TPU v7x, 32 devices: a whole 2x2x4 slice. The times are simulated.
32 devices in a mesh: seq: 4 (over y, core), batch: 8 (over z, x).
Axes of the slice: x: 2, y: 2, z: 4, core: 2. Of those that a mesh axis runs over, the one named last changes fastest.
Arguments:
- inputs: bfloat16 [8, 512, 768], P('batch', 'seq'), may hold values from -6 to 6
- cotangent: bfloat16 [8, 512, 768], P('batch', 'seq'), may hold values from -6 to 6
- weight: bfloat16 [768, 2304], replicated, may hold values from -0.125 to 0.125
Outputs:
- grad_input: bfloat16 [8, 512, 768], P('batch', 'seq')
- grad_weight: float32 [768, 2304], P('seq', 'batch')
All inputs are finite; a program needn't handle non-finite values.
Results may differ from a plain program's by a relative error of at most 0.0026.
Values may be sent and summed in bfloat16 or wider, within the bound.
No kernel may reach another device: no remote copies, remote signals or barrier semaphores. Data moves between devices by JAX's collectives and lax.ppermute only.
A program may use at most 64 MiB of HBM per device.

v0:
```python
import math

import jax
import jax.numpy as jnp
from jax import lax
from jax.sharding import PartitionSpec as P

KW = 3
TAP_SPACING = 64


def extended_2(x, sides, width):
    for axis, dim in sides:
        peers, length = (lax.axis_size(axis), x.shape[dim])
        up = [(i, (i + 1) % peers) for i in range(peers - 1)]
        down = [(j, i) for i, j in up]
        last = lax.slice_in_dim(x, length - width, length, axis=dim)
        first = lax.slice_in_dim(x, 0, width, axis=dim)
        before = lax.ppermute(last, axis, up)
        after = lax.ppermute(first, axis, down)
        x = jnp.concatenate([before, x, after], axis=dim)
    return x


def gelu_factors(values):
    normal_cdf = 0.5 * (1.0 + jax.scipy.special.erf(values / math.sqrt(2.0)))
    density = jnp.exp(-0.5 * values * values) / math.sqrt(2.0 * math.pi)
    return (values * normal_cdf, normal_cdf + values * density)


def body(inputs, cotangent, weight):
    middle_offset = KW // 2
    reach = middle_offset * TAP_SPACING
    length = inputs.shape[1]
    in_width = inputs.shape[2]
    padded_input = extended_2(cotangent, (("seq", 1),), reach)
    extended = padded_input[0]
    values = inputs[0].astype(jnp.float32)
    activation, deriv = gelu_factors(values)
    act = activation.astype(jnp.bfloat16)
    grad_act = jnp.zeros((length, in_width), jnp.float32)
    for tap_index in range(KW):
        window_start = (2 * middle_offset - tap_index) * TAP_SPACING
        window = lax.slice_in_dim(extended, window_start, window_start + length, axis=0)
        grad_act = grad_act + jnp.dot(
            window,
            weight[:, tap_index * in_width : (tap_index + 1) * in_width],
            preferred_element_type=jnp.float32,
        )
    grad_input = (grad_act * deriv).astype(jnp.bfloat16)[None]
    seq_count = lax.axis_size("seq")
    batch_count = lax.axis_size("batch")
    counted = batch_count * inputs.shape[0] * length * seq_count
    factor = 1.0 / math.sqrt(float(counted))
    owned = lax.all_to_all(cotangent, "seq", split_axis=2, concat_axis=1, tiled=True)[0]
    own_rows = owned.shape[1]
    owned_padded = jnp.pad(owned, ((reach, reach), (0, 0)))
    whole_act = lax.all_gather(act[None], "seq", axis=1, tiled=True)[0]
    count = whole_act.shape[0]
    updated = []
    for tap_index in range(KW):
        offset = 0 + (2 * middle_offset - tap_index) * TAP_SPACING
        window = lax.dynamic_slice_in_dim(owned_padded, offset, count, 0)
        updated.append(
            lax.dot_general(
                window, whole_act, (((0,), (0,)), ((), ())), preferred_element_type=jnp.float32
            )
        )
    taps_sum = jnp.stack(updated, axis=0)
    local_rows = jnp.transpose(taps_sum, (1, 0, 2)).reshape(own_rows, KW * in_width) * factor
    grad_weight = lax.psum_scatter(local_rows, "batch", scatter_dimension=1, tiled=True)
    return (grad_input, grad_weight)


def solution(mesh):
    placed = (P("batch", "seq", None), P("batch", "seq", None), P())
    return jax.shard_map(
        body,
        mesh=mesh,
        in_specs=placed,
        out_specs=(P("batch", "seq", None), P("seq", "batch")),
        check_vma=False,
    )
```

profile of v0, /device:TPU:0, one launch (start us, length us, event | category | flops | bytes accessed | tf_op | source)
XLA Modules:
  0.0 108.4 jit_solution(3602889035647854858)
XLA Ops:
  7.2 0.0 copy-start.1
  7.2 1.3 %copy.8 = bf16[1,128,768]{1,0,2:T(2,128)(2,1)S(1)} copy(bf16[1,128,768]{2,1,0:T(8,128)(2,1)} %param.4) | data formatting | bytes 393216 | tf_op args[1]
  8.5 0.5 broadcast.11
  9.0 1.8 %reduce = bf16[768,128]{1,0:T(8,128)(2,1)S(1)} reduce(bf16[768,1,128]{2,1,0:T(2,128)(2,1)S(1)} %bitcast.81, bf16[]{:T(256)} %broadcast.11), dimensions={1}, to_apply=%bitcast.72.reduce_sub_computation | reduce | bytes 393218
  10.8 0.7 reshape.16
  11.5 4.2 %all-to-all-start = ((bf16[4,2,12288]{2,1,0:T(2,128)(2,1)}), bf16[4,2,12288]{2,1,0:T(2,128)(2,1)S(1)}, u32[]{:S(2)}, u32[]{:S(2)}) async-start(bf16[4,2,12288]{2,1,0:T(2,128)(2,1)} %reshape.16), calls=%async_computation | async-start | bytes 393216 | tf_op jit(solution)/shard_map/all_to_all | solution.py:55
  15.8 0.0 reduce-scatter.4.cloned.1.call-start
  15.8 0.0 copy-done.1
  15.8 0.1 fusion.30
  15.9 10.3 %all_gather.3 = bf16[1,512,768]{2,1,0:T(8,128)(2,1)S(1)} all-gather(bf16[1,128,768]{2,1,0:T(8,128)(2,1)S(1)} %fusion.30), channel_id=1, replica_groups=mesh['seq'=4,'batch'=8] {'seq'}, dimensions={1}, use_global_device_ids=true | all-gather | bytes 983040 | tf_op jit(solution)/shard_map/all_gather | solution.py:58
  26.2 0.0 all-to-all-done
  26.2 0.2 reshape.17
  26.4 0.2 copy.9
  26.6 0.4 convolution_bitcast_fusion.1
  27.0 0.4 convolution_bitcast_fusion.2
  27.4 0.3 convolution_bitcast_fusion
  27.7 0.1 fusion
  27.8 1.9 %copy.13 = f32[192,3,768]{0,2,1:T(8,128)} copy(f32[192,3,768]{2,0,1:T(8,128)S(1)} %fusion) | data formatting | bytes 3538944
  29.8 0.0 copy-start
  29.8 0.0 reduce-scatter.4.cloned.1.call-update
  29.8 0.9 copy-done
  30.7 2.3 %collective-permute-start.1 = (bf16[1,64,768]{2,1,0:T(8,128)(2,1)S(1)}, bf16[1,64,768]{2,1,0:T(8,128)(2,1)S(1)}, u32[]{:S(2)}, u32[]{:S(2)}) collective-permute-start(bf16[1,64,768]{2,1,0:T(8,128)(2,1)S(1)} %get-tuple-element.3), channel_id=1, source_target_pairs={{0,8},{8,16},{16,24},{1,9},{9,17},{17,25},{2,10},{10,18},{18,26},{... | collective-permute-start | bytes 294920 | tf_op jit(solution)/shard_map/ppermute | solution.py:19
  33.0 1.3 %collective-permute-start = (bf16[1,64,768]{2,1,0:T(8,128)(2,1)S(1)}, bf16[1,64,768]{2,1,0:T(8,128)(2,1)S(1)}, u32[]{:S(2)}, u32[]{:S(2)}) collective-permute-start(bf16[1,64,768]{2,1,0:T(8,128)(2,1)S(1)} %get-tuple-element.2), channel_id=1, source_target_pairs={{8,0},{16,8},{24,16},{9,1},{17,9},{25,17},{10,2},{18,10},{26,18},{... | collective-permute-start | bytes 294920 | tf_op jit(solution)/shard_map/ppermute | solution.py:20
  34.3 1.6 %fusion.5 = f32[128,768]{1,0:T(8,128)S(1)} fusion(bf16[768,2304]{1,0:T(8,128)(2,1)} %param.5, bf16[1,128,768]{2,1,0:T(8,128)(2,1)S(1)} %copy-done), kind=kOutput, calls=%fused_computation.10 | convolution fusion | flops 150994944 | bytes 1769472 | tf_op jit(solution)/shard_map/dot_general | solution.py:45
  35.9 0.0 collective-permute-done.1
  35.9 1.6 %fusion.3 = f32[128,768]{1,0:T(8,128)S(1)} fusion(bf16[768,2304]{1,0:T(8,128)(2,1)} %param.5, bf16[1,128,768]{2,1,0:T(8,128)(2,1)S(1)} %copy-done, bf16[1,64,768]{2,1,0:T(8,128)(2,1)S(1)} %collective-permute-done.1), kind=kOutput, calls=%fused_computation.8 | convolution fusion | flops 151388160 | bytes 1867776 | tf_op jit(solution)/shard_map/dot_general | solution.py:45
  37.5 0.0 collective-permute-done
  37.5 2.4 %fusion.11 = bf16[1,128,768]{2,1,0:T(8,128)(2,1)} fusion(f32[128,768]{1,0:T(8,128)S(1)} %fusion.3, f32[128,768]{1,0:T(8,128)S(1)} %fusion.5, bf16[768,2304]{1,0:T(8,128)(2,1)} %param.5, bf16[1,128,768]{2,1,0:T(8,128)(2,1)S(1)} %copy-done.1, bf16[1,64,768]{2,1,0:T(8,128)(2,1)S(1)} %collective-permute-done, bf16[1,128,768]{2,1,0:T(8,128)(2,1)S(1)} %copy-done), kind=kOutput, calls=%fused_computation.14 | convolution fusion | flops 152666112 | bytes 2654208 | tf_op jit(solution)/shard_map/dot_general | solution.py:45
  39.9 59.8 %reduce-scatter.4.cloned.1.call-done = f32[288,192]{1,0:T(8,128)} async-done(((f32[2304,192]{1,0:T(8,128)}), f32[288,192]{1,0:T(8,128)}) %reduce-scatter.4.cloned.1.call-update) | async-done | bytes 221200
  99.8 1.8 %copy.12 = f32[192,288]{1,0:T(8,128)} copy(f32[192,288]{0,1:T(8,128)} %bitcast.83) | data formatting | bytes 442368
  (3 shorter events, 0.1 us)
Async XLA Ops:
  7.2 8.6 %copy-start.1 = (bf16[1,128,768]{2,1,0:T(8,128)(2,1)S(1)}, bf16[1,128,768]{2,1,0:T(8,128)(2,1)}, u32[]{:S(2)}) copy-start(bf16[1,128,768]{2,1,0:T(8,128)(2,1)} %param.3) | copy-start | bytes 589828
  11.5 14.7 %all-to-all-start = ((bf16[4,2,12288]{2,1,0:T(2,128)(2,1)}), bf16[4,2,12288]{2,1,0:T(2,128)(2,1)S(1)}, u32[]{:S(2)}, u32[]{:S(2)}) async-start(bf16[4,2,12288]{2,1,0:T(2,128)(2,1)} %reshape.16), calls=%async_computation | async-start | bytes 393216 | tf_op jit(solution)/shard_map/all_to_all | solution.py:55
  15.8 84.0 %reduce-scatter.4.cloned.1.call-start = ((), (), s32[]{:S(2)}) async-start(), calls=%async_computation.2 | async-start | bytes 2654208
  29.8 0.9 copy-start
  30.7 5.2 %collective-permute-start.1 = (bf16[1,64,768]{2,1,0:T(8,128)(2,1)S(1)}, bf16[1,64,768]{2,1,0:T(8,128)(2,1)S(1)}, u32[]{:S(2)}, u32[]{:S(2)}) collective-permute-start(bf16[1,64,768]{2,1,0:T(8,128)(2,1)S(1)} %get-tuple-element.3), channel_id=1, source_target_pairs={{0,8},{8,16},{16,24},{1,9},{9,17},{17,25},{2,10},{10,18},{18,26},{... | collective-permute-start | bytes 294920 | tf_op jit(solution)/shard_map/ppermute | solution.py:19
  33.0 4.5 %collective-permute-start = (bf16[1,64,768]{2,1,0:T(8,128)(2,1)S(1)}, bf16[1,64,768]{2,1,0:T(8,128)(2,1)S(1)}, u32[]{:S(2)}, u32[]{:S(2)}) collective-permute-start(bf16[1,64,768]{2,1,0:T(8,128)(2,1)S(1)} %get-tuple-element.2), channel_id=1, source_target_pairs={{8,0},{16,8},{24,16},{9,1},{17,9},{25,17},{10,2},{18,10},{26,18},{... | collective-permute-start | bytes 294920 | tf_op jit(solution)/shard_map/ppermute | solution.py:20
Sparse Core Ops, SparseCore 0:
  29.9 69.7 reduce-scatter.3
where the time goes:
time: 109 us; the launch traced here: 108 us
  waiting for transfers between devices  59.9 us (55%)
  between operations  14.1 us (13%)
  blocking collectives  10.3 us (9%)
  starting transfers between devices  7.79 us (7%)
  local copies, waits for them, and re-layouts  7.63 us (7%)
  matrix products  6.66 us (6%)
  other arithmetic  2.01 us (2%)
    unnamed x2, waiting for transfers between devices  59.9 us
    all_gather x1, blocking collectives, body(): whole_act = lax.all_gather(act[None], 'seq', axis=1, tiled=True)[0]  10.3 us
    unnamed x12, local copies, waits for them, and re-layouts  7.46 us
    dot_general x3, matrix products, body(): jnp.dot(window, weight[:, tap_index * in_width:(tap_index + 1) * in_width...  5.58 us
    all_to_all x1, starting transfers between devices, body(): lax.all_to_all(cotangent, 'seq', split_axis=2, concat_axis=1, tiled=True)[0]  4.24 us
    ppermute x1, starting transfers between devices, extended_2(): before = lax.ppermute(last, axis, up)  2.26 us
  transfers between devices with their start and end apart: 4, of which 1 were waited for; matrix products, arithmetic and copies ran while one was open for 5% of the time, Pallas kernels for 0%

commit v1 on v0

--- a/solution.py
+++ b/solution.py
@@ -68,7 +68,9 @@
         )
     taps_sum = jnp.stack(updated, axis=0)
     local_rows = jnp.transpose(taps_sum, (1, 0, 2)).reshape(own_rows, KW * in_width) * factor
-    grad_weight = lax.psum_scatter(local_rows, "batch", scatter_dimension=1, tiled=True)
+    pieces = local_rows.reshape(own_rows, batch_count, -1)
+    swapped = lax.all_to_all(pieces, "batch", split_axis=1, concat_axis=1, tiled=True)
+    grad_weight = jnp.sum(swapped, axis=1)
     return (grad_input, grad_weight)
 
 

time: 109 us -> 85.6 us (0.79)
  waiting for transfers between devices: 59.9 us -> 45.5 us
  between operations: 14.1 us -> 0.77 us
  starting transfers between devices: 7.79 us -> 14 us
  local copies, waits for them, and re-layouts: 7.63 us -> 5.77 us
    unnamed x2 -> x0, waiting for transfers between devices: 59.9 us -> none
    all_to_all x0 -> x1, waiting for transfers between devices: none -> 45.5 us  [body(): lax.all_to_all(pieces, 'batch', split_axis=1, concat_axis=1, tiled=True)]
    all_to_all x0 -> x1, starting transfers between devices: none -> 6.48 us  [body(): lax.all_to_all(pieces, 'batch', split_axis=1, concat_axis=1, tiled=True)]
    unnamed x12 -> x11, local copies, waits for them, and re-layouts: 7.46 us -> 3.66 us
    mul x0 -> x1, local copies, waits for them, and re-layouts: none -> 1.95 us  [body(): jnp.transpose(taps_sum, (1, 0, 2)).reshape(own_rows, KW * in_width) * factor]
  transfers between devices with their start and end apart: 4 -> 4, of which waited for: 1 -> 1; matrix products, arithmetic and copies ran while one was open for 5% -> 7% of each run, Pallas kernels for 0% -> 0%
where the time goes in v1:
time: 85.6 us; the launch traced here: 85.2 us
  waiting for transfers between devices  45.5 us (53%)
  starting transfers between devices  14 us (16%)
  blocking collectives  10.3 us (12%)
  matrix products  6.62 us (8%)
  local copies, waits for them, and re-layouts  5.77 us (7%)
  other arithmetic  2.18 us (3%)
    all_to_all x1, waiting for transfers between devices, body(): lax.all_to_all(pieces, 'batch', split_axis=1, concat_axis=1, tiled=True)  45.5 us
    all_gather x1, blocking collectives, body(): whole_act = lax.all_gather(act[None], 'seq', axis=1, tiled=True)[0]  10.3 us
    all_to_all x1, starting transfers between devices, body(): lax.all_to_all(pieces, 'batch', split_axis=1, concat_axis=1, tiled=True)  6.48 us
    dot_general x3, matrix products, body(): jnp.dot(window, weight[:, tap_index * in_width:(tap_index + 1) * in_width...  5.54 us
    all_to_all x1, starting transfers between devices, body(): lax.all_to_all(cotangent, 'seq', split_axis=2, concat_axis=1, tiled=True)[0]  4.24 us
    unnamed x11, local copies, waits for them, and re-layouts  3.66 us
    ppermute x1, starting transfers between devices, extended_2(): before = lax.ppermute(last, axis, up)  1.98 us
    mul x1, local copies, waits for them, and re-layouts, body(): jnp.transpose(taps_sum, (1, 0, 2)).reshape(own_rows, KW * in_width) * factor  1.95 us
  transfers between devices with their start and end apart: 4, of which 1 were waited for; matrix products, arithmetic and copies ran while one was open for 7% of the time, Pallas kernels for 0%

profile of v1, /device:TPU:0, one launch (start us, length us, event | category | flops | bytes accessed | tf_op | source)
XLA Modules:
  0.0 85.2 jit_solution(1251447381360411007)
XLA Ops:
  0.6 0.0 copy-start.1
  0.6 1.3 %copy.8 = bf16[1,128,768]{1,0,2:T(2,128)(2,1)S(1)} copy(bf16[1,128,768]{2,1,0:T(8,128)(2,1)} %param.4) | data formatting | bytes 393216 | tf_op args[1]
  2.0 0.5 broadcast.12
  2.5 1.8 %reduce = bf16[768,128]{1,0:T(8,128)(2,1)S(1)} reduce(bf16[768,1,128]{2,1,0:T(2,128)(2,1)S(1)} %bitcast.78, bf16[]{:T(256)} %broadcast.12), dimensions={1}, to_apply=%bitcast.69.reduce_sub_computation | reduce | bytes 393218
  4.3 0.7 reshape.16
  5.0 4.2 %all-to-all-start = ((bf16[4,2,12288]{2,1,0:T(2,128)(2,1)}), bf16[4,2,12288]{2,1,0:T(2,128)(2,1)S(1)}, u32[]{:S(2)}, u32[]{:S(2)}) async-start(bf16[4,2,12288]{2,1,0:T(2,128)(2,1)} %reshape.16), calls=%async_computation | async-start | bytes 393216 | tf_op jit(solution)/shard_map/all_to_all | solution.py:55
  9.2 0.0 copy-done.1
  9.2 0.1 fusion.30
  9.3 10.3 %all_gather.3 = bf16[1,512,768]{2,1,0:T(8,128)(2,1)S(1)} all-gather(bf16[1,128,768]{2,1,0:T(8,128)(2,1)S(1)} %fusion.30), channel_id=1, replica_groups=mesh['seq'=4,'batch'=8] {'seq'}, dimensions={1}, use_global_device_ids=true | all-gather | bytes 983040 | tf_op jit(solution)/shard_map/all_gather | solution.py:58
  19.7 0.0 all-to-all-done
  19.7 0.2 reshape.17
  19.9 0.2 copy.9
  20.1 0.4 convolution_bitcast_fusion.1
  20.5 0.4 convolution_bitcast_fusion.2
  20.8 0.3 convolution_bitcast_fusion
  21.2 0.1 fusion
  21.3 1.9 %copy.10 = f32[192,3,768]{0,2,1:T(8,128)} copy(f32[192,3,768]{2,0,1:T(8,128)S(1)} %fusion) | data formatting | bytes 3538944 | tf_op jit(solution)/shard_map/mul | solution.py:70
  23.3 0.0 copy-start
  23.3 6.5 %all-to-all-start.1 = ((f32[192,8,288]{0,2,1:T(8,128)}), f32[192,8,288]{0,2,1:T(8,128)S(1)}, u32[]{:S(2)}, u32[]{:S(2)}) async-start(f32[192,8,288]{0,2,1:T(8,128)} %bitcast.72), calls=%async_computation.1 | async-start | bytes 4718592 | tf_op jit(solution)/shard_map/all_to_all | solution.py:72
  29.7 0.0 copy-done
  29.8 2.0 %collective-permute-start.1 = (bf16[1,64,768]{2,1,0:T(8,128)(2,1)S(1)}, bf16[1,64,768]{2,1,0:T(8,128)(2,1)S(1)}, u32[]{:S(2)}, u32[]{:S(2)}) collective-permute-start(bf16[1,64,768]{2,1,0:T(8,128)(2,1)S(1)} %get-tuple-element.5), channel_id=1, source_target_pairs={{0,8},{8,16},{16,24},{1,9},{9,17},{17,25},{2,10},{10,18},{18,26},{... | collective-permute-start | bytes 294920 | tf_op jit(solution)/shard_map/ppermute | solution.py:19
  31.8 1.3 %collective-permute-start = (bf16[1,64,768]{2,1,0:T(8,128)(2,1)S(1)}, bf16[1,64,768]{2,1,0:T(8,128)(2,1)S(1)}, u32[]{:S(2)}, u32[]{:S(2)}) collective-permute-start(bf16[1,64,768]{2,1,0:T(8,128)(2,1)S(1)} %get-tuple-element.4), channel_id=1, source_target_pairs={{8,0},{16,8},{24,16},{9,1},{17,9},{25,17},{10,2},{18,10},{26,18},{... | collective-permute-start | bytes 294920 | tf_op jit(solution)/shard_map/ppermute | solution.py:20
  33.1 1.6 %fusion.5 = f32[128,768]{1,0:T(8,128)S(1)} fusion(bf16[768,2304]{1,0:T(8,128)(2,1)} %param.5, bf16[1,128,768]{2,1,0:T(8,128)(2,1)S(1)} %copy-done), kind=kOutput, calls=%fused_computation.10 | convolution fusion | flops 150994944 | bytes 1769472 | tf_op jit(solution)/shard_map/dot_general | solution.py:45
  34.7 0.0 collective-permute-done.1
  34.7 1.6 %fusion.3 = f32[128,768]{1,0:T(8,128)S(1)} fusion(bf16[768,2304]{1,0:T(8,128)(2,1)} %param.5, bf16[1,128,768]{2,1,0:T(8,128)(2,1)S(1)} %copy-done, bf16[1,64,768]{2,1,0:T(8,128)(2,1)S(1)} %collective-permute-done.1), kind=kOutput, calls=%fused_computation.8 | convolution fusion | flops 151388160 | bytes 1867776 | tf_op jit(solution)/shard_map/dot_general | solution.py:45
  36.3 0.0 collective-permute-done
  36.3 2.4 %fusion.11 = bf16[1,128,768]{2,1,0:T(8,128)(2,1)} fusion(f32[128,768]{1,0:T(8,128)S(1)} %fusion.3, f32[128,768]{1,0:T(8,128)S(1)} %fusion.5, bf16[768,2304]{1,0:T(8,128)(2,1)} %param.5, bf16[1,128,768]{2,1,0:T(8,128)(2,1)S(1)} %copy-done.1, bf16[1,64,768]{2,1,0:T(8,128)(2,1)S(1)} %collective-permute-done, bf16[1,128,768]{2,1,0:T(8,128)(2,1)S(1)} %copy-done), kind=kOutput, calls=%fused_computation.14 | convolution fusion | flops 152666112 | bytes 2654208 | tf_op jit(solution)/shard_map/dot_general | solution.py:45
  38.6 45.5 %all-to-all-done.1 = f32[192,8,288]{0,2,1:T(8,128)S(1)} async-done(((f32[192,8,288]{0,2,1:T(8,128)}), f32[192,8,288]{0,2,1:T(8,128)S(1)}, u32[]{:S(2)}, u32[]{:S(2)}) %all-to-all-start.1) | async-done | bytes 1769504 | tf_op jit(solution)/shard_map/all_to_all | solution.py:72
  84.1 0.2 reduce_sum.9
  84.3 0.9 %copy.11 = f32[192,288]{1,0:T(8,128)} copy(f32[192,288]{0,1:T(8,128)S(1)} %reduce_sum.9) | data formatting | bytes 442368
  (3 shorter events, 0.1 us)
Async XLA Ops:
  0.6 8.6 %copy-start.1 = (bf16[1,128,768]{2,1,0:T(8,128)(2,1)S(1)}, bf16[1,128,768]{2,1,0:T(8,128)(2,1)}, u32[]{:S(2)}) copy-start(bf16[1,128,768]{2,1,0:T(8,128)(2,1)} %param.3) | copy-start | bytes 589828
  5.0 14.7 %all-to-all-start = ((bf16[4,2,12288]{2,1,0:T(2,128)(2,1)}), bf16[4,2,12288]{2,1,0:T(2,128)(2,1)S(1)}, u32[]{:S(2)}, u32[]{:S(2)}) async-start(bf16[4,2,12288]{2,1,0:T(2,128)(2,1)} %reshape.16), calls=%async_computation | async-start | bytes 393216 | tf_op jit(solution)/shard_map/all_to_all | solution.py:55
  23.3 6.5 %copy-start = (bf16[1,128,768]{2,1,0:T(8,128)(2,1)S(1)}, bf16[1,128,768]{2,1,0:T(8,128)(2,1)}, u32[]{:S(2)}) copy-start(bf16[1,128,768]{2,1,0:T(8,128)(2,1)} %param.4) | copy-start | bytes 589828
  23.3 60.9 %all-to-all-start.1 = ((f32[192,8,288]{0,2,1:T(8,128)}), f32[192,8,288]{0,2,1:T(8,128)S(1)}, u32[]{:S(2)}, u32[]{:S(2)}) async-start(f32[192,8,288]{0,2,1:T(8,128)} %bitcast.72), calls=%async_computation.1 | async-start | bytes 4718592 | tf_op jit(solution)/shard_map/all_to_all | solution.py:72
  29.8 4.9 %collective-permute-start.1 = (bf16[1,64,768]{2,1,0:T(8,128)(2,1)S(1)}, bf16[1,64,768]{2,1,0:T(8,128)(2,1)S(1)}, u32[]{:S(2)}, u32[]{:S(2)}) collective-permute-start(bf16[1,64,768]{2,1,0:T(8,128)(2,1)S(1)} %get-tuple-element.5), channel_id=1, source_target_pairs={{0,8},{8,16},{16,24},{1,9},{9,17},{17,25},{2,10},{10,18},{18,26},{... | collective-permute-start | bytes 294920 | tf_op jit(solution)/shard_map/ppermute | solution.py:19
  31.8 4.5 %collective-permute-start = (bf16[1,64,768]{2,1,0:T(8,128)(2,1)S(1)}, bf16[1,64,768]{2,1,0:T(8,128)(2,1)S(1)}, u32[]{:S(2)}, u32[]{:S(2)}) collective-permute-start(bf16[1,64,768]{2,1,0:T(8,128)(2,1)S(1)} %get-tuple-element.4), channel_id=1, source_target_pairs={{8,0},{16,8},{24,16},{9,1},{17,9},{25,17},{10,2},{18,10},{26,18},{... | collective-permute-start | bytes 294920 | tf_op jit(solution)/shard_map/ppermute | solution.py:20

commit v2 on v0

--- a/solution.py
+++ b/solution.py
@@ -26,6 +26,25 @@
     normal_cdf = 0.5 * (1.0 + jax.scipy.special.erf(values / math.sqrt(2.0)))
     density = jnp.exp(-0.5 * values * values) / math.sqrt(2.0 * math.pi)
     return (values * normal_cdf, normal_cdf + values * density)
+
+
+def reduce_over_batch(rows):
+    count = lax.axis_size("batch")
+    outer = count // 2
+    me = lax.axis_index("batch")
+    x = me % 2
+    z = me // 2
+    blocks = rows.reshape(rows.shape[0], outer, 2, -1)
+    mine = lax.dynamic_index_in_dim(blocks, x, axis=2, keepdims=False)
+    theirs = lax.dynamic_index_in_dim(blocks, 1 - x, axis=2, keepdims=False)
+    pairs = [(i, i ^ 1) for i in range(count)]
+    summed = mine + lax.ppermute(theirs, "batch", pairs)
+    total = lax.dynamic_index_in_dim(summed, z, axis=1, keepdims=False)
+    for shift in range(1, outer):
+        target = lax.dynamic_index_in_dim(summed, (z + shift) % outer, axis=1, keepdims=False)
+        perm = [(2 * q + p, 2 * ((q + shift) % outer) + p) for q in range(outer) for p in range(2)]
+        total = total + lax.ppermute(target, "batch", perm)
+    return total
 
 
 def body(inputs, cotangent, weight):
@@ -68,7 +87,12 @@
         )
     taps_sum = jnp.stack(updated, axis=0)
     local_rows = jnp.transpose(taps_sum, (1, 0, 2)).reshape(own_rows, KW * in_width) * factor
-    grad_weight = lax.psum_scatter(local_rows, "batch", scatter_dimension=1, tiled=True)
+    if batch_count == 8:
+        grad_weight = reduce_over_batch(local_rows)
+    else:
+        pieces = local_rows.reshape(own_rows, batch_count, -1)
+        swapped = lax.all_to_all(pieces, "batch", split_axis=1, concat_axis=1, tiled=True)
+        grad_weight = jnp.sum(swapped, axis=1)
     return (grad_input, grad_weight)
 
 

time: 109 us -> 84.7 us (0.78)
  the two profiles are of different devices: /device:TPU:0 before, /device:TPU:11 now
where the time goes in v2:
time: 84.7 us; the launch traced here: 84.2 us
  waiting for transfers between devices  41.1 us (49%)
  starting transfers between devices  12.6 us (15%)
  blocking collectives  10.2 us (12%)
  matrix products  7.36 us (9%)
  local copies, waits for them, and re-layouts  6.67 us (8%)
  other arithmetic  5.45 us (6%)
  between operations  0.89 us (1%)
    ppermute x3, waiting for transfers between devices, reduce_over_batch(): total = total + lax.ppermute(target, 'batch', perm)  22.1 us
    ppermute x1, waiting for transfers between devices, reduce_over_batch(): summed = mine + lax.ppermute(theirs, 'batch', pairs)  19.1 us
    all_gather x1, blocking collectives, body(): whole_act = lax.all_gather(act[None], 'seq', axis=1, tiled=True)[0]  10.2 us
    dot_general x3, matrix products, body(): jnp.dot(window, weight[:, tap_index * in_width:(tap_index + 1) * in_width...  6.29 us
    all_to_all x1, starting transfers between devices, body(): lax.all_to_all(cotangent, 'seq', split_axis=2, concat_axis=1, tiled=True)[0]  4.01 us
    ppermute x3, starting transfers between devices, reduce_over_batch(): total = total + lax.ppermute(target, 'batch', perm)  3.95 us
    unnamed x12, local copies, waits for them, and re-layouts  2.8 us
    ppermute x1, starting transfers between devices, extended_2(): before = lax.ppermute(last, axis, up)  2.3 us
  transfers between devices with their start and end apart: 7, of which 4 were waited for; matrix products, arithmetic and copies ran while one was open for 10% of the time, Pallas kernels for 0%

profile of v2, /device:TPU:11, one launch (start us, length us, event | category | flops | bytes accessed | tf_op | source)
XLA Modules:
  0.0 84.2 jit_solution(3743374876291688411)
XLA Ops:
  0.6 1.3 %copy.12 = bf16[1,128,768]{1,0,2:T(2,128)(2,1)S(1)} copy(bf16[1,128,768]{2,1,0:T(8,128)(2,1)} %param.4) | data formatting | bytes 393216 | tf_op args[1]
  2.0 0.5 broadcast.17
  2.5 1.8 %reduce = bf16[768,128]{1,0:T(8,128)(2,1)S(1)} reduce(bf16[768,1,128]{2,1,0:T(2,128)(2,1)S(1)} %bitcast.92, bf16[]{:T(256)} %broadcast.17), dimensions={1}, to_apply=%bitcast.82.reduce_sub_computation | reduce | bytes 393218
  4.3 0.7 reshape.16
  5.0 4.0 %all-to-all-start = ((bf16[4,2,12288]{2,1,0:T(2,128)(2,1)}), bf16[4,2,12288]{2,1,0:T(2,128)(2,1)S(1)}, u32[]{:S(2)}, u32[]{:S(2)}) async-start(bf16[4,2,12288]{2,1,0:T(2,128)(2,1)} %reshape.16), calls=%async_computation | async-start | bytes 393216 | tf_op jit(solution)/shard_map/all_to_all | solution.py:74
  9.1 10.2 %all_gather.3 = bf16[1,512,768]{2,1,0:T(8,128)(2,1)S(1)} all-gather(bf16[1,128,768]{2,1,0:T(8,128)(2,1)S(1)} %fusion.30), channel_id=1, replica_groups=mesh['seq'=4,'batch'=8] {'seq'}, dimensions={1}, use_global_device_ids=true | all-gather | bytes 983040 | tf_op jit(solution)/shard_map/all_gather | solution.py:77
  19.3 0.2 reshape.17
  19.5 0.2 copy.13
  19.7 0.4 convolution_bitcast_fusion.1
  20.1 0.4 convolution_bitcast_fusion.2
  20.5 0.3 convolution_bitcast_fusion
  20.8 1.4 %fusion = f32[192,3,768]{2,0,1:T(8,128)} fusion(f32[1,192,768]{2,1,0:T(8,128)S(1)} %convolution_bitcast_fusion.1, f32[1,192,768]{2,1,0:T(8,128)S(1)} %convolution_bitcast_fusion, f32[1,192,768]{2,1,0:T(8,128)S(1)} %convolution_bitcast_fusion.2), kind=kLoop, calls=%fused_computation.1 | loop fusion | flops 1327104 | bytes 3538944 | tf_op jit(solution)/shard_map/mul | solution.py:89
  22.2 1.9 %copy.14 = f32[192,3,768]{0,2,1:T(8,128)S(1)} copy(f32[192,3,768]{2,0,1:T(8,128)} %fusion) | data formatting | bytes 3538944 | tf_op jit(solution)/shard_map/mul | solution.py:89
  24.1 1.1 %dynamic-slice_bitcast_fusion = f32[192,4,288]{0,2,1:T(8,128)} fusion(f32[192,4,2,288]{0,3,2,1:T(8,128)S(1)} %bitcast.85, s32[]{:T(128)S(6)} %select_n.45), kind=kLoop, calls=%fused_computation.9 | loop fusion | bytes 1769476 | tf_op jit(solution)/shard_map/jit(dynamic_index_in_dim)/squeeze | solution.py:39
  25.2 0.3 collective-permute-start.2
  25.5 2.3 %collective-permute-start.1 = (bf16[1,64,768]{2,1,0:T(8,128)(2,1)S(1)}, bf16[1,64,768]{2,1,0:T(8,128)(2,1)S(1)}, u32[]{:S(2)}, u32[]{:S(2)}) collective-permute-start(bf16[1,64,768]{2,1,0:T(8,128)(2,1)S(1)} %get-tuple-element.7), channel_id=1, source_target_pairs={{0,8},{8,16},{16,24},{1,9},{9,17},{17,25},{2,10},{10,18},{18,26},{... | collective-permute-start | bytes 294920 | tf_op jit(solution)/shard_map/ppermute | solution.py:19
  27.8 2.0 %collective-permute-start = (bf16[1,64,768]{2,1,0:T(8,128)(2,1)S(1)}, bf16[1,64,768]{2,1,0:T(8,128)(2,1)S(1)}, u32[]{:S(2)}, u32[]{:S(2)}) collective-permute-start(bf16[1,64,768]{2,1,0:T(8,128)(2,1)S(1)} %get-tuple-element.6), channel_id=1, source_target_pairs={{8,0},{16,8},{24,16},{9,1},{17,9},{25,17},{10,2},{18,10},{26,18},{... | collective-permute-start | bytes 294920 | tf_op jit(solution)/shard_map/ppermute | solution.py:20
  29.8 1.6 %fusion.5 = f32[128,768]{1,0:T(8,128)S(1)} fusion(bf16[768,2304]{1,0:T(8,128)(2,1)} %param.5, bf16[1,128,768]{2,1,0:T(8,128)(2,1)S(1)} %copy-done), kind=kOutput, calls=%fused_computation.12 | convolution fusion | flops 150994944 | bytes 1769472 | tf_op jit(solution)/shard_map/dot_general | solution.py:64
  31.5 2.3 %fusion.3 = f32[128,768]{1,0:T(8,128)} fusion(bf16[768,2304]{1,0:T(8,128)(2,1)} %param.5, bf16[1,128,768]{2,1,0:T(8,128)(2,1)S(1)} %copy-done, bf16[1,64,768]{2,1,0:T(8,128)(2,1)S(1)} %collective-permute-done.1), kind=kOutput, calls=%fused_computation.10 | convolution fusion | flops 151388160 | bytes 1867776 | tf_op jit(solution)/shard_map/dot_general | solution.py:64
  33.9 19.1 %collective-permute-done.2 = f32[192,4,288]{0,2,1:T(8,128)} collective-permute-done((f32[192,4,288]{0,2,1:T(8,128)}, f32[192,4,288]{0,2,1:T(8,128)}, u32[]{:S(2)}, u32[]{:S(2)}) %collective-permute-start.2) | collective-permute-done | bytes 884768 | tf_op jit(solution)/shard_map/ppermute | solution.py:41
  52.9 1.4 %bitcast_add_fusion = f32[192,4,288]{0,2,1:T(8,128)S(1)} fusion(f32[192,4,288]{0,2,1:T(8,128)} %collective-permute-done.2, f32[192,4,2,288]{0,3,2,1:T(8,128)S(1)} %bitcast.86, s32[]{:T(128)S(6)} %select_n.44), kind=kLoop, calls=%fused_computation.8 | loop fusion | flops 221184 | bytes 2654212 | tf_op jit(solution)/shard_map/add | solution.py:41
  54.5 0.1 copy.16
  54.6 1.3 %collective-permute-start.3 = (f32[192,288]{1,0:T(8,128)S(1)}, f32[192,288]{1,0:T(8,128)S(1)}, u32[]{:S(2)}, u32[]{:S(2)}) collective-permute-start(f32[192,288]{1,0:T(8,128)S(1)} %bitcast.94), channel_id=1, source_target_pairs={{0,2},{1,3},{2,4},{3,5},{4,6},{5,7},{6,0},{7,1},{8,10},{9,11},{10,... | collective-permute-start | bytes 663560 | tf_op jit(solution)/shard_map/ppermute | solution.py:46
  56.0 0.1 copy.17
  56.1 1.1 %collective-permute-start.4 = (f32[192,288]{1,0:T(8,128)S(1)}, f32[192,288]{1,0:T(8,128)S(1)}, u32[]{:S(2)}, u32[]{:S(2)}) collective-permute-start(f32[192,288]{1,0:T(8,128)S(1)} %bitcast.95), channel_id=1, source_target_pairs={{0,4},{1,5},{2,6},{3,7},{4,0},{5,1},{6,2},{7,3},{8,12},{9,13},{10,... | collective-permute-start | bytes 663560 | tf_op jit(solution)/shard_map/ppermute | solution.py:46
  57.2 0.1 copy.18
  57.4 1.5 %collective-permute-start.5 = (f32[192,288]{1,0:T(8,128)S(1)}, f32[192,288]{1,0:T(8,128)S(1)}, u32[]{:S(2)}, u32[]{:S(2)}) collective-permute-start(f32[192,288]{1,0:T(8,128)S(1)} %bitcast.96), channel_id=1, source_target_pairs={{0,6},{1,7},{2,0},{3,1},{4,2},{5,3},{6,4},{7,5},{8,14},{9,15},{10,... | collective-permute-start | bytes 663560 | tf_op jit(solution)/shard_map/ppermute | solution.py:46
  58.9 2.3 %fusion.11 = bf16[1,128,768]{2,1,0:T(8,128)(2,1)} fusion(f32[128,768]{1,0:T(8,128)S(1)} %copy-done.2, f32[128,768]{1,0:T(8,128)S(1)} %fusion.5, bf16[768,2304]{1,0:T(8,128)(2,1)} %param.5, bf16[1,128,768]{2,1,0:T(8,128)(2,1)S(1)} %copy-done.1, bf16[1,64,768]{2,1,0:T(8,128)(2,1)S(1)} %collective-permute-done, bf16[1,128,768]{2,1,0:T(8,128)(2,1)S(1)} %copy-done), kind=kOutput, calls=%fused_computation.16 | convolution fusion | flops 152666112 | bytes 2654208 | tf_op jit(solution)/shard_map/dot_general | solution.py:64
  61.4 0.8 collective-permute-done.3
  62.2 18.0 %collective-permute-done.4 = f32[192,288]{1,0:T(8,128)S(1)} collective-permute-done((f32[192,288]{1,0:T(8,128)S(1)}, f32[192,288]{1,0:T(8,128)S(1)}, u32[]{:S(2)}, u32[]{:S(2)}) %collective-permute-start.4) | collective-permute-done | bytes 221216 | tf_op jit(solution)/shard_map/ppermute | solution.py:46
  80.3 3.2 %collective-permute-done.5 = f32[192,288]{1,0:T(8,128)S(1)} collective-permute-done((f32[192,288]{1,0:T(8,128)S(1)}, f32[192,288]{1,0:T(8,128)S(1)}, u32[]{:S(2)}, u32[]{:S(2)}) %collective-permute-start.5) | collective-permute-done | bytes 221216 | tf_op jit(solution)/shard_map/ppermute | solution.py:46
  83.5 0.8 fusion.32
  (15 shorter events, 0.4 us)
Async XLA Ops:
  0.6 8.4 %copy-start.1 = (bf16[1,128,768]{2,1,0:T(8,128)(2,1)S(1)}, bf16[1,128,768]{2,1,0:T(8,128)(2,1)}, u32[]{:S(2)}) copy-start(bf16[1,128,768]{2,1,0:T(8,128)(2,1)} %param.3) | copy-start | bytes 589828
  5.0 14.3 %all-to-all-start = ((bf16[4,2,12288]{2,1,0:T(2,128)(2,1)}), bf16[4,2,12288]{2,1,0:T(2,128)(2,1)S(1)}, u32[]{:S(2)}, u32[]{:S(2)}) async-start(bf16[4,2,12288]{2,1,0:T(2,128)(2,1)} %reshape.16), calls=%async_computation | async-start | bytes 393216 | tf_op jit(solution)/shard_map/all_to_all | solution.py:74
  24.1 1.4 %copy-start = (bf16[1,128,768]{2,1,0:T(8,128)(2,1)S(1)}, bf16[1,128,768]{2,1,0:T(8,128)(2,1)}, u32[]{:S(2)}) copy-start(bf16[1,128,768]{2,1,0:T(8,128)(2,1)} %param.4) | copy-start | bytes 589828
  25.2 27.7 %collective-permute-start.2 = (f32[192,4,288]{0,2,1:T(8,128)}, f32[192,4,288]{0,2,1:T(8,128)}, u32[]{:S(2)}, u32[]{:S(2)}) collective-permute-start(f32[192,4,288]{0,2,1:T(8,128)} %dynamic-slice_bitcast_fusion), channel_id=1, source_target_pairs={{0,1},{1,0},{2,3},{3,2},{4,5},{5,4},{6,7},{7,6},{8,9},{9,8},{10,11... | collective-permute-start | bytes 2654216 | tf_op jit(solution)/shard_map/ppermute | solution.py:41
  25.5 6.0 %collective-permute-start.1 = (bf16[1,64,768]{2,1,0:T(8,128)(2,1)S(1)}, bf16[1,64,768]{2,1,0:T(8,128)(2,1)S(1)}, u32[]{:S(2)}, u32[]{:S(2)}) collective-permute-start(bf16[1,64,768]{2,1,0:T(8,128)(2,1)S(1)} %get-tuple-element.7), channel_id=1, source_target_pairs={{0,8},{8,16},{16,24},{1,9},{9,17},{17,25},{2,10},{10,18},{18,26},{... | collective-permute-start | bytes 294920 | tf_op jit(solution)/shard_map/ppermute | solution.py:19
  27.8 31.1 %collective-permute-start = (bf16[1,64,768]{2,1,0:T(8,128)(2,1)S(1)}, bf16[1,64,768]{2,1,0:T(8,128)(2,1)S(1)}, u32[]{:S(2)}, u32[]{:S(2)}) collective-permute-start(bf16[1,64,768]{2,1,0:T(8,128)(2,1)S(1)} %get-tuple-element.6), channel_id=1, source_target_pairs={{8,0},{16,8},{24,16},{9,1},{17,9},{25,17},{10,2},{18,10},{26,18},{... | collective-permute-start | bytes 294920 | tf_op jit(solution)/shard_map/ppermute | solution.py:20
  54.4 4.5 %copy-start.2 = (f32[128,768]{1,0:T(8,128)S(1)}, f32[128,768]{1,0:T(8,128)}, u32[]{:S(2)}) copy-start(f32[128,768]{1,0:T(8,128)} %fusion.3) | copy-start | bytes 1179652
  54.6 7.6 %collective-permute-start.3 = (f32[192,288]{1,0:T(8,128)S(1)}, f32[192,288]{1,0:T(8,128)S(1)}, u32[]{:S(2)}, u32[]{:S(2)}) collective-permute-start(f32[192,288]{1,0:T(8,128)S(1)} %bitcast.94), channel_id=1, source_target_pairs={{0,2},{1,3},{2,4},{3,5},{4,6},{5,7},{6,0},{7,1},{8,10},{9,11},{10,... | collective-permute-start | bytes 663560 | tf_op jit(solution)/shard_map/ppermute | solution.py:46
  56.1 24.2 %collective-permute-start.4 = (f32[192,288]{1,0:T(8,128)S(1)}, f32[192,288]{1,0:T(8,128)S(1)}, u32[]{:S(2)}, u32[]{:S(2)}) collective-permute-start(f32[192,288]{1,0:T(8,128)S(1)} %bitcast.95), channel_id=1, source_target_pairs={{0,4},{1,5},{2,6},{3,7},{4,0},{5,1},{6,2},{7,3},{8,12},{9,13},{10,... | collective-permute-start | bytes 663560 | tf_op jit(solution)/shard_map/ppermute | solution.py:46
  57.4 26.1 %collective-permute-start.5 = (f32[192,288]{1,0:T(8,128)S(1)}, f32[192,288]{1,0:T(8,128)S(1)}, u32[]{:S(2)}, u32[]{:S(2)}) collective-permute-start(f32[192,288]{1,0:T(8,128)S(1)} %bitcast.96), channel_id=1, source_target_pairs={{0,6},{1,7},{2,0},{3,1},{4,2},{5,3},{6,4},{7,5},{8,14},{9,15},{10,... | collective-permute-start | bytes 663560 | tf_op jit(solution)/shard_map/ppermute | solution.py:46

commit v3 on v2

--- a/solution.py
+++ b/solution.py
@@ -7,6 +7,7 @@
 
 KW = 3
 TAP_SPACING = 64
+CHUNKS = 4
 
 
 def extended_2(x, sides, width):
@@ -28,23 +29,33 @@
     return (values * normal_cdf, normal_cdf + values * density)
 
 
-def reduce_over_batch(rows):
+def reduce_over_batch(rows, chunks):
     count = lax.axis_size("batch")
     outer = count // 2
     me = lax.axis_index("batch")
     x = me % 2
     z = me // 2
-    blocks = rows.reshape(rows.shape[0], outer, 2, -1)
-    mine = lax.dynamic_index_in_dim(blocks, x, axis=2, keepdims=False)
-    theirs = lax.dynamic_index_in_dim(blocks, 1 - x, axis=2, keepdims=False)
     pairs = [(i, i ^ 1) for i in range(count)]
-    summed = mine + lax.ppermute(theirs, "batch", pairs)
-    total = lax.dynamic_index_in_dim(summed, z, axis=1, keepdims=False)
-    for shift in range(1, outer):
-        target = lax.dynamic_index_in_dim(summed, (z + shift) % outer, axis=1, keepdims=False)
-        perm = [(2 * q + p, 2 * ((q + shift) % outer) + p) for q in range(outer) for p in range(2)]
-        total = total + lax.ppermute(target, "batch", perm)
-    return total
+    step = rows.shape[0] // chunks
+    results = []
+    previous = None
+    for chunk in range(chunks):
+        part = rows[chunk * step : (chunk + 1) * step]
+        blocks = part.reshape(step, outer, 2, -1)
+        mine = lax.dynamic_index_in_dim(blocks, x, axis=2, keepdims=False)
+        theirs = lax.dynamic_index_in_dim(blocks, 1 - x, axis=2, keepdims=False)
+        if previous is not None:
+            previous, theirs = lax.optimization_barrier((previous, theirs))
+        arrived = lax.ppermute(theirs, "batch", pairs)
+        previous = arrived
+        summed = mine + arrived
+        total = lax.dynamic_index_in_dim(summed, z, axis=1, keepdims=False)
+        for shift in range(1, outer):
+            target = lax.dynamic_index_in_dim(summed, (z + shift) % outer, axis=1, keepdims=False)
+            perm = [(2 * q + p, 2 * ((q + shift) % outer) + p) for q in range(outer) for p in range(2)]
+            total = total + lax.ppermute(target, "batch", perm)
+        results.append(total)
+    return jnp.concatenate(results, axis=0)
 
 
 def body(inputs, cotangent, weight):
@@ -88,7 +99,7 @@
     taps_sum = jnp.stack(updated, axis=0)
     local_rows = jnp.transpose(taps_sum, (1, 0, 2)).reshape(own_rows, KW * in_width) * factor
     if batch_count == 8:
-        grad_weight = reduce_over_batch(local_rows)
+        grad_weight = reduce_over_batch(local_rows, CHUNKS)
     else:
         pieces = local_rows.reshape(own_rows, batch_count, -1)
         swapped = lax.all_to_all(pieces, "batch", split_axis=1, concat_axis=1, tiled=True)

time: 84.7 us -> 83.6 us (0.987)
  the two profiles are of different devices: /device:TPU:11 before, /device:TPU:0 now
where the time goes in v3:
time: 83.6 us; the launch traced here: 83.2 us
  starting transfers between devices  33.1 us (40%)
  waiting for transfers between devices  13.7 us (16%)
  local copies, waits for them, and re-layouts  12.4 us (15%)
  blocking collectives  11.5 us (14%)
  matrix products  8.19 us (10%)
  other arithmetic  3.25 us (4%)
  between operations  0.99 us (1%)
    ppermute x12, starting transfers between devices, reduce_over_batch(): total = total + lax.ppermute(target, 'batch', perm)  18.5 us
    all_gather x1, blocking collectives, body(): whole_act = lax.all_gather(act[None], 'seq', axis=1, tiled=True)[0]  11.5 us
    dot_general x3, matrix products, body(): jnp.dot(window, weight[:, tap_index * in_width:(tap_index + 1) * in_width...  7.12 us
    ppermute x12, waiting for transfers between devices, reduce_over_batch(): total = total + lax.ppermute(target, 'batch', perm)  6.92 us
    ppermute x4, waiting for transfers between devices, reduce_over_batch(): arrived = lax.ppermute(theirs, 'batch', pairs)  6.81 us
    ppermute x4, starting transfers between devices, reduce_over_batch(): arrived = lax.ppermute(theirs, 'batch', pairs)  6.68 us
    unnamed x34, local copies, waits for them, and re-layouts  4.65 us
    all_to_all x1, starting transfers between devices, body(): lax.all_to_all(cotangent, 'seq', split_axis=2, concat_axis=1, tiled=True)[0]  4.24 us
  transfers between devices with their start and end apart: 19, of which 10 were waited for; matrix products, arithmetic and copies ran while one was open for 22% of the time, Pallas kernels for 0%

profile of v3, /device:TPU:0, one launch (start us, length us, event | category | flops | bytes accessed | tf_op | source)
XLA Modules:
  0.0 83.2 jit_solution(541887866762764827)
XLA Ops:
  0.7 1.3 %copy.11 = bf16[1,128,768]{1,0,2:T(2,128)(2,1)S(1)} copy(bf16[1,128,768]{2,1,0:T(8,128)(2,1)} %param.4) | data formatting | bytes 393216 | tf_op args[1]
  2.5 1.8 %reduce = bf16[768,128]{1,0:T(8,128)(2,1)S(1)} reduce(bf16[768,1,128]{2,1,0:T(2,128)(2,1)S(1)} %bitcast.156, bf16[]{:T(256)} %broadcast.16), dimensions={1}, to_apply=%bitcast.132.reduce_sub_computation | reduce | bytes 393218
  5.0 4.2 %all-to-all-start = ((bf16[4,2,12288]{2,1,0:T(2,128)(2,1)}), bf16[4,2,12288]{2,1,0:T(2,128)(2,1)S(1)}, u32[]{:S(2)}, u32[]{:S(2)}) async-start(bf16[4,2,12288]{2,1,0:T(2,128)(2,1)} %reshape.38), calls=%async_computation | async-start | bytes 393216 | tf_op jit(solution)/shard_map/all_to_all | solution.py:85
  9.3 2.4 %collective-permute-start.1 = (bf16[1,64,768]{2,1,0:T(8,128)(2,1)S(1)}, bf16[1,64,768]{2,1,0:T(8,128)(2,1)S(1)}, u32[]{:S(2)}, u32[]{:S(2)}) collective-permute-start(bf16[1,64,768]{2,1,0:T(8,128)(2,1)S(1)} %get-tuple-element.37), channel_id=1, source_target_pairs={{0,8},{8,16},{16,24},{1,9},{9,17},{17,25},{2,10},{10,18},{18,26},{... | collective-permute-start | bytes 294920 | tf_op jit(solution)/shard_map/ppermute | solution.py:20
  11.7 1.3 %collective-permute-start = (bf16[1,64,768]{2,1,0:T(8,128)(2,1)S(1)}, bf16[1,64,768]{2,1,0:T(8,128)(2,1)}, u32[]{:S(2)}, u32[]{:S(2)}) collective-permute-start(bf16[1,64,768]{2,1,0:T(8,128)(2,1)S(1)} %get-tuple-element.36), channel_id=1, source_target_pairs={{8,0},{16,8},{24,16},{9,1},{17,9},{25,17},{10,2},{18,10},{26,18},{... | collective-permute-start | bytes 294920 | tf_op jit(solution)/shard_map/ppermute | solution.py:21
  13.1 11.5 %all_gather.3 = bf16[1,512,768]{2,1,0:T(8,128)(2,1)S(1)} all-gather(bf16[1,128,768]{2,1,0:T(8,128)(2,1)S(1)} %fusion.30), channel_id=1, replica_groups=mesh['seq'=4,'batch'=8] {'seq'}, dimensions={1}, use_global_device_ids=true | all-gather | bytes 983040 | tf_op jit(solution)/shard_map/all_gather | solution.py:88
  24.6 2.4 %fusion.5 = f32[128,768]{1,0:T(8,128)} fusion(bf16[768,2304]{1,0:T(8,128)(2,1)} %param.5, bf16[1,128,768]{2,1,0:T(8,128)(2,1)S(1)} %copy-done), kind=kOutput, calls=%fused_computation.10 | convolution fusion | flops 150994944 | bytes 1769472 | tf_op jit(solution)/shard_map/dot_general | solution.py:75
  27.0 2.4 %fusion.3 = f32[128,768]{1,0:T(8,128)} fusion(bf16[768,2304]{1,0:T(8,128)(2,1)} %param.5, bf16[1,128,768]{2,1,0:T(8,128)(2,1)S(1)} %copy-done, bf16[1,64,768]{2,1,0:T(8,128)(2,1)S(1)} %collective-permute-done.1), kind=kOutput, calls=%fused_computation.8 | convolution fusion | flops 151388160 | bytes 1867776 | tf_op jit(solution)/shard_map/dot_general | solution.py:75
  31.4 0.8 reshape.33
  33.4 1.0 %constant_dynamic-slice_fusion.17 = (f32[48,4,1,288]{3,2,1,0:T(1,128)S(1)}, f32[48,4,1,288]{3,2,1,0:T(1,128)S(1)}, f32[48,4,1,288]{3,2,1,0:T(1,128)S(1)}, f32[48,4,1,288]{3,2,1,0:T(1,128)S(1)}) fusion(f32[48,4,2,288]{3,2,1,0:T(2,128)S(1)} %reshape.34, s32[]{:T(128)S(6)} %select_n.80, s32[]{:T(128)S(6)} %select_n.81, f32[48,4,2,288]{3,2,1,0:T(2,128)S(1)} %reshape.33), kind=kLoop, calls=%fused_computation.95 | loop fusion | bytes 1769480 | tf_op jit(solution)/shard_map/jit(dynamic_index_in_dim)/dynamic_slice | solution.py:45
  34.4 0.8 copy.72
  35.2 2.0 %collective-permute-start.2 = (f32[48,4,288]{2,1,0:T(4,128)}, f32[48,4,288]{2,1,0:T(4,128)S(1)}, u32[]{:S(2)}, u32[]{:S(2)}) collective-permute-start(f32[48,4,288]{2,1,0:T(4,128)} %bitcast.137), channel_id=1, source_target_pairs={{0,1},{1,0},{2,3},{3,2},{4,5},{5,4},{6,7},{7,6},{8,9},{9,8},{10,11... | collective-permute-start | bytes 663560 | tf_op jit(solution)/shard_map/ppermute | solution.py:49
  37.2 2.4 %fusion.11 = bf16[1,128,768]{2,1,0:T(8,128)(2,1)} fusion(f32[128,768]{1,0:T(8,128)S(1)} %copy-done.5, f32[128,768]{1,0:T(8,128)S(1)} %copy-done.1, bf16[768,2304]{1,0:T(8,128)(2,1)} %param.5, bf16[1,128,768]{2,1,0:T(8,128)(2,1)S(1)} %copy-done.4, bf16[1,64,768]{2,1,0:T(8,128)(2,1)} %collective-permute-done, bf16[1,128,768]{2,1,0:T(8,128)(2,1)S(1)} %copy-done), kind=kOutput, calls=%fused_computation.14 | convolution fusion | flops 152666112 | bytes 2654208 | tf_op jit(solution)/shard_map/dot_general | solution.py:75
  42.6 1.0 %constant_dynamic-slice_fusion.5 = (f32[48,4,1,288]{3,2,1,0:T(1,128)S(1)}, f32[48,4,1,288]{3,2,1,0:T(1,128)S(1)}, f32[48,4,1,288]{3,2,1,0:T(1,128)S(1)}, f32[48,4,1,288]{3,2,1,0:T(1,128)S(1)}) fusion(f32[48,4,2,288]{3,2,1,0:T(2,128)S(1)} %reshape.36, s32[]{:T(128)S(6)} %select_n.80, s32[]{:T(128)S(6)} %select_n.81, f32[48,4,2,288]{3,2,1,0:T(2,128)S(1)} %reshape.35), kind=kLoop, calls=%fused_computation.83 | loop fusion | bytes 1769480 | tf_op jit(solution)/shard_map/jit(dynamic_index_in_dim)/dynamic_slice | solution.py:45
  43.8 1.1 %collective-permute-done.2 = f32[48,4,288]{2,1,0:T(4,128)S(1)} collective-permute-done((f32[48,4,288]{2,1,0:T(4,128)}, f32[48,4,288]{2,1,0:T(4,128)S(1)}, u32[]{:S(2)}, u32[]{:S(2)}) %collective-permute-start.2) | collective-permute-done | bytes 221216 | tf_op jit(solution)/shard_map/ppermute | solution.py:49
  44.9 1.7 %collective-permute-start.6 = (f32[48,4,288]{2,1,0:T(4,128)S(1)}, f32[48,4,288]{2,1,0:T(4,128)S(1)}, u32[]{:S(2)}, u32[]{:S(2)}) collective-permute-start(f32[48,4,288]{2,1,0:T(4,128)S(1)} %bitcast.160), channel_id=1, source_target_pairs={{0,1},{1,0},{2,3},{3,2},{4,5},{5,4},{6,7},{7,6},{8,9},{9,8},{10,11... | collective-permute-start | bytes 663560 | tf_op jit(solution)/shard_map/ppermute | solution.py:49
  47.0 1.6 %collective-permute-start.3 = (f32[48,288]{1,0:T(8,128)S(1)}, f32[48,288]{1,0:T(8,128)S(1)}, u32[]{:S(2)}, u32[]{:S(2)}) collective-permute-start(f32[48,288]{1,0:T(8,128)S(1)} %bitcast.165), channel_id=1, source_target_pairs={{0,2},{1,3},{2,4},{3,5},{4,6},{5,7},{6,0},{7,1},{8,10},{9,11},{10,... | collective-permute-start | bytes 165896 | tf_op jit(solution)/shard_map/ppermute | solution.py:56
  48.7 2.6 %collective-permute-start.4 = (f32[48,288]{1,0:T(8,128)S(1)}, f32[48,288]{1,0:T(8,128)S(1)}, u32[]{:S(2)}, u32[]{:S(2)}) collective-permute-start(f32[48,288]{1,0:T(8,128)S(1)} %bitcast.164), channel_id=1, source_target_pairs={{0,4},{1,5},{2,6},{3,7},{4,0},{5,1},{6,2},{7,3},{8,12},{9,13},{10,... | collective-permute-start | bytes 165896 | tf_op jit(solution)/shard_map/ppermute | solution.py:56
  51.3 1.3 %collective-permute-start.5 = (f32[48,288]{1,0:T(8,128)S(1)}, f32[48,288]{1,0:T(8,128)S(1)}, u32[]{:S(2)}, u32[]{:S(2)}) collective-permute-start(f32[48,288]{1,0:T(8,128)S(1)} %bitcast.166), channel_id=1, source_target_pairs={{0,6},{1,7},{2,0},{3,1},{4,2},{5,3},{6,4},{7,5},{8,14},{9,15},{10,... | collective-permute-start | bytes 165896 | tf_op jit(solution)/shard_map/ppermute | solution.py:56
  52.6 1.0 %collective-permute-done.6 = f32[48,4,288]{2,1,0:T(4,128)S(1)} collective-permute-done((f32[48,4,288]{2,1,0:T(4,128)S(1)}, f32[48,4,288]{2,1,0:T(4,128)S(1)}, u32[]{:S(2)}, u32[]{:S(2)}) %collective-permute-start.6) | collective-permute-done | bytes 221216 | tf_op jit(solution)/shard_map/ppermute | solution.py:49
  54.0 1.6 %collective-permute-start.7 = (f32[48,288]{1,0:T(8,128)S(1)}, f32[48,288]{1,0:T(8,128)S(1)}, u32[]{:S(2)}, u32[]{:S(2)}) collective-permute-start(f32[48,288]{1,0:T(8,128)S(1)} %bitcast.167), channel_id=1, source_target_pairs={{0,2},{1,3},{2,4},{3,5},{4,6},{5,7},{6,0},{7,1},{8,10},{9,11},{10,... | collective-permute-start | bytes 165896 | tf_op jit(solution)/shard_map/ppermute | solution.py:56
  55.6 2.6 %collective-permute-start.8 = (f32[48,288]{1,0:T(8,128)S(1)}, f32[48,288]{1,0:T(8,128)S(1)}, u32[]{:S(2)}, u32[]{:S(2)}) collective-permute-start(f32[48,288]{1,0:T(8,128)S(1)} %bitcast.168), channel_id=1, source_target_pairs={{0,4},{1,5},{2,6},{3,7},{4,0},{5,1},{6,2},{7,3},{8,12},{9,13},{10,... | collective-permute-start | bytes 165896 | tf_op jit(solution)/shard_map/ppermute | solution.py:56
  58.2 1.4 %collective-permute-start.9 = (f32[48,288]{1,0:T(8,128)S(1)}, f32[48,288]{1,0:T(8,128)S(1)}, u32[]{:S(2)}, u32[]{:S(2)}) collective-permute-start(f32[48,288]{1,0:T(8,128)S(1)} %bitcast.169), channel_id=1, source_target_pairs={{0,6},{1,7},{2,0},{3,1},{4,2},{5,3},{6,4},{7,5},{8,14},{9,15},{10,... | collective-permute-start | bytes 165896 | tf_op jit(solution)/shard_map/ppermute | solution.py:56
  59.7 1.5 %collective-permute-start.10 = (f32[48,4,288]{2,1,0:T(4,128)S(1)}, f32[48,4,288]{2,1,0:T(4,128)S(1)}, u32[]{:S(2)}, u32[]{:S(2)}) collective-permute-start(f32[48,4,288]{2,1,0:T(4,128)S(1)} %bitcast.159), channel_id=1, source_target_pairs={{0,1},{1,0},{2,3},{3,2},{4,5},{5,4},{6,7},{7,6},{8,9},{9,8},{10,11... | collective-permute-start | bytes 663560 | tf_op jit(solution)/shard_map/ppermute | solution.py:49
  61.2 1.8 %collective-permute-done.8 = f32[48,288]{1,0:T(8,128)S(1)} collective-permute-done((f32[48,288]{1,0:T(8,128)S(1)}, f32[48,288]{1,0:T(8,128)S(1)}, u32[]{:S(2)}, u32[]{:S(2)}) %collective-permute-start.8) | collective-permute-done | bytes 55328 | tf_op jit(solution)/shard_map/ppermute | solution.py:56
  63.2 3.8 %collective-permute-done.10 = f32[48,4,288]{2,1,0:T(4,128)S(1)} collective-permute-done((f32[48,4,288]{2,1,0:T(4,128)S(1)}, f32[48,4,288]{2,1,0:T(4,128)S(1)}, u32[]{:S(2)}, u32[]{:S(2)}) %collective-permute-start.10) | collective-permute-done | bytes 221216 | tf_op jit(solution)/shard_map/ppermute | solution.py:49
  67.0 1.4 %collective-permute-start.14 = (f32[48,4,288]{2,1,0:T(4,128)S(1)}, f32[48,4,288]{2,1,0:T(4,128)S(1)}, u32[]{:S(2)}, u32[]{:S(2)}) collective-permute-start(f32[48,4,288]{2,1,0:T(4,128)S(1)} %bitcast.158), channel_id=1, source_target_pairs={{0,1},{1,0},{2,3},{3,2},{4,5},{5,4},{6,7},{7,6},{8,9},{9,8},{10,11... | collective-permute-start | bytes 663560 | tf_op jit(solution)/shard_map/ppermute | solution.py:49
  69.8 2.9 %collective-permute-start.13 = (f32[48,288]{1,0:T(8,128)S(1)}, f32[48,288]{1,0:T(8,128)S(1)}, u32[]{:S(2)}, u32[]{:S(2)}) collective-permute-start(f32[48,288]{1,0:T(8,128)S(1)} %bitcast.163), channel_id=1, source_target_pairs={{0,6},{1,7},{2,0},{3,1},{4,2},{5,3},{6,4},{7,5},{8,14},{9,15},{10,... | collective-permute-start | bytes 165896 | tf_op jit(solution)/shard_map/ppermute | solution.py:56
  72.8 0.9 %collective-permute-done.14 = f32[48,4,288]{2,1,0:T(4,128)S(1)} collective-permute-done((f32[48,4,288]{2,1,0:T(4,128)S(1)}, f32[48,4,288]{2,1,0:T(4,128)S(1)}, u32[]{:S(2)}, u32[]{:S(2)}) %collective-permute-start.14) | collective-permute-done | bytes 221216 | tf_op jit(solution)/shard_map/ppermute | solution.py:49
  75.9 2.2 %collective-permute-start.17 = (f32[48,288]{1,0:T(8,128)S(1)}, f32[48,288]{1,0:T(8,128)S(1)}, u32[]{:S(2)}, u32[]{:S(2)}) collective-permute-start(f32[48,288]{1,0:T(8,128)S(1)} %bitcast.172), channel_id=1, source_target_pairs={{0,6},{1,7},{2,0},{3,1},{4,2},{5,3},{6,4},{7,5},{8,14},{9,15},{10,... | collective-permute-start | bytes 165896 | tf_op jit(solution)/shard_map/ppermute | solution.py:56
  78.7 1.7 %collective-permute-done.15 = f32[48,288]{1,0:T(8,128)S(1)} collective-permute-done((f32[48,288]{1,0:T(8,128)S(1)}, f32[48,288]{1,0:T(8,128)S(1)}, u32[]{:S(2)}, u32[]{:S(2)}) %collective-permute-start.15) | collective-permute-done | bytes 55328 | tf_op jit(solution)/shard_map/ppermute | solution.py:56
  80.4 2.0 %collective-permute-done.16 = f32[48,288]{1,0:T(8,128)S(1)} collective-permute-done((f32[48,288]{1,0:T(8,128)S(1)}, f32[48,288]{1,0:T(8,128)S(1)}, u32[]{:S(2)}, u32[]{:S(2)}) %collective-permute-start.16) | collective-permute-done | bytes 55328 | tf_op jit(solution)/shard_map/ppermute | solution.py:56
  (76 shorter events, 13.5 us)
Async XLA Ops:
  0.6 8.6 %copy-start = (bf16[1,128,768]{2,1,0:T(8,128)(2,1)S(1)}, bf16[1,128,768]{2,1,0:T(8,128)(2,1)}, u32[]{:S(2)}) copy-start(bf16[1,128,768]{2,1,0:T(8,128)(2,1)} %param.4) | copy-start | bytes 589828
  0.6 12.4 %copy-start.3 = (bf16[1,128,768]{2,1,0:T(8,128)(2,1)S(1)}, bf16[1,128,768]{2,1,0:T(8,128)(2,1)}, u32[]{:S(2)}) copy-start(bf16[1,128,768]{2,1,0:T(8,128)(2,1)} %param.3) | copy-start | bytes 589828
  5.0 24.3 %all-to-all-start = ((bf16[4,2,12288]{2,1,0:T(2,128)(2,1)}), bf16[4,2,12288]{2,1,0:T(2,128)(2,1)S(1)}, u32[]{:S(2)}, u32[]{:S(2)}) async-start(bf16[4,2,12288]{2,1,0:T(2,128)(2,1)} %reshape.38), calls=%async_computation | async-start | bytes 393216 | tf_op jit(solution)/shard_map/all_to_all | solution.py:85
  9.3 17.7 %collective-permute-start.1 = (bf16[1,64,768]{2,1,0:T(8,128)(2,1)S(1)}, bf16[1,64,768]{2,1,0:T(8,128)(2,1)S(1)}, u32[]{:S(2)}, u32[]{:S(2)}) collective-permute-start(bf16[1,64,768]{2,1,0:T(8,128)(2,1)S(1)} %get-tuple-element.37), channel_id=1, source_target_pairs={{0,8},{8,16},{16,24},{1,9},{9,17},{17,25},{2,10},{10,18},{18,26},{... | collective-permute-start | bytes 294920 | tf_op jit(solution)/shard_map/ppermute | solution.py:20
  11.7 25.5 %collective-permute-start = (bf16[1,64,768]{2,1,0:T(8,128)(2,1)S(1)}, bf16[1,64,768]{2,1,0:T(8,128)(2,1)}, u32[]{:S(2)}, u32[]{:S(2)}) collective-permute-start(bf16[1,64,768]{2,1,0:T(8,128)(2,1)S(1)} %get-tuple-element.36), channel_id=1, source_target_pairs={{8,0},{16,8},{24,16},{9,1},{17,9},{25,17},{10,2},{18,10},{26,18},{... | collective-permute-start | bytes 294920 | tf_op jit(solution)/shard_map/ppermute | solution.py:21
  33.3 3.8 %copy-start.1 = (f32[128,768]{1,0:T(8,128)S(1)}, f32[128,768]{1,0:T(8,128)}, u32[]{:S(2)}) copy-start(f32[128,768]{1,0:T(8,128)} %fusion.5) | copy-start | bytes 1179652
  33.3 3.8 %copy-start.4 = (bf16[1,128,768]{2,1,0:T(8,128)(2,1)S(1)}, bf16[1,128,768]{2,1,0:T(8,128)(2,1)}, u32[]{:S(2)}) copy-start(bf16[1,128,768]{2,1,0:T(8,128)(2,1)} %param.3) | copy-start | bytes 589828
  33.4 3.8 %copy-start.5 = (f32[128,768]{1,0:T(8,128)S(1)}, f32[128,768]{1,0:T(8,128)}, u32[]{:S(2)}) copy-start(f32[128,768]{1,0:T(8,128)} %fusion.3) | copy-start | bytes 1179652
  35.2 9.7 %collective-permute-start.2 = (f32[48,4,288]{2,1,0:T(4,128)}, f32[48,4,288]{2,1,0:T(4,128)S(1)}, u32[]{:S(2)}, u32[]{:S(2)}) collective-permute-start(f32[48,4,288]{2,1,0:T(4,128)} %bitcast.137), channel_id=1, source_target_pairs={{0,1},{1,0},{2,3},{3,2},{4,5},{5,4},{6,7},{7,6},{8,9},{9,8},{10,11... | collective-permute-start | bytes 663560 | tf_op jit(solution)/shard_map/ppermute | solution.py:49
  42.6 2.3 %copy-start.2 = (f32[48,4,1,288]{3,1,2,0:T(4,128)S(1)}, f32[48,4,1,288]{3,1,2,0:T(4,128)}, u32[]{:S(2)}) copy-start(f32[48,4,1,288]{3,1,2,0:T(4,128)} %copy.71) | copy-start | bytes 663556
  44.9 8.7 %collective-permute-start.6 = (f32[48,4,288]{2,1,0:T(4,128)S(1)}, f32[48,4,288]{2,1,0:T(4,128)S(1)}, u32[]{:S(2)}, u32[]{:S(2)}) collective-permute-start(f32[48,4,288]{2,1,0:T(4,128)S(1)} %bitcast.160), channel_id=1, source_target_pairs={{0,1},{1,0},{2,3},{3,2},{4,5},{5,4},{6,7},{7,6},{8,9},{9,8},{10,11... | collective-permute-start | bytes 663560 | tf_op jit(solution)/shard_map/ppermute | solution.py:49
  47.0 11.2 %collective-permute-start.3 = (f32[48,288]{1,0:T(8,128)S(1)}, f32[48,288]{1,0:T(8,128)S(1)}, u32[]{:S(2)}, u32[]{:S(2)}) collective-permute-start(f32[48,288]{1,0:T(8,128)S(1)} %bitcast.165), channel_id=1, source_target_pairs={{0,2},{1,3},{2,4},{3,5},{4,6},{5,7},{6,0},{7,1},{8,10},{9,11},{10,... | collective-permute-start | bytes 165896 | tf_op jit(solution)/shard_map/ppermute | solution.py:56
  48.7 11.0 %collective-permute-start.4 = (f32[48,288]{1,0:T(8,128)S(1)}, f32[48,288]{1,0:T(8,128)S(1)}, u32[]{:S(2)}, u32[]{:S(2)}) collective-permute-start(f32[48,288]{1,0:T(8,128)S(1)} %bitcast.164), channel_id=1, source_target_pairs={{0,4},{1,5},{2,6},{3,7},{4,0},{5,1},{6,2},{7,3},{8,12},{9,13},{10,... | collective-permute-start | bytes 165896 | tf_op jit(solution)/shard_map/ppermute | solution.py:56
  51.3 8.4 %collective-permute-start.5 = (f32[48,288]{1,0:T(8,128)S(1)}, f32[48,288]{1,0:T(8,128)S(1)}, u32[]{:S(2)}, u32[]{:S(2)}) collective-permute-start(f32[48,288]{1,0:T(8,128)S(1)} %bitcast.166), channel_id=1, source_target_pairs={{0,6},{1,7},{2,0},{3,1},{4,2},{5,3},{6,4},{7,5},{8,14},{9,15},{10,... | collective-permute-start | bytes 165896 | tf_op jit(solution)/shard_map/ppermute | solution.py:56
  54.0 7.2 %collective-permute-start.7 = (f32[48,288]{1,0:T(8,128)S(1)}, f32[48,288]{1,0:T(8,128)S(1)}, u32[]{:S(2)}, u32[]{:S(2)}) collective-permute-start(f32[48,288]{1,0:T(8,128)S(1)} %bitcast.167), channel_id=1, source_target_pairs={{0,2},{1,3},{2,4},{3,5},{4,6},{5,7},{6,0},{7,1},{8,10},{9,11},{10,... | collective-permute-start | bytes 165896 | tf_op jit(solution)/shard_map/ppermute | solution.py:56
  55.6 7.4 %collective-permute-start.8 = (f32[48,288]{1,0:T(8,128)S(1)}, f32[48,288]{1,0:T(8,128)S(1)}, u32[]{:S(2)}, u32[]{:S(2)}) collective-permute-start(f32[48,288]{1,0:T(8,128)S(1)} %bitcast.168), channel_id=1, source_target_pairs={{0,4},{1,5},{2,6},{3,7},{4,0},{5,1},{6,2},{7,3},{8,12},{9,13},{10,... | collective-permute-start | bytes 165896 | tf_op jit(solution)/shard_map/ppermute | solution.py:56
  58.2 4.9 %collective-permute-start.9 = (f32[48,288]{1,0:T(8,128)S(1)}, f32[48,288]{1,0:T(8,128)S(1)}, u32[]{:S(2)}, u32[]{:S(2)}) collective-permute-start(f32[48,288]{1,0:T(8,128)S(1)} %bitcast.169), channel_id=1, source_target_pairs={{0,6},{1,7},{2,0},{3,1},{4,2},{5,3},{6,4},{7,5},{8,14},{9,15},{10,... | collective-permute-start | bytes 165896 | tf_op jit(solution)/shard_map/ppermute | solution.py:56
  59.7 7.3 %collective-permute-start.10 = (f32[48,4,288]{2,1,0:T(4,128)S(1)}, f32[48,4,288]{2,1,0:T(4,128)S(1)}, u32[]{:S(2)}, u32[]{:S(2)}) collective-permute-start(f32[48,4,288]{2,1,0:T(4,128)S(1)} %bitcast.159), channel_id=1, source_target_pairs={{0,1},{1,0},{2,3},{3,2},{4,5},{5,4},{6,7},{7,6},{8,9},{9,8},{10,11... | collective-permute-start | bytes 663560 | tf_op jit(solution)/shard_map/ppermute | solution.py:49
  67.0 6.7 %collective-permute-start.14 = (f32[48,4,288]{2,1,0:T(4,128)S(1)}, f32[48,4,288]{2,1,0:T(4,128)S(1)}, u32[]{:S(2)}, u32[]{:S(2)}) collective-permute-start(f32[48,4,288]{2,1,0:T(4,128)S(1)} %bitcast.158), channel_id=1, source_target_pairs={{0,1},{1,0},{2,3},{3,2},{4,5},{5,4},{6,7},{7,6},{8,9},{9,8},{10,11... | collective-permute-start | bytes 663560 | tf_op jit(solution)/shard_map/ppermute | solution.py:49
  68.8 7.1 %collective-permute-start.11 = (f32[48,288]{1,0:T(8,128)S(1)}, f32[48,288]{1,0:T(8,128)S(1)}, u32[]{:S(2)}, u32[]{:S(2)}) collective-permute-start(f32[48,288]{1,0:T(8,128)S(1)} %bitcast.162), channel_id=1, source_target_pairs={{0,2},{1,3},{2,4},{3,5},{4,6},{5,7},{6,0},{7,1},{8,10},{9,11},{10,... | collective-permute-start | bytes 165896 | tf_op jit(solution)/shard_map/ppermute | solution.py:56
  69.5 9.2 %collective-permute-start.12 = (f32[48,288]{1,0:T(8,128)S(1)}, f32[48,288]{1,0:T(8,128)S(1)}, u32[]{:S(2)}, u32[]{:S(2)}) collective-permute-start(f32[48,288]{1,0:T(8,128)S(1)} %bitcast.161), channel_id=1, source_target_pairs={{0,4},{1,5},{2,6},{3,7},{4,0},{5,1},{6,2},{7,3},{8,12},{9,13},{10,... | collective-permute-start | bytes 165896 | tf_op jit(solution)/shard_map/ppermute | solution.py:56
  69.8 8.9 %collective-permute-start.13 = (f32[48,288]{1,0:T(8,128)S(1)}, f32[48,288]{1,0:T(8,128)S(1)}, u32[]{:S(2)}, u32[]{:S(2)}) collective-permute-start(f32[48,288]{1,0:T(8,128)S(1)} %bitcast.163), channel_id=1, source_target_pairs={{0,6},{1,7},{2,0},{3,1},{4,2},{5,3},{6,4},{7,5},{8,14},{9,15},{10,... | collective-permute-start | bytes 165896 | tf_op jit(solution)/shard_map/ppermute | solution.py:56
  74.1 6.3 %collective-permute-start.15 = (f32[48,288]{1,0:T(8,128)S(1)}, f32[48,288]{1,0:T(8,128)S(1)}, u32[]{:S(2)}, u32[]{:S(2)}) collective-permute-start(f32[48,288]{1,0:T(8,128)S(1)} %bitcast.170), channel_id=1, source_target_pairs={{0,2},{1,3},{2,4},{3,5},{4,6},{5,7},{6,0},{7,1},{8,10},{9,11},{10,... | collective-permute-start | bytes 165896 | tf_op jit(solution)/shard_map/ppermute | solution.py:56
  74.7 7.8 %collective-permute-start.16 = (f32[48,288]{1,0:T(8,128)S(1)}, f32[48,288]{1,0:T(8,128)S(1)}, u32[]{:S(2)}, u32[]{:S(2)}) collective-permute-start(f32[48,288]{1,0:T(8,128)S(1)} %bitcast.171), channel_id=1, source_target_pairs={{0,4},{1,5},{2,6},{3,7},{4,0},{5,1},{6,2},{7,3},{8,12},{9,13},{10,... | collective-permute-start | bytes 165896 | tf_op jit(solution)/shard_map/ppermute | solution.py:56
  75.9 6.5 %collective-permute-start.17 = (f32[48,288]{1,0:T(8,128)S(1)}, f32[48,288]{1,0:T(8,128)S(1)}, u32[]{:S(2)}, u32[]{:S(2)}) collective-permute-start(f32[48,288]{1,0:T(8,128)S(1)} %bitcast.172), channel_id=1, source_target_pairs={{0,6},{1,7},{2,0},{3,1},{4,2},{5,3},{6,4},{7,5},{8,14},{9,15},{10,... | collective-permute-start | bytes 165896 | tf_op jit(solution)/shard_map/ppermute | solution.py:56

commit v4 on v3

--- a/solution.py
+++ b/solution.py
@@ -7,7 +7,8 @@
 
 KW = 3
 TAP_SPACING = 64
-CHUNKS = 4
+CHUNKS = 2
+HEADROOM = 12.0
 
 
 def extended_2(x, sides, width):
@@ -29,6 +30,23 @@
     return (values * normal_cdf, normal_cdf + values * density)
 
 
+def encode(values):
+    biggest = jnp.maximum(jnp.max(jnp.abs(values)), 1e-30)
+    exponent = jnp.floor(jnp.log2(biggest))
+    scaled = (values * jnp.exp2(HEADROOM - exponent)).astype(jnp.float16)
+    tag = jnp.full((1,) + values.shape[1:], exponent, jnp.float16)
+    return jnp.concatenate([tag, scaled], axis=0)
+
+
+def decode(packed):
+    exponent = packed[0].reshape(-1)[0].astype(jnp.float32)
+    return packed[1:].astype(jnp.float32) * jnp.exp2(exponent - HEADROOM)
+
+
+def send(values, perm):
+    return decode(lax.ppermute(encode(values), "batch", perm))
+
+
 def reduce_over_batch(rows, chunks):
     count = lax.axis_size("batch")
     outer = count // 2
@@ -37,24 +55,29 @@
     z = me // 2
     pairs = [(i, i ^ 1) for i in range(count)]
     step = rows.shape[0] // chunks
+
+    def finish(mine, packed):
+        summed = mine + decode(packed)
+        total = lax.dynamic_index_in_dim(summed, z, axis=1, keepdims=False)
+        for shift in range(1, outer):
+            target = lax.dynamic_index_in_dim(summed, (z + shift) % outer, axis=1, keepdims=False)
+            perm = [(2 * q + p, 2 * ((q + shift) % outer) + p) for q in range(outer) for p in range(2)]
+            total = total + send(target, perm)
+        return total
+
     results = []
-    previous = None
+    pending = None
     for chunk in range(chunks):
         part = rows[chunk * step : (chunk + 1) * step]
         blocks = part.reshape(step, outer, 2, -1)
         mine = lax.dynamic_index_in_dim(blocks, x, axis=2, keepdims=False)
-        theirs = lax.dynamic_index_in_dim(blocks, 1 - x, axis=2, keepdims=False)
-        if previous is not None:
-            previous, theirs = lax.optimization_barrier((previous, theirs))
-        arrived = lax.ppermute(theirs, "batch", pairs)
-        previous = arrived
-        summed = mine + arrived
-        total = lax.dynamic_index_in_dim(summed, z, axis=1, keepdims=False)
-        for shift in range(1, outer):
-            target = lax.dynamic_index_in_dim(summed, (z + shift) % outer, axis=1, keepdims=False)
-            perm = [(2 * q + p, 2 * ((q + shift) % outer) + p) for q in range(outer) for p in range(2)]
-            total = total + lax.ppermute(target, "batch", perm)
-        results.append(total)
+        theirs = encode(lax.dynamic_index_in_dim(blocks, 1 - x, axis=2, keepdims=False))
+        if pending is not None:
+            kept, arrived = pending
+            arrived, theirs = lax.optimization_barrier((arrived, theirs))
+            results.append(finish(kept, arrived))
+        pending = (mine, lax.ppermute(theirs, "batch", pairs))
+    results.append(finish(*pending))
     return jnp.concatenate(results, axis=0)
 
 

time: 83.6 us -> 82.2 us (0.983)
  starting transfers between devices: 33.1 us -> 21.4 us
  between operations: 0.99 us -> 12.4 us
  waiting for transfers between devices: 13.7 us -> 8.61 us
  other arithmetic: 3.25 us -> 6.49 us
    ppermute x16 -> x8, starting transfers between devices: 25.2 us -> 13.5 us  [the longest x6 9.71 us: send(): return decode(lax.ppermute(encode(values), 'batch', perm))]
    slice x0 -> x10, local copies, waits for them, and re-layouts: none -> 5.69 us  [decode(): exponent = packed[0].reshape(-1)[0].astype(jnp.float32)]
    ppermute x16 -> x8, waiting for transfers between devices: 13.7 us -> 8.6 us  [the longest x2 8.58 us: reduce_over_batch(): pending = (mine, lax.ppermute(theirs, 'batch', pairs))]
    reshape x4 -> x0, local copies, waits for them, and re-layouts: 3.16 us -> none  [reduce_over_batch(): blocks = part.reshape(step, outer, 2, -1)]
    dynamic_slice x6 -> x0, local copies, waits for them, and re-layouts: 3.08 us -> none  [the longest x2 2.04 us: reduce_over_batch(): mine = lax.dynamic_index_in_dim(blocks, x, axis=2, keepdims=False)]
    concatenate x0 -> x8, local copies, waits for them, and re-layouts: none -> 2.52 us  [encode(): return jnp.concatenate([tag, scaled], axis=0)]
    reduce_max x0 -> x3, other arithmetic: none -> 2.3 us  [encode(): biggest = jnp.maximum(jnp.max(jnp.abs(values)), 1e-30)]
    add x8 -> x4, other arithmetic: 0.49 us -> 1.77 us  [the longest x2 1.4 us: finish(): summed = mine + decode(packed)]
  transfers between devices with their start and end apart: 19 -> 11, of which waited for: 10 -> 2; matrix products, arithmetic and copies ran while one was open for 22% -> 26% of each run, Pallas kernels for 0% -> 0%
where the time goes in v4:
time: 82.2 us; the launch traced here: 81.6 us
  starting transfers between devices  21.4 us (26%)
  local copies, waits for them, and re-layouts  13.1 us (16%)
  between operations  12.4 us (15%)
  blocking collectives  11.4 us (14%)
  waiting for transfers between devices  8.61 us (10%)
  matrix products  8.17 us (10%)
  other arithmetic  6.49 us (8%)
    all_gather x1, blocking collectives, body(): whole_act = lax.all_gather(act[None], 'seq', axis=1, tiled=True)[0]  11.4 us
    ppermute x6, starting transfers between devices, send(): return decode(lax.ppermute(encode(values), 'batch', perm))  9.71 us
    ppermute x2, waiting for transfers between devices, reduce_over_batch(): pending = (mine, lax.ppermute(theirs, 'batch', pairs))  8.58 us
    dot_general x3, matrix products, body(): jnp.dot(window, weight[:, tap_index * in_width:(tap_index + 1) * in_width...  7.1 us
    slice x10, local copies, waits for them, and re-layouts, decode(): exponent = packed[0].reshape(-1)[0].astype(jnp.float32)  5.69 us
    all_to_all x1, starting transfers between devices, body(): lax.all_to_all(cotangent, 'seq', split_axis=2, concat_axis=1, tiled=True)[0]  4.24 us
    ppermute x2, starting transfers between devices, reduce_over_batch(): pending = (mine, lax.ppermute(theirs, 'batch', pairs))  3.76 us
    unnamed x17, local copies, waits for them, and re-layouts  3.69 us
  transfers between devices with their start and end apart: 11, of which 2 were waited for; matrix products, arithmetic and copies ran while one was open for 26% of the time, Pallas kernels for 0%

profile of v4, /device:TPU:0, one launch (start us, length us, event | category | flops | bytes accessed | tf_op | source)
XLA Modules:
  0.0 81.6 jit_solution(18400280370088884823)
XLA Ops:
  0.7 1.3 %copy.11 = bf16[1,128,768]{1,0,2:T(2,128)(2,1)S(1)} copy(bf16[1,128,768]{2,1,0:T(8,128)(2,1)} %param.4) | data formatting | bytes 393216 | tf_op args[1]
  2.5 1.8 %reduce.12 = bf16[768,128]{1,0:T(8,128)(2,1)S(1)} reduce(bf16[768,1,128]{2,1,0:T(2,128)(2,1)S(1)} %bitcast.133, bf16[]{:T(256)} %broadcast.50), dimensions={1}, to_apply=%bitcast.119.reduce_sub_computation | reduce | bytes 393218
  4.3 0.7 reshape.120
  5.0 4.2 %all-to-all-start = ((bf16[4,2,12288]{2,1,0:T(2,128)(2,1)}), bf16[4,2,12288]{2,1,0:T(2,128)(2,1)S(1)}, u32[]{:S(2)}, u32[]{:S(2)}) async-start(bf16[4,2,12288]{2,1,0:T(2,128)(2,1)} %reshape.120), calls=%async_computation | async-start | bytes 393216 | tf_op jit(solution)/shard_map/all_to_all | solution.py:108
  9.3 2.4 %collective-permute-start.1 = (bf16[1,64,768]{2,1,0:T(8,128)(2,1)S(1)}, bf16[1,64,768]{2,1,0:T(8,128)(2,1)S(1)}, u32[]{:S(2)}, u32[]{:S(2)}) collective-permute-start(bf16[1,64,768]{2,1,0:T(8,128)(2,1)S(1)} %get-tuple-element.25), channel_id=1, source_target_pairs={{0,8},{8,16},{16,24},{1,9},{9,17},{17,25},{2,10},{10,18},{18,26},{... | collective-permute-start | bytes 294920 | tf_op jit(solution)/shard_map/ppermute | solution.py:21
  11.7 1.3 %collective-permute-start = (bf16[1,64,768]{2,1,0:T(8,128)(2,1)S(1)}, bf16[1,64,768]{2,1,0:T(8,128)(2,1)}, u32[]{:S(2)}, u32[]{:S(2)}) collective-permute-start(bf16[1,64,768]{2,1,0:T(8,128)(2,1)S(1)} %get-tuple-element.24), channel_id=1, source_target_pairs={{8,0},{16,8},{24,16},{9,1},{17,9},{25,17},{10,2},{18,10},{26,18},{... | collective-permute-start | bytes 294920 | tf_op jit(solution)/shard_map/ppermute | solution.py:22
  13.2 11.4 %all_gather.3 = bf16[1,512,768]{2,1,0:T(8,128)(2,1)S(1)} all-gather(bf16[1,128,768]{2,1,0:T(8,128)(2,1)S(1)} %fusion.32), channel_id=1, replica_groups=mesh['seq'=4,'batch'=8] {'seq'}, dimensions={1}, use_global_device_ids=true | all-gather | bytes 983040 | tf_op jit(solution)/shard_map/all_gather | solution.py:111
  24.6 2.3 %fusion.5 = f32[128,768]{1,0:T(8,128)} fusion(bf16[768,2304]{1,0:T(8,128)(2,1)} %param.5, bf16[1,128,768]{2,1,0:T(8,128)(2,1)S(1)} %copy-done), kind=kOutput, calls=%fused_computation.10 | convolution fusion | flops 150994944 | bytes 1769472 | tf_op jit(solution)/shard_map/dot_general | solution.py:98
  29.1 0.8 abs_reduce_fusion
  30.7 0.9 %concatenate.36 = f16[97,4,288]{0,2,1:T(8,128)(2,1)} pad(f16[96,4,288]{0,2,1:T(8,128)(2,1)S(1)} %fusion.33, f16[]{:T(256)S(6)} %convert_element_type.153), padding=1_0x0_0x0_0 | pad | bytes 444674 | tf_op jit(solution)/shard_map/concatenate | solution.py:38
  31.6 2.0 %collective-permute-start.2 = (f16[97,4,288]{0,2,1:T(8,128)(2,1)}, f16[97,4,288]{0,2,1:T(8,128)(2,1)}, u32[]{:S(2)}, u32[]{:S(2)}) collective-permute-start(f16[97,4,288]{0,2,1:T(8,128)(2,1)} %concatenate.36), channel_id=1, source_target_pairs={{0,1},{1,0},{2,3},{3,2},{4,5},{5,4},{6,7},{7,6},{8,9},{9,8},{10,11... | collective-permute-start | bytes 670472 | tf_op jit(solution)/shard_map/ppermute | solution.py:79
  33.6 2.3 %fusion.3 = f32[128,768]{1,0:T(8,128)} fusion(bf16[768,2304]{1,0:T(8,128)(2,1)} %param.5, bf16[1,128,768]{2,1,0:T(8,128)(2,1)S(1)} %copy-done, bf16[1,64,768]{2,1,0:T(8,128)(2,1)S(1)} %collective-permute-done.1), kind=kOutput, calls=%fused_computation.8 | convolution fusion | flops 151388160 | bytes 1867776 | tf_op jit(solution)/shard_map/dot_general | solution.py:98
  36.3 0.8 fusion.21
  37.9 0.9 %concatenate.37 = f16[97,4,288]{0,2,1:T(8,128)(2,1)} pad(f16[96,4,288]{0,2,1:T(8,128)(2,1)S(1)} %fusion.34, f16[]{:T(256)S(6)} %convert_element_type.156), padding=1_0x0_0x0_0 | pad | bytes 444674 | tf_op jit(solution)/shard_map/concatenate | solution.py:38
  38.8 2.6 %collective-permute-done.2 = f16[97,4,288]{0,2,1:T(8,128)(2,1)} collective-permute-done((f16[97,4,288]{0,2,1:T(8,128)(2,1)}, f16[97,4,288]{0,2,1:T(8,128)(2,1)}, u32[]{:S(2)}, u32[]{:S(2)}) %collective-permute-start.2) | collective-permute-done | bytes 223520 | tf_op jit(solution)/shard_map/ppermute | solution.py:79
  41.4 1.2 %slice_reduce_fusion.1 = f16[4,288]{1,0:T(4,128)(2,1)S(1)} fusion(f16[97,4,288]{0,2,1:T(8,128)(2,1)} %collective-permute-done.2), kind=kLoop, calls=%fused_computation.47 | loop fusion | bytes 4608 | tf_op jit(solution)/shard_map/slice | solution.py:42
  42.8 0.5 slice.145
  44.0 1.8 %collective-permute-start.6 = (f16[97,4,288]{0,2,1:T(8,128)(2,1)}, f16[97,4,288]{0,2,1:T(8,128)(2,1)S(1)}, u32[]{:S(2)}, u32[]{:S(2)}) collective-permute-start(f16[97,4,288]{0,2,1:T(8,128)(2,1)} %concatenate.37), channel_id=1, source_target_pairs={{0,1},{1,0},{2,3},{3,2},{4,5},{5,4},{6,7},{7,6},{8,9},{9,8},{10,11... | collective-permute-start | bytes 670472 | tf_op jit(solution)/shard_map/ppermute | solution.py:79
  45.8 1.2 %bitcast_add_fusion.1 = f32[96,4,288]{0,2,1:T(8,128)S(1)} fusion(f32[96,4,2,288]{0,3,2,1:T(8,128)S(1)} %bitcast.124, s32[]{:T(128)S(6)} %select_n.56, f32[]{:T(128)} %bitcast.17, f16[97,4,288]{0,2,1:T(8,128)(2,1)} %collective-permute-done.2), kind=kLoop, calls=%fused_computation.30 | loop fusion | flops 331776 | bytes 1105928 | tf_op jit(solution)/shard_map/add | solution.py:60
  47.0 6.0 %collective-permute-done.6 = f16[97,4,288]{0,2,1:T(8,128)(2,1)S(1)} collective-permute-done((f16[97,4,288]{0,2,1:T(8,128)(2,1)}, f16[97,4,288]{0,2,1:T(8,128)(2,1)S(1)}, u32[]{:S(2)}, u32[]{:S(2)}) %collective-permute-start.6) | collective-permute-done | bytes 223520 | tf_op jit(solution)/shard_map/ppermute | solution.py:79
  53.3 0.5 slice.154
  54.8 0.8 abs_reduce_fusion.3
  59.9 1.6 %collective-permute-start.3 = (f16[97,288]{0,1:T(8,128)(2,1)S(1)}, f16[97,288]{0,1:T(8,128)(2,1)S(1)}, u32[]{:S(2)}, u32[]{:S(2)}) collective-permute-start(f16[97,288]{0,1:T(8,128)(2,1)S(1)} %concatenate.38), channel_id=1, source_target_pairs={{0,2},{1,3},{2,4},{3,5},{4,6},{5,7},{6,0},{7,1},{8,10},{9,11},{10,... | collective-permute-start | bytes 167624 | tf_op jit(solution)/shard_map/ppermute | solution.py:47
  61.7 2.7 %collective-permute-start.4 = (f16[97,288]{0,1:T(8,128)(2,1)S(1)}, f16[97,288]{0,1:T(8,128)(2,1)S(1)}, u32[]{:S(2)}, u32[]{:S(2)}) collective-permute-start(f16[97,288]{0,1:T(8,128)(2,1)S(1)} %concatenate.39), channel_id=1, source_target_pairs={{0,4},{1,5},{2,6},{3,7},{4,0},{5,1},{6,2},{7,3},{8,12},{9,13},{10,... | collective-permute-start | bytes 167624 | tf_op jit(solution)/shard_map/ppermute | solution.py:47
  64.5 1.4 %collective-permute-start.5 = (f16[97,288]{0,1:T(8,128)(2,1)S(1)}, f16[97,288]{0,1:T(8,128)(2,1)S(1)}, u32[]{:S(2)}, u32[]{:S(2)}) collective-permute-start(f16[97,288]{0,1:T(8,128)(2,1)S(1)} %concatenate.40), channel_id=1, source_target_pairs={{0,6},{1,7},{2,0},{3,1},{4,2},{5,3},{6,4},{7,5},{8,14},{9,15},{10,... | collective-permute-start | bytes 167624 | tf_op jit(solution)/shard_map/ppermute | solution.py:47
  66.2 0.7 collective-permute-start.7
  67.5 2.9 %collective-permute-start.9 = (f16[97,288]{0,1:T(8,128)(2,1)S(1)}, f16[97,288]{0,1:T(8,128)(2,1)S(1)}, u32[]{:S(2)}, u32[]{:S(2)}) collective-permute-start(f16[97,288]{0,1:T(8,128)(2,1)S(1)} %concatenate.43), channel_id=1, source_target_pairs={{0,6},{1,7},{2,0},{3,1},{4,2},{5,3},{6,4},{7,5},{8,14},{9,15},{10,... | collective-permute-start | bytes 167624 | tf_op jit(solution)/shard_map/ppermute | solution.py:47
  70.4 2.4 %fusion.11 = bf16[1,128,768]{2,1,0:T(8,128)(2,1)} fusion(f32[128,768]{1,0:T(8,128)S(1)} %copy-done.4, f32[128,768]{1,0:T(8,128)S(1)} %copy-done.1, bf16[768,2304]{1,0:T(8,128)(2,1)} %param.5, bf16[1,128,768]{2,1,0:T(8,128)(2,1)S(1)} %copy-done.3, bf16[1,64,768]{2,1,0:T(8,128)(2,1)} %collective-permute-done, bf16[1,128,768]{2,1,0:T(8,128)(2,1)S(1)} %copy-done), kind=kOutput, calls=%fused_computation.14 | convolution fusion | flops 152666112 | bytes 2654208 | tf_op jit(solution)/shard_map/dot_general | solution.py:98
  74.1 0.5 slice.149
  75.3 0.5 slice.151
  76.5 0.5 slice.156
  80.7 0.9 %copy.16 = f32[192,288]{1,0:T(8,128)} copy(f32[192,288]{0,1:T(8,128)S(1)} %pad_maximum_fusion) | data formatting | bytes 442368
  (54 shorter events, 7.1 us)
Async XLA Ops:
  0.6 8.6 %copy-start = (bf16[1,128,768]{2,1,0:T(8,128)(2,1)S(1)}, bf16[1,128,768]{2,1,0:T(8,128)(2,1)}, u32[]{:S(2)}) copy-start(bf16[1,128,768]{2,1,0:T(8,128)(2,1)} %param.4) | copy-start | bytes 589828
  0.6 12.5 %copy-start.2 = (bf16[1,128,768]{2,1,0:T(8,128)(2,1)S(1)}, bf16[1,128,768]{2,1,0:T(8,128)(2,1)}, u32[]{:S(2)}) copy-start(bf16[1,128,768]{2,1,0:T(8,128)(2,1)} %param.3) | copy-start | bytes 589828
  5.0 21.9 %all-to-all-start = ((bf16[4,2,12288]{2,1,0:T(2,128)(2,1)}), bf16[4,2,12288]{2,1,0:T(2,128)(2,1)S(1)}, u32[]{:S(2)}, u32[]{:S(2)}) async-start(bf16[4,2,12288]{2,1,0:T(2,128)(2,1)} %reshape.120), calls=%async_computation | async-start | bytes 393216 | tf_op jit(solution)/shard_map/all_to_all | solution.py:108
  9.3 24.3 %collective-permute-start.1 = (bf16[1,64,768]{2,1,0:T(8,128)(2,1)S(1)}, bf16[1,64,768]{2,1,0:T(8,128)(2,1)S(1)}, u32[]{:S(2)}, u32[]{:S(2)}) collective-permute-start(bf16[1,64,768]{2,1,0:T(8,128)(2,1)S(1)} %get-tuple-element.25), channel_id=1, source_target_pairs={{0,8},{8,16},{16,24},{1,9},{9,17},{17,25},{2,10},{10,18},{18,26},{... | collective-permute-start | bytes 294920 | tf_op jit(solution)/shard_map/ppermute | solution.py:21
  11.7 55.4 %collective-permute-start = (bf16[1,64,768]{2,1,0:T(8,128)(2,1)S(1)}, bf16[1,64,768]{2,1,0:T(8,128)(2,1)}, u32[]{:S(2)}, u32[]{:S(2)}) collective-permute-start(bf16[1,64,768]{2,1,0:T(8,128)(2,1)S(1)} %get-tuple-element.24), channel_id=1, source_target_pairs={{8,0},{16,8},{24,16},{9,1},{17,9},{25,17},{10,2},{18,10},{26,18},{... | collective-permute-start | bytes 294920 | tf_op jit(solution)/shard_map/ppermute | solution.py:22
  31.6 9.8 %collective-permute-start.2 = (f16[97,4,288]{0,2,1:T(8,128)(2,1)}, f16[97,4,288]{0,2,1:T(8,128)(2,1)}, u32[]{:S(2)}, u32[]{:S(2)}) collective-permute-start(f16[97,4,288]{0,2,1:T(8,128)(2,1)} %concatenate.36), channel_id=1, source_target_pairs={{0,1},{1,0},{2,3},{3,2},{4,5},{5,4},{6,7},{7,6},{8,9},{9,8},{10,11... | collective-permute-start | bytes 670472 | tf_op jit(solution)/shard_map/ppermute | solution.py:79
  44.0 9.0 %collective-permute-start.6 = (f16[97,4,288]{0,2,1:T(8,128)(2,1)}, f16[97,4,288]{0,2,1:T(8,128)(2,1)S(1)}, u32[]{:S(2)}, u32[]{:S(2)}) collective-permute-start(f16[97,4,288]{0,2,1:T(8,128)(2,1)} %concatenate.37), channel_id=1, source_target_pairs={{0,1},{1,0},{2,3},{3,2},{4,5},{5,4},{6,7},{7,6},{8,9},{9,8},{10,11... | collective-permute-start | bytes 670472 | tf_op jit(solution)/shard_map/ppermute | solution.py:79
  54.8 15.6 %copy-start.1 = (f32[128,768]{1,0:T(8,128)S(1)}, f32[128,768]{1,0:T(8,128)}, u32[]{:S(2)}) copy-start(f32[128,768]{1,0:T(8,128)} %fusion.5) | copy-start | bytes 1179652
  54.8 15.6 %copy-start.3 = (bf16[1,128,768]{2,1,0:T(8,128)(2,1)S(1)}, bf16[1,128,768]{2,1,0:T(8,128)(2,1)}, u32[]{:S(2)}) copy-start(bf16[1,128,768]{2,1,0:T(8,128)(2,1)} %param.3) | copy-start | bytes 589828
  54.8 15.6 %copy-start.4 = (f32[128,768]{1,0:T(8,128)S(1)}, f32[128,768]{1,0:T(8,128)}, u32[]{:S(2)}) copy-start(f32[128,768]{1,0:T(8,128)} %fusion.3) | copy-start | bytes 1179652
  59.9 7.6 %collective-permute-start.3 = (f16[97,288]{0,1:T(8,128)(2,1)S(1)}, f16[97,288]{0,1:T(8,128)(2,1)S(1)}, u32[]{:S(2)}, u32[]{:S(2)}) collective-permute-start(f16[97,288]{0,1:T(8,128)(2,1)S(1)} %concatenate.38), channel_id=1, source_target_pairs={{0,2},{1,3},{2,4},{3,5},{4,6},{5,7},{6,0},{7,1},{8,10},{9,11},{10,... | collective-permute-start | bytes 167624 | tf_op jit(solution)/shard_map/ppermute | solution.py:47
  61.7 12.4 %collective-permute-start.4 = (f16[97,288]{0,1:T(8,128)(2,1)S(1)}, f16[97,288]{0,1:T(8,128)(2,1)S(1)}, u32[]{:S(2)}, u32[]{:S(2)}) collective-permute-start(f16[97,288]{0,1:T(8,128)(2,1)S(1)} %concatenate.39), channel_id=1, source_target_pairs={{0,4},{1,5},{2,6},{3,7},{4,0},{5,1},{6,2},{7,3},{8,12},{9,13},{10,... | collective-permute-start | bytes 167624 | tf_op jit(solution)/shard_map/ppermute | solution.py:47
  64.5 10.8 %collective-permute-start.5 = (f16[97,288]{0,1:T(8,128)(2,1)S(1)}, f16[97,288]{0,1:T(8,128)(2,1)S(1)}, u32[]{:S(2)}, u32[]{:S(2)}) collective-permute-start(f16[97,288]{0,1:T(8,128)(2,1)S(1)} %concatenate.40), channel_id=1, source_target_pairs={{0,6},{1,7},{2,0},{3,1},{4,2},{5,3},{6,4},{7,5},{8,14},{9,15},{10,... | collective-permute-start | bytes 167624 | tf_op jit(solution)/shard_map/ppermute | solution.py:47
  66.2 10.3 %collective-permute-start.7 = (f16[97,288]{0,1:T(8,128)(2,1)S(1)}, f16[97,288]{0,1:T(8,128)(2,1)S(1)}, u32[]{:S(2)}, u32[]{:S(2)}) collective-permute-start(f16[97,288]{0,1:T(8,128)(2,1)S(1)} %concatenate.41), channel_id=1, source_target_pairs={{0,2},{1,3},{2,4},{3,5},{4,6},{5,7},{6,0},{7,1},{8,10},{9,11},{10,... | collective-permute-start | bytes 167624 | tf_op jit(solution)/shard_map/ppermute | solution.py:47
  67.1 10.6 %collective-permute-start.8 = (f16[97,288]{0,1:T(8,128)(2,1)S(1)}, f16[97,288]{0,1:T(8,128)(2,1)S(1)}, u32[]{:S(2)}, u32[]{:S(2)}) collective-permute-start(f16[97,288]{0,1:T(8,128)(2,1)S(1)} %concatenate.42), channel_id=1, source_target_pairs={{0,4},{1,5},{2,6},{3,7},{4,0},{5,1},{6,2},{7,3},{8,12},{9,13},{10,... | collective-permute-start | bytes 167624 | tf_op jit(solution)/shard_map/ppermute | solution.py:47
  67.5 11.4 %collective-permute-start.9 = (f16[97,288]{0,1:T(8,128)(2,1)S(1)}, f16[97,288]{0,1:T(8,128)(2,1)S(1)}, u32[]{:S(2)}, u32[]{:S(2)}) collective-permute-start(f16[97,288]{0,1:T(8,128)(2,1)S(1)} %concatenate.43), channel_id=1, source_target_pairs={{0,6},{1,7},{2,0},{3,1},{4,2},{5,3},{6,4},{7,5},{8,14},{9,15},{10,... | collective-permute-start | bytes 167624 | tf_op jit(solution)/shard_map/ppermute | solution.py:47

commit v5 on v4

--- a/solution.py
+++ b/solution.py
@@ -7,7 +7,7 @@
 
 KW = 3
 TAP_SPACING = 64
-CHUNKS = 2
+CHUNKS = 1
 HEADROOM = 12.0
 
 
@@ -86,21 +86,9 @@
     reach = middle_offset * TAP_SPACING
     length = inputs.shape[1]
     in_width = inputs.shape[2]
-    padded_input = extended_2(cotangent, (("seq", 1),), reach)
-    extended = padded_input[0]
     values = inputs[0].astype(jnp.float32)
     activation, deriv = gelu_factors(values)
     act = activation.astype(jnp.bfloat16)
-    grad_act = jnp.zeros((length, in_width), jnp.float32)
-    for tap_index in range(KW):
-        window_start = (2 * middle_offset - tap_index) * TAP_SPACING
-        window = lax.slice_in_dim(extended, window_start, window_start + length, axis=0)
-        grad_act = grad_act + jnp.dot(
-            window,
-            weight[:, tap_index * in_width : (tap_index + 1) * in_width],
-            preferred_element_type=jnp.float32,
-        )
-    grad_input = (grad_act * deriv).astype(jnp.bfloat16)[None]
     seq_count = lax.axis_size("seq")
     batch_count = lax.axis_size("batch")
     counted = batch_count * inputs.shape[0] * length * seq_count
@@ -121,6 +109,19 @@
         )
     taps_sum = jnp.stack(updated, axis=0)
     local_rows = jnp.transpose(taps_sum, (1, 0, 2)).reshape(own_rows, KW * in_width) * factor
+    local_rows, cotangent, deriv = lax.optimization_barrier((local_rows, cotangent, deriv))
+    padded_input = extended_2(cotangent, (("seq", 1),), reach)
+    extended = padded_input[0]
+    grad_act = jnp.zeros((length, in_width), jnp.float32)
+    for tap_index in range(KW):
+        window_start = (2 * middle_offset - tap_index) * TAP_SPACING
+        window = lax.slice_in_dim(extended, window_start, window_start + length, axis=0)
+        grad_act = grad_act + jnp.dot(
+            window,
+            weight[:, tap_index * in_width : (tap_index + 1) * in_width],
+            preferred_element_type=jnp.float32,
+        )
+    grad_input = (grad_act * deriv).astype(jnp.bfloat16)[None]
     if batch_count == 8:
         grad_weight = reduce_over_batch(local_rows, CHUNKS)
     else:

time: 82.2 us -> 79.7 us (0.970)
  waiting for transfers between devices: 8.61 us -> 14.8 us
  between operations: 12.4 us -> 6.62 us
  starting transfers between devices: 21.4 us -> 16.8 us
  local copies, waits for them, and re-layouts: 13.1 us -> 16.6 us
  blocking collectives: 11.4 us -> 10.3 us
  other arithmetic: 6.49 us -> 5.64 us
    ppermute x6 -> x3, waiting for transfers between devices: 0.02 us -> 5.02 us  [send(): return decode(lax.ppermute(encode(values), 'batch', perm))]
    ppermute x6 -> x3, starting transfers between devices: 9.71 us -> 5.52 us  [send(): return decode(lax.ppermute(encode(values), 'batch', perm))]
    reshape x0 -> x1, local copies, waits for them, and re-layouts: none -> 4.05 us  [reduce_over_batch(): blocks = part.reshape(step, outer, 2, -1)]
    slice x10 -> x5, local copies, waits for them, and re-layouts: 5.69 us -> 2.36 us  [decode(): exponent = packed[0].reshape(-1)[0].astype(jnp.float32)]
    dynamic_slice x0 -> x1, local copies, waits for them, and re-layouts: none -> 3.04 us  [reduce_over_batch(): lax.dynamic_index_in_dim(blocks, 1 - x, axis=2, keepdims=False)]
    concatenate x8 -> x4, local copies, waits for them, and re-layouts: 2.52 us -> 0.55 us  [encode(): return jnp.concatenate([tag, scaled], axis=0)]
    ppermute x2 -> x1, starting transfers between devices: 3.76 us -> 2.1 us  [reduce_over_batch(): pending = (mine, lax.ppermute(theirs, 'batch', pairs))]
    mul x0 -> x1, local copies, waits for them, and re-layouts: none -> 1.34 us  [body(): jnp.transpose(taps_sum, (1, 0, 2)).reshape(own_rows, KW * in_width) * factor]
  transfers between devices with their start and end apart: 11 -> 7, of which waited for: 2 -> 3; matrix products, arithmetic and copies ran while one was open for 26% -> 26% of each run, Pallas kernels for 0% -> 0%
where the time goes in v5:
time: 79.7 us; the launch traced here: 78.3 us
  starting transfers between devices  16.8 us (21%)
  local copies, waits for them, and re-layouts  16.6 us (21%)
  waiting for transfers between devices  14.8 us (19%)
  blocking collectives  10.3 us (13%)
  matrix products  7.45 us (9%)
  between operations  6.62 us (8%)
  other arithmetic  5.64 us (7%)
    all_gather x1, blocking collectives, body(): whole_act = lax.all_gather(act[None], 'seq', axis=1, tiled=True)[0]  10.3 us
    ppermute x1, waiting for transfers between devices, reduce_over_batch(): pending = (mine, lax.ppermute(theirs, 'batch', pairs))  9.75 us
    dot_general x3, matrix products, body(): jnp.dot(window, weight[:, tap_index * in_width:(tap_index + 1) * in_width...  6.37 us
    ppermute x3, starting transfers between devices, send(): return decode(lax.ppermute(encode(values), 'batch', perm))  5.52 us
    ppermute x3, waiting for transfers between devices, send(): return decode(lax.ppermute(encode(values), 'batch', perm))  5.02 us
    all_to_all x1, starting transfers between devices, body(): lax.all_to_all(cotangent, 'seq', split_axis=2, concat_axis=1, tiled=True)[0]  4.24 us
    reshape x1, local copies, waits for them, and re-layouts, reduce_over_batch(): blocks = part.reshape(step, outer, 2, -1)  4.05 us
    unnamed x20, local copies, waits for them, and re-layouts  3.98 us
  transfers between devices with their start and end apart: 7, of which 3 were waited for; matrix products, arithmetic and copies ran while one was open for 26% of the time, Pallas kernels for 0%

profile of v5, /device:TPU:0, one launch (start us, length us, event | category | flops | bytes accessed | tf_op | source)
XLA Modules:
  0.0 78.3 jit_solution(14614929384795829708)
XLA Ops:
  0.6 1.3 %copy.26 = bf16[1,128,768]{1,0,2:T(2,128)(2,1)S(1)} copy(bf16[1,128,768]{2,1,0:T(8,128)(2,1)} %param.4) | data formatting | bytes 393216 | tf_op args[1]
  2.0 0.5 broadcast.33
  2.5 1.8 %reduce.6 = bf16[768,128]{1,0:T(8,128)(2,1)S(1)} reduce(bf16[768,1,128]{2,1,0:T(2,128)(2,1)S(1)} %bitcast.93, bf16[]{:T(256)} %broadcast.33), dimensions={1}, to_apply=%bitcast.84.reduce_sub_computation | reduce | bytes 393218
  4.3 0.7 reshape.65
  5.0 4.2 %all-to-all-start = ((bf16[4,2,12288]{2,1,0:T(2,128)(2,1)}), bf16[4,2,12288]{2,1,0:T(2,128)(2,1)S(1)}, u32[]{:S(2)}, u32[]{:S(2)}) async-start(bf16[4,2,12288]{2,1,0:T(2,128)(2,1)} %reshape.65), calls=%async_computation | async-start | bytes 393216 | tf_op jit(solution)/shard_map/all_to_all | solution.py:96
  9.3 10.3 %all_gather.3 = bf16[1,512,768]{2,1,0:T(8,128)(2,1)S(1)} all-gather(bf16[1,128,768]{2,1,0:T(8,128)(2,1)S(1)} %fusion.27), channel_id=1, replica_groups=mesh['seq'=4,'batch'=8] {'seq'}, dimensions={1}, use_global_device_ids=true | all-gather | bytes 983040 | tf_op jit(solution)/shard_map/all_gather | solution.py:99
  19.7 0.9 %fusion.23 = f32[128,768]{1,0:T(8,128)} fusion(bf16[1,128,768]{2,1,0:T(8,128)(2,1)S(1)} %copy-done.4), kind=kLoop, calls=%fused_computation.31 | loop fusion | flops 884736 | bytes 589824 | tf_op jit(solution)/shard_map/add | solution.py:30
  22.2 1.3 %copy.37 = f32[3,24,8,768]{3,2,0,1:T(8,128)} copy(f32[3,24,8,768]{3,2,1,0:T(8,128)S(1)} %fusion) | data formatting | bytes 3538944 | tf_op jit(solution)/shard_map/mul | solution.py:111
  23.6 0.7 fusion.46
  24.3 1.3 %collective-permute-start = (bf16[1,64,768]{2,1,0:T(8,128)(2,1)}, bf16[1,64,768]{2,1,0:T(8,128)(2,1)}, u32[]{:S(2)}, u32[]{:S(2)}) collective-permute-start(bf16[1,64,768]{2,1,0:T(8,128)(2,1)} %get-tuple-element.16), channel_id=1, source_target_pairs={{8,0},{16,8},{24,16},{9,1},{17,9},{25,17},{10,2},{18,10},{26,18},{... | collective-permute-start | bytes 294920 | tf_op jit(solution)/shard_map/ppermute | solution.py:22
  25.6 3.7 %collective-permute-start.1 = (bf16[1,64,768]{2,1,0:T(8,128)(2,1)}, bf16[1,64,768]{2,1,0:T(8,128)(2,1)}, u32[]{:S(2)}, u32[]{:S(2)}) collective-permute-start(bf16[1,64,768]{2,1,0:T(8,128)(2,1)} %get-tuple-element.17), channel_id=1, source_target_pairs={{0,8},{8,16},{16,24},{1,9},{9,17},{17,25},{2,10},{10,18},{18,26},{... | collective-permute-start | bytes 294920 | tf_op jit(solution)/shard_map/ppermute | solution.py:21
  29.2 4.0 %reshape.62 = f32[192,4,2,288]{3,2,1,0:T(2,128)S(1)} reshape(f32[192,2304]{1,0:T(8,128)} %bitcast.87) | data formatting | bytes 3538944 | tf_op jit(solution)/shard_map/reshape | solution.py:72
  33.3 3.0 %constant_dynamic-slice_fusion = (f32[192,4,1,288]{3,2,1,0:T(1,128)S(1)}, f32[192,4,1,288]{3,2,1,0:T(1,128)}) fusion(f32[192,4,2,288]{3,2,1,0:T(2,128)S(1)} %reshape.62, s32[]{:T(128)S(6)} %select_n.45, s32[]{:T(128)S(6)} %select_n.44), kind=kLoop, calls=%fused_computation.61 | loop fusion | bytes 3538952 | tf_op jit(solution)/shard_map/jit(dynamic_index_in_dim)/dynamic_slice | solution.py:74
  36.3 0.8 abs_reduce_fusion
  38.0 0.6 copy.36
  38.9 2.1 %collective-permute-start.2 = (f16[193,4,288]{0,2,1:T(8,128)(2,1)S(1)}, f16[193,4,288]{0,2,1:T(8,128)(2,1)S(1)}, u32[]{:S(2)}, u32[]{:S(2)}) collective-permute-start(f16[193,4,288]{0,2,1:T(8,128)(2,1)S(1)} %concatenate.21.clone), channel_id=1, source_target_pairs={{0,1},{1,0},{2,3},{3,2},{4,5},{5,4},{6,7},{7,6},{8,9},{9,8},{10,11... | collective-permute-start | bytes 1334024 | tf_op jit(solution)/shard_map/ppermute | solution.py:79
  41.0 1.6 %fusion.5 = f32[128,768]{1,0:T(8,128)S(1)} fusion(bf16[768,2304]{1,0:T(8,128)(2,1)} %param.5, bf16[1,128,768]{2,1,0:T(8,128)(2,1)S(1)} %copy-done.2), kind=kOutput, calls=%fused_computation.13 | convolution fusion | flops 150994944 | bytes 1769472 | tf_op jit(solution)/shard_map/dot_general | solution.py:119
  42.6 2.4 %fusion.3 = f32[128,768]{1,0:T(8,128)} fusion(bf16[768,2304]{1,0:T(8,128)(2,1)} %param.5, bf16[1,128,768]{2,1,0:T(8,128)(2,1)S(1)} %copy-done.2, bf16[1,64,768]{2,1,0:T(8,128)(2,1)} %collective-permute-done.1), kind=kOutput, calls=%fused_computation.11 | convolution fusion | flops 151388160 | bytes 1867776 | tf_op jit(solution)/shard_map/dot_general | solution.py:119
  45.1 9.8 %collective-permute-done.2 = f16[193,4,288]{0,2,1:T(8,128)(2,1)S(1)} collective-permute-done((f16[193,4,288]{0,2,1:T(8,128)(2,1)S(1)}, f16[193,4,288]{0,2,1:T(8,128)(2,1)S(1)}, u32[]{:S(2)}, u32[]{:S(2)}) %collective-permute-start.2) | collective-permute-done | bytes 444704 | tf_op jit(solution)/shard_map/ppermute | solution.py:79
  55.2 0.6 copy.35
  56.2 0.5 slice.90
  57.6 0.7 abs_reduce_fusion.3
  60.7 3.4 %collective-permute-start.4 = (f16[193,288]{1,0:T(8,128)(2,1)S(1)}, f16[193,288]{1,0:T(8,128)(2,1)S(1)}, u32[]{:S(2)}, u32[]{:S(2)}) collective-permute-start(f16[193,288]{1,0:T(8,128)(2,1)S(1)} %concatenate.23), channel_id=1, source_target_pairs={{0,4},{1,5},{2,6},{3,7},{4,0},{5,1},{6,2},{7,3},{8,12},{9,13},{10,... | collective-permute-start | bytes 333512 | tf_op jit(solution)/shard_map/ppermute | solution.py:47
  64.2 1.4 %collective-permute-start.5 = (f16[193,288]{1,0:T(8,128)(2,1)S(1)}, f16[193,288]{1,0:T(8,128)(2,1)S(1)}, u32[]{:S(2)}, u32[]{:S(2)}) collective-permute-start(f16[193,288]{1,0:T(8,128)(2,1)S(1)} %concatenate.24), channel_id=1, source_target_pairs={{0,6},{1,7},{2,0},{3,1},{4,2},{5,3},{6,4},{7,5},{8,14},{9,15},{10,... | collective-permute-start | bytes 333512 | tf_op jit(solution)/shard_map/ppermute | solution.py:47
  65.6 0.7 collective-permute-start.3
  66.4 2.3 %fusion.11 = bf16[1,128,768]{2,1,0:T(8,128)(2,1)} fusion(f32[128,768]{1,0:T(8,128)S(1)} %copy-done.3, f32[128,768]{1,0:T(8,128)S(1)} %copy-done.5, f32[128,768]{1,0:T(8,128)S(1)} %fusion.5, bf16[768,2304]{1,0:T(8,128)(2,1)} %param.5, bf16[1,64,768]{2,1,0:T(8,128)(2,1)} %collective-permute-done, bf16[1,128,768]{2,1,0:T(8,128)(2,1)S(1)} %copy-done.2), kind=kOutput, calls=%fused_computation.17 | convolution fusion | flops 151781376 | bytes 2850816 | tf_op jit(solution)/shard_map/dot_general | solution.py:119
  68.7 3.7 %collective-permute-done.4 = f16[193,288]{1,0:T(8,128)(2,1)S(1)} collective-permute-done((f16[193,288]{1,0:T(8,128)(2,1)S(1)}, f16[193,288]{1,0:T(8,128)(2,1)S(1)}, u32[]{:S(2)}, u32[]{:S(2)}) %collective-permute-start.4) | collective-permute-done | bytes 111200 | tf_op jit(solution)/shard_map/ppermute | solution.py:47
  72.4 0.5 slice.94
  73.6 0.5 slice.96
  74.8 1.3 %collective-permute-done.3 = f16[193,288]{1,0:T(8,128)(2,1)S(1)} collective-permute-done((f16[193,288]{1,0:T(8,128)(2,1)S(1)}, f16[193,288]{1,0:T(8,128)(2,1)S(1)}, u32[]{:S(2)}, u32[]{:S(2)}) %collective-permute-start.3) | collective-permute-done | bytes 111200 | tf_op jit(solution)/shard_map/ppermute | solution.py:47
  76.2 0.5 slice.92
  77.4 0.9 %fusion.31 = f32[192,288]{1,0:T(8,128)} fusion(f32[192,4,288]{2,0,1:T(8,128)S(1)} %bitcast_add_fusion, s32[]{:T(128)S(6)} %select_n.47, f16[193,288]{1,0:T(8,128)(2,1)S(1)} %collective-permute-done.5, f16[193,288]{1,0:T(8,128)(2,1)S(1)} %collective-permute-done.4, f16[193,288]{1,0:T(8,128)(2,1)S(1)} %collective-permute-done.3, f32[]{:T(128)} %bitcast.21, ...), kind=kLoop, calls=%fused_computation.41 | loop fusion | flops 497664 | bytes 774160 | tf_op jit(solution)/shard_map/add | solution.py:65
  (35 shorter events, 3.4 us)
Async XLA Ops:
  0.6 8.6 %copy-start.4 = (bf16[1,128,768]{2,1,0:T(8,128)(2,1)S(1)}, bf16[1,128,768]{2,1,0:T(8,128)(2,1)}, u32[]{:S(2)}) copy-start(bf16[1,128,768]{2,1,0:T(8,128)(2,1)} %param.3) | copy-start | bytes 589828
  5.0 15.6 %all-to-all-start = ((bf16[4,2,12288]{2,1,0:T(2,128)(2,1)}), bf16[4,2,12288]{2,1,0:T(2,128)(2,1)S(1)}, u32[]{:S(2)}, u32[]{:S(2)}) async-start(bf16[4,2,12288]{2,1,0:T(2,128)(2,1)} %reshape.65), calls=%async_computation | async-start | bytes 393216 | tf_op jit(solution)/shard_map/all_to_all | solution.py:96
  22.2 1.4 %copy-start.1 = (bf16[1,128,768]{2,1,0:T(8,128)(2,1)S(1)}, bf16[1,128,768]{2,1,0:T(8,128)(2,1)}, u32[]{:S(2)}) copy-start(bf16[1,128,768]{2,1,0:T(8,128)(2,1)} %param.4) | copy-start | bytes 589828
  24.3 42.1 %collective-permute-start = (bf16[1,64,768]{2,1,0:T(8,128)(2,1)}, bf16[1,64,768]{2,1,0:T(8,128)(2,1)}, u32[]{:S(2)}, u32[]{:S(2)}) collective-permute-start(bf16[1,64,768]{2,1,0:T(8,128)(2,1)} %get-tuple-element.16), channel_id=1, source_target_pairs={{8,0},{16,8},{24,16},{9,1},{17,9},{25,17},{10,2},{18,10},{26,18},{... | collective-permute-start | bytes 294920 | tf_op jit(solution)/shard_map/ppermute | solution.py:22
  25.6 17.1 %collective-permute-start.1 = (bf16[1,64,768]{2,1,0:T(8,128)(2,1)}, bf16[1,64,768]{2,1,0:T(8,128)(2,1)}, u32[]{:S(2)}, u32[]{:S(2)}) collective-permute-start(bf16[1,64,768]{2,1,0:T(8,128)(2,1)} %get-tuple-element.17), channel_id=1, source_target_pairs={{0,8},{8,16},{16,24},{1,9},{9,17},{17,25},{2,10},{10,18},{18,26},{... | collective-permute-start | bytes 294920 | tf_op jit(solution)/shard_map/ppermute | solution.py:21
  37.9 3.1 %copy-start.2 = (bf16[1,128,768]{2,1,0:T(8,128)(2,1)S(1)}, bf16[1,128,768]{2,1,0:T(8,128)(2,1)}, u32[]{:S(2)}) copy-start(bf16[1,128,768]{2,1,0:T(8,128)(2,1)} %param.4) | copy-start | bytes 589828
  38.9 15.9 %collective-permute-start.2 = (f16[193,4,288]{0,2,1:T(8,128)(2,1)S(1)}, f16[193,4,288]{0,2,1:T(8,128)(2,1)S(1)}, u32[]{:S(2)}, u32[]{:S(2)}) collective-permute-start(f16[193,4,288]{0,2,1:T(8,128)(2,1)S(1)} %concatenate.21.clone), channel_id=1, source_target_pairs={{0,1},{1,0},{2,3},{3,2},{4,5},{5,4},{6,7},{7,6},{8,9},{9,8},{10,11... | collective-permute-start | bytes 1334024 | tf_op jit(solution)/shard_map/ppermute | solution.py:79
  45.1 12.3 %copy-start = (f32[192,4,1,288]{3,2,1,0:T(1,128)S(1)}, f32[192,4,1,288]{3,2,1,0:T(1,128)}, u32[]{:S(2)}) copy-start(f32[192,4,1,288]{3,2,1,0:T(1,128)} %get-tuple-element.12) | copy-start | bytes 2654212
  58.3 8.1 %copy-start.3 = (f32[128,768]{1,0:T(8,128)S(1)}, f32[128,768]{1,0:T(8,128)}, u32[]{:S(2)}) copy-start(f32[128,768]{1,0:T(8,128)} %fusion.23) | copy-start | bytes 1179652
  58.3 8.1 %copy-start.5 = (f32[128,768]{1,0:T(8,128)S(1)}, f32[128,768]{1,0:T(8,128)}, u32[]{:S(2)}) copy-start(f32[128,768]{1,0:T(8,128)} %fusion.3) | copy-start | bytes 1179652
  60.7 11.7 %collective-permute-start.4 = (f16[193,288]{1,0:T(8,128)(2,1)S(1)}, f16[193,288]{1,0:T(8,128)(2,1)S(1)}, u32[]{:S(2)}, u32[]{:S(2)}) collective-permute-start(f16[193,288]{1,0:T(8,128)(2,1)S(1)} %concatenate.23), channel_id=1, source_target_pairs={{0,4},{1,5},{2,6},{3,7},{4,0},{5,1},{6,2},{7,3},{8,12},{9,13},{10,... | collective-permute-start | bytes 333512 | tf_op jit(solution)/shard_map/ppermute | solution.py:47
  64.2 9.4 %collective-permute-start.5 = (f16[193,288]{1,0:T(8,128)(2,1)S(1)}, f16[193,288]{1,0:T(8,128)(2,1)S(1)}, u32[]{:S(2)}, u32[]{:S(2)}) collective-permute-start(f16[193,288]{1,0:T(8,128)(2,1)S(1)} %concatenate.24), channel_id=1, source_target_pairs={{0,6},{1,7},{2,0},{3,1},{4,2},{5,3},{6,4},{7,5},{8,14},{9,15},{10,... | collective-permute-start | bytes 333512 | tf_op jit(solution)/shard_map/ppermute | solution.py:47
  65.6 10.5 %collective-permute-start.3 = (f16[193,288]{1,0:T(8,128)(2,1)S(1)}, f16[193,288]{1,0:T(8,128)(2,1)S(1)}, u32[]{:S(2)}, u32[]{:S(2)}) collective-permute-start(f16[193,288]{1,0:T(8,128)(2,1)S(1)} %concatenate.22), channel_id=1, source_target_pairs={{0,2},{1,3},{2,4},{3,5},{4,6},{5,7},{6,0},{7,1},{8,10},{9,11},{10,... | collective-permute-start | bytes 333512 | tf_op jit(solution)/shard_map/ppermute | solution.py:47

commit v6 on v5

--- a/solution.py
+++ b/solution.py
@@ -7,8 +7,8 @@
 
 KW = 3
 TAP_SPACING = 64
-CHUNKS = 1
 HEADROOM = 12.0
+TAG = 16
 
 
 def extended_2(x, sides, width):
@@ -34,51 +34,36 @@
     biggest = jnp.maximum(jnp.max(jnp.abs(values)), 1e-30)
     exponent = jnp.floor(jnp.log2(biggest))
     scaled = (values * jnp.exp2(HEADROOM - exponent)).astype(jnp.float16)
-    tag = jnp.full((1,) + values.shape[1:], exponent, jnp.float16)
-    return jnp.concatenate([tag, scaled], axis=0)
+    tag = jnp.full(values.shape[:-2] + (TAG, values.shape[-1]), exponent, jnp.float16)
+    return jnp.concatenate([scaled, tag], axis=-2)
 
 
 def decode(packed):
-    exponent = packed[0].reshape(-1)[0].astype(jnp.float32)
-    return packed[1:].astype(jnp.float32) * jnp.exp2(exponent - HEADROOM)
+    exponent = packed[(0,) * (packed.ndim - 2) + (-TAG, 0)].astype(jnp.float32)
+    return packed[..., :-TAG, :].astype(jnp.float32) * jnp.exp2(exponent - HEADROOM)
 
 
 def send(values, perm):
     return decode(lax.ppermute(encode(values), "batch", perm))
 
 
-def reduce_over_batch(rows, chunks):
+def reduce_over_batch(columns):
     count = lax.axis_size("batch")
     outer = count // 2
     me = lax.axis_index("batch")
     x = me % 2
     z = me // 2
     pairs = [(i, i ^ 1) for i in range(count)]
-    step = rows.shape[0] // chunks
-
-    def finish(mine, packed):
-        summed = mine + decode(packed)
-        total = lax.dynamic_index_in_dim(summed, z, axis=1, keepdims=False)
-        for shift in range(1, outer):
-            target = lax.dynamic_index_in_dim(summed, (z + shift) % outer, axis=1, keepdims=False)
-            perm = [(2 * q + p, 2 * ((q + shift) % outer) + p) for q in range(outer) for p in range(2)]
-            total = total + send(target, perm)
-        return total
-
-    results = []
-    pending = None
-    for chunk in range(chunks):
-        part = rows[chunk * step : (chunk + 1) * step]
-        blocks = part.reshape(step, outer, 2, -1)
-        mine = lax.dynamic_index_in_dim(blocks, x, axis=2, keepdims=False)
-        theirs = encode(lax.dynamic_index_in_dim(blocks, 1 - x, axis=2, keepdims=False))
-        if pending is not None:
-            kept, arrived = pending
-            arrived, theirs = lax.optimization_barrier((arrived, theirs))
-            results.append(finish(kept, arrived))
-        pending = (mine, lax.ppermute(theirs, "batch", pairs))
-    results.append(finish(*pending))
-    return jnp.concatenate(results, axis=0)
+    blocks = columns.reshape(outer, 2, -1, columns.shape[1])
+    mine = lax.dynamic_index_in_dim(blocks, x, axis=1, keepdims=False)
+    theirs = lax.dynamic_index_in_dim(blocks, 1 - x, axis=1, keepdims=False)
+    summed = mine + send(theirs, pairs)
+    total = lax.dynamic_index_in_dim(summed, z, axis=0, keepdims=False)
+    for shift in range(1, outer):
+        target = lax.dynamic_index_in_dim(summed, (z + shift) % outer, axis=0, keepdims=False)
+        perm = [(2 * q + p, 2 * ((q + shift) % outer) + p) for q in range(outer) for p in range(2)]
+        total = total + send(target, perm)
+    return total.T
 
 
 def body(inputs, cotangent, weight):
@@ -104,12 +89,11 @@
         window = lax.dynamic_slice_in_dim(owned_padded, offset, count, 0)
         updated.append(
             lax.dot_general(
-                window, whole_act, (((0,), (0,)), ((), ())), preferred_element_type=jnp.float32
+                whole_act, window, (((0,), (0,)), ((), ())), preferred_element_type=jnp.float32
             )
         )
-    taps_sum = jnp.stack(updated, axis=0)
-    local_rows = jnp.transpose(taps_sum, (1, 0, 2)).reshape(own_rows, KW * in_width) * factor
-    local_rows, cotangent, deriv = lax.optimization_barrier((local_rows, cotangent, deriv))
+    local_columns = jnp.concatenate(updated, axis=0) * factor
+    local_columns, cotangent, deriv = lax.optimization_barrier((local_columns, cotangent, deriv))
     padded_input = extended_2(cotangent, (("seq", 1),), reach)
     extended = padded_input[0]
     grad_act = jnp.zeros((length, in_width), jnp.float32)
@@ -123,11 +107,11 @@
         )
     grad_input = (grad_act * deriv).astype(jnp.bfloat16)[None]
     if batch_count == 8:
-        grad_weight = reduce_over_batch(local_rows, CHUNKS)
+        grad_weight = reduce_over_batch(local_columns)
     else:
-        pieces = local_rows.reshape(own_rows, batch_count, -1)
-        swapped = lax.all_to_all(pieces, "batch", split_axis=1, concat_axis=1, tiled=True)
-        grad_weight = jnp.sum(swapped, axis=1)
+        pieces = local_columns.reshape(batch_count, -1, own_rows)
+        swapped = lax.all_to_all(pieces, "batch", split_axis=0, concat_axis=0, tiled=True)
+        grad_weight = jnp.sum(swapped, axis=0).T
     return (grad_input, grad_weight)
 
 

time: 79.7 us -> 77 us (0.966)
  local copies, waits for them, and re-layouts: 16.6 us -> 13.3 us
  other arithmetic: 5.64 us -> 6.8 us
    ppermute x3 -> x4, waiting for transfers between devices: 5.02 us -> 15.1 us  [send(): return decode(lax.ppermute(encode(values), 'batch', perm))]
    ppermute x1 -> x0, waiting for transfers between devices: 9.75 us -> none  [reduce_over_batch(): pending = (mine, lax.ppermute(theirs, 'batch', pairs))]
    ppermute x3 -> x4, starting transfers between devices: 5.52 us -> 7.69 us  [send(): return decode(lax.ppermute(encode(values), 'batch', perm))]
    ppermute x1 -> x0, starting transfers between devices: 2.1 us -> none  [reduce_over_batch(): pending = (mine, lax.ppermute(theirs, 'batch', pairs))]
    mul x1 -> x0, local copies, waits for them, and re-layouts: 1.34 us -> none  [body(): jnp.transpose(taps_sum, (1, 0, 2)).reshape(own_rows, KW * in_width) * factor]
    mul x0 -> x1, other arithmetic: none -> 1.34 us  [body(): local_columns = jnp.concatenate(updated, axis=0) * factor]
    unnamed x20 -> x16, local copies, waits for them, and re-layouts: 3.98 us -> 2.81 us
    add x2 -> x1, other arithmetic: 1.01 us -> 0.14 us  [reduce_over_batch(): summed = mine + send(theirs, pairs)]
  transfers between devices with their start and end apart: 7 -> 7, of which waited for: 3 -> 3; matrix products, arithmetic and copies ran while one was open for 26% -> 23% of each run, Pallas kernels for 0% -> 0%
where the time goes in v6:
time: 77 us; the launch traced here: 75.7 us
  starting transfers between devices  16.9 us (22%)
  waiting for transfers between devices  15.1 us (20%)
  local copies, waits for them, and re-layouts  13.3 us (17%)
  blocking collectives  10.3 us (13%)
  other arithmetic  6.8 us (9%)
  matrix products  6.75 us (9%)
  between operations  6.56 us (9%)
    ppermute x4, waiting for transfers between devices, send(): return decode(lax.ppermute(encode(values), 'batch', perm))  15.1 us
    all_gather x1, blocking collectives, body(): whole_act = lax.all_gather(act[None], 'seq', axis=1, tiled=True)[0]  10.3 us
    ppermute x4, starting transfers between devices, send(): return decode(lax.ppermute(encode(values), 'batch', perm))  7.69 us
    dot_general x3, matrix products, body(): jnp.dot(window, weight[:, tap_index * in_width:(tap_index + 1) * in_width...  5.68 us
    all_to_all x1, starting transfers between devices, body(): lax.all_to_all(cotangent, 'seq', split_axis=2, concat_axis=1, tiled=True)[0]  4.24 us
    reshape x1, local copies, waits for them, and re-layouts, reduce_over_batch(): blocks = columns.reshape(outer, 2, -1, columns.shape[1])  4.05 us
    ppermute x1, starting transfers between devices, extended_2(): before = lax.ppermute(last, axis, up)  3.67 us
    dynamic_slice x1, local copies, waits for them, and re-layouts, reduce_over_batch(): theirs = lax.dynamic_index_in_dim(blocks, 1 - x, axis=1, keepdims=False)  3.05 us
  transfers between devices with their start and end apart: 7, of which 3 were waited for; matrix products, arithmetic and copies ran while one was open for 23% of the time, Pallas kernels for 0%

profile of v6, /device:TPU:0, one launch (start us, length us, event | category | flops | bytes accessed | tf_op | source)
XLA Modules:
  0.0 75.7 jit_solution(596006210432564610)
XLA Ops:
  0.6 1.3 %copy.11 = bf16[1,128,768]{1,0,2:T(2,128)(2,1)S(1)} copy(bf16[1,128,768]{2,1,0:T(8,128)(2,1)} %param.4) | data formatting | bytes 393216 | tf_op args[1]
  2.0 0.5 broadcast.28
  2.5 1.8 %reduce.4 = bf16[768,128]{1,0:T(8,128)(2,1)S(1)} reduce(bf16[768,1,128]{2,1,0:T(2,128)(2,1)S(1)} %bitcast.86, bf16[]{:T(256)} %broadcast.28), dimensions={1}, to_apply=%bitcast.78.reduce_sub_computation | reduce | bytes 393218
  4.3 0.7 reshape.55
  5.0 4.2 %all-to-all-start = ((bf16[4,2,12288]{2,1,0:T(2,128)(2,1)}), bf16[4,2,12288]{2,1,0:T(2,128)(2,1)S(1)}, u32[]{:S(2)}, u32[]{:S(2)}) async-start(bf16[4,2,12288]{2,1,0:T(2,128)(2,1)} %reshape.55), calls=%async_computation | async-start | bytes 393216 | tf_op jit(solution)/shard_map/all_to_all | solution.py:81
  9.3 10.3 %all_gather.3 = bf16[1,512,768]{2,1,0:T(8,128)(2,1)S(1)} all-gather(bf16[1,128,768]{2,1,0:T(8,128)(2,1)S(1)} %fusion.29), channel_id=1, replica_groups=mesh['seq'=4,'batch'=8] {'seq'}, dimensions={1}, use_global_device_ids=true | all-gather | bytes 983040 | tf_op jit(solution)/shard_map/all_gather | solution.py:84
  19.7 0.9 %fusion.25 = f32[128,768]{1,0:T(8,128)} fusion(bf16[1,128,768]{2,1,0:T(8,128)(2,1)S(1)} %copy-done.4), kind=kLoop, calls=%fused_computation.30 | loop fusion | flops 884736 | bytes 589824 | tf_op jit(solution)/shard_map/add | solution.py:30
  21.3 0.4 fusion.13
  21.7 0.4 fusion.17
  22.1 1.3 %maximum_multiply_fusion = f32[2304,192]{0,1:T(8,128)} fusion(f32[768,192]{0,1:T(8,128)S(1)} %fusion.17, f32[768,192]{0,1:T(8,128)S(1)} %fusion.15, f32[768,192]{0,1:T(8,128)S(1)} %fusion.13), kind=kLoop, calls=%fused_computation | loop fusion | flops 1327104 | bytes 3538944 | tf_op jit(solution)/shard_map/mul | solution.py:95
  23.4 0.7 fusion.49
  24.1 1.3 %collective-permute-start = (bf16[1,64,768]{2,1,0:T(8,128)(2,1)}, bf16[1,64,768]{2,1,0:T(8,128)(2,1)}, u32[]{:S(2)}, u32[]{:S(2)}) collective-permute-start(bf16[1,64,768]{2,1,0:T(8,128)(2,1)} %get-tuple-element.16), channel_id=1, source_target_pairs={{8,0},{16,8},{24,16},{9,1},{17,9},{25,17},{10,2},{18,10},{26,18},{... | collective-permute-start | bytes 294920 | tf_op jit(solution)/shard_map/ppermute | solution.py:22
  25.4 3.7 %collective-permute-start.1 = (bf16[1,64,768]{2,1,0:T(8,128)(2,1)}, bf16[1,64,768]{2,1,0:T(8,128)(2,1)}, u32[]{:S(2)}, u32[]{:S(2)}) collective-permute-start(bf16[1,64,768]{2,1,0:T(8,128)(2,1)} %get-tuple-element.17), channel_id=1, source_target_pairs={{0,8},{8,16},{16,24},{1,9},{9,17},{17,25},{2,10},{10,18},{18,26},{... | collective-permute-start | bytes 294920 | tf_op jit(solution)/shard_map/ppermute | solution.py:21
  29.1 4.0 %reshape.53 = f32[4,2,288,192]{2,1,0,3:T(2,128)S(1)} reshape(f32[2304,192]{0,1:T(8,128)} %maximum_multiply_fusion) | data formatting | bytes 3538944 | tf_op jit(solution)/shard_map/reshape | solution.py:57
  33.1 3.0 %constant_dynamic-slice_fusion = (f32[4,1,288,192]{2,1,0,3:T(1,128)S(1)}, f32[4,1,288,192]{2,1,0,3:T(1,128)}) fusion(f32[4,2,288,192]{2,1,0,3:T(2,128)S(1)} %reshape.53, s32[]{:T(128)S(6)} %select_n.45, s32[]{:T(128)S(6)} %select_n.44), kind=kLoop, calls=%fused_computation.60 | loop fusion | bytes 3538952 | tf_op jit(solution)/shard_map/jit(dynamic_index_in_dim)/dynamic_slice | solution.py:59
  36.2 0.8 %abs_reduce_fusion = f32[]{:T(128)} fusion(f32[4,1,288,192]{2,1,0,3:T(1,128)S(1)} %get-tuple-element.11), kind=kLoop, calls=%fused_computation.6 | loop fusion | flops 442367 | bytes 884740 | tf_op jit(solution)/shard_map/reduce_max | solution.py:34
  38.0 2.1 %collective-permute-start.2 = (f16[4,304,192]{1,2,0:T(8,128)(2,1)S(1)}, f16[4,304,192]{1,2,0:T(8,128)(2,1)S(1)}, u32[]{:S(2)}, u32[]{:S(2)}) collective-permute-start(f16[4,304,192]{1,2,0:T(8,128)(2,1)S(1)} %concatenate.25), channel_id=1, source_target_pairs={{0,1},{1,0},{2,3},{3,2},{4,5},{5,4},{6,7},{7,6},{8,9},{9,8},{10,11... | collective-permute-start | bytes 1400840 | tf_op jit(solution)/shard_map/ppermute | solution.py:47
  40.1 1.6 %fusion.4 = f32[128,768]{1,0:T(8,128)S(1)} fusion(bf16[768,2304]{1,0:T(8,128)(2,1)} %param.5, bf16[1,128,768]{2,1,0:T(8,128)(2,1)S(1)} %copy-done.2), kind=kOutput, calls=%fused_computation.9 | convolution fusion | flops 150994944 | bytes 1769472 | tf_op jit(solution)/shard_map/dot_general | solution.py:103
  41.7 1.7 %fusion.2 = f32[128,768]{1,0:T(8,128)S(1)} fusion(bf16[768,2304]{1,0:T(8,128)(2,1)} %param.5, bf16[1,128,768]{2,1,0:T(8,128)(2,1)S(1)} %copy-done.2, bf16[1,64,768]{2,1,0:T(8,128)(2,1)} %collective-permute-done.1), kind=kOutput, calls=%fused_computation.7 | convolution fusion | flops 151388160 | bytes 1867776 | tf_op jit(solution)/shard_map/dot_general | solution.py:103
  43.5 10.5 %collective-permute-done.2 = f16[4,304,192]{1,2,0:T(8,128)(2,1)S(1)} collective-permute-done((f16[4,304,192]{1,2,0:T(8,128)(2,1)S(1)}, f16[4,304,192]{1,2,0:T(8,128)(2,1)S(1)}, u32[]{:S(2)}, u32[]{:S(2)}) %collective-permute-start.2) | collective-permute-done | bytes 466976 | tf_op jit(solution)/shard_map/ppermute | solution.py:47
  54.0 0.6 slice.76
  55.4 0.7 abs_reduce_fusion.3
  58.5 3.4 %collective-permute-start.4 = (f16[304,192]{0,1:T(8,128)(2,1)S(1)}, f16[304,192]{0,1:T(8,128)(2,1)S(1)}, u32[]{:S(2)}, u32[]{:S(2)}) collective-permute-start(f16[304,192]{0,1:T(8,128)(2,1)S(1)} %concatenate.27), channel_id=1, source_target_pairs={{0,4},{1,5},{2,6},{3,7},{4,0},{5,1},{6,2},{7,3},{8,12},{9,13},{10,... | collective-permute-start | bytes 350216 | tf_op jit(solution)/shard_map/ppermute | solution.py:47
  62.0 1.4 %collective-permute-start.5 = (f16[304,192]{0,1:T(8,128)(2,1)S(1)}, f16[304,192]{0,1:T(8,128)(2,1)S(1)}, u32[]{:S(2)}, u32[]{:S(2)}) collective-permute-start(f16[304,192]{0,1:T(8,128)(2,1)S(1)} %concatenate.28), channel_id=1, source_target_pairs={{0,6},{1,7},{2,0},{3,1},{4,2},{5,3},{6,4},{7,5},{8,14},{9,15},{10,... | collective-permute-start | bytes 350216 | tf_op jit(solution)/shard_map/ppermute | solution.py:47
  63.4 0.7 collective-permute-start.3
  64.2 2.3 %fusion.10 = bf16[1,128,768]{2,1,0:T(8,128)(2,1)} fusion(f32[128,768]{1,0:T(8,128)S(1)} %copy-done.3, f32[128,768]{1,0:T(8,128)S(1)} %fusion.2, f32[128,768]{1,0:T(8,128)S(1)} %fusion.4, bf16[768,2304]{1,0:T(8,128)(2,1)} %param.5, bf16[1,64,768]{2,1,0:T(8,128)(2,1)} %collective-permute-done, bf16[1,128,768]{2,1,0:T(8,128)(2,1)S(1)} %copy-done.2), kind=kOutput, calls=%fused_computation.13 | convolution fusion | flops 151781376 | bytes 2850816 | tf_op jit(solution)/shard_map/dot_general | solution.py:103
  66.5 3.5 %collective-permute-done.4 = f16[304,192]{0,1:T(8,128)(2,1)S(1)} collective-permute-done((f16[304,192]{0,1:T(8,128)(2,1)S(1)}, f16[304,192]{0,1:T(8,128)(2,1)S(1)}, u32[]{:S(2)}, u32[]{:S(2)}) %collective-permute-start.4) | collective-permute-done | bytes 116768 | tf_op jit(solution)/shard_map/ppermute | solution.py:47
  70.0 0.6 slice.80
  71.3 0.6 slice.82
  72.6 1.0 %collective-permute-done.3 = f16[304,192]{0,1:T(8,128)(2,1)S(1)} collective-permute-done((f16[304,192]{0,1:T(8,128)(2,1)S(1)}, f16[304,192]{0,1:T(8,128)(2,1)S(1)}, u32[]{:S(2)}, u32[]{:S(2)}) %collective-permute-start.3) | collective-permute-done | bytes 116768 | tf_op jit(solution)/shard_map/ppermute | solution.py:47
  73.6 0.6 slice.78
  74.9 0.8 %fusion.34 = f32[192,288]{1,0:T(8,128)} fusion(f32[4,288,192]{1,2,0:T(8,128)S(1)} %bitcast_add_fusion, s32[]{:T(128)S(6)} %select_n.47, f16[304,192]{0,1:T(8,128)(2,1)S(1)} %collective-permute-done.5, f16[304,192]{0,1:T(8,128)(2,1)S(1)} %collective-permute-done.4, f16[304,192]{0,1:T(8,128)(2,1)S(1)} %collective-permute-done.3, f32[]{:T(128)} %bitcast.16, ...), kind=kLoop, calls=%fused_computation.40 | loop fusion | flops 497664 | bytes 774160 | tf_op jit(solution)/shard_map/transpose | solution.py:66
  (27 shorter events, 1.4 us)
Async XLA Ops:
  0.6 8.6 %copy-start.4 = (bf16[1,128,768]{2,1,0:T(8,128)(2,1)S(1)}, bf16[1,128,768]{2,1,0:T(8,128)(2,1)}, u32[]{:S(2)}) copy-start(bf16[1,128,768]{2,1,0:T(8,128)(2,1)} %param.3) | copy-start | bytes 589828
  5.0 15.6 %all-to-all-start = ((bf16[4,2,12288]{2,1,0:T(2,128)(2,1)}), bf16[4,2,12288]{2,1,0:T(2,128)(2,1)S(1)}, u32[]{:S(2)}, u32[]{:S(2)}) async-start(bf16[4,2,12288]{2,1,0:T(2,128)(2,1)} %reshape.55), calls=%async_computation | async-start | bytes 393216 | tf_op jit(solution)/shard_map/all_to_all | solution.py:81
  22.1 1.4 %copy-start.1 = (bf16[1,128,768]{2,1,0:T(8,128)(2,1)S(1)}, bf16[1,128,768]{2,1,0:T(8,128)(2,1)}, u32[]{:S(2)}) copy-start(bf16[1,128,768]{2,1,0:T(8,128)(2,1)} %param.4) | copy-start | bytes 589828
  24.1 40.0 %collective-permute-start = (bf16[1,64,768]{2,1,0:T(8,128)(2,1)}, bf16[1,64,768]{2,1,0:T(8,128)(2,1)}, u32[]{:S(2)}, u32[]{:S(2)}) collective-permute-start(bf16[1,64,768]{2,1,0:T(8,128)(2,1)} %get-tuple-element.16), channel_id=1, source_target_pairs={{8,0},{16,8},{24,16},{9,1},{17,9},{25,17},{10,2},{18,10},{26,18},{... | collective-permute-start | bytes 294920 | tf_op jit(solution)/shard_map/ppermute | solution.py:22
  25.4 16.3 %collective-permute-start.1 = (bf16[1,64,768]{2,1,0:T(8,128)(2,1)}, bf16[1,64,768]{2,1,0:T(8,128)(2,1)}, u32[]{:S(2)}, u32[]{:S(2)}) collective-permute-start(bf16[1,64,768]{2,1,0:T(8,128)(2,1)} %get-tuple-element.17), channel_id=1, source_target_pairs={{0,8},{8,16},{16,24},{1,9},{9,17},{17,25},{2,10},{10,18},{18,26},{... | collective-permute-start | bytes 294920 | tf_op jit(solution)/shard_map/ppermute | solution.py:21
  37.7 2.4 %copy-start.2 = (bf16[1,128,768]{2,1,0:T(8,128)(2,1)S(1)}, bf16[1,128,768]{2,1,0:T(8,128)(2,1)}, u32[]{:S(2)}) copy-start(bf16[1,128,768]{2,1,0:T(8,128)(2,1)} %param.4) | copy-start | bytes 589828
  38.0 16.0 %collective-permute-start.2 = (f16[4,304,192]{1,2,0:T(8,128)(2,1)S(1)}, f16[4,304,192]{1,2,0:T(8,128)(2,1)S(1)}, u32[]{:S(2)}, u32[]{:S(2)}) collective-permute-start(f16[4,304,192]{1,2,0:T(8,128)(2,1)S(1)} %concatenate.25), channel_id=1, source_target_pairs={{0,1},{1,0},{2,3},{3,2},{4,5},{5,4},{6,7},{7,6},{8,9},{9,8},{10,11... | collective-permute-start | bytes 1400840 | tf_op jit(solution)/shard_map/ppermute | solution.py:47
  41.7 13.6 %copy-start = (f32[4,1,288,192]{2,1,0,3:T(1,128)S(1)}, f32[4,1,288,192]{2,1,0,3:T(1,128)}, u32[]{:S(2)}) copy-start(f32[4,1,288,192]{2,1,0,3:T(1,128)} %get-tuple-element.12) | copy-start | bytes 2654212
  56.2 8.0 %copy-start.3 = (f32[128,768]{1,0:T(8,128)S(1)}, f32[128,768]{1,0:T(8,128)}, u32[]{:S(2)}) copy-start(f32[128,768]{1,0:T(8,128)} %fusion.25) | copy-start | bytes 1179652
  58.5 11.5 %collective-permute-start.4 = (f16[304,192]{0,1:T(8,128)(2,1)S(1)}, f16[304,192]{0,1:T(8,128)(2,1)S(1)}, u32[]{:S(2)}, u32[]{:S(2)}) collective-permute-start(f16[304,192]{0,1:T(8,128)(2,1)S(1)} %concatenate.27), channel_id=1, source_target_pairs={{0,4},{1,5},{2,6},{3,7},{4,0},{5,1},{6,2},{7,3},{8,12},{9,13},{10,... | collective-permute-start | bytes 350216 | tf_op jit(solution)/shard_map/ppermute | solution.py:47
  62.0 9.3 %collective-permute-start.5 = (f16[304,192]{0,1:T(8,128)(2,1)S(1)}, f16[304,192]{0,1:T(8,128)(2,1)S(1)}, u32[]{:S(2)}, u32[]{:S(2)}) collective-permute-start(f16[304,192]{0,1:T(8,128)(2,1)S(1)} %concatenate.28), channel_id=1, source_target_pairs={{0,6},{1,7},{2,0},{3,1},{4,2},{5,3},{6,4},{7,5},{8,14},{9,15},{10,... | collective-permute-start | bytes 350216 | tf_op jit(solution)/shard_map/ppermute | solution.py:47
  63.4 10.2 %collective-permute-start.3 = (f16[304,192]{0,1:T(8,128)(2,1)S(1)}, f16[304,192]{0,1:T(8,128)(2,1)S(1)}, u32[]{:S(2)}, u32[]{:S(2)}) collective-permute-start(f16[304,192]{0,1:T(8,128)(2,1)S(1)} %concatenate.26), channel_id=1, source_target_pairs={{0,2},{1,3},{2,4},{3,5},{4,6},{5,7},{6,0},{7,1},{8,10},{9,11},{10,... | collective-permute-start | bytes 350216 | tf_op jit(solution)/shard_map/ppermute | solution.py:47

commit v7 on v6

--- a/solution.py
+++ b/solution.py
@@ -3,6 +3,7 @@
 import jax
 import jax.numpy as jnp
 from jax import lax
+from jax.experimental.layout import Layout, with_layout_constraint
 from jax.sharding import PartitionSpec as P
 
 KW = 3
@@ -31,20 +32,23 @@
 
 
 def encode(values):
-    biggest = jnp.maximum(jnp.max(jnp.abs(values)), 1e-30)
+    flat = values.reshape(-1, values.shape[-1])
+    biggest = jnp.maximum(jnp.max(jnp.abs(flat)), 1e-30)
     exponent = jnp.floor(jnp.log2(biggest))
-    scaled = (values * jnp.exp2(HEADROOM - exponent)).astype(jnp.float16)
-    tag = jnp.full(values.shape[:-2] + (TAG, values.shape[-1]), exponent, jnp.float16)
-    return jnp.concatenate([scaled, tag], axis=-2)
+    scaled = (flat * jnp.exp2(HEADROOM - exponent)).astype(jnp.float16)
+    tag = jnp.full((TAG, flat.shape[-1]), exponent, jnp.float16)
+    return with_layout_constraint(jnp.concatenate([scaled, tag], axis=0), Layout((0, 1)))
 
 
-def decode(packed):
-    exponent = packed[(0,) * (packed.ndim - 2) + (-TAG, 0)].astype(jnp.float32)
-    return packed[..., :-TAG, :].astype(jnp.float32) * jnp.exp2(exponent - HEADROOM)
+def decode(packed, shape):
+    exponent = packed[-TAG, 0].astype(jnp.float32)
+    values = packed[:-TAG].astype(jnp.float32) * jnp.exp2(exponent - HEADROOM)
+    return values.reshape(shape)
 
 
 def send(values, perm):
-    return decode(lax.ppermute(encode(values), "batch", perm))
+    arrived = lax.ppermute(encode(values), "batch", perm)
+    return decode(with_layout_constraint(arrived, Layout((0, 1))), values.shape)
 
 
 def reduce_over_batch(columns):
@@ -57,13 +61,13 @@
     blocks = columns.reshape(outer, 2, -1, columns.shape[1])
     mine = lax.dynamic_index_in_dim(blocks, x, axis=1, keepdims=False)
     theirs = lax.dynamic_index_in_dim(blocks, 1 - x, axis=1, keepdims=False)
-    summed = mine + send(theirs, pairs)
+    summed = with_layout_constraint(mine + send(theirs, pairs), Layout((0, 1, 2)))
     total = lax.dynamic_index_in_dim(summed, z, axis=0, keepdims=False)
     for shift in range(1, outer):
         target = lax.dynamic_index_in_dim(summed, (z + shift) % outer, axis=0, keepdims=False)
         perm = [(2 * q + p, 2 * ((q + shift) % outer) + p) for q in range(outer) for p in range(2)]
         total = total + send(target, perm)
-    return total.T
+    return with_layout_constraint(total, Layout((0, 1))).T
 
 
 def body(inputs, cotangent, weight):
@@ -93,6 +97,7 @@
             )
         )
     local_columns = jnp.concatenate(updated, axis=0) * factor
+    local_columns = with_layout_constraint(local_columns, Layout((0, 1)))
     local_columns, cotangent, deriv = lax.optimization_barrier((local_columns, cotangent, deriv))
     padded_input = extended_2(cotangent, (("seq", 1),), reach)
     extended = padded_input[0]

time: 77 us -> 70.9 us (0.921)
  starting transfers between devices: 16.9 us -> 14.9 us
  other arithmetic: 6.8 us -> 5.08 us
  waiting for transfers between devices: 15.1 us -> 13.4 us
  matrix products: 6.75 us -> 8.42 us
  local copies, waits for them, and re-layouts: 13.3 us -> 11.7 us
    reshape x1 -> x0, local copies, waits for them, and re-layouts: 4.05 us -> none  [reduce_over_batch(): blocks = columns.reshape(outer, 2, -1, columns.shape[1])]
    unnamed x16 -> x23, local copies, waits for them, and re-layouts: 2.81 us -> 6.8 us
    dynamic_slice x1 -> x0, local copies, waits for them, and re-layouts: 3.05 us -> none  [reduce_over_batch(): theirs = lax.dynamic_index_in_dim(blocks, 1 - x, axis=1, keepdims=False)]
    ppermute x4, waiting for transfers between devices: 15.1 us -> 13.3 us  [send(): arrived = lax.ppermute(encode(values), 'batch', perm)]
    ppermute x1, starting transfers between devices: 3.67 us -> 2.25 us  [extended_2(): before = lax.ppermute(last, axis, up)]
    dot_general x3, matrix products: 5.68 us -> 7.07 us  [body(): jnp.dot(window, weight[:, tap_index * in_width:(tap_index + 1) * in_width...]
    mul x1, other arithmetic: 1.34 us -> 0.18 us  [body(): local_columns = jnp.concatenate(updated, axis=0) * factor]
    concatenate x4, local copies, waits for them, and re-layouts: 0.23 us -> 1.2 us  [encode(): jnp.concatenate([scaled, tag], axis=0)]
  transfers between devices with their start and end apart: 7 -> 7, of which waited for: 3 -> 3; matrix products, arithmetic and copies ran while one was open for 23% -> 22% of each run, Pallas kernels for 0% -> 0%
where the time goes in v7:
time: 70.9 us; the launch traced here: 70.3 us
  starting transfers between devices  14.9 us (21%)
  waiting for transfers between devices  13.4 us (19%)
  local copies, waits for them, and re-layouts  11.7 us (17%)
  blocking collectives  10.3 us (15%)
  matrix products  8.42 us (12%)
  between operations  6.58 us (9%)
  other arithmetic  5.08 us (7%)
    ppermute x4, waiting for transfers between devices, send(): arrived = lax.ppermute(encode(values), 'batch', perm)  13.3 us
    all_gather x1, blocking collectives, body(): whole_act = lax.all_gather(act[None], 'seq', axis=1, tiled=True)[0]  10.3 us
    ppermute x4, starting transfers between devices, send(): arrived = lax.ppermute(encode(values), 'batch', perm)  7.11 us
    dot_general x3, matrix products, body(): jnp.dot(window, weight[:, tap_index * in_width:(tap_index + 1) * in_width...  7.07 us
    unnamed x23, local copies, waits for them, and re-layouts  6.8 us
    all_to_all x1, starting transfers between devices, body(): lax.all_to_all(cotangent, 'seq', split_axis=2, concat_axis=1, tiled=True)[0]  4.24 us
    slice x4, local copies, waits for them, and re-layouts, decode(): exponent = packed[-TAG, 0].astype(jnp.float32)  2.78 us
    ppermute x1, starting transfers between devices, extended_2(): before = lax.ppermute(last, axis, up)  2.25 us
  transfers between devices with their start and end apart: 7, of which 3 were waited for; matrix products, arithmetic and copies ran while one was open for 22% of the time, Pallas kernels for 0%

profile of v7, /device:TPU:0, one launch (start us, length us, event | category | flops | bytes accessed | tf_op | source)
XLA Modules:
  0.0 70.3 jit_solution(11992312325881288849)
XLA Ops:
  0.6 1.3 %copy.19 = bf16[1,128,768]{1,0,2:T(2,128)(2,1)S(1)} copy(bf16[1,128,768]{2,1,0:T(8,128)(2,1)} %param.4) | data formatting | bytes 393216 | tf_op args[1]
  2.0 0.5 broadcast.28
  2.5 1.8 %reduce.4 = bf16[768,128]{1,0:T(8,128)(2,1)S(1)} reduce(bf16[768,1,128]{2,1,0:T(2,128)(2,1)S(1)} %bitcast.100, bf16[]{:T(256)} %broadcast.28), dimensions={1}, to_apply=%bitcast.87.reduce_sub_computation | reduce | bytes 393218
  4.3 0.7 %reshape.60 = bf16[4,2,12288]{2,1,0:T(2,128)(2,1)} reshape(bf16[768,128]{1,0:T(8,128)(2,1)S(1)} %reduce.4) | data formatting | bytes 393216
  5.0 4.2 %all-to-all-start = ((bf16[4,2,12288]{2,1,0:T(2,128)(2,1)}), bf16[4,2,12288]{2,1,0:T(2,128)(2,1)S(1)}, u32[]{:S(2)}, u32[]{:S(2)}) async-start(bf16[4,2,12288]{2,1,0:T(2,128)(2,1)} %reshape.60), calls=%async_computation | async-start | bytes 393216 | tf_op jit(solution)/shard_map/all_to_all | solution.py:85
  9.3 10.3 %all_gather.3 = bf16[1,512,768]{2,1,0:T(8,128)(2,1)S(1)} all-gather(bf16[1,128,768]{2,1,0:T(8,128)(2,1)S(1)} %fusion.30), channel_id=1, replica_groups=mesh['seq'=4,'batch'=8] {'seq'}, dimensions={1}, use_global_device_ids=true | all-gather | bytes 983040 | tf_op jit(solution)/shard_map/all_gather | solution.py:88
  19.7 0.9 %fusion.26 = f32[128,768]{1,0:T(8,128)} fusion(bf16[1,128,768]{2,1,0:T(8,128)(2,1)S(1)} %copy-done.4), kind=kLoop, calls=%fused_computation.32 | loop fusion | flops 884736 | bytes 589824 | tf_op jit(solution)/shard_map/add | solution.py:31
  21.4 0.5 fusion.15
  22.6 0.7 %copy-done = bf16[1,128,768]{2,1,0:T(8,128)(2,1)S(1)} copy-done((bf16[1,128,768]{2,1,0:T(8,128)(2,1)S(1)}, bf16[1,128,768]{2,1,0:T(8,128)(2,1)}, u32[]{:S(2)}) %copy-start) | copy-done | bytes 196632
  23.3 0.7 fusion.50
  24.0 2.2 %collective-permute-start.1 = (bf16[1,64,768]{2,1,0:T(8,128)(2,1)S(1)}, bf16[1,64,768]{2,1,0:T(8,128)(2,1)S(1)}, u32[]{:S(2)}, u32[]{:S(2)}) collective-permute-start(bf16[1,64,768]{2,1,0:T(8,128)(2,1)S(1)} %get-tuple-element.21), channel_id=1, source_target_pairs={{0,8},{8,16},{16,24},{1,9},{9,17},{17,25},{2,10},{10,18},{18,26},{... | collective-permute-start | bytes 294920 | tf_op jit(solution)/shard_map/ppermute | solution.py:22
  26.2 0.8 %fusion.2 = f32[]{:T(128)} fusion(f32[4,2,288,192]{3,2,1,0:T(8,128)S(1)} %bitcast.90, s32[]{:T(128)S(6)} %select_n.45), kind=kLoop, calls=%fused_computation.7 | loop fusion | flops 442367 | bytes 884744 | tf_op jit(solution)/shard_map/reduce_max | solution.py:36
  27.9 1.1 %copy.37 = f16[1152,192]{0,1:T(8,128)(2,1)} copy(f16[1152,192]{1,0:T(8,128)(2,1)S(1)} %bitcast.94) | data formatting | bytes 884736
  29.0 1.1 %concatenate.25.clone = f16[1168,192]{0,1:T(8,128)(2,1)S(1)} pad(f16[1152,192]{0,1:T(8,128)(2,1)} %copy.37, f16[]{:T(256)S(6)} %convert_element_type.89), padding=0_16x0_0 | pad | bytes 890882 | tf_op jit(solution)/shard_map/concatenate | solution.py:40
  30.1 2.1 %collective-permute-start.2 = (f16[1168,192]{0,1:T(8,128)(2,1)S(1)}, f16[1168,192]{0,1:T(8,128)(2,1)S(1)}, u32[]{:S(2)}, u32[]{:S(2)}) collective-permute-start(f16[1168,192]{0,1:T(8,128)(2,1)S(1)} %concatenate.25.clone), channel_id=1, source_target_pairs={{0,1},{1,0},{2,3},{3,2},{4,5},{5,4},{6,7},{7,6},{8,9},{9,8},{10,11... | collective-permute-start | bytes 1345544 | tf_op jit(solution)/shard_map/ppermute | solution.py:50
  32.2 2.4 %fusion.6 = f32[128,768]{1,0:T(8,128)} fusion(bf16[768,2304]{1,0:T(8,128)(2,1)} %param.5, bf16[1,128,768]{2,1,0:T(8,128)(2,1)S(1)} %copy-done), kind=kOutput, calls=%fused_computation.12 | convolution fusion | flops 150994944 | bytes 1769472 | tf_op jit(solution)/shard_map/dot_general | solution.py:108
  34.6 1.3 %collective-permute-start = (bf16[1,64,768]{2,1,0:T(8,128)(2,1)}, bf16[1,64,768]{2,1,0:T(8,128)(2,1)}, u32[]{:S(2)}, u32[]{:S(2)}) collective-permute-start(bf16[1,64,768]{2,1,0:T(8,128)(2,1)} %get-tuple-element.20), channel_id=1, source_target_pairs={{8,0},{16,8},{24,16},{9,1},{17,9},{25,17},{10,2},{18,10},{26,18},{... | collective-permute-start | bytes 294920 | tf_op jit(solution)/shard_map/ppermute | solution.py:23
  35.9 2.4 %fusion.4 = f32[128,768]{1,0:T(8,128)} fusion(bf16[768,2304]{1,0:T(8,128)(2,1)} %param.5, bf16[1,128,768]{2,1,0:T(8,128)(2,1)S(1)} %copy-done, bf16[1,64,768]{2,1,0:T(8,128)(2,1)S(1)} %collective-permute-done.1), kind=kOutput, calls=%fused_computation.10 | convolution fusion | flops 151388160 | bytes 1867776 | tf_op jit(solution)/shard_map/dot_general | solution.py:108
  38.3 5.5 %collective-permute-done.2 = f16[1168,192]{0,1:T(8,128)(2,1)S(1)} collective-permute-done((f16[1168,192]{0,1:T(8,128)(2,1)S(1)}, f16[1168,192]{0,1:T(8,128)(2,1)S(1)}, u32[]{:S(2)}, u32[]{:S(2)}) %collective-permute-start.2) | collective-permute-done | bytes 448544 | tf_op jit(solution)/shard_map/ppermute | solution.py:50
  43.7 0.8 %copy-done.5 = f16[1168,192]{0,1:T(8,128)(2,1)} copy-done((f16[1168,192]{0,1:T(8,128)(2,1)}, f16[1168,192]{0,1:T(8,128)(2,1)S(1)}, u32[]{:S(2)}) %copy-start.5) | copy-done | bytes 448536
  44.6 0.5 copy.35
  45.1 1.2 %slice.76 = f16[1,1]{0,1:T(2,128)(2,1)} slice(f16[1168,192]{0,1:T(8,128)(2,1)} %copy-done.5), slice={[1152:1153], [0:1]} | slice | bytes 4 | tf_op jit(solution)/shard_map/slice | solution.py:44
  47.2 0.7 %abs_reduce_fusion.2 = (f32[]{:T(128)}, f32[]{:T(128)}, f32[]{:T(128)}) fusion(f32[4,288,192]{2,1,0:T(8,128)S(1)} %bitcast_add_fusion, s32[]{:T(128)S(6)} %select_n.49, s32[]{:T(128)S(6)} %select_n.51, s32[]{:T(128)S(6)} %select_n.53), kind=kLoop, calls=%fused_computation.48 | loop fusion | flops 331773 | bytes 663576 | tf_op jit(solution)/shard_map/reduce_max | solution.py:36
  50.4 3.9 %collective-permute-start.5 = (f16[304,192]{1,0:T(8,128)(2,1)S(1)}, f16[304,192]{1,0:T(8,128)(2,1)S(1)}, u32[]{:S(2)}, u32[]{:S(2)}) collective-permute-start(f16[304,192]{1,0:T(8,128)(2,1)S(1)} %concatenate.28), channel_id=1, source_target_pairs={{0,6},{1,7},{2,0},{3,1},{4,2},{5,3},{6,4},{7,5},{8,14},{9,15},{10,... | collective-permute-start | bytes 350216 | tf_op jit(solution)/shard_map/ppermute | solution.py:50
  54.4 1.0 %collective-permute-start.3 = (f16[304,192]{1,0:T(8,128)(2,1)S(1)}, f16[304,192]{1,0:T(8,128)(2,1)S(1)}, u32[]{:S(2)}, u32[]{:S(2)}) collective-permute-start(f16[304,192]{1,0:T(8,128)(2,1)S(1)} %concatenate.26), channel_id=1, source_target_pairs={{0,2},{1,3},{2,4},{3,5},{4,6},{5,7},{6,0},{7,1},{8,10},{9,11},{10,... | collective-permute-start | bytes 350216 | tf_op jit(solution)/shard_map/ppermute | solution.py:50
  55.5 2.3 %fusion.12 = bf16[1,128,768]{2,1,0:T(8,128)(2,1)} fusion(f32[128,768]{1,0:T(8,128)S(1)} %copy-done.3, f32[128,768]{1,0:T(8,128)S(1)} %copy-done.6, f32[128,768]{1,0:T(8,128)S(1)} %copy-done.2, bf16[768,2304]{1,0:T(8,128)(2,1)} %param.5, bf16[1,64,768]{2,1,0:T(8,128)(2,1)} %collective-permute-done, bf16[1,128,768]{2,1,0:T(8,128)(2,1)S(1)} %copy-done.1), kind=kOutput, calls=%fused_computation.16 | convolution fusion | flops 151781376 | bytes 2850816 | tf_op jit(solution)/shard_map/dot_general | solution.py:108
  57.9 0.9 %collective-permute-done.5 = f16[304,192]{1,0:T(8,128)(2,1)S(1)} collective-permute-done((f16[304,192]{1,0:T(8,128)(2,1)S(1)}, f16[304,192]{1,0:T(8,128)(2,1)S(1)}, u32[]{:S(2)}, u32[]{:S(2)}) %collective-permute-start.5) | collective-permute-done | bytes 116768 | tf_op jit(solution)/shard_map/ppermute | solution.py:50
  58.8 0.5 slice.82
  60.0 7.0 %collective-permute-done.4 = f16[304,192]{1,0:T(8,128)(2,1)S(1)} collective-permute-done((f16[304,192]{1,0:T(8,128)(2,1)S(1)}, f16[304,192]{1,0:T(8,128)(2,1)S(1)}, u32[]{:S(2)}, u32[]{:S(2)}) %collective-permute-start.4) | collective-permute-done | bytes 116768 | tf_op jit(solution)/shard_map/ppermute | solution.py:50
  66.9 0.5 slice.80
  68.1 0.5 slice.78
  69.4 0.9 %copy.28 = f32[192,288]{1,0:T(8,128)} copy(f32[192,288]{0,1:T(8,128)S(1)} %fusion.35) | data formatting | bytes 442368
  (34 shorter events, 2.4 us)
Async XLA Ops:
  0.6 8.6 %copy-start.4 = (bf16[1,128,768]{2,1,0:T(8,128)(2,1)S(1)}, bf16[1,128,768]{2,1,0:T(8,128)(2,1)}, u32[]{:S(2)}) copy-start(bf16[1,128,768]{2,1,0:T(8,128)(2,1)} %param.3) | copy-start | bytes 589828
  5.0 15.6 %all-to-all-start = ((bf16[4,2,12288]{2,1,0:T(2,128)(2,1)}), bf16[4,2,12288]{2,1,0:T(2,128)(2,1)S(1)}, u32[]{:S(2)}, u32[]{:S(2)}) async-start(bf16[4,2,12288]{2,1,0:T(2,128)(2,1)} %reshape.60), calls=%async_computation | async-start | bytes 393216 | tf_op jit(solution)/shard_map/all_to_all | solution.py:85
  22.4 0.9 %copy-start = (bf16[1,128,768]{2,1,0:T(8,128)(2,1)S(1)}, bf16[1,128,768]{2,1,0:T(8,128)(2,1)}, u32[]{:S(2)}) copy-start(bf16[1,128,768]{2,1,0:T(8,128)(2,1)} %param.4) | copy-start | bytes 589828
  24.0 11.9 %collective-permute-start.1 = (bf16[1,64,768]{2,1,0:T(8,128)(2,1)S(1)}, bf16[1,64,768]{2,1,0:T(8,128)(2,1)S(1)}, u32[]{:S(2)}, u32[]{:S(2)}) collective-permute-start(bf16[1,64,768]{2,1,0:T(8,128)(2,1)S(1)} %get-tuple-element.21), channel_id=1, source_target_pairs={{0,8},{8,16},{16,24},{1,9},{9,17},{17,25},{2,10},{10,18},{18,26},{... | collective-permute-start | bytes 294920 | tf_op jit(solution)/shard_map/ppermute | solution.py:22
  30.1 13.6 %collective-permute-start.2 = (f16[1168,192]{0,1:T(8,128)(2,1)S(1)}, f16[1168,192]{0,1:T(8,128)(2,1)S(1)}, u32[]{:S(2)}, u32[]{:S(2)}) collective-permute-start(f16[1168,192]{0,1:T(8,128)(2,1)S(1)} %concatenate.25.clone), channel_id=1, source_target_pairs={{0,1},{1,0},{2,3},{3,2},{4,5},{5,4},{6,7},{7,6},{8,9},{9,8},{10,11... | collective-permute-start | bytes 1345544 | tf_op jit(solution)/shard_map/ppermute | solution.py:50
  34.6 20.9 %collective-permute-start = (bf16[1,64,768]{2,1,0:T(8,128)(2,1)}, bf16[1,64,768]{2,1,0:T(8,128)(2,1)}, u32[]{:S(2)}, u32[]{:S(2)}) collective-permute-start(bf16[1,64,768]{2,1,0:T(8,128)(2,1)} %get-tuple-element.20), channel_id=1, source_target_pairs={{8,0},{16,8},{24,16},{9,1},{17,9},{25,17},{10,2},{18,10},{26,18},{... | collective-permute-start | bytes 294920 | tf_op jit(solution)/shard_map/ppermute | solution.py:23
  43.7 0.8 %copy-start.5 = (f16[1168,192]{0,1:T(8,128)(2,1)}, f16[1168,192]{0,1:T(8,128)(2,1)S(1)}, u32[]{:S(2)}) copy-start(f16[1168,192]{0,1:T(8,128)(2,1)S(1)} %collective-permute-done.2) | copy-start | bytes 1345540
  48.0 7.5 %copy-start.1 = (bf16[1,128,768]{2,1,0:T(8,128)(2,1)S(1)}, bf16[1,128,768]{2,1,0:T(8,128)(2,1)}, u32[]{:S(2)}) copy-start(bf16[1,128,768]{2,1,0:T(8,128)(2,1)} %param.4) | copy-start | bytes 589828
  48.0 7.5 %copy-start.2 = (f32[128,768]{1,0:T(8,128)S(1)}, f32[128,768]{1,0:T(8,128)}, u32[]{:S(2)}) copy-start(f32[128,768]{1,0:T(8,128)} %fusion.6) | copy-start | bytes 1179652
  48.0 7.5 %copy-start.3 = (f32[128,768]{1,0:T(8,128)S(1)}, f32[128,768]{1,0:T(8,128)}, u32[]{:S(2)}) copy-start(f32[128,768]{1,0:T(8,128)} %fusion.26) | copy-start | bytes 1179652
  48.0 7.5 %copy-start.6 = (f32[128,768]{1,0:T(8,128)S(1)}, f32[128,768]{1,0:T(8,128)}, u32[]{:S(2)}) copy-start(f32[128,768]{1,0:T(8,128)} %fusion.4) | copy-start | bytes 1179652
  50.4 8.4 %collective-permute-start.5 = (f16[304,192]{1,0:T(8,128)(2,1)S(1)}, f16[304,192]{1,0:T(8,128)(2,1)S(1)}, u32[]{:S(2)}, u32[]{:S(2)}) collective-permute-start(f16[304,192]{1,0:T(8,128)(2,1)S(1)} %concatenate.28), channel_id=1, source_target_pairs={{0,6},{1,7},{2,0},{3,1},{4,2},{5,3},{6,4},{7,5},{8,14},{9,15},{10,... | collective-permute-start | bytes 350216 | tf_op jit(solution)/shard_map/ppermute | solution.py:50
  54.3 12.6 %collective-permute-start.4 = (f16[304,192]{1,0:T(8,128)(2,1)S(1)}, f16[304,192]{1,0:T(8,128)(2,1)S(1)}, u32[]{:S(2)}, u32[]{:S(2)}) collective-permute-start(f16[304,192]{1,0:T(8,128)(2,1)S(1)} %concatenate.27), channel_id=1, source_target_pairs={{0,4},{1,5},{2,6},{3,7},{4,0},{5,1},{6,2},{7,3},{8,12},{9,13},{10,... | collective-permute-start | bytes 350216 | tf_op jit(solution)/shard_map/ppermute | solution.py:50
  54.4 13.7 %collective-permute-start.3 = (f16[304,192]{1,0:T(8,128)(2,1)S(1)}, f16[304,192]{1,0:T(8,128)(2,1)S(1)}, u32[]{:S(2)}, u32[]{:S(2)}) collective-permute-start(f16[304,192]{1,0:T(8,128)(2,1)S(1)} %concatenate.26), channel_id=1, source_target_pairs={{0,2},{1,3},{2,4},{3,5},{4,6},{5,7},{6,0},{7,1},{8,10},{9,11},{10,... | collective-permute-start | bytes 350216 | tf_op jit(solution)/shard_map/ppermute | solution.py:50

commit v8 on v7

--- a/solution.py
+++ b/solution.py
@@ -82,10 +82,11 @@
     batch_count = lax.axis_size("batch")
     counted = batch_count * inputs.shape[0] * length * seq_count
     factor = 1.0 / math.sqrt(float(counted))
-    owned = lax.all_to_all(cotangent, "seq", split_axis=2, concat_axis=1, tiled=True)[0]
-    own_rows = owned.shape[1]
+    both = lax.all_gather(jnp.concatenate([act[None], cotangent], axis=0), "seq", axis=1, tiled=True)
+    whole_act = both[0]
+    own_rows = cotangent.shape[2] // seq_count
+    owned = lax.dynamic_slice_in_dim(both[1], lax.axis_index("seq") * own_rows, own_rows, axis=1)
     owned_padded = jnp.pad(owned, ((reach, reach), (0, 0)))
-    whole_act = lax.all_gather(act[None], "seq", axis=1, tiled=True)[0]
     count = whole_act.shape[0]
     updated = []
     for tap_index in range(KW):
@@ -98,7 +99,6 @@
         )
     local_columns = jnp.concatenate(updated, axis=0) * factor
     local_columns = with_layout_constraint(local_columns, Layout((0, 1)))
-    local_columns, cotangent, deriv = lax.optimization_barrier((local_columns, cotangent, deriv))
     padded_input = extended_2(cotangent, (("seq", 1),), reach)
     extended = padded_input[0]
     grad_act = jnp.zeros((length, in_width), jnp.float32)

time: 70.9 us -> 85.5 us (1.21)
  waiting for transfers between devices: 13.4 us -> 30.2 us
  between operations: 6.58 us -> 19.9 us
  blocking collectives: 10.3 us -> 0 us
  starting transfers between devices: 14.9 us -> 10.7 us
  local copies, waits for them, and re-layouts: 11.7 us -> 9.46 us
  matrix products: 8.42 us -> 9.61 us
    all_gather x0 -> x1, waiting for transfers between devices: none -> 18.2 us  [body(): lax.all_gather(jnp.concatenate([act[None], cotangent], axis=0), 'seq', ax...]
    all_gather x1 -> x0, blocking collectives: 10.3 us -> none  [body(): whole_act = lax.all_gather(act[None], 'seq', axis=1, tiled=True)[0]]
    unnamed x23 -> x13, local copies, waits for them, and re-layouts: 6.8 us -> 2.51 us
    all_to_all x1 -> x0, starting transfers between devices: 4.24 us -> none  [body(): lax.all_to_all(cotangent, 'seq', split_axis=2, concat_axis=1, tiled=True)[0]]
    unnamed x1 -> x0, other arithmetic: 1.81 us -> none
    concatenate x0 -> x1, other arithmetic: none -> 1.72 us  [body(): jnp.concatenate([act[None], cotangent], axis=0)]
    ppermute x4, waiting for transfers between devices: 13.3 us -> 12 us  [send(): arrived = lax.ppermute(encode(values), 'batch', perm)]
    slice x0 -> x2, local copies, waits for them, and re-layouts: none -> 1.13 us  [body(): both[1]]
  transfers between devices with their start and end apart: 7 -> 7, of which waited for: 3 -> 4; matrix products, arithmetic and copies ran while one was open for 22% -> 22% of each run, Pallas kernels for 0% -> 0%
where the time goes in v8:
time: 85.5 us; the launch traced here: 85 us
  waiting for transfers between devices  30.2 us (35%)
  between operations  19.9 us (23%)
  starting transfers between devices  10.7 us (13%)
  matrix products  9.61 us (11%)
  local copies, waits for them, and re-layouts  9.46 us (11%)
  other arithmetic  5.11 us (6%)
    all_gather x1, waiting for transfers between devices, body(): lax.all_gather(jnp.concatenate([act[None], cotangent], axis=0), 'seq', ax...  18.2 us
    ppermute x4, waiting for transfers between devices, send(): arrived = lax.ppermute(encode(values), 'batch', perm)  12 us
    dot_general x3, matrix products, body(): jnp.dot(window, weight[:, tap_index * in_width:(tap_index + 1) * in_width...  7.16 us
    ppermute x4, starting transfers between devices, send(): arrived = lax.ppermute(encode(values), 'batch', perm)  7.04 us
    slice x4, local copies, waits for them, and re-layouts, decode(): exponent = packed[-TAG, 0].astype(jnp.float32)  2.73 us
    unnamed x13, local copies, waits for them, and re-layouts  2.51 us
    dot_general x3, matrix products, body(): lax.dot_general(whole_act, window, (((0,), (0,)), ((), ())), preferred_el...  2.44 us
    ppermute x1, starting transfers between devices, extended_2(): before = lax.ppermute(last, axis, up)  2.35 us
  transfers between devices with their start and end apart: 7, of which 4 were waited for; matrix products, arithmetic and copies ran while one was open for 22% of the time, Pallas kernels for 0%

profile of v8, /device:TPU:0, one launch (start us, length us, event | category | flops | bytes accessed | tf_op | source)
XLA Modules:
  0.0 85.0 jit_solution(3425084594294148215)
XLA Ops:
  7.2 1.1 %fusion.31 = bf16[1,128,768]{2,1,0:T(8,128)(2,1)S(1)} fusion(bf16[1,128,768]{2,1,0:T(8,128)(2,1)} %param.3), kind=kLoop, calls=%fused_computation.37 | loop fusion | flops 589824 | bytes 393216 | tf_op jit(solution)/shard_map/convert_element_type | solution.py:80
  8.3 1.7 %pad_maximum_fusion = bf16[2,128,768]{2,1,0:T(8,128)(2,1)} fusion(bf16[1,128,768]{2,1,0:T(8,128)(2,1)} %param.4, bf16[1,128,768]{2,1,0:T(8,128)(2,1)S(1)} %fusion.31), kind=kLoop, calls=%fused_computation.38 | loop fusion | flops 196608 | bytes 786432 | tf_op jit(solution)/shard_map/concatenate | solution.py:85
  10.0 0.7 fusion.49
  10.7 2.4 %collective-permute-start.1 = (bf16[1,64,768]{2,1,0:T(8,128)(2,1)S(1)}, bf16[1,64,768]{2,1,0:T(8,128)(2,1)S(1)}, u32[]{:S(2)}, u32[]{:S(2)}) collective-permute-start(bf16[1,64,768]{2,1,0:T(8,128)(2,1)S(1)} %get-tuple-element.13), channel_id=1, source_target_pairs={{0,8},{8,16},{16,24},{1,9},{9,17},{17,25},{2,10},{10,18},{18,26},{... | collective-permute-start | bytes 294920 | tf_op jit(solution)/shard_map/ppermute | solution.py:22
  13.0 1.3 %collective-permute-start = (bf16[1,64,768]{2,1,0:T(8,128)(2,1)}, bf16[1,64,768]{2,1,0:T(8,128)(2,1)}, u32[]{:S(2)}, u32[]{:S(2)}) collective-permute-start(bf16[1,64,768]{2,1,0:T(8,128)(2,1)} %get-tuple-element.12), channel_id=1, source_target_pairs={{8,0},{16,8},{24,16},{9,1},{17,9},{25,17},{10,2},{18,10},{26,18},{... | collective-permute-start | bytes 294920 | tf_op jit(solution)/shard_map/ppermute | solution.py:23
  14.4 18.2 %all-gather.2.cloned.1.call-done = bf16[2,512,768]{2,1,0:T(8,128)(2,1)} async-done(((bf16[2,128,768]{2,1,0:T(8,128)(2,1)}), bf16[2,512,768]{2,1,0:T(8,128)(2,1)}) %all-gather.2.cloned.1.call-update) | async-done | bytes 1572880 | tf_op jit(solution)/shard_map/all_gather | solution.py:85
  32.5 1.1 %slice-done = bf16[1,512,768]{2,1,0:T(8,128)(2,1)S(1)} async-done(((bf16[2,512,768]{2,1,0:T(8,128)(2,1)}), bf16[1,512,768]{2,1,0:T(8,128)(2,1)S(1)}, s32[]{:S(2)}) %slice-start) | async-done | bytes 786456 | tf_op jit(solution)/shard_map/slice | solution.py:88
  33.8 1.6 %fusion.15 = f32[768,192]{1,0:T(8,128)S(1)} fusion(bf16[2,512,768]{2,1,0:T(8,128)(2,1)} %all-gather.2.cloned.1.call-done, bf16[512,192]{1,0:T(8,128)(2,1)S(1)} %dynamic-slice_bitcast_fusion), kind=kOutput, calls=%fused_computation.18 | convolution fusion | flops 150994944 | bytes 1572864 | tf_op jit(solution)/shard_map/dot_general | solution.py:96
  35.5 0.4 fusion.16
  35.9 0.4 fusion.17
  36.3 0.2 maximum_multiply_fusion
  36.5 0.8 fusion.2
  38.2 1.1 %copy.26 = f16[1152,192]{0,1:T(8,128)(2,1)} copy(f16[1152,192]{1,0:T(8,128)(2,1)S(1)} %bitcast.88) | data formatting | bytes 884736
  39.3 1.1 %concatenate.29.clone = f16[1168,192]{0,1:T(8,128)(2,1)S(1)} pad(f16[1152,192]{0,1:T(8,128)(2,1)} %copy.26, f16[]{:T(256)S(6)} %convert_element_type.89), padding=0_16x0_0 | pad | bytes 890882 | tf_op jit(solution)/shard_map/concatenate | solution.py:40
  40.4 1.5 %collective-permute-start.2 = (f16[1168,192]{0,1:T(8,128)(2,1)S(1)}, f16[1168,192]{0,1:T(8,128)(2,1)}, u32[]{:S(2)}, u32[]{:S(2)}) collective-permute-start(f16[1168,192]{0,1:T(8,128)(2,1)S(1)} %concatenate.29.clone), channel_id=1, source_target_pairs={{0,1},{1,0},{2,3},{3,2},{4,5},{5,4},{6,7},{7,6},{8,9},{9,8},{10,11... | collective-permute-start | bytes 1345544 | tf_op jit(solution)/shard_map/ppermute | solution.py:50
  41.9 2.3 %fusion.6 = f32[128,768]{1,0:T(8,128)} fusion(bf16[768,2304]{1,0:T(8,128)(2,1)} %param.5, bf16[1,128,768]{2,1,0:T(8,128)(2,1)S(1)} %copy-done), kind=kOutput, calls=%fused_computation.12 | convolution fusion | flops 150994944 | bytes 1769472 | tf_op jit(solution)/shard_map/dot_general | solution.py:108
  44.3 2.3 %fusion.4 = f32[128,768]{1,0:T(8,128)} fusion(bf16[768,2304]{1,0:T(8,128)(2,1)} %param.5, bf16[1,128,768]{2,1,0:T(8,128)(2,1)S(1)} %copy-done, bf16[1,64,768]{2,1,0:T(8,128)(2,1)S(1)} %collective-permute-done.1), kind=kOutput, calls=%fused_computation.10 | convolution fusion | flops 151388160 | bytes 1867776 | tf_op jit(solution)/shard_map/dot_general | solution.py:108
  46.6 7.3 %collective-permute-done.2 = f16[1168,192]{0,1:T(8,128)(2,1)} collective-permute-done((f16[1168,192]{0,1:T(8,128)(2,1)S(1)}, f16[1168,192]{0,1:T(8,128)(2,1)}, u32[]{:S(2)}, u32[]{:S(2)}) %collective-permute-start.2) | collective-permute-done | bytes 448544 | tf_op jit(solution)/shard_map/ppermute | solution.py:50
  53.9 1.1 %slice.85 = f16[1152,192]{0,1:T(8,128)(2,1)S(1)} slice(f16[1168,192]{0,1:T(8,128)(2,1)} %collective-permute-done.2), slice={[0:1152], [0:192]} | slice | bytes 884736 | tf_op jit(solution)/shard_map/slice | solution.py:45
  55.0 0.5 copy.24
  55.5 1.2 %slice.86 = f16[1,1]{0,1:T(2,128)(2,1)} slice(f16[1168,192]{0,1:T(8,128)(2,1)} %collective-permute-done.2), slice={[1152:1153], [0:1]} | slice | bytes 4 | tf_op jit(solution)/shard_map/slice | solution.py:44
  57.7 0.8 abs_reduce_fusion.2
  60.8 1.5 %collective-permute-start.3 = (f16[304,192]{1,0:T(8,128)(2,1)S(1)}, f16[304,192]{1,0:T(8,128)(2,1)S(1)}, u32[]{:S(2)}, u32[]{:S(2)}) collective-permute-start(f16[304,192]{1,0:T(8,128)(2,1)S(1)} %concatenate.30), channel_id=1, source_target_pairs={{0,2},{1,3},{2,4},{3,5},{4,6},{5,7},{6,0},{7,1},{8,10},{9,11},{10,... | collective-permute-start | bytes 350216 | tf_op jit(solution)/shard_map/ppermute | solution.py:50
  62.4 2.5 %collective-permute-start.4 = (f16[304,192]{1,0:T(8,128)(2,1)S(1)}, f16[304,192]{1,0:T(8,128)(2,1)S(1)}, u32[]{:S(2)}, u32[]{:S(2)}) collective-permute-start(f16[304,192]{1,0:T(8,128)(2,1)S(1)} %concatenate.31), channel_id=1, source_target_pairs={{0,4},{1,5},{2,6},{3,7},{4,0},{5,1},{6,2},{7,3},{8,12},{9,13},{10,... | collective-permute-start | bytes 350216 | tf_op jit(solution)/shard_map/ppermute | solution.py:50
  64.9 1.5 %collective-permute-start.5 = (f16[304,192]{1,0:T(8,128)(2,1)S(1)}, f16[304,192]{1,0:T(8,128)(2,1)S(1)}, u32[]{:S(2)}, u32[]{:S(2)}) collective-permute-start(f16[304,192]{1,0:T(8,128)(2,1)S(1)} %concatenate.32), channel_id=1, source_target_pairs={{0,6},{1,7},{2,0},{3,1},{4,2},{5,3},{6,4},{7,5},{8,14},{9,15},{10,... | collective-permute-start | bytes 350216 | tf_op jit(solution)/shard_map/ppermute | solution.py:50
  66.4 2.5 %fusion.12 = bf16[1,128,768]{2,1,0:T(8,128)(2,1)} fusion(f32[128,768]{1,0:T(8,128)} %fusion.4, f32[128,768]{1,0:T(8,128)S(1)} %copy-done.3, bf16[768,2304]{1,0:T(8,128)(2,1)} %param.5, bf16[1,128,768]{2,1,0:T(8,128)(2,1)S(1)} %copy-done.4, bf16[1,64,768]{2,1,0:T(8,128)(2,1)} %collective-permute-done, bf16[1,128,768]{2,1,0:T(8,128)(2,1)S(1)} %copy-done.1), kind=kOutput, calls=%fused_computation.16 | convolution fusion | flops 152666112 | bytes 2654208 | tf_op jit(solution)/shard_map/dot_general | solution.py:108
  68.8 0.8 collective-permute-done.3
  69.7 0.5 slice.88
  70.9 3.8 %collective-permute-done.4 = f16[304,192]{1,0:T(8,128)(2,1)S(1)} collective-permute-done((f16[304,192]{1,0:T(8,128)(2,1)S(1)}, f16[304,192]{1,0:T(8,128)(2,1)S(1)}, u32[]{:S(2)}, u32[]{:S(2)}) %collective-permute-start.4) | collective-permute-done | bytes 116768 | tf_op jit(solution)/shard_map/ppermute | solution.py:50
  74.7 0.5 slice.90
  76.0 0.5 slice.92
  77.3 0.9 %copy.18 = f32[192,288]{1,0:T(8,128)} copy(f32[192,288]{0,1:T(8,128)S(1)} %fusion.34) | data formatting | bytes 442368
  (25 shorter events, 0.9 us)
Async XLA Ops:
  7.2 2.9 %copy-start = (bf16[1,128,768]{2,1,0:T(8,128)(2,1)S(1)}, bf16[1,128,768]{2,1,0:T(8,128)(2,1)}, u32[]{:S(2)}) copy-start(bf16[1,128,768]{2,1,0:T(8,128)(2,1)} %param.4) | copy-start | bytes 589828
  7.2 25.4 %all-gather.2.cloned.1.call-start = ((), (), s32[]{:S(2)}) async-start(), calls=%async_computation | async-start | bytes 1966080 | tf_op jit(solution)/shard_map/all_gather | solution.py:85
  10.7 33.6 %collective-permute-start.1 = (bf16[1,64,768]{2,1,0:T(8,128)(2,1)S(1)}, bf16[1,64,768]{2,1,0:T(8,128)(2,1)S(1)}, u32[]{:S(2)}, u32[]{:S(2)}) collective-permute-start(bf16[1,64,768]{2,1,0:T(8,128)(2,1)S(1)} %get-tuple-element.13), channel_id=1, source_target_pairs={{0,8},{8,16},{16,24},{1,9},{9,17},{17,25},{2,10},{10,18},{18,26},{... | collective-permute-start | bytes 294920 | tf_op jit(solution)/shard_map/ppermute | solution.py:22
  13.0 53.3 %collective-permute-start = (bf16[1,64,768]{2,1,0:T(8,128)(2,1)}, bf16[1,64,768]{2,1,0:T(8,128)(2,1)}, u32[]{:S(2)}, u32[]{:S(2)}) collective-permute-start(bf16[1,64,768]{2,1,0:T(8,128)(2,1)} %get-tuple-element.12), channel_id=1, source_target_pairs={{8,0},{16,8},{24,16},{9,1},{17,9},{25,17},{10,2},{18,10},{26,18},{... | collective-permute-start | bytes 294920 | tf_op jit(solution)/shard_map/ppermute | solution.py:23
  32.5 1.1 %slice-start = ((bf16[2,512,768]{2,1,0:T(8,128)(2,1)}), bf16[1,512,768]{2,1,0:T(8,128)(2,1)S(1)}, s32[]{:S(2)}) async-start(bf16[2,512,768]{2,1,0:T(8,128)(2,1)} %all-gather.2.cloned.1.call-done), calls=%async_computation.1 | async-start | bytes 1572864 | tf_op jit(solution)/shard_map/slice | solution.py:88
  33.7 1.8 %copy-start.2 = (bf16[2,512,768]{2,1,0:T(8,128)(2,1)S(1)}, bf16[2,512,768]{2,1,0:T(8,128)(2,1)}, u32[]{:S(2)}) copy-start(bf16[2,512,768]{2,1,0:T(8,128)(2,1)} %all-gather.2.cloned.1.call-done) | copy-start | bytes 4718596
  40.4 13.5 %collective-permute-start.2 = (f16[1168,192]{0,1:T(8,128)(2,1)S(1)}, f16[1168,192]{0,1:T(8,128)(2,1)}, u32[]{:S(2)}, u32[]{:S(2)}) collective-permute-start(f16[1168,192]{0,1:T(8,128)(2,1)S(1)} %concatenate.29.clone), channel_id=1, source_target_pairs={{0,1},{1,0},{2,3},{3,2},{4,5},{5,4},{6,7},{7,6},{8,9},{9,8},{10,11... | collective-permute-start | bytes 1345544 | tf_op jit(solution)/shard_map/ppermute | solution.py:50
  57.7 8.7 %copy-start.1 = (bf16[1,128,768]{2,1,0:T(8,128)(2,1)S(1)}, bf16[1,128,768]{2,1,0:T(8,128)(2,1)}, u32[]{:S(2)}) copy-start(bf16[1,128,768]{2,1,0:T(8,128)(2,1)} %param.4) | copy-start | bytes 589828
  57.7 8.7 %copy-start.3 = (f32[128,768]{1,0:T(8,128)S(1)}, f32[128,768]{1,0:T(8,128)}, u32[]{:S(2)}) copy-start(f32[128,768]{1,0:T(8,128)} %fusion.6) | copy-start | bytes 1179652
  57.7 8.7 %copy-start.4 = (bf16[1,128,768]{2,1,0:T(8,128)(2,1)S(1)}, bf16[1,128,768]{2,1,0:T(8,128)(2,1)}, u32[]{:S(2)}) copy-start(bf16[1,128,768]{2,1,0:T(8,128)(2,1)} %param.3) | copy-start | bytes 589828
  60.8 8.9 %collective-permute-start.3 = (f16[304,192]{1,0:T(8,128)(2,1)S(1)}, f16[304,192]{1,0:T(8,128)(2,1)S(1)}, u32[]{:S(2)}, u32[]{:S(2)}) collective-permute-start(f16[304,192]{1,0:T(8,128)(2,1)S(1)} %concatenate.30), channel_id=1, source_target_pairs={{0,2},{1,3},{2,4},{3,5},{4,6},{5,7},{6,0},{7,1},{8,10},{9,11},{10,... | collective-permute-start | bytes 350216 | tf_op jit(solution)/shard_map/ppermute | solution.py:50
  62.4 12.4 %collective-permute-start.4 = (f16[304,192]{1,0:T(8,128)(2,1)S(1)}, f16[304,192]{1,0:T(8,128)(2,1)S(1)}, u32[]{:S(2)}, u32[]{:S(2)}) collective-permute-start(f16[304,192]{1,0:T(8,128)(2,1)S(1)} %concatenate.31), channel_id=1, source_target_pairs={{0,4},{1,5},{2,6},{3,7},{4,0},{5,1},{6,2},{7,3},{8,12},{9,13},{10,... | collective-permute-start | bytes 350216 | tf_op jit(solution)/shard_map/ppermute | solution.py:50
  64.9 11.1 %collective-permute-start.5 = (f16[304,192]{1,0:T(8,128)(2,1)S(1)}, f16[304,192]{1,0:T(8,128)(2,1)S(1)}, u32[]{:S(2)}, u32[]{:S(2)}) collective-permute-start(f16[304,192]{1,0:T(8,128)(2,1)S(1)} %concatenate.32), channel_id=1, source_target_pairs={{0,6},{1,7},{2,0},{3,1},{4,2},{5,3},{6,4},{7,5},{8,14},{9,15},{10,... | collective-permute-start | bytes 350216 | tf_op jit(solution)/shard_map/ppermute | solution.py:50
Sparse Core Ops, SparseCore 0:
  10.1 22.3 all-gather.1

commit v9 on v7

--- a/solution.py
+++ b/solution.py
@@ -58,15 +58,41 @@
     x = me % 2
     z = me // 2
     pairs = [(i, i ^ 1) for i in range(count)]
+    perms = [
+        [(2 * q + p, 2 * ((q + shift) % outer) + p) for q in range(outer) for p in range(2)]
+        for shift in range(1, outer)
+    ]
     blocks = columns.reshape(outer, 2, -1, columns.shape[1])
+    half = blocks.shape[2] // 2
     mine = lax.dynamic_index_in_dim(blocks, x, axis=1, keepdims=False)
     theirs = lax.dynamic_index_in_dim(blocks, 1 - x, axis=1, keepdims=False)
-    summed = with_layout_constraint(mine + send(theirs, pairs), Layout((0, 1, 2)))
-    total = lax.dynamic_index_in_dim(summed, z, axis=0, keepdims=False)
-    for shift in range(1, outer):
-        target = lax.dynamic_index_in_dim(summed, (z + shift) % outer, axis=0, keepdims=False)
-        perm = [(2 * q + p, 2 * ((q + shift) % outer) + p) for q in range(outer) for p in range(2)]
-        total = total + send(target, perm)
+    parts = [(mine[:, :half], theirs[:, :half]), (mine[:, half:], theirs[:, half:])]
+
+    def z_packets(summed):
+        targets = [
+            lax.dynamic_index_in_dim(summed, (z + shift) % outer, axis=0, keepdims=False)
+            for shift in range(1, outer)
+        ]
+        return [encode(t) for t in targets]
+
+    def z_finish(summed, packets):
+        total = lax.dynamic_index_in_dim(summed, z, axis=0, keepdims=False)
+        for packet, perm in zip(packets, perms):
+            arrived = lax.ppermute(packet, "batch", perm)
+            total = total + decode(with_layout_constraint(arrived, Layout((0, 1))), total.shape)
+        return total
+
+    first_mine, first_theirs = parts[0]
+    second_mine, second_theirs = parts[1]
+    first_summed = first_mine + send(first_theirs, pairs)
+    first_packets = z_packets(first_summed)
+    second_packet = encode(second_theirs)
+    first_packets, second_packet = lax.optimization_barrier((first_packets, second_packet))
+    arrived = lax.ppermute(second_packet, "batch", pairs)
+    first_total = z_finish(first_summed, first_packets)
+    second_summed = second_mine + decode(with_layout_constraint(arrived, Layout((0, 1))), second_theirs.shape)
+    second_total = z_finish(second_summed, z_packets(second_summed))
+    total = jnp.concatenate([first_total, second_total], axis=0)
     return with_layout_constraint(total, Layout((0, 1))).T
 
 

time: 70.9 us -> 79.3 us (1.12)
  between operations: 6.58 us -> 12.3 us
  starting transfers between devices: 14.9 us -> 20.6 us
  local copies, waits for them, and re-layouts: 11.7 us -> 9.2 us
  other arithmetic: 5.08 us -> 6.66 us
  matrix products: 8.42 us -> 6.94 us
  blocking collectives: 10.3 us -> 9.41 us
    ppermute x0 -> x7, starting transfers between devices: none -> 10 us  [the longest x6 7.74 us: z_finish(): arrived = lax.ppermute(packet, 'batch', perm)]
    ppermute x0 -> x7, waiting for transfers between devices: none -> 7.75 us  [the longest x6 7.75 us: z_finish(): arrived = lax.ppermute(packet, 'batch', perm)]
    ppermute x4 -> x1, waiting for transfers between devices: 13.3 us -> 5.93 us  [send(): arrived = lax.ppermute(encode(values), 'batch', perm)]
    ppermute x4 -> x1, starting transfers between devices: 7.11 us -> 2.11 us  [send(): arrived = lax.ppermute(encode(values), 'batch', perm)]
    unnamed x23 -> x21, local copies, waits for them, and re-layouts: 6.8 us -> 3.68 us
    dot_general x3, matrix products: 7.07 us -> 5.59 us  [body(): jnp.dot(window, weight[:, tap_index * in_width:(tap_index + 1) * in_width...]
    slice x4 -> x8, local copies, waits for them, and re-layouts: 2.78 us -> 4.24 us  [decode(): exponent = packed[-TAG, 0].astype(jnp.float32)]
    concatenate x4 -> x8, local copies, waits for them, and re-layouts: 1.2 us -> 0.27 us  [encode(): jnp.concatenate([scaled, tag], axis=0)]
  transfers between devices with their start and end apart: 7 -> 11, of which waited for: 3 -> 4; matrix products, arithmetic and copies ran while one was open for 22% -> 15% of each run, Pallas kernels for 0% -> 0%
where the time goes in v9:
time: 79.3 us; the launch traced here: 78.7 us
  starting transfers between devices  20.6 us (26%)
  waiting for transfers between devices  13.7 us (17%)
  between operations  12.3 us (16%)
  blocking collectives  9.41 us (12%)
  local copies, waits for them, and re-layouts  9.2 us (12%)
  matrix products  6.94 us (9%)
  other arithmetic  6.66 us (8%)
    all_gather x1, blocking collectives, body(): whole_act = lax.all_gather(act[None], 'seq', axis=1, tiled=True)[0]  9.41 us
    ppermute x6, waiting for transfers between devices, z_finish(): arrived = lax.ppermute(packet, 'batch', perm)  7.75 us
    ppermute x6, starting transfers between devices, z_finish(): arrived = lax.ppermute(packet, 'batch', perm)  7.74 us
    ppermute x1, waiting for transfers between devices, send(): arrived = lax.ppermute(encode(values), 'batch', perm)  5.93 us
    dot_general x3, matrix products, body(): jnp.dot(window, weight[:, tap_index * in_width:(tap_index + 1) * in_width...  5.59 us
    slice x8, local copies, waits for them, and re-layouts, decode(): exponent = packed[-TAG, 0].astype(jnp.float32)  4.24 us
    all_to_all x1, starting transfers between devices, body(): lax.all_to_all(cotangent, 'seq', split_axis=2, concat_axis=1, tiled=True)[0]  4.24 us
    unnamed x21, local copies, waits for them, and re-layouts  3.68 us
  transfers between devices with their start and end apart: 11, of which 4 were waited for; matrix products, arithmetic and copies ran while one was open for 15% of the time, Pallas kernels for 0%

profile of v9, /device:TPU:0, one launch (start us, length us, event | category | flops | bytes accessed | tf_op | source)
XLA Modules:
  0.0 78.7 jit_solution(14074597502077022443)
XLA Ops:
  0.6 1.3 %copy.17 = bf16[1,128,768]{1,0,2:T(2,128)(2,1)S(1)} copy(bf16[1,128,768]{2,1,0:T(8,128)(2,1)} %param.4) | data formatting | bytes 393216 | tf_op args[1]
  2.5 1.8 %reduce.8 = bf16[768,128]{1,0:T(8,128)(2,1)S(1)} reduce(bf16[768,1,128]{2,1,0:T(2,128)(2,1)S(1)} %bitcast.108, bf16[]{:T(256)} %broadcast.44), dimensions={1}, to_apply=%bitcast.97.reduce_sub_computation | reduce | bytes 393218
  4.3 0.7 reshape.103
  5.0 4.2 %all-to-all-start = ((bf16[4,2,12288]{2,1,0:T(2,128)(2,1)}), bf16[4,2,12288]{2,1,0:T(2,128)(2,1)S(1)}, u32[]{:S(2)}, u32[]{:S(2)}) async-start(bf16[4,2,12288]{2,1,0:T(2,128)(2,1)} %reshape.103), calls=%async_computation | async-start | bytes 393216 | tf_op jit(solution)/shard_map/all_to_all | solution.py:111
  9.2 1.0 %fusion.28 = bf16[1,128,768]{2,1,0:T(8,128)(2,1)S(1)} fusion(bf16[1,128,768]{2,1,0:T(8,128)(2,1)} %param.3), kind=kLoop, calls=%fused_computation.40 | loop fusion | flops 589824 | bytes 393216 | tf_op jit(solution)/shard_map/convert_element_type | solution.py:106
  10.3 9.4 %all_gather.3 = bf16[1,512,768]{2,1,0:T(8,128)(2,1)S(1)} all-gather(bf16[1,128,768]{2,1,0:T(8,128)(2,1)S(1)} %fusion.28), channel_id=1, replica_groups=mesh['seq'=4,'batch'=8] {'seq'}, dimensions={1}, use_global_device_ids=true | all-gather | bytes 983040 | tf_op jit(solution)/shard_map/all_gather | solution.py:114
  19.7 0.9 %fusion.24 = f32[128,768]{1,0:T(8,128)} fusion(bf16[1,128,768]{2,1,0:T(8,128)(2,1)S(1)} %copy-done.2), kind=kLoop, calls=%fused_computation.36 | loop fusion | flops 884736 | bytes 589824 | tf_op jit(solution)/shard_map/add | solution.py:31
  22.7 0.7 abs_reduce_fusion
  24.9 0.7 fusion.52
  25.6 2.9 %collective-permute-start.1 = (bf16[1,64,768]{2,1,0:T(8,128)(2,1)}, bf16[1,64,768]{2,1,0:T(8,128)(2,1)}, u32[]{:S(2)}, u32[]{:S(2)}) collective-permute-start(bf16[1,64,768]{2,1,0:T(8,128)(2,1)} %get-tuple-element.41), channel_id=1, source_target_pairs={{0,8},{8,16},{16,24},{1,9},{9,17},{17,25},{2,10},{10,18},{18,26},{... | collective-permute-start | bytes 294920 | tf_op jit(solution)/shard_map/ppermute | solution.py:22
  28.5 1.6 %fusion.4 = f32[128,768]{1,0:T(8,128)S(1)} fusion(bf16[768,2304]{1,0:T(8,128)(2,1)} %param.5, bf16[1,128,768]{2,1,0:T(8,128)(2,1)S(1)} %copy-done), kind=kOutput, calls=%fused_computation.8 | convolution fusion | flops 150994944 | bytes 1769472 | tf_op jit(solution)/shard_map/dot_general | solution.py:134
  30.1 1.3 %collective-permute-start = (bf16[1,64,768]{2,1,0:T(8,128)(2,1)}, bf16[1,64,768]{2,1,0:T(8,128)(2,1)}, u32[]{:S(2)}, u32[]{:S(2)}) collective-permute-start(bf16[1,64,768]{2,1,0:T(8,128)(2,1)} %get-tuple-element.40), channel_id=1, source_target_pairs={{8,0},{16,8},{24,16},{9,1},{17,9},{25,17},{10,2},{18,10},{26,18},{... | collective-permute-start | bytes 294920 | tf_op jit(solution)/shard_map/ppermute | solution.py:23
  31.7 2.1 %collective-permute-start.2 = (f16[592,192]{1,0:T(8,128)(2,1)S(1)}, f16[592,192]{1,0:T(8,128)(2,1)S(1)}, u32[]{:S(2)}, u32[]{:S(2)}) collective-permute-start(f16[592,192]{1,0:T(8,128)(2,1)S(1)} %concatenate.40), channel_id=1, source_target_pairs={{0,1},{1,0},{2,3},{3,2},{4,5},{5,4},{6,7},{7,6},{8,9},{9,8},{10,11... | collective-permute-start | bytes 681992 | tf_op jit(solution)/shard_map/ppermute | solution.py:50
  33.9 1.7 %fusion.2 = f32[128,768]{1,0:T(8,128)S(1)} fusion(bf16[768,2304]{1,0:T(8,128)(2,1)} %param.5, bf16[1,128,768]{2,1,0:T(8,128)(2,1)S(1)} %copy-done, bf16[1,64,768]{2,1,0:T(8,128)(2,1)} %collective-permute-done.1), kind=kOutput, calls=%fused_computation.6 | convolution fusion | flops 151388160 | bytes 1867776 | tf_op jit(solution)/shard_map/dot_general | solution.py:134
  35.5 5.9 %collective-permute-done.2 = f16[592,192]{1,0:T(8,128)(2,1)S(1)} collective-permute-done((f16[592,192]{1,0:T(8,128)(2,1)S(1)}, f16[592,192]{1,0:T(8,128)(2,1)S(1)}, u32[]{:S(2)}, u32[]{:S(2)}) %collective-permute-start.2) | collective-permute-done | bytes 227360 | tf_op jit(solution)/shard_map/ppermute | solution.py:50
  42.8 0.7 abs_reduce_fusion.5
  45.9 2.3 %collective-permute-start.6 = (f16[592,192]{1,0:T(8,128)(2,1)S(1)}, f16[592,192]{1,0:T(8,128)(2,1)S(1)}, u32[]{:S(2)}, u32[]{:S(2)}) collective-permute-start(f16[592,192]{1,0:T(8,128)(2,1)S(1)} %concatenate.44), channel_id=1, source_target_pairs={{0,1},{1,0},{2,3},{3,2},{4,5},{5,4},{6,7},{7,6},{8,9},{9,8},{10,11... | collective-permute-start | bytes 681992 | tf_op jit(solution)/shard_map/ppermute | solution.py:91
  48.2 3.6 %collective-permute-start.5 = (f16[160,192]{1,0:T(8,128)(2,1)S(1)}, f16[160,192]{1,0:T(8,128)(2,1)S(1)}, u32[]{:S(2)}, u32[]{:S(2)}) collective-permute-start(f16[160,192]{1,0:T(8,128)(2,1)S(1)} %concatenate.43), channel_id=1, source_target_pairs={{0,6},{1,7},{2,0},{3,1},{4,2},{5,3},{6,4},{7,5},{8,14},{9,15},{10,... | collective-permute-start | bytes 184328 | tf_op jit(solution)/shard_map/ppermute | solution.py:81
  51.8 1.0 %collective-permute-start.3 = (f16[160,192]{1,0:T(8,128)(2,1)S(1)}, f16[160,192]{1,0:T(8,128)(2,1)S(1)}, u32[]{:S(2)}, u32[]{:S(2)}) collective-permute-start(f16[160,192]{1,0:T(8,128)(2,1)S(1)} %concatenate.41), channel_id=1, source_target_pairs={{0,2},{1,3},{2,4},{3,5},{4,6},{5,7},{6,0},{7,1},{8,10},{9,11},{10,... | collective-permute-start | bytes 184328 | tf_op jit(solution)/shard_map/ppermute | solution.py:81
  52.8 2.3 %fusion.10 = bf16[1,128,768]{2,1,0:T(8,128)(2,1)} fusion(f32[128,768]{1,0:T(8,128)S(1)} %copy-done.1, f32[128,768]{1,0:T(8,128)S(1)} %fusion.2, f32[128,768]{1,0:T(8,128)S(1)} %fusion.4, bf16[768,2304]{1,0:T(8,128)(2,1)} %param.5, bf16[1,64,768]{2,1,0:T(8,128)(2,1)} %collective-permute-done, bf16[1,128,768]{2,1,0:T(8,128)(2,1)S(1)} %copy-done), kind=kOutput, calls=%fused_computation.12 | convolution fusion | flops 151781376 | bytes 2850816 | tf_op jit(solution)/shard_map/dot_general | solution.py:134
  55.2 0.5 slice.133
  56.4 2.9 %collective-permute-done.4 = f16[160,192]{1,0:T(8,128)(2,1)S(1)} collective-permute-done((f16[160,192]{1,0:T(8,128)(2,1)S(1)}, f16[160,192]{1,0:T(8,128)(2,1)S(1)}, u32[]{:S(2)}, u32[]{:S(2)}) %collective-permute-start.4) | collective-permute-done | bytes 61472 | tf_op jit(solution)/shard_map/ppermute | solution.py:81
  59.3 0.5 slice.131
  60.5 0.5 slice.129
  61.6 0.6 slice.136
  63.1 0.7 abs_reduce_fusion.4
  66.1 2.2 %collective-permute-start.9 = (f16[160,192]{1,0:T(8,128)(2,1)S(1)}, f16[160,192]{1,0:T(8,128)(2,1)S(1)}, u32[]{:S(2)}, u32[]{:S(2)}) collective-permute-start(f16[160,192]{1,0:T(8,128)(2,1)S(1)} %concatenate.47), channel_id=1, source_target_pairs={{0,6},{1,7},{2,0},{3,1},{4,2},{5,3},{6,4},{7,5},{8,14},{9,15},{10,... | collective-permute-start | bytes 184328 | tf_op jit(solution)/shard_map/ppermute | solution.py:81
  68.4 0.9 %collective-permute-start.7 = (f16[160,192]{1,0:T(8,128)(2,1)S(1)}, f16[160,192]{1,0:T(8,128)(2,1)S(1)}, u32[]{:S(2)}, u32[]{:S(2)}) collective-permute-start(f16[160,192]{1,0:T(8,128)(2,1)S(1)} %concatenate.45), channel_id=1, source_target_pairs={{0,2},{1,3},{2,4},{3,5},{4,6},{5,7},{6,0},{7,1},{8,10},{9,11},{10,... | collective-permute-start | bytes 184328 | tf_op jit(solution)/shard_map/ppermute | solution.py:81
  69.4 2.0 %collective-permute-done.9 = f16[160,192]{1,0:T(8,128)(2,1)S(1)} collective-permute-done((f16[160,192]{1,0:T(8,128)(2,1)S(1)}, f16[160,192]{1,0:T(8,128)(2,1)S(1)}, u32[]{:S(2)}, u32[]{:S(2)}) %collective-permute-start.9) | collective-permute-done | bytes 61472 | tf_op jit(solution)/shard_map/ppermute | solution.py:81
  72.6 2.8 %collective-permute-done.8 = f16[160,192]{1,0:T(8,128)(2,1)S(1)} collective-permute-done((f16[160,192]{1,0:T(8,128)(2,1)S(1)}, f16[160,192]{1,0:T(8,128)(2,1)S(1)}, u32[]{:S(2)}, u32[]{:S(2)}) %collective-permute-start.8) | collective-permute-done | bytes 61472 | tf_op jit(solution)/shard_map/ppermute | solution.py:81
  76.5 0.5 slice.138
  77.8 0.9 %copy.23 = f32[192,288]{1,0:T(8,128)} copy(f32[192,288]{0,1:T(8,128)S(1)} %maximum_bitcast_fusion) | data formatting | bytes 442368
  (54 shorter events, 5.1 us)
Async XLA Ops:
  0.6 19.1 %copy-start.2 = (bf16[1,128,768]{2,1,0:T(8,128)(2,1)S(1)}, bf16[1,128,768]{2,1,0:T(8,128)(2,1)}, u32[]{:S(2)}) copy-start(bf16[1,128,768]{2,1,0:T(8,128)(2,1)} %param.3) | copy-start | bytes 589828
  5.0 15.6 %all-to-all-start = ((bf16[4,2,12288]{2,1,0:T(2,128)(2,1)}), bf16[4,2,12288]{2,1,0:T(2,128)(2,1)S(1)}, u32[]{:S(2)}, u32[]{:S(2)}) async-start(bf16[4,2,12288]{2,1,0:T(2,128)(2,1)} %reshape.103), calls=%async_computation | async-start | bytes 393216 | tf_op jit(solution)/shard_map/all_to_all | solution.py:111
  22.6 2.3 %copy-start = (bf16[1,128,768]{2,1,0:T(8,128)(2,1)S(1)}, bf16[1,128,768]{2,1,0:T(8,128)(2,1)}, u32[]{:S(2)}) copy-start(bf16[1,128,768]{2,1,0:T(8,128)(2,1)} %param.4) | copy-start | bytes 589828
  25.6 8.3 %collective-permute-start.1 = (bf16[1,64,768]{2,1,0:T(8,128)(2,1)}, bf16[1,64,768]{2,1,0:T(8,128)(2,1)}, u32[]{:S(2)}, u32[]{:S(2)}) collective-permute-start(bf16[1,64,768]{2,1,0:T(8,128)(2,1)} %get-tuple-element.41), channel_id=1, source_target_pairs={{0,8},{8,16},{16,24},{1,9},{9,17},{17,25},{2,10},{10,18},{18,26},{... | collective-permute-start | bytes 294920 | tf_op jit(solution)/shard_map/ppermute | solution.py:22
  30.1 22.8 %collective-permute-start = (bf16[1,64,768]{2,1,0:T(8,128)(2,1)}, bf16[1,64,768]{2,1,0:T(8,128)(2,1)}, u32[]{:S(2)}, u32[]{:S(2)}) collective-permute-start(bf16[1,64,768]{2,1,0:T(8,128)(2,1)} %get-tuple-element.40), channel_id=1, source_target_pairs={{8,0},{16,8},{24,16},{9,1},{17,9},{25,17},{10,2},{18,10},{26,18},{... | collective-permute-start | bytes 294920 | tf_op jit(solution)/shard_map/ppermute | solution.py:23
  31.7 9.8 %collective-permute-start.2 = (f16[592,192]{1,0:T(8,128)(2,1)S(1)}, f16[592,192]{1,0:T(8,128)(2,1)S(1)}, u32[]{:S(2)}, u32[]{:S(2)}) collective-permute-start(f16[592,192]{1,0:T(8,128)(2,1)S(1)} %concatenate.40), channel_id=1, source_target_pairs={{0,1},{1,0},{2,3},{3,2},{4,5},{5,4},{6,7},{7,6},{8,9},{9,8},{10,11... | collective-permute-start | bytes 681992 | tf_op jit(solution)/shard_map/ppermute | solution.py:50
  35.5 17.3 %copy-start.1 = (f32[128,768]{1,0:T(8,128)S(1)}, f32[128,768]{1,0:T(8,128)}, u32[]{:S(2)}) copy-start(f32[128,768]{1,0:T(8,128)} %fusion.24) | copy-start | bytes 1179652
  45.9 15.7 %collective-permute-start.6 = (f16[592,192]{1,0:T(8,128)(2,1)S(1)}, f16[592,192]{1,0:T(8,128)(2,1)S(1)}, u32[]{:S(2)}, u32[]{:S(2)}) collective-permute-start(f16[592,192]{1,0:T(8,128)(2,1)S(1)} %concatenate.44), channel_id=1, source_target_pairs={{0,1},{1,0},{2,3},{3,2},{4,5},{5,4},{6,7},{7,6},{8,9},{9,8},{10,11... | collective-permute-start | bytes 681992 | tf_op jit(solution)/shard_map/ppermute | solution.py:91
  48.2 7.0 %collective-permute-start.5 = (f16[160,192]{1,0:T(8,128)(2,1)S(1)}, f16[160,192]{1,0:T(8,128)(2,1)S(1)}, u32[]{:S(2)}, u32[]{:S(2)}) collective-permute-start(f16[160,192]{1,0:T(8,128)(2,1)S(1)} %concatenate.43), channel_id=1, source_target_pairs={{0,6},{1,7},{2,0},{3,1},{4,2},{5,3},{6,4},{7,5},{8,14},{9,15},{10,... | collective-permute-start | bytes 184328 | tf_op jit(solution)/shard_map/ppermute | solution.py:81
  51.8 7.5 %collective-permute-start.4 = (f16[160,192]{1,0:T(8,128)(2,1)S(1)}, f16[160,192]{1,0:T(8,128)(2,1)S(1)}, u32[]{:S(2)}, u32[]{:S(2)}) collective-permute-start(f16[160,192]{1,0:T(8,128)(2,1)S(1)} %concatenate.42), channel_id=1, source_target_pairs={{0,4},{1,5},{2,6},{3,7},{4,0},{5,1},{6,2},{7,3},{8,12},{9,13},{10,... | collective-permute-start | bytes 184328 | tf_op jit(solution)/shard_map/ppermute | solution.py:81
  51.8 8.7 %collective-permute-start.3 = (f16[160,192]{1,0:T(8,128)(2,1)S(1)}, f16[160,192]{1,0:T(8,128)(2,1)S(1)}, u32[]{:S(2)}, u32[]{:S(2)}) collective-permute-start(f16[160,192]{1,0:T(8,128)(2,1)S(1)} %concatenate.41), channel_id=1, source_target_pairs={{0,2},{1,3},{2,4},{3,5},{4,6},{5,7},{6,0},{7,1},{8,10},{9,11},{10,... | collective-permute-start | bytes 184328 | tf_op jit(solution)/shard_map/ppermute | solution.py:81
  59.3 3.6 %copy-start.3 = (f16[160,192]{1,0:T(8,128)(2,1)}, f16[160,192]{1,0:T(8,128)(2,1)S(1)}, u32[]{:S(2)}) copy-start(f16[160,192]{1,0:T(8,128)(2,1)S(1)} %collective-permute-done.4) | copy-start | bytes 184324
  60.5 2.5 %copy-start.5 = (f16[160,192]{1,0:T(8,128)(2,1)}, f16[160,192]{1,0:T(8,128)(2,1)S(1)}, u32[]{:S(2)}) copy-start(f16[160,192]{1,0:T(8,128)(2,1)S(1)} %collective-permute-done.3) | copy-start | bytes 184324
  63.0 6.4 %copy-start.4 = (f16[160,192]{1,0:T(8,128)(2,1)S(1)}, f16[160,192]{1,0:T(8,128)(2,1)}, u32[]{:S(2)}) copy-start(f16[160,192]{1,0:T(8,128)(2,1)} %copy-done.3) | copy-start | bytes 184324
  63.0 6.3 %copy-start.6 = (f16[160,192]{1,0:T(8,128)(2,1)S(1)}, f16[160,192]{1,0:T(8,128)(2,1)}, u32[]{:S(2)}) copy-start(f16[160,192]{1,0:T(8,128)(2,1)} %copy-done.5) | copy-start | bytes 184324
  66.1 5.2 %collective-permute-start.9 = (f16[160,192]{1,0:T(8,128)(2,1)S(1)}, f16[160,192]{1,0:T(8,128)(2,1)S(1)}, u32[]{:S(2)}, u32[]{:S(2)}) collective-permute-start(f16[160,192]{1,0:T(8,128)(2,1)S(1)} %concatenate.47), channel_id=1, source_target_pairs={{0,6},{1,7},{2,0},{3,1},{4,2},{5,3},{6,4},{7,5},{8,14},{9,15},{10,... | collective-permute-start | bytes 184328 | tf_op jit(solution)/shard_map/ppermute | solution.py:81
  68.3 7.1 %collective-permute-start.8 = (f16[160,192]{1,0:T(8,128)(2,1)S(1)}, f16[160,192]{1,0:T(8,128)(2,1)S(1)}, u32[]{:S(2)}, u32[]{:S(2)}) collective-permute-start(f16[160,192]{1,0:T(8,128)(2,1)S(1)} %concatenate.46), channel_id=1, source_target_pairs={{0,4},{1,5},{2,6},{3,7},{4,0},{5,1},{6,2},{7,3},{8,12},{9,13},{10,... | collective-permute-start | bytes 184328 | tf_op jit(solution)/shard_map/ppermute | solution.py:81
  68.4 8.1 %collective-permute-start.7 = (f16[160,192]{1,0:T(8,128)(2,1)S(1)}, f16[160,192]{1,0:T(8,128)(2,1)S(1)}, u32[]{:S(2)}, u32[]{:S(2)}) collective-permute-start(f16[160,192]{1,0:T(8,128)(2,1)S(1)} %concatenate.45), channel_id=1, source_target_pairs={{0,2},{1,3},{2,4},{3,5},{4,6},{5,7},{6,0},{7,1},{8,10},{9,11},{10,... | collective-permute-start | bytes 184328 | tf_op jit(solution)/shard_map/ppermute | solution.py:81

commit v10 on v7

--- a/solution.py
+++ b/solution.py
@@ -62,11 +62,15 @@
     mine = lax.dynamic_index_in_dim(blocks, x, axis=1, keepdims=False)
     theirs = lax.dynamic_index_in_dim(blocks, 1 - x, axis=1, keepdims=False)
     summed = with_layout_constraint(mine + send(theirs, pairs), Layout((0, 1, 2)))
-    total = lax.dynamic_index_in_dim(summed, z, axis=0, keepdims=False)
-    for shift in range(1, outer):
-        target = lax.dynamic_index_in_dim(summed, (z + shift) % outer, axis=0, keepdims=False)
-        perm = [(2 * q + p, 2 * ((q + shift) % outer) + p) for q in range(outer) for p in range(2)]
-        total = total + send(target, perm)
+    packets = jnp.stack([encode(summed[j]) for j in range(outer)])
+    packets = with_layout_constraint(packets, Layout((0, 1, 2)))
+    groups = [[2 * q + p for q in range(outer)] for p in range(2)]
+    swapped = lax.all_to_all(jnp.swapaxes(packets, 1, 2), "batch", 0, 0, axis_index_groups=groups, tiled=True)
+    arrived = with_layout_constraint(jnp.swapaxes(swapped, 1, 2), Layout((0, 1, 2)))
+    others = jnp.stack([decode(arrived[j], summed.shape[1:]) for j in range(outer)])
+    others = jnp.where((jnp.arange(outer) == z)[:, None, None], 0.0, others)
+    own = lax.dynamic_index_in_dim(summed, z, axis=0, keepdims=False)
+    total = own + jnp.sum(others, axis=0)
     return with_layout_constraint(total, Layout((0, 1))).T
 
 

time: 70.9 us -> 77.8 us (1.097)
  waiting for transfers between devices: 13.4 us -> 17.1 us
  local copies, waits for them, and re-layouts: 11.7 us -> 13.8 us
  matrix products: 8.42 us -> 6.92 us
  between operations: 6.58 us -> 7.91 us
    all_to_all x0 -> x1, waiting for transfers between devices: none -> 8.33 us  [reduce_over_batch(): lax.all_to_all(jnp.swapaxes(packets, 1, 2), 'batch', 0, 0, axis_index_gro...]
    all_to_all x0 -> x1, starting transfers between devices: none -> 5.11 us  [reduce_over_batch(): lax.all_to_all(jnp.swapaxes(packets, 1, 2), 'batch', 0, 0, axis_index_gro...]
    ppermute x4 -> x1, starting transfers between devices: 7.11 us -> 2.11 us  [send(): arrived = lax.ppermute(encode(values), 'batch', perm)]
    ppermute x4 -> x1, waiting for transfers between devices: 13.3 us -> 8.54 us  [send(): arrived = lax.ppermute(encode(values), 'batch', perm)]
    dot_general x3, matrix products: 7.07 us -> 5.57 us  [body(): jnp.dot(window, weight[:, tap_index * in_width:(tap_index + 1) * in_width...]
    unnamed x23 -> x19, local copies, waits for them, and re-layouts: 6.8 us -> 5.3 us
    transpose x0 -> x1, local copies, waits for them, and re-layouts: none -> 1.27 us  [reduce_over_batch(): jnp.swapaxes(packets, 1, 2)]
    slice x1, local copies, waits for them, and re-layouts: 0.08 us -> 1.09 us  [decode(): values = packed[:-TAG].astype(jnp.float32) * jnp.exp2(exponent - HEADROOM)]
  transfers between devices with their start and end apart: 7 -> 5, of which waited for: 3 -> 3; matrix products, arithmetic and copies ran while one was open for 22% -> 17% of each run, Pallas kernels for 0% -> 0%
where the time goes in v10:
time: 77.8 us; the launch traced here: 77.2 us
  waiting for transfers between devices  17.1 us (22%)
  starting transfers between devices  15.5 us (20%)
  local copies, waits for them, and re-layouts  13.8 us (18%)
  blocking collectives  10.3 us (13%)
  between operations  7.91 us (10%)
  matrix products  6.92 us (9%)
  other arithmetic  5.6 us (7%)
    all_gather x1, blocking collectives, body(): whole_act = lax.all_gather(act[None], 'seq', axis=1, tiled=True)[0]  10.3 us
    ppermute x1, waiting for transfers between devices, send(): arrived = lax.ppermute(encode(values), 'batch', perm)  8.54 us
    all_to_all x1, waiting for transfers between devices, reduce_over_batch(): lax.all_to_all(jnp.swapaxes(packets, 1, 2), 'batch', 0, 0, axis_index_gro...  8.33 us
    dot_general x3, matrix products, body(): jnp.dot(window, weight[:, tap_index * in_width:(tap_index + 1) * in_width...  5.57 us
    unnamed x19, local copies, waits for them, and re-layouts  5.3 us
    all_to_all x1, starting transfers between devices, reduce_over_batch(): lax.all_to_all(jnp.swapaxes(packets, 1, 2), 'batch', 0, 0, axis_index_gro...  5.11 us
    all_to_all x1, starting transfers between devices, body(): lax.all_to_all(cotangent, 'seq', split_axis=2, concat_axis=1, tiled=True)[0]  4.24 us
    slice x5, local copies, waits for them, and re-layouts, decode(): exponent = packed[-TAG, 0].astype(jnp.float32)  3.35 us
  transfers between devices with their start and end apart: 5, of which 3 were waited for; matrix products, arithmetic and copies ran while one was open for 17% of the time, Pallas kernels for 0%

profile of v10, /device:TPU:0, one launch (start us, length us, event | category | flops | bytes accessed | tf_op | source)
XLA Modules:
  0.0 77.2 jit_solution(15140333509642331945)
XLA Ops:
  0.6 1.3 %copy.19 = bf16[1,128,768]{1,0,2:T(2,128)(2,1)S(1)} copy(bf16[1,128,768]{2,1,0:T(8,128)(2,1)} %param.4) | data formatting | bytes 393216 | tf_op args[1]
  2.0 0.5 broadcast.37
  2.5 1.8 %reduce.5 = bf16[768,128]{1,0:T(8,128)(2,1)S(1)} reduce(bf16[768,1,128]{2,1,0:T(2,128)(2,1)S(1)} %bitcast.120, bf16[]{:T(256)} %broadcast.37), dimensions={1}, to_apply=%bitcast.105.reduce_sub_computation | reduce | bytes 393218
  4.3 0.7 reshape.78
  5.0 4.2 %all-to-all-start = ((bf16[4,2,12288]{2,1,0:T(2,128)(2,1)}), bf16[4,2,12288]{2,1,0:T(2,128)(2,1)S(1)}, u32[]{:S(2)}, u32[]{:S(2)}) async-start(bf16[4,2,12288]{2,1,0:T(2,128)(2,1)} %reshape.78), calls=%async_computation | async-start | bytes 393216 | tf_op jit(solution)/shard_map/all_to_all | solution.py:89
  9.3 10.3 %all_gather.3 = bf16[1,512,768]{2,1,0:T(8,128)(2,1)S(1)} all-gather(bf16[1,128,768]{2,1,0:T(8,128)(2,1)S(1)} %fusion.31), channel_id=1, replica_groups=mesh['seq'=4,'batch'=8] {'seq'}, dimensions={1}, use_global_device_ids=true | all-gather | bytes 983040 | tf_op jit(solution)/shard_map/all_gather | solution.py:92
  19.7 0.9 %fusion.27 = f32[128,768]{1,0:T(8,128)} fusion(bf16[1,128,768]{2,1,0:T(8,128)(2,1)S(1)} %copy-done.3), kind=kLoop, calls=%fused_computation.35 | loop fusion | flops 884736 | bytes 589824 | tf_op jit(solution)/shard_map/add | solution.py:31
  21.4 0.5 fusion.16
  22.6 0.8 %fusion.3 = f32[]{:T(128)} fusion(f32[4,2,288,192]{3,2,1,0:T(8,128)S(1)} %bitcast.108, s32[]{:T(128)S(6)} %select_n.28), kind=kLoop, calls=%fused_computation.9 | loop fusion | flops 442367 | bytes 884744 | tf_op jit(solution)/shard_map/reduce_max | solution.py:36
  24.3 1.1 %copy.39 = f16[1152,192]{0,1:T(8,128)(2,1)} copy(f16[1152,192]{1,0:T(8,128)(2,1)S(1)} %bitcast.114) | data formatting | bytes 884736
  25.4 1.1 %concatenate.28.clone = f16[1168,192]{0,1:T(8,128)(2,1)S(1)} pad(f16[1152,192]{0,1:T(8,128)(2,1)} %copy.39, f16[]{:T(256)S(6)} %convert_element_type.109), padding=0_16x0_0 | pad | bytes 890882 | tf_op jit(solution)/shard_map/concatenate | solution.py:40
  26.5 2.1 %collective-permute-start.2 = (f16[1168,192]{0,1:T(8,128)(2,1)S(1)}, f16[1168,192]{0,1:T(8,128)(2,1)}, u32[]{:S(2)}, u32[]{:S(2)}) collective-permute-start(f16[1168,192]{0,1:T(8,128)(2,1)S(1)} %concatenate.28.clone), channel_id=1, source_target_pairs={{0,1},{1,0},{2,3},{3,2},{4,5},{5,4},{6,7},{7,6},{8,9},{9,8},{10,11... | collective-permute-start | bytes 1345544 | tf_op jit(solution)/shard_map/ppermute | solution.py:50
  28.6 0.7 fusion.50
  29.3 2.6 %collective-permute-start.1 = (bf16[1,64,768]{2,1,0:T(8,128)(2,1)}, bf16[1,64,768]{2,1,0:T(8,128)(2,1)}, u32[]{:S(2)}, u32[]{:S(2)}) collective-permute-start(bf16[1,64,768]{2,1,0:T(8,128)(2,1)} %get-tuple-element.31), channel_id=1, source_target_pairs={{0,8},{8,16},{16,24},{1,9},{9,17},{17,25},{2,10},{10,18},{18,26},{... | collective-permute-start | bytes 294920 | tf_op jit(solution)/shard_map/ppermute | solution.py:22
  31.9 8.5 %collective-permute-done.2 = f16[1168,192]{0,1:T(8,128)(2,1)} collective-permute-done((f16[1168,192]{0,1:T(8,128)(2,1)S(1)}, f16[1168,192]{0,1:T(8,128)(2,1)}, u32[]{:S(2)}, u32[]{:S(2)}) %collective-permute-start.2) | collective-permute-done | bytes 448544 | tf_op jit(solution)/shard_map/ppermute | solution.py:50
  40.4 1.1 %slice.123 = f16[1152,192]{0,1:T(8,128)(2,1)S(1)} slice(f16[1168,192]{0,1:T(8,128)(2,1)} %collective-permute-done.2), slice={[0:1152], [0:192]} | slice | bytes 884736 | tf_op jit(solution)/shard_map/slice | solution.py:45
  41.5 0.5 copy.37
  42.0 1.2 %slice.124 = f16[1,1]{0,1:T(2,128)(2,1)} slice(f16[1168,192]{0,1:T(8,128)(2,1)} %collective-permute-done.2), slice={[1152:1153], [0:1]} | slice | bytes 4 | tf_op jit(solution)/shard_map/slice | solution.py:44
  44.2 0.8 abs_reduce_fusion.3
  48.3 1.3 %copy.28 = f16[4,192,304]{2,1,0:T(8,128)(2,1)} copy(f16[4,192,304]{1,2,0:T(8,128)(2,1)S(1)} %maximum_bitcast_fusion) | data formatting | bytes 933888 | tf_op jit(solution)/shard_map/transpose | solution.py:68
  49.6 5.1 %all-to-all-start.1 = ((f16[4,192,304]{2,1,0:T(8,128)(2,1)}), f16[4,192,304]{2,1,0:T(8,128)(2,1)S(1)}, u32[]{:S(2)}, u32[]{:S(2)}) async-start(f16[4,192,304]{2,1,0:T(8,128)(2,1)} %copy.28), calls=%async_computation.1 | async-start | bytes 1179648 | tf_op jit(solution)/shard_map/all_to_all | solution.py:68
  54.7 1.6 %fusion.7 = f32[128,768]{1,0:T(8,128)S(1)} fusion(bf16[768,2304]{1,0:T(8,128)(2,1)} %param.5, bf16[1,128,768]{2,1,0:T(8,128)(2,1)S(1)} %copy-done.1), kind=kOutput, calls=%fused_computation.14 | convolution fusion | flops 150994944 | bytes 1769472 | tf_op jit(solution)/shard_map/dot_general | solution.py:112
  56.4 1.4 %collective-permute-start = (bf16[1,64,768]{2,1,0:T(8,128)(2,1)S(1)}, bf16[1,64,768]{2,1,0:T(8,128)(2,1)S(1)}, u32[]{:S(2)}, u32[]{:S(2)}) collective-permute-start(bf16[1,64,768]{2,1,0:T(8,128)(2,1)S(1)} %copy-done.4), channel_id=1, source_target_pairs={{8,0},{16,8},{24,16},{9,1},{17,9},{25,17},{10,2},{18,10},{26,18},{... | collective-permute-start | bytes 294920 | tf_op jit(solution)/shard_map/ppermute | solution.py:23
  57.8 1.7 %fusion.5 = f32[128,768]{1,0:T(8,128)S(1)} fusion(bf16[768,2304]{1,0:T(8,128)(2,1)} %param.5, bf16[1,128,768]{2,1,0:T(8,128)(2,1)S(1)} %copy-done.1, bf16[1,64,768]{2,1,0:T(8,128)(2,1)} %collective-permute-done.1), kind=kOutput, calls=%fused_computation.12 | convolution fusion | flops 151388160 | bytes 1867776 | tf_op jit(solution)/shard_map/dot_general | solution.py:112
  59.7 2.3 %fusion.13 = bf16[1,128,768]{2,1,0:T(8,128)(2,1)} fusion(f32[128,768]{1,0:T(8,128)S(1)} %copy-done.2, f32[128,768]{1,0:T(8,128)S(1)} %fusion.5, f32[128,768]{1,0:T(8,128)S(1)} %fusion.7, bf16[768,2304]{1,0:T(8,128)(2,1)} %param.5, bf16[1,64,768]{2,1,0:T(8,128)(2,1)S(1)} %collective-permute-done, bf16[1,128,768]{2,1,0:T(8,128)(2,1)S(1)} %copy-done.1), kind=kOutput, calls=%fused_computation.18 | convolution fusion | flops 151781376 | bytes 2850816 | tf_op jit(solution)/shard_map/dot_general | solution.py:112
  62.0 8.3 %all-to-all-done.1 = f16[4,192,304]{2,1,0:T(8,128)(2,1)S(1)} async-done(((f16[4,192,304]{2,1,0:T(8,128)(2,1)}), f16[4,192,304]{2,1,0:T(8,128)(2,1)S(1)}, u32[]{:S(2)}, u32[]{:S(2)}) %all-to-all-start.1) | async-done | bytes 466976 | tf_op jit(solution)/shard_map/all_to_all | solution.py:68
  70.3 0.6 copy.29
  71.1 0.5 slice.131
  72.3 0.6 slice.140
  73.6 0.5 slice.137
  74.7 0.5 slice.134
  76.3 0.9 %copy.30 = f32[192,288]{1,0:T(8,128)} copy(f32[192,288]{0,1:T(8,128)S(1)} %fusion.34) | data formatting | bytes 442368
  (33 shorter events, 3.1 us)
Async XLA Ops:
  0.6 8.6 %copy-start.3 = (bf16[1,128,768]{2,1,0:T(8,128)(2,1)S(1)}, bf16[1,128,768]{2,1,0:T(8,128)(2,1)}, u32[]{:S(2)}) copy-start(bf16[1,128,768]{2,1,0:T(8,128)(2,1)} %param.3) | copy-start | bytes 589828
  5.0 15.6 %all-to-all-start = ((bf16[4,2,12288]{2,1,0:T(2,128)(2,1)}), bf16[4,2,12288]{2,1,0:T(2,128)(2,1)S(1)}, u32[]{:S(2)}, u32[]{:S(2)}) async-start(bf16[4,2,12288]{2,1,0:T(2,128)(2,1)} %reshape.78), calls=%async_computation | async-start | bytes 393216 | tf_op jit(solution)/shard_map/all_to_all | solution.py:89
  24.3 4.4 %copy-start = (bf16[1,128,768]{2,1,0:T(8,128)(2,1)S(1)}, bf16[1,128,768]{2,1,0:T(8,128)(2,1)}, u32[]{:S(2)}) copy-start(bf16[1,128,768]{2,1,0:T(8,128)(2,1)} %param.4) | copy-start | bytes 589828
  26.5 13.9 %collective-permute-start.2 = (f16[1168,192]{0,1:T(8,128)(2,1)S(1)}, f16[1168,192]{0,1:T(8,128)(2,1)}, u32[]{:S(2)}, u32[]{:S(2)}) collective-permute-start(f16[1168,192]{0,1:T(8,128)(2,1)S(1)} %concatenate.28.clone), channel_id=1, source_target_pairs={{0,1},{1,0},{2,3},{3,2},{4,5},{5,4},{6,7},{7,6},{8,9},{9,8},{10,11... | collective-permute-start | bytes 1345544 | tf_op jit(solution)/shard_map/ppermute | solution.py:50
  29.3 28.5 %collective-permute-start.1 = (bf16[1,64,768]{2,1,0:T(8,128)(2,1)}, bf16[1,64,768]{2,1,0:T(8,128)(2,1)}, u32[]{:S(2)}, u32[]{:S(2)}) collective-permute-start(bf16[1,64,768]{2,1,0:T(8,128)(2,1)} %get-tuple-element.31), channel_id=1, source_target_pairs={{0,8},{8,16},{16,24},{1,9},{9,17},{17,25},{2,10},{10,18},{18,26},{... | collective-permute-start | bytes 294920 | tf_op jit(solution)/shard_map/ppermute | solution.py:22
  48.3 6.4 %copy-start.1 = (bf16[1,128,768]{2,1,0:T(8,128)(2,1)S(1)}, bf16[1,128,768]{2,1,0:T(8,128)(2,1)}, u32[]{:S(2)}) copy-start(bf16[1,128,768]{2,1,0:T(8,128)(2,1)} %param.4) | copy-start | bytes 589828
  49.6 20.7 %all-to-all-start.1 = ((f16[4,192,304]{2,1,0:T(8,128)(2,1)}), f16[4,192,304]{2,1,0:T(8,128)(2,1)S(1)}, u32[]{:S(2)}, u32[]{:S(2)}) async-start(f16[4,192,304]{2,1,0:T(8,128)(2,1)} %copy.28), calls=%async_computation.1 | async-start | bytes 1179648 | tf_op jit(solution)/shard_map/all_to_all | solution.py:68
  54.7 1.7 %copy-start.4 = (bf16[1,64,768]{2,1,0:T(8,128)(2,1)S(1)}, bf16[1,64,768]{2,1,0:T(8,128)(2,1)}, u32[]{:S(2)}) copy-start(bf16[1,64,768]{2,1,0:T(8,128)(2,1)} %get-tuple-element.30) | copy-start | bytes 294916
  56.4 3.3 %copy-start.2 = (f32[128,768]{1,0:T(8,128)S(1)}, f32[128,768]{1,0:T(8,128)}, u32[]{:S(2)}) copy-start(f32[128,768]{1,0:T(8,128)} %fusion.27) | copy-start | bytes 1179652
  56.4 3.3 %collective-permute-start = (bf16[1,64,768]{2,1,0:T(8,128)(2,1)S(1)}, bf16[1,64,768]{2,1,0:T(8,128)(2,1)S(1)}, u32[]{:S(2)}, u32[]{:S(2)}) collective-permute-start(bf16[1,64,768]{2,1,0:T(8,128)(2,1)S(1)} %copy-done.4), channel_id=1, source_target_pairs={{8,0},{16,8},{24,16},{9,1},{17,9},{25,17},{10,2},{18,10},{26,18},{... | collective-permute-start | bytes 294920 | tf_op jit(solution)/shard_map/ppermute | solution.py:23

commit v11 on v7

--- a/solution.py
+++ b/solution.py
@@ -82,18 +82,19 @@
     batch_count = lax.axis_size("batch")
     counted = batch_count * inputs.shape[0] * length * seq_count
     factor = 1.0 / math.sqrt(float(counted))
-    owned = lax.all_to_all(cotangent, "seq", split_axis=2, concat_axis=1, tiled=True)[0]
-    own_rows = owned.shape[1]
-    owned_padded = jnp.pad(owned, ((reach, reach), (0, 0)))
+    channels = cotangent[0].T.reshape(seq_count, -1, length)
+    arrived = lax.all_to_all(channels, "seq", 0, 0, tiled=True)
+    own_rows = arrived.shape[1]
+    owned = jnp.transpose(arrived, (1, 0, 2)).reshape(own_rows, -1)
     whole_act = lax.all_gather(act[None], "seq", axis=1, tiled=True)[0]
     count = whole_act.shape[0]
+    act_padded = jnp.pad(whole_act, ((reach, reach), (0, 0)))
     updated = []
     for tap_index in range(KW):
-        offset = 0 + (2 * middle_offset - tap_index) * TAP_SPACING
-        window = lax.dynamic_slice_in_dim(owned_padded, offset, count, 0)
+        window = lax.slice_in_dim(act_padded, tap_index * TAP_SPACING, tap_index * TAP_SPACING + count, axis=0)
         updated.append(
             lax.dot_general(
-                whole_act, window, (((0,), (0,)), ((), ())), preferred_element_type=jnp.float32
+                window, owned, (((0,), (1,)), ((), ())), preferred_element_type=jnp.float32
             )
         )
     local_columns = jnp.concatenate(updated, axis=0) * factor

time: 70.9 us -> 69.3 us (0.977)
  local copies, waits for them, and re-layouts: 11.7 us -> 10.5 us
  waiting for transfers between devices: 13.4 us -> 14.4 us
  blocking collectives: 10.3 us -> 9.41 us
  other arithmetic: 5.08 us -> 4.25 us
    unnamed x1 -> x0, other arithmetic: 1.81 us -> none
    ppermute x4, waiting for transfers between devices: 13.3 us -> 14.4 us  [send(): arrived = lax.ppermute(encode(values), 'batch', perm)]
    unnamed x23 -> x18, local copies, waits for them, and re-layouts: 6.8 us -> 5.79 us
    convert_element_type x1, other arithmetic: 0.09 us -> 1.02 us  [body(): act = activation.astype(jnp.bfloat16)]
    all_gather x1, blocking collectives: 10.3 us -> 9.41 us  [body(): whole_act = lax.all_gather(act[None], 'seq', axis=1, tiled=True)[0]]
  transfers between devices with their start and end apart: 7 -> 7, of which waited for: 3 -> 3; matrix products, arithmetic and copies ran while one was open for 22% -> 24% of each run, Pallas kernels for 0% -> 0%
where the time goes in v11:
time: 69.3 us; the launch traced here: 68.8 us
  starting transfers between devices  15.3 us (22%)
  waiting for transfers between devices  14.4 us (21%)
  local copies, waits for them, and re-layouts  10.5 us (15%)
  blocking collectives  9.41 us (14%)
  matrix products  8.28 us (12%)
  between operations  6.58 us (9%)
  other arithmetic  4.25 us (6%)
    ppermute x4, waiting for transfers between devices, send(): arrived = lax.ppermute(encode(values), 'batch', perm)  14.4 us
    all_gather x1, blocking collectives, body(): whole_act = lax.all_gather(act[None], 'seq', axis=1, tiled=True)[0]  9.41 us
    ppermute x4, starting transfers between devices, send(): arrived = lax.ppermute(encode(values), 'batch', perm)  7.54 us
    dot_general x3, matrix products, body(): jnp.dot(window, weight[:, tap_index * in_width:(tap_index + 1) * in_width...  7.06 us
    unnamed x18, local copies, waits for them, and re-layouts  5.79 us
    all_to_all x1, starting transfers between devices, body(): arrived = lax.all_to_all(channels, 'seq', 0, 0, tiled=True)  4.24 us
    slice x4, local copies, waits for them, and re-layouts, decode(): exponent = packed[-TAG, 0].astype(jnp.float32)  2.79 us
    ppermute x1, starting transfers between devices, extended_2(): before = lax.ppermute(last, axis, up)  2.25 us
  transfers between devices with their start and end apart: 7, of which 3 were waited for; matrix products, arithmetic and copies ran while one was open for 24% of the time, Pallas kernels for 0%

profile of v11, /device:TPU:0, one launch (start us, length us, event | category | flops | bytes accessed | tf_op | source)
XLA Modules:
  0.0 68.8 jit_solution(18019066204142757158)
XLA Ops:
  0.6 1.8 %copy.19 = bf16[1,128,768]{1,2,0:T(8,128)(2,1)} copy(bf16[1,128,768]{2,1,0:T(8,128)(2,1)} %param.4) | data formatting | bytes 393216 | tf_op args[1]
  2.4 4.2 %all-to-all-start = ((bf16[4,192,128]{2,1,0:T(8,128)(2,1)}), bf16[4,192,128]{2,1,0:T(8,128)(2,1)S(1)}, u32[]{:S(2)}, u32[]{:S(2)}) async-start(bf16[4,192,128]{2,1,0:T(8,128)(2,1)} %bitcast.3), calls=%async_computation | async-start | bytes 393216 | tf_op jit(solution)/shard_map/all_to_all | solution.py:86
  6.7 1.0 %fusion.26 = bf16[1,128,768]{2,1,0:T(8,128)(2,1)S(1)} fusion(bf16[1,128,768]{2,1,0:T(8,128)(2,1)} %param.3), kind=kLoop, calls=%fused_computation.34 | loop fusion | flops 589824 | bytes 393216 | tf_op jit(solution)/shard_map/convert_element_type | solution.py:80
  7.7 9.4 %all_gather.3 = bf16[1,512,768]{2,1,0:T(8,128)(2,1)S(1)} all-gather(bf16[1,128,768]{2,1,0:T(8,128)(2,1)S(1)} %fusion.26), channel_id=1, replica_groups=mesh['seq'=4,'batch'=8] {'seq'}, dimensions={1}, use_global_device_ids=true | all-gather | bytes 983040 | tf_op jit(solution)/shard_map/all_gather | solution.py:89
  17.1 0.9 %fusion.22 = f32[128,768]{1,0:T(8,128)} fusion(bf16[1,128,768]{2,1,0:T(8,128)(2,1)S(1)} %copy-done.4), kind=kLoop, calls=%fused_computation.30 | loop fusion | flops 884736 | bytes 589824 | tf_op jit(solution)/shard_map/add | solution.py:31
  18.0 0.4 fusion.33
  18.4 0.4 fusion.16
  18.8 0.4 fusion.15
  19.4 0.7 %copy-done = bf16[1,128,768]{2,1,0:T(8,128)(2,1)S(1)} copy-done((bf16[1,128,768]{2,1,0:T(8,128)(2,1)S(1)}, bf16[1,128,768]{2,1,0:T(8,128)(2,1)}, u32[]{:S(2)}) %copy-start) | copy-done | bytes 196632
  20.2 0.7 fusion.54
  20.8 2.2 %collective-permute-start.1 = (bf16[1,64,768]{2,1,0:T(8,128)(2,1)S(1)}, bf16[1,64,768]{2,1,0:T(8,128)(2,1)S(1)}, u32[]{:S(2)}, u32[]{:S(2)}) collective-permute-start(bf16[1,64,768]{2,1,0:T(8,128)(2,1)S(1)} %get-tuple-element.21), channel_id=1, source_target_pairs={{0,8},{8,16},{16,24},{1,9},{9,17},{17,25},{2,10},{10,18},{18,26},{... | collective-permute-start | bytes 294920 | tf_op jit(solution)/shard_map/ppermute | solution.py:22
  23.1 0.8 %fusion.2 = f32[]{:T(128)} fusion(f32[4,2,288,192]{3,2,1,0:T(8,128)S(1)} %bitcast.96, s32[]{:T(128)S(6)} %select_n.45), kind=kLoop, calls=%fused_computation.7 | loop fusion | flops 442367 | bytes 884744 | tf_op jit(solution)/shard_map/reduce_max | solution.py:36
  24.8 1.1 %copy.36 = f16[1152,192]{0,1:T(8,128)(2,1)} copy(f16[1152,192]{1,0:T(8,128)(2,1)S(1)} %bitcast.102) | data formatting | bytes 884736
  25.9 1.1 %concatenate.25.clone = f16[1168,192]{0,1:T(8,128)(2,1)S(1)} pad(f16[1152,192]{0,1:T(8,128)(2,1)} %copy.36, f16[]{:T(256)S(6)} %convert_element_type.89), padding=0_16x0_0 | pad | bytes 890882 | tf_op jit(solution)/shard_map/concatenate | solution.py:40
  27.0 2.1 %collective-permute-start.2 = (f16[1168,192]{0,1:T(8,128)(2,1)S(1)}, f16[1168,192]{0,1:T(8,128)(2,1)S(1)}, u32[]{:S(2)}, u32[]{:S(2)}) collective-permute-start(f16[1168,192]{0,1:T(8,128)(2,1)S(1)} %concatenate.25.clone), channel_id=1, source_target_pairs={{0,1},{1,0},{2,3},{3,2},{4,5},{5,4},{6,7},{7,6},{8,9},{9,8},{10,11... | collective-permute-start | bytes 1345544 | tf_op jit(solution)/shard_map/ppermute | solution.py:50
  29.1 2.4 %fusion.6 = f32[128,768]{1,0:T(8,128)} fusion(bf16[768,2304]{1,0:T(8,128)(2,1)} %param.5, bf16[1,128,768]{2,1,0:T(8,128)(2,1)S(1)} %copy-done), kind=kOutput, calls=%fused_computation.12 | convolution fusion | flops 150994944 | bytes 1769472 | tf_op jit(solution)/shard_map/dot_general | solution.py:109
  31.4 1.3 %collective-permute-start = (bf16[1,64,768]{2,1,0:T(8,128)(2,1)}, bf16[1,64,768]{2,1,0:T(8,128)(2,1)}, u32[]{:S(2)}, u32[]{:S(2)}) collective-permute-start(bf16[1,64,768]{2,1,0:T(8,128)(2,1)} %get-tuple-element.20), channel_id=1, source_target_pairs={{8,0},{16,8},{24,16},{9,1},{17,9},{25,17},{10,2},{18,10},{26,18},{... | collective-permute-start | bytes 294920 | tf_op jit(solution)/shard_map/ppermute | solution.py:23
  32.7 2.4 %fusion.4 = f32[128,768]{1,0:T(8,128)} fusion(bf16[768,2304]{1,0:T(8,128)(2,1)} %param.5, bf16[1,128,768]{2,1,0:T(8,128)(2,1)S(1)} %copy-done, bf16[1,64,768]{2,1,0:T(8,128)(2,1)S(1)} %collective-permute-done.1), kind=kOutput, calls=%fused_computation.10 | convolution fusion | flops 151388160 | bytes 1867776 | tf_op jit(solution)/shard_map/dot_general | solution.py:109
  35.1 5.8 %collective-permute-done.2 = f16[1168,192]{0,1:T(8,128)(2,1)S(1)} collective-permute-done((f16[1168,192]{0,1:T(8,128)(2,1)S(1)}, f16[1168,192]{0,1:T(8,128)(2,1)S(1)}, u32[]{:S(2)}, u32[]{:S(2)}) %collective-permute-start.2) | collective-permute-done | bytes 448544 | tf_op jit(solution)/shard_map/ppermute | solution.py:50
  41.0 0.8 %copy-done.5 = f16[1168,192]{0,1:T(8,128)(2,1)} copy-done((f16[1168,192]{0,1:T(8,128)(2,1)}, f16[1168,192]{0,1:T(8,128)(2,1)S(1)}, u32[]{:S(2)}) %copy-start.5) | copy-done | bytes 448536
  41.8 0.5 copy.34
  42.3 1.2 %slice.85 = f16[1,1]{0,1:T(2,128)(2,1)} slice(f16[1168,192]{0,1:T(8,128)(2,1)} %copy-done.5), slice={[1152:1153], [0:1]} | slice | bytes 4 | tf_op jit(solution)/shard_map/slice | solution.py:44
  44.4 0.8 %abs_reduce_fusion.2 = (f32[]{:T(128)}, f32[]{:T(128)}, f32[]{:T(128)}) fusion(f32[4,288,192]{2,1,0:T(8,128)S(1)} %bitcast_add_fusion, s32[]{:T(128)S(6)} %select_n.49, s32[]{:T(128)S(6)} %select_n.51, s32[]{:T(128)S(6)} %select_n.53), kind=kLoop, calls=%fused_computation.46 | loop fusion | flops 331773 | bytes 663576 | tf_op jit(solution)/shard_map/reduce_max | solution.py:36
  47.6 4.3 %collective-permute-start.5 = (f16[304,192]{1,0:T(8,128)(2,1)S(1)}, f16[304,192]{1,0:T(8,128)(2,1)S(1)}, u32[]{:S(2)}, u32[]{:S(2)}) collective-permute-start(f16[304,192]{1,0:T(8,128)(2,1)S(1)} %concatenate.28), channel_id=1, source_target_pairs={{0,6},{1,7},{2,0},{3,1},{4,2},{5,3},{6,4},{7,5},{8,14},{9,15},{10,... | collective-permute-start | bytes 350216 | tf_op jit(solution)/shard_map/ppermute | solution.py:50
  52.1 1.0 %collective-permute-start.3 = (f16[304,192]{1,0:T(8,128)(2,1)S(1)}, f16[304,192]{1,0:T(8,128)(2,1)S(1)}, u32[]{:S(2)}, u32[]{:S(2)}) collective-permute-start(f16[304,192]{1,0:T(8,128)(2,1)S(1)} %concatenate.26), channel_id=1, source_target_pairs={{0,2},{1,3},{2,4},{3,5},{4,6},{5,7},{6,0},{7,1},{8,10},{9,11},{10,... | collective-permute-start | bytes 350216 | tf_op jit(solution)/shard_map/ppermute | solution.py:50
  53.2 2.3 %fusion.12 = bf16[1,128,768]{2,1,0:T(8,128)(2,1)} fusion(f32[128,768]{1,0:T(8,128)S(1)} %copy-done.3, f32[128,768]{1,0:T(8,128)S(1)} %copy-done.6, f32[128,768]{1,0:T(8,128)S(1)} %copy-done.2, bf16[768,2304]{1,0:T(8,128)(2,1)} %param.5, bf16[1,64,768]{2,1,0:T(8,128)(2,1)} %collective-permute-done, bf16[1,128,768]{2,1,0:T(8,128)(2,1)S(1)} %copy-done.1), kind=kOutput, calls=%fused_computation.16 | convolution fusion | flops 151781376 | bytes 2850816 | tf_op jit(solution)/shard_map/dot_general | solution.py:109
  55.5 0.9 %collective-permute-done.5 = f16[304,192]{1,0:T(8,128)(2,1)S(1)} collective-permute-done((f16[304,192]{1,0:T(8,128)(2,1)S(1)}, f16[304,192]{1,0:T(8,128)(2,1)S(1)}, u32[]{:S(2)}, u32[]{:S(2)}) %collective-permute-start.5) | collective-permute-done | bytes 116768 | tf_op jit(solution)/shard_map/ppermute | solution.py:50
  56.4 0.5 slice.91
  57.7 7.7 %collective-permute-done.4 = f16[304,192]{1,0:T(8,128)(2,1)S(1)} collective-permute-done((f16[304,192]{1,0:T(8,128)(2,1)S(1)}, f16[304,192]{1,0:T(8,128)(2,1)S(1)}, u32[]{:S(2)}, u32[]{:S(2)}) %collective-permute-start.4) | collective-permute-done | bytes 116768 | tf_op jit(solution)/shard_map/ppermute | solution.py:50
  65.3 0.6 slice.89
  66.7 0.5 slice.87
  67.9 0.9 %copy.28 = f32[192,288]{1,0:T(8,128)} copy(f32[192,288]{0,1:T(8,128)S(1)} %fusion.31) | data formatting | bytes 442368
  (27 shorter events, 1.1 us)
Async XLA Ops:
  0.6 16.5 %copy-start.4 = (bf16[1,128,768]{2,1,0:T(8,128)(2,1)S(1)}, bf16[1,128,768]{2,1,0:T(8,128)(2,1)}, u32[]{:S(2)}) copy-start(bf16[1,128,768]{2,1,0:T(8,128)(2,1)} %param.3) | copy-start | bytes 589828
  2.4 15.6 %all-to-all-start = ((bf16[4,192,128]{2,1,0:T(8,128)(2,1)}), bf16[4,192,128]{2,1,0:T(8,128)(2,1)S(1)}, u32[]{:S(2)}, u32[]{:S(2)}) async-start(bf16[4,192,128]{2,1,0:T(8,128)(2,1)} %bitcast.3), calls=%async_computation | async-start | bytes 393216 | tf_op jit(solution)/shard_map/all_to_all | solution.py:86
  19.2 0.9 %copy-start = (bf16[1,128,768]{2,1,0:T(8,128)(2,1)S(1)}, bf16[1,128,768]{2,1,0:T(8,128)(2,1)}, u32[]{:S(2)}) copy-start(bf16[1,128,768]{2,1,0:T(8,128)(2,1)} %param.4) | copy-start | bytes 589828
  20.8 11.9 %collective-permute-start.1 = (bf16[1,64,768]{2,1,0:T(8,128)(2,1)S(1)}, bf16[1,64,768]{2,1,0:T(8,128)(2,1)S(1)}, u32[]{:S(2)}, u32[]{:S(2)}) collective-permute-start(bf16[1,64,768]{2,1,0:T(8,128)(2,1)S(1)} %get-tuple-element.21), channel_id=1, source_target_pairs={{0,8},{8,16},{16,24},{1,9},{9,17},{17,25},{2,10},{10,18},{18,26},{... | collective-permute-start | bytes 294920 | tf_op jit(solution)/shard_map/ppermute | solution.py:22
  27.0 14.0 %collective-permute-start.2 = (f16[1168,192]{0,1:T(8,128)(2,1)S(1)}, f16[1168,192]{0,1:T(8,128)(2,1)S(1)}, u32[]{:S(2)}, u32[]{:S(2)}) collective-permute-start(f16[1168,192]{0,1:T(8,128)(2,1)S(1)} %concatenate.25.clone), channel_id=1, source_target_pairs={{0,1},{1,0},{2,3},{3,2},{4,5},{5,4},{6,7},{7,6},{8,9},{9,8},{10,11... | collective-permute-start | bytes 1345544 | tf_op jit(solution)/shard_map/ppermute | solution.py:50
  31.4 21.7 %collective-permute-start = (bf16[1,64,768]{2,1,0:T(8,128)(2,1)}, bf16[1,64,768]{2,1,0:T(8,128)(2,1)}, u32[]{:S(2)}, u32[]{:S(2)}) collective-permute-start(bf16[1,64,768]{2,1,0:T(8,128)(2,1)} %get-tuple-element.20), channel_id=1, source_target_pairs={{8,0},{16,8},{24,16},{9,1},{17,9},{25,17},{10,2},{18,10},{26,18},{... | collective-permute-start | bytes 294920 | tf_op jit(solution)/shard_map/ppermute | solution.py:23
  41.0 0.8 %copy-start.5 = (f16[1168,192]{0,1:T(8,128)(2,1)}, f16[1168,192]{0,1:T(8,128)(2,1)S(1)}, u32[]{:S(2)}) copy-start(f16[1168,192]{0,1:T(8,128)(2,1)S(1)} %collective-permute-done.2) | copy-start | bytes 1345540
  45.2 8.0 %copy-start.1 = (bf16[1,128,768]{2,1,0:T(8,128)(2,1)S(1)}, bf16[1,128,768]{2,1,0:T(8,128)(2,1)}, u32[]{:S(2)}) copy-start(bf16[1,128,768]{2,1,0:T(8,128)(2,1)} %param.4) | copy-start | bytes 589828
  45.2 8.0 %copy-start.2 = (f32[128,768]{1,0:T(8,128)S(1)}, f32[128,768]{1,0:T(8,128)}, u32[]{:S(2)}) copy-start(f32[128,768]{1,0:T(8,128)} %fusion.6) | copy-start | bytes 1179652
  45.2 8.0 %copy-start.3 = (f32[128,768]{1,0:T(8,128)S(1)}, f32[128,768]{1,0:T(8,128)}, u32[]{:S(2)}) copy-start(f32[128,768]{1,0:T(8,128)} %fusion.22) | copy-start | bytes 1179652
  45.2 8.0 %copy-start.6 = (f32[128,768]{1,0:T(8,128)S(1)}, f32[128,768]{1,0:T(8,128)}, u32[]{:S(2)}) copy-start(f32[128,768]{1,0:T(8,128)} %fusion.4) | copy-start | bytes 1179652
  47.6 8.8 %collective-permute-start.5 = (f16[304,192]{1,0:T(8,128)(2,1)S(1)}, f16[304,192]{1,0:T(8,128)(2,1)S(1)}, u32[]{:S(2)}, u32[]{:S(2)}) collective-permute-start(f16[304,192]{1,0:T(8,128)(2,1)S(1)} %concatenate.28), channel_id=1, source_target_pairs={{0,6},{1,7},{2,0},{3,1},{4,2},{5,3},{6,4},{7,5},{8,14},{9,15},{10,... | collective-permute-start | bytes 350216 | tf_op jit(solution)/shard_map/ppermute | solution.py:50
  52.0 13.3 %collective-permute-start.4 = (f16[304,192]{1,0:T(8,128)(2,1)S(1)}, f16[304,192]{1,0:T(8,128)(2,1)S(1)}, u32[]{:S(2)}, u32[]{:S(2)}) collective-permute-start(f16[304,192]{1,0:T(8,128)(2,1)S(1)} %concatenate.27), channel_id=1, source_target_pairs={{0,4},{1,5},{2,6},{3,7},{4,0},{5,1},{6,2},{7,3},{8,12},{9,13},{10,... | collective-permute-start | bytes 350216 | tf_op jit(solution)/shard_map/ppermute | solution.py:50
  52.1 14.6 %collective-permute-start.3 = (f16[304,192]{1,0:T(8,128)(2,1)S(1)}, f16[304,192]{1,0:T(8,128)(2,1)S(1)}, u32[]{:S(2)}, u32[]{:S(2)}) collective-permute-start(f16[304,192]{1,0:T(8,128)(2,1)S(1)} %concatenate.26), channel_id=1, source_target_pairs={{0,2},{1,3},{2,4},{3,5},{4,6},{5,7},{6,0},{7,1},{8,10},{9,11},{10,... | collective-permute-start | bytes 350216 | tf_op jit(solution)/shard_map/ppermute | solution.py:50

commit v12 on v11

--- a/solution.py
+++ b/solution.py
@@ -63,7 +63,7 @@
     theirs = lax.dynamic_index_in_dim(blocks, 1 - x, axis=1, keepdims=False)
     summed = with_layout_constraint(mine + send(theirs, pairs), Layout((0, 1, 2)))
     total = lax.dynamic_index_in_dim(summed, z, axis=0, keepdims=False)
-    for shift in range(1, outer):
+    for shift in sorted(range(1, outer), key=lambda d: (min(d, outer - d), -d)):
         target = lax.dynamic_index_in_dim(summed, (z + shift) % outer, axis=0, keepdims=False)
         perm = [(2 * q + p, 2 * ((q + shift) % outer) + p) for q in range(outer) for p in range(2)]
         total = total + send(target, perm)

time: 69.3 us -> 68 us (0.981)
  waiting for transfers between devices: 14.4 us -> 11 us
  starting transfers between devices: 15.3 us -> 17.1 us
    ppermute x4, waiting for transfers between devices: 14.4 us -> 11 us  [send(): arrived = lax.ppermute(encode(values), 'batch', perm)]
    ppermute x4, starting transfers between devices: 7.54 us -> 9.35 us  [send(): arrived = lax.ppermute(encode(values), 'batch', perm)]
  transfers between devices with their start and end apart: 7 -> 7, of which waited for: 3 -> 2; matrix products, arithmetic and copies ran while one was open for 24% -> 24% of each run, Pallas kernels for 0% -> 0%
where the time goes in v12:
time: 68 us; the launch traced here: 67.2 us
  starting transfers between devices  17.1 us (25%)
  waiting for transfers between devices  11 us (16%)
  local copies, waits for them, and re-layouts  10.5 us (15%)
  blocking collectives  9.41 us (14%)
  matrix products  8.28 us (12%)
  between operations  6.57 us (10%)
  other arithmetic  4.25 us (6%)
    ppermute x4, waiting for transfers between devices, send(): arrived = lax.ppermute(encode(values), 'batch', perm)  11 us
    all_gather x1, blocking collectives, body(): whole_act = lax.all_gather(act[None], 'seq', axis=1, tiled=True)[0]  9.41 us
    ppermute x4, starting transfers between devices, send(): arrived = lax.ppermute(encode(values), 'batch', perm)  9.35 us
    dot_general x3, matrix products, body(): jnp.dot(window, weight[:, tap_index * in_width:(tap_index + 1) * in_width...  7.06 us
    unnamed x18, local copies, waits for them, and re-layouts  5.79 us
    all_to_all x1, starting transfers between devices, body(): arrived = lax.all_to_all(channels, 'seq', 0, 0, tiled=True)  4.24 us
    slice x4, local copies, waits for them, and re-layouts, decode(): exponent = packed[-TAG, 0].astype(jnp.float32)  2.79 us
    ppermute x1, starting transfers between devices, extended_2(): before = lax.ppermute(last, axis, up)  2.25 us
  transfers between devices with their start and end apart: 7, of which 2 were waited for; matrix products, arithmetic and copies ran while one was open for 24% of the time, Pallas kernels for 0%

profile of v12, /device:TPU:0, one launch (start us, length us, event | category | flops | bytes accessed | tf_op | source)
XLA Modules:
  0.0 67.2 jit_solution(76794939901761697)
XLA Ops:
  0.6 1.8 %copy.19 = bf16[1,128,768]{1,2,0:T(8,128)(2,1)} copy(bf16[1,128,768]{2,1,0:T(8,128)(2,1)} %param.4) | data formatting | bytes 393216 | tf_op args[1]
  2.4 4.2 %all-to-all-start = ((bf16[4,192,128]{2,1,0:T(8,128)(2,1)}), bf16[4,192,128]{2,1,0:T(8,128)(2,1)S(1)}, u32[]{:S(2)}, u32[]{:S(2)}) async-start(bf16[4,192,128]{2,1,0:T(8,128)(2,1)} %bitcast.3), calls=%async_computation | async-start | bytes 393216 | tf_op jit(solution)/shard_map/all_to_all | solution.py:86
  6.7 1.0 %fusion.26 = bf16[1,128,768]{2,1,0:T(8,128)(2,1)S(1)} fusion(bf16[1,128,768]{2,1,0:T(8,128)(2,1)} %param.3), kind=kLoop, calls=%fused_computation.34 | loop fusion | flops 589824 | bytes 393216 | tf_op jit(solution)/shard_map/convert_element_type | solution.py:80
  7.7 9.4 %all_gather.3 = bf16[1,512,768]{2,1,0:T(8,128)(2,1)S(1)} all-gather(bf16[1,128,768]{2,1,0:T(8,128)(2,1)S(1)} %fusion.26), channel_id=1, replica_groups=mesh['seq'=4,'batch'=8] {'seq'}, dimensions={1}, use_global_device_ids=true | all-gather | bytes 983040 | tf_op jit(solution)/shard_map/all_gather | solution.py:89
  17.1 0.9 %fusion.22 = f32[128,768]{1,0:T(8,128)} fusion(bf16[1,128,768]{2,1,0:T(8,128)(2,1)S(1)} %copy-done.4), kind=kLoop, calls=%fused_computation.30 | loop fusion | flops 884736 | bytes 589824 | tf_op jit(solution)/shard_map/add | solution.py:31
  18.0 0.4 fusion.33
  18.4 0.4 fusion.16
  18.8 0.4 fusion.15
  19.4 0.7 %copy-done = bf16[1,128,768]{2,1,0:T(8,128)(2,1)S(1)} copy-done((bf16[1,128,768]{2,1,0:T(8,128)(2,1)S(1)}, bf16[1,128,768]{2,1,0:T(8,128)(2,1)}, u32[]{:S(2)}) %copy-start) | copy-done | bytes 196632
  20.2 0.7 fusion.54
  20.8 2.2 %collective-permute-start.1 = (bf16[1,64,768]{2,1,0:T(8,128)(2,1)S(1)}, bf16[1,64,768]{2,1,0:T(8,128)(2,1)S(1)}, u32[]{:S(2)}, u32[]{:S(2)}) collective-permute-start(bf16[1,64,768]{2,1,0:T(8,128)(2,1)S(1)} %get-tuple-element.21), channel_id=1, source_target_pairs={{0,8},{8,16},{16,24},{1,9},{9,17},{17,25},{2,10},{10,18},{18,26},{... | collective-permute-start | bytes 294920 | tf_op jit(solution)/shard_map/ppermute | solution.py:22
  23.1 0.8 %fusion.2 = f32[]{:T(128)} fusion(f32[4,2,288,192]{3,2,1,0:T(8,128)S(1)} %bitcast.96, s32[]{:T(128)S(6)} %select_n.45), kind=kLoop, calls=%fused_computation.7 | loop fusion | flops 442367 | bytes 884744 | tf_op jit(solution)/shard_map/reduce_max | solution.py:36
  24.8 1.1 %copy.36 = f16[1152,192]{0,1:T(8,128)(2,1)} copy(f16[1152,192]{1,0:T(8,128)(2,1)S(1)} %bitcast.102) | data formatting | bytes 884736
  25.9 1.1 %concatenate.25.clone = f16[1168,192]{0,1:T(8,128)(2,1)S(1)} pad(f16[1152,192]{0,1:T(8,128)(2,1)} %copy.36, f16[]{:T(256)S(6)} %convert_element_type.89), padding=0_16x0_0 | pad | bytes 890882 | tf_op jit(solution)/shard_map/concatenate | solution.py:40
  27.0 2.1 %collective-permute-start.2 = (f16[1168,192]{0,1:T(8,128)(2,1)S(1)}, f16[1168,192]{0,1:T(8,128)(2,1)S(1)}, u32[]{:S(2)}, u32[]{:S(2)}) collective-permute-start(f16[1168,192]{0,1:T(8,128)(2,1)S(1)} %concatenate.25.clone), channel_id=1, source_target_pairs={{0,1},{1,0},{2,3},{3,2},{4,5},{5,4},{6,7},{7,6},{8,9},{9,8},{10,11... | collective-permute-start | bytes 1345544 | tf_op jit(solution)/shard_map/ppermute | solution.py:50
  29.1 2.4 %fusion.6 = f32[128,768]{1,0:T(8,128)} fusion(bf16[768,2304]{1,0:T(8,128)(2,1)} %param.5, bf16[1,128,768]{2,1,0:T(8,128)(2,1)S(1)} %copy-done), kind=kOutput, calls=%fused_computation.12 | convolution fusion | flops 150994944 | bytes 1769472 | tf_op jit(solution)/shard_map/dot_general | solution.py:109
  31.4 1.3 %collective-permute-start = (bf16[1,64,768]{2,1,0:T(8,128)(2,1)}, bf16[1,64,768]{2,1,0:T(8,128)(2,1)}, u32[]{:S(2)}, u32[]{:S(2)}) collective-permute-start(bf16[1,64,768]{2,1,0:T(8,128)(2,1)} %get-tuple-element.20), channel_id=1, source_target_pairs={{8,0},{16,8},{24,16},{9,1},{17,9},{25,17},{10,2},{18,10},{26,18},{... | collective-permute-start | bytes 294920 | tf_op jit(solution)/shard_map/ppermute | solution.py:23
  32.7 2.4 %fusion.4 = f32[128,768]{1,0:T(8,128)} fusion(bf16[768,2304]{1,0:T(8,128)(2,1)} %param.5, bf16[1,128,768]{2,1,0:T(8,128)(2,1)S(1)} %copy-done, bf16[1,64,768]{2,1,0:T(8,128)(2,1)S(1)} %collective-permute-done.1), kind=kOutput, calls=%fused_computation.10 | convolution fusion | flops 151388160 | bytes 1867776 | tf_op jit(solution)/shard_map/dot_general | solution.py:109
  35.1 5.8 %collective-permute-done.2 = f16[1168,192]{0,1:T(8,128)(2,1)S(1)} collective-permute-done((f16[1168,192]{0,1:T(8,128)(2,1)S(1)}, f16[1168,192]{0,1:T(8,128)(2,1)S(1)}, u32[]{:S(2)}, u32[]{:S(2)}) %collective-permute-start.2) | collective-permute-done | bytes 448544 | tf_op jit(solution)/shard_map/ppermute | solution.py:50
  41.0 0.8 %copy-done.5 = f16[1168,192]{0,1:T(8,128)(2,1)} copy-done((f16[1168,192]{0,1:T(8,128)(2,1)}, f16[1168,192]{0,1:T(8,128)(2,1)S(1)}, u32[]{:S(2)}) %copy-start.5) | copy-done | bytes 448536
  41.8 0.5 copy.34
  42.3 1.2 %slice.85 = f16[1,1]{0,1:T(2,128)(2,1)} slice(f16[1168,192]{0,1:T(8,128)(2,1)} %copy-done.5), slice={[1152:1153], [0:1]} | slice | bytes 4 | tf_op jit(solution)/shard_map/slice | solution.py:44
  44.4 0.8 %abs_reduce_fusion.2 = (f32[]{:T(128)}, f32[]{:T(128)}, f32[]{:T(128)}) fusion(f32[4,288,192]{2,1,0:T(8,128)S(1)} %bitcast_add_fusion, s32[]{:T(128)S(6)} %select_n.49, s32[]{:T(128)S(6)} %select_n.51, s32[]{:T(128)S(6)} %select_n.53), kind=kLoop, calls=%fused_computation.46 | loop fusion | flops 331773 | bytes 663576 | tf_op jit(solution)/shard_map/reduce_max | solution.py:36
  47.6 3.3 %collective-permute-start.5 = (f16[304,192]{1,0:T(8,128)(2,1)S(1)}, f16[304,192]{1,0:T(8,128)(2,1)S(1)}, u32[]{:S(2)}, u32[]{:S(2)}) collective-permute-start(f16[304,192]{1,0:T(8,128)(2,1)S(1)} %concatenate.28), channel_id=1, source_target_pairs={{0,4},{1,5},{2,6},{3,7},{4,0},{5,1},{6,2},{7,3},{8,12},{9,13},{10,... | collective-permute-start | bytes 350216 | tf_op jit(solution)/shard_map/ppermute | solution.py:50
  51.0 1.6 %collective-permute-start.4 = (f16[304,192]{1,0:T(8,128)(2,1)S(1)}, f16[304,192]{1,0:T(8,128)(2,1)S(1)}, u32[]{:S(2)}, u32[]{:S(2)}) collective-permute-start(f16[304,192]{1,0:T(8,128)(2,1)S(1)} %concatenate.27), channel_id=1, source_target_pairs={{0,2},{1,3},{2,4},{3,5},{4,6},{5,7},{6,0},{7,1},{8,10},{9,11},{10,... | collective-permute-start | bytes 350216 | tf_op jit(solution)/shard_map/ppermute | solution.py:50
  52.7 2.3 %collective-permute-start.3 = (f16[304,192]{1,0:T(8,128)(2,1)S(1)}, f16[304,192]{1,0:T(8,128)(2,1)S(1)}, u32[]{:S(2)}, u32[]{:S(2)}) collective-permute-start(f16[304,192]{1,0:T(8,128)(2,1)S(1)} %concatenate.26), channel_id=1, source_target_pairs={{0,6},{1,7},{2,0},{3,1},{4,2},{5,3},{6,4},{7,5},{8,14},{9,15},{10,... | collective-permute-start | bytes 350216 | tf_op jit(solution)/shard_map/ppermute | solution.py:50
  55.0 2.3 %fusion.12 = bf16[1,128,768]{2,1,0:T(8,128)(2,1)} fusion(f32[128,768]{1,0:T(8,128)S(1)} %copy-done.3, f32[128,768]{1,0:T(8,128)S(1)} %copy-done.6, f32[128,768]{1,0:T(8,128)S(1)} %copy-done.2, bf16[768,2304]{1,0:T(8,128)(2,1)} %param.5, bf16[1,64,768]{2,1,0:T(8,128)(2,1)} %collective-permute-done, bf16[1,128,768]{2,1,0:T(8,128)(2,1)S(1)} %copy-done.1), kind=kOutput, calls=%fused_computation.16 | convolution fusion | flops 151781376 | bytes 2850816 | tf_op jit(solution)/shard_map/dot_general | solution.py:109
  57.3 5.2 %collective-permute-done.5 = f16[304,192]{1,0:T(8,128)(2,1)S(1)} collective-permute-done((f16[304,192]{1,0:T(8,128)(2,1)S(1)}, f16[304,192]{1,0:T(8,128)(2,1)S(1)}, u32[]{:S(2)}, u32[]{:S(2)}) %collective-permute-start.5) | collective-permute-done | bytes 116768 | tf_op jit(solution)/shard_map/ppermute | solution.py:50
  62.5 0.5 slice.91
  63.7 0.6 slice.89
  65.1 0.5 slice.87
  66.3 0.9 %copy.28 = f32[192,288]{1,0:T(8,128)} copy(f32[192,288]{0,1:T(8,128)S(1)} %fusion.31) | data formatting | bytes 442368
  (27 shorter events, 1.0 us)
Async XLA Ops:
  0.6 16.5 %copy-start.4 = (bf16[1,128,768]{2,1,0:T(8,128)(2,1)S(1)}, bf16[1,128,768]{2,1,0:T(8,128)(2,1)}, u32[]{:S(2)}) copy-start(bf16[1,128,768]{2,1,0:T(8,128)(2,1)} %param.3) | copy-start | bytes 589828
  2.4 15.6 %all-to-all-start = ((bf16[4,192,128]{2,1,0:T(8,128)(2,1)}), bf16[4,192,128]{2,1,0:T(8,128)(2,1)S(1)}, u32[]{:S(2)}, u32[]{:S(2)}) async-start(bf16[4,192,128]{2,1,0:T(8,128)(2,1)} %bitcast.3), calls=%async_computation | async-start | bytes 393216 | tf_op jit(solution)/shard_map/all_to_all | solution.py:86
  19.2 0.9 %copy-start = (bf16[1,128,768]{2,1,0:T(8,128)(2,1)S(1)}, bf16[1,128,768]{2,1,0:T(8,128)(2,1)}, u32[]{:S(2)}) copy-start(bf16[1,128,768]{2,1,0:T(8,128)(2,1)} %param.4) | copy-start | bytes 589828
  20.8 11.9 %collective-permute-start.1 = (bf16[1,64,768]{2,1,0:T(8,128)(2,1)S(1)}, bf16[1,64,768]{2,1,0:T(8,128)(2,1)S(1)}, u32[]{:S(2)}, u32[]{:S(2)}) collective-permute-start(bf16[1,64,768]{2,1,0:T(8,128)(2,1)S(1)} %get-tuple-element.21), channel_id=1, source_target_pairs={{0,8},{8,16},{16,24},{1,9},{9,17},{17,25},{2,10},{10,18},{18,26},{... | collective-permute-start | bytes 294920 | tf_op jit(solution)/shard_map/ppermute | solution.py:22
  27.0 14.0 %collective-permute-start.2 = (f16[1168,192]{0,1:T(8,128)(2,1)S(1)}, f16[1168,192]{0,1:T(8,128)(2,1)S(1)}, u32[]{:S(2)}, u32[]{:S(2)}) collective-permute-start(f16[1168,192]{0,1:T(8,128)(2,1)S(1)} %concatenate.25.clone), channel_id=1, source_target_pairs={{0,1},{1,0},{2,3},{3,2},{4,5},{5,4},{6,7},{7,6},{8,9},{9,8},{10,11... | collective-permute-start | bytes 1345544 | tf_op jit(solution)/shard_map/ppermute | solution.py:50
  31.4 23.5 %collective-permute-start = (bf16[1,64,768]{2,1,0:T(8,128)(2,1)}, bf16[1,64,768]{2,1,0:T(8,128)(2,1)}, u32[]{:S(2)}, u32[]{:S(2)}) collective-permute-start(bf16[1,64,768]{2,1,0:T(8,128)(2,1)} %get-tuple-element.20), channel_id=1, source_target_pairs={{8,0},{16,8},{24,16},{9,1},{17,9},{25,17},{10,2},{18,10},{26,18},{... | collective-permute-start | bytes 294920 | tf_op jit(solution)/shard_map/ppermute | solution.py:23
  41.0 0.8 %copy-start.5 = (f16[1168,192]{0,1:T(8,128)(2,1)}, f16[1168,192]{0,1:T(8,128)(2,1)S(1)}, u32[]{:S(2)}) copy-start(f16[1168,192]{0,1:T(8,128)(2,1)S(1)} %collective-permute-done.2) | copy-start | bytes 1345540
  45.2 9.8 %copy-start.1 = (bf16[1,128,768]{2,1,0:T(8,128)(2,1)S(1)}, bf16[1,128,768]{2,1,0:T(8,128)(2,1)}, u32[]{:S(2)}) copy-start(bf16[1,128,768]{2,1,0:T(8,128)(2,1)} %param.4) | copy-start | bytes 589828
  45.2 9.8 %copy-start.2 = (f32[128,768]{1,0:T(8,128)S(1)}, f32[128,768]{1,0:T(8,128)}, u32[]{:S(2)}) copy-start(f32[128,768]{1,0:T(8,128)} %fusion.6) | copy-start | bytes 1179652
  45.2 9.8 %copy-start.3 = (f32[128,768]{1,0:T(8,128)S(1)}, f32[128,768]{1,0:T(8,128)}, u32[]{:S(2)}) copy-start(f32[128,768]{1,0:T(8,128)} %fusion.22) | copy-start | bytes 1179652
  45.2 9.8 %copy-start.6 = (f32[128,768]{1,0:T(8,128)S(1)}, f32[128,768]{1,0:T(8,128)}, u32[]{:S(2)}) copy-start(f32[128,768]{1,0:T(8,128)} %fusion.4) | copy-start | bytes 1179652
  47.6 14.9 %collective-permute-start.5 = (f16[304,192]{1,0:T(8,128)(2,1)S(1)}, f16[304,192]{1,0:T(8,128)(2,1)S(1)}, u32[]{:S(2)}, u32[]{:S(2)}) collective-permute-start(f16[304,192]{1,0:T(8,128)(2,1)S(1)} %concatenate.28), channel_id=1, source_target_pairs={{0,4},{1,5},{2,6},{3,7},{4,0},{5,1},{6,2},{7,3},{8,12},{9,13},{10,... | collective-permute-start | bytes 350216 | tf_op jit(solution)/shard_map/ppermute | solution.py:50
  51.0 12.7 %collective-permute-start.4 = (f16[304,192]{1,0:T(8,128)(2,1)S(1)}, f16[304,192]{1,0:T(8,128)(2,1)S(1)}, u32[]{:S(2)}, u32[]{:S(2)}) collective-permute-start(f16[304,192]{1,0:T(8,128)(2,1)S(1)} %concatenate.27), channel_id=1, source_target_pairs={{0,2},{1,3},{2,4},{3,5},{4,6},{5,7},{6,0},{7,1},{8,10},{9,11},{10,... | collective-permute-start | bytes 350216 | tf_op jit(solution)/shard_map/ppermute | solution.py:50
  52.7 12.4 %collective-permute-start.3 = (f16[304,192]{1,0:T(8,128)(2,1)S(1)}, f16[304,192]{1,0:T(8,128)(2,1)S(1)}, u32[]{:S(2)}, u32[]{:S(2)}) collective-permute-start(f16[304,192]{1,0:T(8,128)(2,1)S(1)} %concatenate.26), channel_id=1, source_target_pairs={{0,6},{1,7},{2,0},{3,1},{4,2},{5,3},{6,4},{7,5},{8,14},{9,15},{10,... | collective-permute-start | bytes 350216 | tf_op jit(solution)/shard_map/ppermute | solution.py:50

commit v13 on v12

--- a/solution.py
+++ b/solution.py
@@ -31,23 +31,27 @@
     return (values * normal_cdf, normal_cdf + values * density)
 
 
-def encode(values):
+def exponent_of(values):
     flat = values.reshape(-1, values.shape[-1])
-    biggest = jnp.maximum(jnp.max(jnp.abs(flat)), 1e-30)
-    exponent = jnp.floor(jnp.log2(biggest))
+    biggest = jnp.max(jnp.max(jnp.abs(flat), axis=0, keepdims=True), axis=1, keepdims=True)
+    return jnp.floor(jnp.log2(jnp.maximum(biggest, 1e-30)))
+
+
+def encode(values, exponent):
+    flat = values.reshape(-1, values.shape[-1])
     scaled = (flat * jnp.exp2(HEADROOM - exponent)).astype(jnp.float16)
-    tag = jnp.full((TAG, flat.shape[-1]), exponent, jnp.float16)
+    tag = jnp.broadcast_to(exponent.astype(jnp.float16), (TAG, flat.shape[-1]))
     return with_layout_constraint(jnp.concatenate([scaled, tag], axis=0), Layout((0, 1)))
 
 
 def decode(packed, shape):
-    exponent = packed[-TAG, 0].astype(jnp.float32)
+    exponent = packed[-TAG:1 - TAG, 0:1].astype(jnp.float32)
     values = packed[:-TAG].astype(jnp.float32) * jnp.exp2(exponent - HEADROOM)
     return values.reshape(shape)
 
 
-def send(values, perm):
-    arrived = lax.ppermute(encode(values), "batch", perm)
+def send(values, perm, exponent):
+    arrived = lax.ppermute(encode(values, exponent), "batch", perm)
     return decode(with_layout_constraint(arrived, Layout((0, 1))), values.shape)
 
 
@@ -61,12 +65,13 @@
     blocks = columns.reshape(outer, 2, -1, columns.shape[1])
     mine = lax.dynamic_index_in_dim(blocks, x, axis=1, keepdims=False)
     theirs = lax.dynamic_index_in_dim(blocks, 1 - x, axis=1, keepdims=False)
-    summed = with_layout_constraint(mine + send(theirs, pairs), Layout((0, 1, 2)))
+    summed = with_layout_constraint(mine + send(theirs, pairs, exponent_of(theirs)), Layout((0, 1, 2)))
+    spread = exponent_of(summed)
     total = lax.dynamic_index_in_dim(summed, z, axis=0, keepdims=False)
     for shift in sorted(range(1, outer), key=lambda d: (min(d, outer - d), -d)):
         target = lax.dynamic_index_in_dim(summed, (z + shift) % outer, axis=0, keepdims=False)
         perm = [(2 * q + p, 2 * ((q + shift) % outer) + p) for q in range(outer) for p in range(2)]
-        total = total + send(target, perm)
+        total = total + send(target, perm, spread)
     return with_layout_constraint(total, Layout((0, 1))).T
 
 

time: 68 us -> 66.4 us (0.976)
  between operations: 6.57 us -> 5.09 us
  transfers between devices with their start and end apart: 7 -> 7, of which waited for: 2 -> 2; matrix products, arithmetic and copies ran while one was open for 24% -> 25% of each run, Pallas kernels for 0% -> 0%
where the time goes in v13:
time: 66.4 us; the launch traced here: 65.6 us
  starting transfers between devices  17.1 us (26%)
  waiting for transfers between devices  11 us (17%)
  local copies, waits for them, and re-layouts  10.5 us (16%)
  blocking collectives  9.41 us (14%)
  matrix products  8.26 us (12%)
  between operations  5.09 us (8%)
  other arithmetic  4.18 us (6%)
    ppermute x4, waiting for transfers between devices, send(): arrived = lax.ppermute(encode(values, exponent), 'batch', perm)  11 us
    all_gather x1, blocking collectives, body(): whole_act = lax.all_gather(act[None], 'seq', axis=1, tiled=True)[0]  9.41 us
    ppermute x4, starting transfers between devices, send(): arrived = lax.ppermute(encode(values, exponent), 'batch', perm)  9.34 us
    dot_general x3, matrix products, body(): jnp.dot(window, weight[:, tap_index * in_width:(tap_index + 1) * in_width...  7.05 us
    unnamed x18, local copies, waits for them, and re-layouts  5.81 us
    all_to_all x1, starting transfers between devices, body(): arrived = lax.all_to_all(channels, 'seq', 0, 0, tiled=True)  4.24 us
    slice x4, local copies, waits for them, and re-layouts, decode(): exponent = packed[-TAG:1 - TAG, 0:1].astype(jnp.float32)  2.76 us
    ppermute x1, starting transfers between devices, extended_2(): before = lax.ppermute(last, axis, up)  2.25 us
  transfers between devices with their start and end apart: 7, of which 2 were waited for; matrix products, arithmetic and copies ran while one was open for 25% of the time, Pallas kernels for 0%

profile of v13, /device:TPU:0, one launch (start us, length us, event | category | flops | bytes accessed | tf_op | source)
XLA Modules:
  0.0 65.6 jit_solution(526850169295480659)
XLA Ops:
  0.6 1.8 %copy.19 = bf16[1,128,768]{1,2,0:T(8,128)(2,1)} copy(bf16[1,128,768]{2,1,0:T(8,128)(2,1)} %param.4) | data formatting | bytes 393216 | tf_op args[1]
  2.4 4.2 %all-to-all-start = ((bf16[4,192,128]{2,1,0:T(8,128)(2,1)}), bf16[4,192,128]{2,1,0:T(8,128)(2,1)S(1)}, u32[]{:S(2)}, u32[]{:S(2)}) async-start(bf16[4,192,128]{2,1,0:T(8,128)(2,1)} %bitcast.3), calls=%async_computation | async-start | bytes 393216 | tf_op jit(solution)/shard_map/all_to_all | solution.py:91
  6.7 1.0 %fusion.26 = bf16[1,128,768]{2,1,0:T(8,128)(2,1)S(1)} fusion(bf16[1,128,768]{2,1,0:T(8,128)(2,1)} %param.3), kind=kLoop, calls=%fused_computation.35 | loop fusion | flops 589824 | bytes 393216 | tf_op jit(solution)/shard_map/convert_element_type | solution.py:85
  7.7 9.4 %all_gather.3 = bf16[1,512,768]{2,1,0:T(8,128)(2,1)S(1)} all-gather(bf16[1,128,768]{2,1,0:T(8,128)(2,1)S(1)} %fusion.26), channel_id=1, replica_groups=mesh['seq'=4,'batch'=8] {'seq'}, dimensions={1}, use_global_device_ids=true | all-gather | bytes 983040 | tf_op jit(solution)/shard_map/all_gather | solution.py:94
  17.1 0.9 %fusion.22 = f32[128,768]{1,0:T(8,128)} fusion(bf16[1,128,768]{2,1,0:T(8,128)(2,1)S(1)} %copy-done.4), kind=kLoop, calls=%fused_computation.31 | loop fusion | flops 884736 | bytes 589824 | tf_op jit(solution)/shard_map/add | solution.py:31
  18.0 0.4 fusion.33
  18.4 0.4 fusion.16
  18.8 0.4 fusion.15
  19.4 0.7 %copy-done = bf16[1,128,768]{2,1,0:T(8,128)(2,1)S(1)} copy-done((bf16[1,128,768]{2,1,0:T(8,128)(2,1)S(1)}, bf16[1,128,768]{2,1,0:T(8,128)(2,1)}, u32[]{:S(2)}) %copy-start) | copy-done | bytes 196632
  20.2 0.7 fusion.54
  20.8 2.2 %collective-permute-start.1 = (bf16[1,64,768]{2,1,0:T(8,128)(2,1)S(1)}, bf16[1,64,768]{2,1,0:T(8,128)(2,1)S(1)}, u32[]{:S(2)}, u32[]{:S(2)}) collective-permute-start(bf16[1,64,768]{2,1,0:T(8,128)(2,1)S(1)} %get-tuple-element.20), channel_id=1, source_target_pairs={{0,8},{8,16},{16,24},{1,9},{9,17},{17,25},{2,10},{10,18},{18,26},{... | collective-permute-start | bytes 294920 | tf_op jit(solution)/shard_map/ppermute | solution.py:22
  23.1 0.8 %fusion.2 = f32[]{:T(128)} fusion(f32[4,2,288,192]{3,2,1,0:T(8,128)S(1)} %bitcast.97, s32[]{:T(128)S(6)} %select_n.45), kind=kLoop, calls=%fused_computation.7 | loop fusion | flops 442367 | bytes 884744 | tf_op jit(solution)/shard_map/reduce_max | solution.py:36
  24.8 1.1 %copy.36 = f16[1152,192]{0,1:T(8,128)(2,1)} copy(f16[1152,192]{1,0:T(8,128)(2,1)S(1)} %bitcast.103) | data formatting | bytes 884736
  25.9 1.1 %concatenate.25.clone = f16[1168,192]{0,1:T(8,128)(2,1)S(1)} pad(f16[1152,192]{0,1:T(8,128)(2,1)} %copy.36, f16[]{:T(256)S(6)} %convert_element_type.98), padding=0_16x0_0 | pad | bytes 890882 | tf_op jit(solution)/shard_map/concatenate | solution.py:44
  27.0 2.1 %collective-permute-start.2 = (f16[1168,192]{0,1:T(8,128)(2,1)S(1)}, f16[1168,192]{0,1:T(8,128)(2,1)S(1)}, u32[]{:S(2)}, u32[]{:S(2)}) collective-permute-start(f16[1168,192]{0,1:T(8,128)(2,1)S(1)} %concatenate.25.clone), channel_id=1, source_target_pairs={{0,1},{1,0},{2,3},{3,2},{4,5},{5,4},{6,7},{7,6},{8,9},{9,8},{10,11... | collective-permute-start | bytes 1345544 | tf_op jit(solution)/shard_map/ppermute | solution.py:54
  29.1 2.3 %fusion.6 = f32[128,768]{1,0:T(8,128)} fusion(bf16[768,2304]{1,0:T(8,128)(2,1)} %param.5, bf16[1,128,768]{2,1,0:T(8,128)(2,1)S(1)} %copy-done), kind=kOutput, calls=%fused_computation.13 | convolution fusion | flops 150994944 | bytes 1769472 | tf_op jit(solution)/shard_map/dot_general | solution.py:114
  31.4 1.3 %collective-permute-start = (bf16[1,64,768]{2,1,0:T(8,128)(2,1)}, bf16[1,64,768]{2,1,0:T(8,128)(2,1)}, u32[]{:S(2)}, u32[]{:S(2)}) collective-permute-start(bf16[1,64,768]{2,1,0:T(8,128)(2,1)} %get-tuple-element.19), channel_id=1, source_target_pairs={{8,0},{16,8},{24,16},{9,1},{17,9},{25,17},{10,2},{18,10},{26,18},{... | collective-permute-start | bytes 294920 | tf_op jit(solution)/shard_map/ppermute | solution.py:23
  32.7 2.4 %fusion.4 = f32[128,768]{1,0:T(8,128)} fusion(bf16[768,2304]{1,0:T(8,128)(2,1)} %param.5, bf16[1,128,768]{2,1,0:T(8,128)(2,1)S(1)} %copy-done, bf16[1,64,768]{2,1,0:T(8,128)(2,1)S(1)} %collective-permute-done.1), kind=kOutput, calls=%fused_computation.11 | convolution fusion | flops 151388160 | bytes 1867776 | tf_op jit(solution)/shard_map/dot_general | solution.py:114
  35.1 5.9 %collective-permute-done.2 = f16[1168,192]{0,1:T(8,128)(2,1)S(1)} collective-permute-done((f16[1168,192]{0,1:T(8,128)(2,1)S(1)}, f16[1168,192]{0,1:T(8,128)(2,1)S(1)}, u32[]{:S(2)}, u32[]{:S(2)}) %collective-permute-start.2) | collective-permute-done | bytes 448544 | tf_op jit(solution)/shard_map/ppermute | solution.py:54
  41.0 0.8 %copy-done.5 = f16[1168,192]{0,1:T(8,128)(2,1)} copy-done((f16[1168,192]{0,1:T(8,128)(2,1)}, f16[1168,192]{0,1:T(8,128)(2,1)S(1)}, u32[]{:S(2)}) %copy-start.5) | copy-done | bytes 448536
  41.8 0.5 copy.34
  42.3 1.2 %slice.85 = f16[1,1]{0,1:T(2,128)(2,1)} slice(f16[1168,192]{0,1:T(8,128)(2,1)} %copy-done.5), slice={[1152:1153], [0:1]} | slice | bytes 4 | tf_op jit(solution)/shard_map/slice | solution.py:48
  44.3 0.8 %abs_reduce_fusion = (f32[]{:T(128)}, f32[4,288,192]{2,1,0:T(8,128)S(1)}) fusion(f32[4,288,192]{2,1,0:T(8,128)S(1)} %bitcast.102, f32[4,2,288,192]{3,2,1,0:T(8,128)S(1)} %bitcast.99, s32[]{:T(128)S(6)} %select_n.44), kind=kLoop, calls=%fused_computation.9 | loop fusion | flops 663551 | bytes 2654216 | tf_op jit(solution)/shard_map/reduce_max | solution.py:36
  46.2 3.3 %collective-permute-start.5 = (f16[304,192]{1,0:T(8,128)(2,1)S(1)}, f16[304,192]{1,0:T(8,128)(2,1)S(1)}, u32[]{:S(2)}, u32[]{:S(2)}) collective-permute-start(f16[304,192]{1,0:T(8,128)(2,1)S(1)} %concatenate.28), channel_id=1, source_target_pairs={{0,4},{1,5},{2,6},{3,7},{4,0},{5,1},{6,2},{7,3},{8,12},{9,13},{10,... | collective-permute-start | bytes 350216 | tf_op jit(solution)/shard_map/ppermute | solution.py:54
  49.5 1.6 %collective-permute-start.4 = (f16[304,192]{1,0:T(8,128)(2,1)S(1)}, f16[304,192]{1,0:T(8,128)(2,1)S(1)}, u32[]{:S(2)}, u32[]{:S(2)}) collective-permute-start(f16[304,192]{1,0:T(8,128)(2,1)S(1)} %concatenate.27), channel_id=1, source_target_pairs={{0,2},{1,3},{2,4},{3,5},{4,6},{5,7},{6,0},{7,1},{8,10},{9,11},{10,... | collective-permute-start | bytes 350216 | tf_op jit(solution)/shard_map/ppermute | solution.py:54
  51.2 2.3 %collective-permute-start.3 = (f16[304,192]{1,0:T(8,128)(2,1)S(1)}, f16[304,192]{1,0:T(8,128)(2,1)S(1)}, u32[]{:S(2)}, u32[]{:S(2)}) collective-permute-start(f16[304,192]{1,0:T(8,128)(2,1)S(1)} %concatenate.26), channel_id=1, source_target_pairs={{0,6},{1,7},{2,0},{3,1},{4,2},{5,3},{6,4},{7,5},{8,14},{9,15},{10,... | collective-permute-start | bytes 350216 | tf_op jit(solution)/shard_map/ppermute | solution.py:54
  53.5 2.3 %fusion.12 = bf16[1,128,768]{2,1,0:T(8,128)(2,1)} fusion(f32[128,768]{1,0:T(8,128)S(1)} %copy-done.3, f32[128,768]{1,0:T(8,128)S(1)} %copy-done.6, f32[128,768]{1,0:T(8,128)S(1)} %copy-done.2, bf16[768,2304]{1,0:T(8,128)(2,1)} %param.5, bf16[1,64,768]{2,1,0:T(8,128)(2,1)} %collective-permute-done, bf16[1,128,768]{2,1,0:T(8,128)(2,1)S(1)} %copy-done.1), kind=kOutput, calls=%fused_computation.17 | convolution fusion | flops 151781376 | bytes 2850816 | tf_op jit(solution)/shard_map/dot_general | solution.py:114
  55.9 5.2 %collective-permute-done.5 = f16[304,192]{1,0:T(8,128)(2,1)S(1)} collective-permute-done((f16[304,192]{1,0:T(8,128)(2,1)S(1)}, f16[304,192]{1,0:T(8,128)(2,1)S(1)}, u32[]{:S(2)}, u32[]{:S(2)}) %collective-permute-start.5) | collective-permute-done | bytes 116768 | tf_op jit(solution)/shard_map/ppermute | solution.py:54
  61.0 0.5 slice.91
  62.2 0.5 slice.89
  63.5 0.5 slice.87
  64.7 0.9 %copy.28 = f32[192,288]{1,0:T(8,128)} copy(f32[192,288]{0,1:T(8,128)S(1)} %fusion.31) | data formatting | bytes 442368
  (26 shorter events, 0.8 us)
Async XLA Ops:
  0.6 16.5 %copy-start.4 = (bf16[1,128,768]{2,1,0:T(8,128)(2,1)S(1)}, bf16[1,128,768]{2,1,0:T(8,128)(2,1)}, u32[]{:S(2)}) copy-start(bf16[1,128,768]{2,1,0:T(8,128)(2,1)} %param.3) | copy-start | bytes 589828
  2.4 15.6 %all-to-all-start = ((bf16[4,192,128]{2,1,0:T(8,128)(2,1)}), bf16[4,192,128]{2,1,0:T(8,128)(2,1)S(1)}, u32[]{:S(2)}, u32[]{:S(2)}) async-start(bf16[4,192,128]{2,1,0:T(8,128)(2,1)} %bitcast.3), calls=%async_computation | async-start | bytes 393216 | tf_op jit(solution)/shard_map/all_to_all | solution.py:91
  19.2 0.9 %copy-start = (bf16[1,128,768]{2,1,0:T(8,128)(2,1)S(1)}, bf16[1,128,768]{2,1,0:T(8,128)(2,1)}, u32[]{:S(2)}) copy-start(bf16[1,128,768]{2,1,0:T(8,128)(2,1)} %param.4) | copy-start | bytes 589828
  20.8 11.9 %collective-permute-start.1 = (bf16[1,64,768]{2,1,0:T(8,128)(2,1)S(1)}, bf16[1,64,768]{2,1,0:T(8,128)(2,1)S(1)}, u32[]{:S(2)}, u32[]{:S(2)}) collective-permute-start(bf16[1,64,768]{2,1,0:T(8,128)(2,1)S(1)} %get-tuple-element.20), channel_id=1, source_target_pairs={{0,8},{8,16},{16,24},{1,9},{9,17},{17,25},{2,10},{10,18},{18,26},{... | collective-permute-start | bytes 294920 | tf_op jit(solution)/shard_map/ppermute | solution.py:22
  27.0 14.0 %collective-permute-start.2 = (f16[1168,192]{0,1:T(8,128)(2,1)S(1)}, f16[1168,192]{0,1:T(8,128)(2,1)S(1)}, u32[]{:S(2)}, u32[]{:S(2)}) collective-permute-start(f16[1168,192]{0,1:T(8,128)(2,1)S(1)} %concatenate.25.clone), channel_id=1, source_target_pairs={{0,1},{1,0},{2,3},{3,2},{4,5},{5,4},{6,7},{7,6},{8,9},{9,8},{10,11... | collective-permute-start | bytes 1345544 | tf_op jit(solution)/shard_map/ppermute | solution.py:54
  31.4 22.1 %collective-permute-start = (bf16[1,64,768]{2,1,0:T(8,128)(2,1)}, bf16[1,64,768]{2,1,0:T(8,128)(2,1)}, u32[]{:S(2)}, u32[]{:S(2)}) collective-permute-start(bf16[1,64,768]{2,1,0:T(8,128)(2,1)} %get-tuple-element.19), channel_id=1, source_target_pairs={{8,0},{16,8},{24,16},{9,1},{17,9},{25,17},{10,2},{18,10},{26,18},{... | collective-permute-start | bytes 294920 | tf_op jit(solution)/shard_map/ppermute | solution.py:23
  41.0 0.8 %copy-start.5 = (f16[1168,192]{0,1:T(8,128)(2,1)}, f16[1168,192]{0,1:T(8,128)(2,1)S(1)}, u32[]{:S(2)}) copy-start(f16[1168,192]{0,1:T(8,128)(2,1)S(1)} %collective-permute-done.2) | copy-start | bytes 1345540
  45.2 8.3 %copy-start.1 = (bf16[1,128,768]{2,1,0:T(8,128)(2,1)S(1)}, bf16[1,128,768]{2,1,0:T(8,128)(2,1)}, u32[]{:S(2)}) copy-start(bf16[1,128,768]{2,1,0:T(8,128)(2,1)} %param.4) | copy-start | bytes 589828
  45.2 8.3 %copy-start.2 = (f32[128,768]{1,0:T(8,128)S(1)}, f32[128,768]{1,0:T(8,128)}, u32[]{:S(2)}) copy-start(f32[128,768]{1,0:T(8,128)} %fusion.6) | copy-start | bytes 1179652
  45.2 8.3 %copy-start.3 = (f32[128,768]{1,0:T(8,128)S(1)}, f32[128,768]{1,0:T(8,128)}, u32[]{:S(2)}) copy-start(f32[128,768]{1,0:T(8,128)} %fusion.22) | copy-start | bytes 1179652
  45.2 8.3 %copy-start.6 = (f32[128,768]{1,0:T(8,128)S(1)}, f32[128,768]{1,0:T(8,128)}, u32[]{:S(2)}) copy-start(f32[128,768]{1,0:T(8,128)} %fusion.4) | copy-start | bytes 1179652
  46.2 14.9 %collective-permute-start.5 = (f16[304,192]{1,0:T(8,128)(2,1)S(1)}, f16[304,192]{1,0:T(8,128)(2,1)S(1)}, u32[]{:S(2)}, u32[]{:S(2)}) collective-permute-start(f16[304,192]{1,0:T(8,128)(2,1)S(1)} %concatenate.28), channel_id=1, source_target_pairs={{0,4},{1,5},{2,6},{3,7},{4,0},{5,1},{6,2},{7,3},{8,12},{9,13},{10,... | collective-permute-start | bytes 350216 | tf_op jit(solution)/shard_map/ppermute | solution.py:54
  49.5 12.7 %collective-permute-start.4 = (f16[304,192]{1,0:T(8,128)(2,1)S(1)}, f16[304,192]{1,0:T(8,128)(2,1)S(1)}, u32[]{:S(2)}, u32[]{:S(2)}) collective-permute-start(f16[304,192]{1,0:T(8,128)(2,1)S(1)} %concatenate.27), channel_id=1, source_target_pairs={{0,2},{1,3},{2,4},{3,5},{4,6},{5,7},{6,0},{7,1},{8,10},{9,11},{10,... | collective-permute-start | bytes 350216 | tf_op jit(solution)/shard_map/ppermute | solution.py:54
  51.2 12.3 %collective-permute-start.3 = (f16[304,192]{1,0:T(8,128)(2,1)S(1)}, f16[304,192]{1,0:T(8,128)(2,1)S(1)}, u32[]{:S(2)}, u32[]{:S(2)}) collective-permute-start(f16[304,192]{1,0:T(8,128)(2,1)S(1)} %concatenate.26), channel_id=1, source_target_pairs={{0,6},{1,7},{2,0},{3,1},{4,2},{5,3},{6,4},{7,5},{8,14},{9,15},{10,... | collective-permute-start | bytes 350216 | tf_op jit(solution)/shard_map/ppermute | solution.py:54

commit v14 on v13

--- a/solution.py
+++ b/solution.py
@@ -47,7 +47,7 @@
 def decode(packed, shape):
     exponent = packed[-TAG:1 - TAG, 0:1].astype(jnp.float32)
     values = packed[:-TAG].astype(jnp.float32) * jnp.exp2(exponent - HEADROOM)
-    return values.reshape(shape)
+    return values.reshape(shape), exponent
 
 
 def send(values, perm, exponent):
@@ -65,13 +65,14 @@
     blocks = columns.reshape(outer, 2, -1, columns.shape[1])
     mine = lax.dynamic_index_in_dim(blocks, x, axis=1, keepdims=False)
     theirs = lax.dynamic_index_in_dim(blocks, 1 - x, axis=1, keepdims=False)
-    summed = with_layout_constraint(mine + send(theirs, pairs, exponent_of(theirs)), Layout((0, 1, 2)))
-    spread = exponent_of(summed)
+    received, partner = send(theirs, pairs, exponent_of(theirs))
+    summed = with_layout_constraint(mine + received, Layout((0, 1, 2)))
+    spread = jnp.maximum(exponent_of(mine), partner) + 1.0
     total = lax.dynamic_index_in_dim(summed, z, axis=0, keepdims=False)
     for shift in sorted(range(1, outer), key=lambda d: (min(d, outer - d), -d)):
         target = lax.dynamic_index_in_dim(summed, (z + shift) % outer, axis=0, keepdims=False)
         perm = [(2 * q + p, 2 * ((q + shift) % outer) + p) for q in range(outer) for p in range(2)]
-        total = total + send(target, perm, spread)
+        total = total + send(target, perm, spread)[0]
     return with_layout_constraint(total, Layout((0, 1))).T
 
 

time: 66.4 us -> 67 us (level)
  local copies, waits for them, and re-layouts: 10.5 us -> 12.6 us
  matrix products: 8.26 us -> 7.56 us
    slice x1, local copies, waits for them, and re-layouts: 0.08 us -> 1.85 us  [decode(): values = packed[:-TAG].astype(jnp.float32) * jnp.exp2(exponent - HEADROOM)]
    reduce_max x2 -> x1, other arithmetic: 1.64 us -> 0.89 us  [exponent_of(): jnp.max(jnp.max(jnp.abs(flat), axis=0, keepdims=True), axis=1, keepdims=T...]
    dot_general x3, matrix products: 7.05 us -> 6.34 us  [body(): jnp.dot(window, weight[:, tap_index * in_width:(tap_index + 1) * in_width...]
    unnamed x18 -> x12, local copies, waits for them, and re-layouts: 5.81 us -> 6.01 us
  transfers between devices with their start and end apart: 7 -> 7, of which waited for: 2 -> 2; matrix products, arithmetic and copies ran while one was open for 25% -> 27% of each run, Pallas kernels for 0% -> 0%
where the time goes in v14:
time: 67 us; the launch traced here: 66.4 us
  starting transfers between devices  17.4 us (26%)
  local copies, waits for them, and re-layouts  12.6 us (19%)
  waiting for transfers between devices  10.9 us (16%)
  blocking collectives  9.41 us (14%)
  matrix products  7.56 us (11%)
  between operations  4.96 us (7%)
  other arithmetic  3.61 us (5%)
    ppermute x4, waiting for transfers between devices, send(): arrived = lax.ppermute(encode(values, exponent), 'batch', perm)  10.9 us
    all_gather x1, blocking collectives, body(): whole_act = lax.all_gather(act[None], 'seq', axis=1, tiled=True)[0]  9.41 us
    ppermute x4, starting transfers between devices, send(): arrived = lax.ppermute(encode(values, exponent), 'batch', perm)  8.94 us
    dot_general x3, matrix products, body(): jnp.dot(window, weight[:, tap_index * in_width:(tap_index + 1) * in_width...  6.34 us
    unnamed x12, local copies, waits for them, and re-layouts  6.01 us
    all_to_all x1, starting transfers between devices, body(): arrived = lax.all_to_all(channels, 'seq', 0, 0, tiled=True)  4.24 us
    ppermute x1, starting transfers between devices, extended_2(): before = lax.ppermute(last, axis, up)  2.88 us
    slice x4, local copies, waits for them, and re-layouts, decode(): exponent = packed[-TAG:1 - TAG, 0:1].astype(jnp.float32)  2.82 us
  transfers between devices with their start and end apart: 7, of which 2 were waited for; matrix products, arithmetic and copies ran while one was open for 27% of the time, Pallas kernels for 0%

profile of v14, /device:TPU:0, one launch (start us, length us, event | category | flops | bytes accessed | tf_op | source)
XLA Modules:
  0.0 66.4 jit_solution(11219515026722585547)
XLA Ops:
  0.6 1.8 %copy.19 = bf16[1,128,768]{1,2,0:T(8,128)(2,1)} copy(bf16[1,128,768]{2,1,0:T(8,128)(2,1)} %param.4) | data formatting | bytes 393216 | tf_op args[1]
  2.4 4.2 %all-to-all-start = ((bf16[4,192,128]{2,1,0:T(8,128)(2,1)}), bf16[4,192,128]{2,1,0:T(8,128)(2,1)S(1)}, u32[]{:S(2)}, u32[]{:S(2)}) async-start(bf16[4,192,128]{2,1,0:T(8,128)(2,1)} %bitcast.3), calls=%async_computation | async-start | bytes 393216 | tf_op jit(solution)/shard_map/all_to_all | solution.py:92
  6.7 1.0 %fusion.27 = bf16[1,128,768]{2,1,0:T(8,128)(2,1)S(1)} fusion(bf16[1,128,768]{2,1,0:T(8,128)(2,1)} %param.3), kind=kLoop, calls=%fused_computation.36 | loop fusion | flops 589824 | bytes 393216 | tf_op jit(solution)/shard_map/convert_element_type | solution.py:86
  7.7 9.4 %all_gather.3 = bf16[1,512,768]{2,1,0:T(8,128)(2,1)S(1)} all-gather(bf16[1,128,768]{2,1,0:T(8,128)(2,1)S(1)} %fusion.27), channel_id=1, replica_groups=mesh['seq'=4,'batch'=8] {'seq'}, dimensions={1}, use_global_device_ids=true | all-gather | bytes 983040 | tf_op jit(solution)/shard_map/all_gather | solution.py:95
  17.1 0.9 %fusion.23 = f32[128,768]{1,0:T(8,128)} fusion(bf16[1,128,768]{2,1,0:T(8,128)(2,1)S(1)} %copy-done.2), kind=kLoop, calls=%fused_computation.32 | loop fusion | flops 884736 | bytes 589824 | tf_op jit(solution)/shard_map/add | solution.py:31
  18.0 0.4 fusion.34
  18.4 0.4 fusion.17
  18.8 0.4 fusion.16
  19.3 0.2 maximum_multiply_fusion
  19.4 0.7 %copy-done = bf16[1,128,768]{2,1,0:T(8,128)(2,1)S(1)} copy-done((bf16[1,128,768]{2,1,0:T(8,128)(2,1)S(1)}, bf16[1,128,768]{2,1,0:T(8,128)(2,1)}, u32[]{:S(2)}) %copy-start) | copy-done | bytes 196632
  20.2 0.7 %fusion.55 = (bf16[1,64,768]{2,1,0:T(8,128)(2,1)}, bf16[1,64,768]{2,1,0:T(8,128)(2,1)}) fusion(bf16[1,128,768]{2,1,0:T(8,128)(2,1)S(1)} %copy-done), kind=kLoop, calls=%fused_computation.68 | loop fusion | bytes 393216 | tf_op jit(solution)/shard_map/slice | solution.py:21
  20.9 2.9 %collective-permute-start.1 = (bf16[1,64,768]{2,1,0:T(8,128)(2,1)}, bf16[1,64,768]{2,1,0:T(8,128)(2,1)}, u32[]{:S(2)}, u32[]{:S(2)}) collective-permute-start(bf16[1,64,768]{2,1,0:T(8,128)(2,1)} %get-tuple-element.20), channel_id=1, source_target_pairs={{0,8},{8,16},{16,24},{1,9},{9,17},{17,25},{2,10},{10,18},{18,26},{... | collective-permute-start | bytes 294920 | tf_op jit(solution)/shard_map/ppermute | solution.py:22
  23.7 0.9 %fusion.2 = (f32[]{:T(128)}, f32[]{:T(128)}) fusion(f32[4,2,288,192]{3,2,1,0:T(8,128)S(1)} %bitcast.102, s32[]{:T(128)S(6)} %select_n.44, s32[]{:T(128)S(6)} %select_n.45), kind=kLoop, calls=%fused_computation.6 | loop fusion | flops 884734 | bytes 1769488 | tf_op jit(solution)/shard_map/reduce_max | solution.py:36
  25.4 1.1 %copy.36 = f16[1152,192]{0,1:T(8,128)(2,1)} copy(f16[1152,192]{1,0:T(8,128)(2,1)S(1)} %bitcast.108) | data formatting | bytes 884736
  26.5 1.1 %concatenate.25.clone = f16[1168,192]{0,1:T(8,128)(2,1)S(1)} pad(f16[1152,192]{0,1:T(8,128)(2,1)} %copy.36, f16[]{:T(256)S(6)} %convert_element_type.98), padding=0_16x0_0 | pad | bytes 890882 | tf_op jit(solution)/shard_map/concatenate | solution.py:44
  27.6 2.1 %collective-permute-start.2 = (f16[1168,192]{0,1:T(8,128)(2,1)S(1)}, f16[1168,192]{0,1:T(8,128)(2,1)}, u32[]{:S(2)}, u32[]{:S(2)}) collective-permute-start(f16[1168,192]{0,1:T(8,128)(2,1)S(1)} %concatenate.25.clone), channel_id=1, source_target_pairs={{0,1},{1,0},{2,3},{3,2},{4,5},{5,4},{6,7},{7,6},{8,9},{9,8},{10,11... | collective-permute-start | bytes 1345544 | tf_op jit(solution)/shard_map/ppermute | solution.py:54
  29.8 1.6 %fusion.7 = f32[128,768]{1,0:T(8,128)S(1)} fusion(bf16[768,2304]{1,0:T(8,128)(2,1)} %param.5, bf16[1,128,768]{2,1,0:T(8,128)(2,1)S(1)} %copy-done), kind=kOutput, calls=%fused_computation.14 | convolution fusion | flops 150994944 | bytes 1769472 | tf_op jit(solution)/shard_map/dot_general | solution.py:115
  31.4 1.3 %collective-permute-start = (bf16[1,64,768]{2,1,0:T(8,128)(2,1)}, bf16[1,64,768]{2,1,0:T(8,128)(2,1)}, u32[]{:S(2)}, u32[]{:S(2)}) collective-permute-start(bf16[1,64,768]{2,1,0:T(8,128)(2,1)} %get-tuple-element.19), channel_id=1, source_target_pairs={{8,0},{16,8},{24,16},{9,1},{17,9},{25,17},{10,2},{18,10},{26,18},{... | collective-permute-start | bytes 294920 | tf_op jit(solution)/shard_map/ppermute | solution.py:23
  33.4 2.4 %fusion.5 = f32[128,768]{1,0:T(8,128)} fusion(bf16[768,2304]{1,0:T(8,128)(2,1)} %param.5, bf16[1,128,768]{2,1,0:T(8,128)(2,1)S(1)} %copy-done, bf16[1,64,768]{2,1,0:T(8,128)(2,1)} %collective-permute-done.1), kind=kOutput, calls=%fused_computation.12 | convolution fusion | flops 151388160 | bytes 1867776 | tf_op jit(solution)/shard_map/dot_general | solution.py:115
  35.8 5.7 %collective-permute-done.2 = f16[1168,192]{0,1:T(8,128)(2,1)} collective-permute-done((f16[1168,192]{0,1:T(8,128)(2,1)S(1)}, f16[1168,192]{0,1:T(8,128)(2,1)}, u32[]{:S(2)}, u32[]{:S(2)}) %collective-permute-start.2) | collective-permute-done | bytes 448544 | tf_op jit(solution)/shard_map/ppermute | solution.py:54
  41.5 1.9 %slice.84 = f16[1152,192]{0,1:T(8,128)(2,1)} slice(f16[1168,192]{0,1:T(8,128)(2,1)} %collective-permute-done.2), slice={[0:1152], [0:192]} | slice | bytes 884736 | tf_op jit(solution)/shard_map/slice | solution.py:49
  43.4 1.5 %copy.34 = f16[1152,192]{1,0:T(8,128)(2,1)S(1)} copy(f16[1152,192]{0,1:T(8,128)(2,1)} %slice.84) | data formatting | bytes 884736
  44.9 1.2 %slice.85 = f16[1,1]{0,1:T(2,128)(2,1)} slice(f16[1168,192]{0,1:T(8,128)(2,1)} %collective-permute-done.2), slice={[1152:1153], [0:1]} | slice | bytes 4 | tf_op jit(solution)/shard_map/slice | solution.py:48
  47.3 2.9 %collective-permute-start.5 = (f16[304,192]{1,0:T(8,128)(2,1)S(1)}, f16[304,192]{1,0:T(8,128)(2,1)S(1)}, u32[]{:S(2)}, u32[]{:S(2)}) collective-permute-start(f16[304,192]{1,0:T(8,128)(2,1)S(1)} %concatenate.28), channel_id=1, source_target_pairs={{0,4},{1,5},{2,6},{3,7},{4,0},{5,1},{6,2},{7,3},{8,12},{9,13},{10,... | collective-permute-start | bytes 350216 | tf_op jit(solution)/shard_map/ppermute | solution.py:54
  50.2 1.6 %collective-permute-start.4 = (f16[304,192]{1,0:T(8,128)(2,1)S(1)}, f16[304,192]{1,0:T(8,128)(2,1)S(1)}, u32[]{:S(2)}, u32[]{:S(2)}) collective-permute-start(f16[304,192]{1,0:T(8,128)(2,1)S(1)} %concatenate.27), channel_id=1, source_target_pairs={{0,2},{1,3},{2,4},{3,5},{4,6},{5,7},{6,0},{7,1},{8,10},{9,11},{10,... | collective-permute-start | bytes 350216 | tf_op jit(solution)/shard_map/ppermute | solution.py:54
  51.9 2.3 %collective-permute-start.3 = (f16[304,192]{1,0:T(8,128)(2,1)S(1)}, f16[304,192]{1,0:T(8,128)(2,1)S(1)}, u32[]{:S(2)}, u32[]{:S(2)}) collective-permute-start(f16[304,192]{1,0:T(8,128)(2,1)S(1)} %concatenate.26), channel_id=1, source_target_pairs={{0,6},{1,7},{2,0},{3,1},{4,2},{5,3},{6,4},{7,5},{8,14},{9,15},{10,... | collective-permute-start | bytes 350216 | tf_op jit(solution)/shard_map/ppermute | solution.py:54
  54.2 2.3 %fusion.13 = bf16[1,128,768]{2,1,0:T(8,128)(2,1)} fusion(f32[128,768]{1,0:T(8,128)S(1)} %copy-done.1, f32[128,768]{1,0:T(8,128)S(1)} %copy-done.3, f32[128,768]{1,0:T(8,128)S(1)} %fusion.7, bf16[768,2304]{1,0:T(8,128)(2,1)} %param.5, bf16[1,64,768]{2,1,0:T(8,128)(2,1)} %collective-permute-done, bf16[1,128,768]{2,1,0:T(8,128)(2,1)S(1)} %copy-done), kind=kOutput, calls=%fused_computation.18 | convolution fusion | flops 151781376 | bytes 2850816 | tf_op jit(solution)/shard_map/dot_general | solution.py:115
  56.5 5.2 %collective-permute-done.5 = f16[304,192]{1,0:T(8,128)(2,1)S(1)} collective-permute-done((f16[304,192]{1,0:T(8,128)(2,1)S(1)}, f16[304,192]{1,0:T(8,128)(2,1)S(1)}, u32[]{:S(2)}, u32[]{:S(2)}) %collective-permute-start.5) | collective-permute-done | bytes 116768 | tf_op jit(solution)/shard_map/ppermute | solution.py:54
  61.7 0.5 slice.91
  62.9 0.6 slice.89
  64.2 0.5 slice.87
  65.5 0.9 %copy.28 = f32[192,288]{1,0:T(8,128)} copy(f32[192,288]{0,1:T(8,128)S(1)} %fusion.32) | data formatting | bytes 442368
  (20 shorter events, 0.7 us)
Async XLA Ops:
  0.6 16.5 %copy-start.2 = (bf16[1,128,768]{2,1,0:T(8,128)(2,1)S(1)}, bf16[1,128,768]{2,1,0:T(8,128)(2,1)}, u32[]{:S(2)}) copy-start(bf16[1,128,768]{2,1,0:T(8,128)(2,1)} %param.3) | copy-start | bytes 589828
  2.4 15.6 %all-to-all-start = ((bf16[4,192,128]{2,1,0:T(8,128)(2,1)}), bf16[4,192,128]{2,1,0:T(8,128)(2,1)S(1)}, u32[]{:S(2)}, u32[]{:S(2)}) async-start(bf16[4,192,128]{2,1,0:T(8,128)(2,1)} %bitcast.3), calls=%async_computation | async-start | bytes 393216 | tf_op jit(solution)/shard_map/all_to_all | solution.py:92
  19.2 0.9 %copy-start = (bf16[1,128,768]{2,1,0:T(8,128)(2,1)S(1)}, bf16[1,128,768]{2,1,0:T(8,128)(2,1)}, u32[]{:S(2)}) copy-start(bf16[1,128,768]{2,1,0:T(8,128)(2,1)} %param.4) | copy-start | bytes 589828
  20.9 12.5 %collective-permute-start.1 = (bf16[1,64,768]{2,1,0:T(8,128)(2,1)}, bf16[1,64,768]{2,1,0:T(8,128)(2,1)}, u32[]{:S(2)}, u32[]{:S(2)}) collective-permute-start(bf16[1,64,768]{2,1,0:T(8,128)(2,1)} %get-tuple-element.20), channel_id=1, source_target_pairs={{0,8},{8,16},{16,24},{1,9},{9,17},{17,25},{2,10},{10,18},{18,26},{... | collective-permute-start | bytes 294920 | tf_op jit(solution)/shard_map/ppermute | solution.py:22
  27.6 13.9 %collective-permute-start.2 = (f16[1168,192]{0,1:T(8,128)(2,1)S(1)}, f16[1168,192]{0,1:T(8,128)(2,1)}, u32[]{:S(2)}, u32[]{:S(2)}) collective-permute-start(f16[1168,192]{0,1:T(8,128)(2,1)S(1)} %concatenate.25.clone), channel_id=1, source_target_pairs={{0,1},{1,0},{2,3},{3,2},{4,5},{5,4},{6,7},{7,6},{8,9},{9,8},{10,11... | collective-permute-start | bytes 1345544 | tf_op jit(solution)/shard_map/ppermute | solution.py:54
  31.4 22.8 %collective-permute-start = (bf16[1,64,768]{2,1,0:T(8,128)(2,1)}, bf16[1,64,768]{2,1,0:T(8,128)(2,1)}, u32[]{:S(2)}, u32[]{:S(2)}) collective-permute-start(bf16[1,64,768]{2,1,0:T(8,128)(2,1)} %get-tuple-element.19), channel_id=1, source_target_pairs={{8,0},{16,8},{24,16},{9,1},{17,9},{25,17},{10,2},{18,10},{26,18},{... | collective-permute-start | bytes 294920 | tf_op jit(solution)/shard_map/ppermute | solution.py:23
  47.0 7.1 %copy-start.1 = (f32[128,768]{1,0:T(8,128)S(1)}, f32[128,768]{1,0:T(8,128)}, u32[]{:S(2)}) copy-start(f32[128,768]{1,0:T(8,128)} %fusion.23) | copy-start | bytes 1179652
  47.0 7.1 %copy-start.3 = (f32[128,768]{1,0:T(8,128)S(1)}, f32[128,768]{1,0:T(8,128)}, u32[]{:S(2)}) copy-start(f32[128,768]{1,0:T(8,128)} %fusion.5) | copy-start | bytes 1179652
  47.3 14.4 %collective-permute-start.5 = (f16[304,192]{1,0:T(8,128)(2,1)S(1)}, f16[304,192]{1,0:T(8,128)(2,1)S(1)}, u32[]{:S(2)}, u32[]{:S(2)}) collective-permute-start(f16[304,192]{1,0:T(8,128)(2,1)S(1)} %concatenate.28), channel_id=1, source_target_pairs={{0,4},{1,5},{2,6},{3,7},{4,0},{5,1},{6,2},{7,3},{8,12},{9,13},{10,... | collective-permute-start | bytes 350216 | tf_op jit(solution)/shard_map/ppermute | solution.py:54
  50.2 12.7 %collective-permute-start.4 = (f16[304,192]{1,0:T(8,128)(2,1)S(1)}, f16[304,192]{1,0:T(8,128)(2,1)S(1)}, u32[]{:S(2)}, u32[]{:S(2)}) collective-permute-start(f16[304,192]{1,0:T(8,128)(2,1)S(1)} %concatenate.27), channel_id=1, source_target_pairs={{0,2},{1,3},{2,4},{3,5},{4,6},{5,7},{6,0},{7,1},{8,10},{9,11},{10,... | collective-permute-start | bytes 350216 | tf_op jit(solution)/shard_map/ppermute | solution.py:54
  51.9 12.3 %collective-permute-start.3 = (f16[304,192]{1,0:T(8,128)(2,1)S(1)}, f16[304,192]{1,0:T(8,128)(2,1)S(1)}, u32[]{:S(2)}, u32[]{:S(2)}) collective-permute-start(f16[304,192]{1,0:T(8,128)(2,1)S(1)} %concatenate.26), channel_id=1, source_target_pairs={{0,6},{1,7},{2,0},{3,1},{4,2},{5,3},{6,4},{7,5},{8,14},{9,15},{10,... | collective-permute-start | bytes 350216 | tf_op jit(solution)/shard_map/ppermute | solution.py:54

commit v15 on v13

--- a/solution.py
+++ b/solution.py
@@ -80,6 +80,7 @@
     reach = middle_offset * TAP_SPACING
     length = inputs.shape[1]
     in_width = inputs.shape[2]
+    halo_source = cotangent
     values = inputs[0].astype(jnp.float32)
     activation, deriv = gelu_factors(values)
     act = activation.astype(jnp.bfloat16)
@@ -104,9 +105,8 @@
         )
     local_columns = jnp.concatenate(updated, axis=0) * factor
     local_columns = with_layout_constraint(local_columns, Layout((0, 1)))
-    local_columns, cotangent, deriv = lax.optimization_barrier((local_columns, cotangent, deriv))
-    padded_input = extended_2(cotangent, (("seq", 1),), reach)
-    extended = padded_input[0]
+    extended = extended_2(halo_source, (("seq", 1),), reach)[0]
+    local_columns, extended, deriv = lax.optimization_barrier((local_columns, extended, deriv))
     grad_act = jnp.zeros((length, in_width), jnp.float32)
     for tap_index in range(KW):
         window_start = (2 * middle_offset - tap_index) * TAP_SPACING

time: 66.4 us -> 64.9 us (0.977)
  local copies, waits for them, and re-layouts: 10.5 us -> 8.41 us
  waiting for transfers between devices: 11 us -> 12.6 us
  matrix products: 8.26 us -> 7.55 us
    ppermute x4, waiting for transfers between devices: 11 us -> 12.6 us  [send(): arrived = lax.ppermute(encode(values, exponent), 'batch', perm)]
    unnamed x18, local copies, waits for them, and re-layouts: 5.81 us -> 4.4 us
    concatenate x4, local copies, waits for them, and re-layouts: 1.19 us -> 0.18 us  [encode(): jnp.concatenate([scaled, tag], axis=0)]
    convert_element_type x1, other arithmetic: 1.02 us -> 0.09 us  [body(): act = activation.astype(jnp.bfloat16)]
    ppermute x1, starting transfers between devices: 2.25 us -> 3.05 us  [extended_2(): before = lax.ppermute(last, axis, up)]
    squeeze x0 -> x1, other arithmetic: none -> 0.79 us  [body(): extended = extended_2(halo_source, (('seq', 1),), reach)[0]]
    dot_general x3, matrix products: 7.05 us -> 6.34 us  [body(): jnp.dot(window, weight[:, tap_index * in_width:(tap_index + 1) * in_width...]
  transfers between devices with their start and end apart: 7 -> 7, of which waited for: 2 -> 2; matrix products, arithmetic and copies ran while one was open for 25% -> 16% of each run, Pallas kernels for 0% -> 0%
where the time goes in v15:
time: 64.9 us; the launch traced here: 64.2 us
  starting transfers between devices  17.5 us (27%)
  waiting for transfers between devices  12.6 us (19%)
  blocking collectives  9.08 us (14%)
  local copies, waits for them, and re-layouts  8.41 us (13%)
  matrix products  7.55 us (12%)
  between operations  5.09 us (8%)
  other arithmetic  4.04 us (6%)
    ppermute x4, waiting for transfers between devices, send(): arrived = lax.ppermute(encode(values, exponent), 'batch', perm)  12.6 us
    all_gather x1, blocking collectives, body(): whole_act = lax.all_gather(act[None], 'seq', axis=1, tiled=True)[0]  9.08 us
    ppermute x4, starting transfers between devices, send(): arrived = lax.ppermute(encode(values, exponent), 'batch', perm)  8.9 us
    dot_general x3, matrix products, body(): jnp.dot(window, weight[:, tap_index * in_width:(tap_index + 1) * in_width...  6.34 us
    unnamed x18, local copies, waits for them, and re-layouts  4.4 us
    all_to_all x1, starting transfers between devices, body(): arrived = lax.all_to_all(channels, 'seq', 0, 0, tiled=True)  4.24 us
    ppermute x1, starting transfers between devices, extended_2(): before = lax.ppermute(last, axis, up)  3.05 us
    slice x4, local copies, waits for them, and re-layouts, decode(): exponent = packed[-TAG:1 - TAG, 0:1].astype(jnp.float32)  2.76 us
  transfers between devices with their start and end apart: 7, of which 2 were waited for; matrix products, arithmetic and copies ran while one was open for 16% of the time, Pallas kernels for 0%

profile of v15, /device:TPU:0, one launch (start us, length us, event | category | flops | bytes accessed | tf_op | source)
XLA Modules:
  0.0 64.2 jit_solution(5420582189454266538)
XLA Ops:
  0.6 1.8 %copy.19 = bf16[1,128,768]{1,2,0:T(8,128)(2,1)} copy(bf16[1,128,768]{2,1,0:T(8,128)(2,1)} %param.4) | data formatting | bytes 393216 | tf_op args[1]
  2.4 4.2 %all-to-all-start = ((bf16[4,192,128]{2,1,0:T(8,128)(2,1)}), bf16[4,192,128]{2,1,0:T(8,128)(2,1)S(1)}, u32[]{:S(2)}, u32[]{:S(2)}) async-start(bf16[4,192,128]{2,1,0:T(8,128)(2,1)} %bitcast.3), calls=%async_computation | async-start | bytes 393216 | tf_op jit(solution)/shard_map/all_to_all | solution.py:92
  6.7 1.0 %fusion.46 = (bf16[1,64,768]{2,1,0:T(8,128)(2,1)S(1)}, bf16[1,64,768]{2,1,0:T(8,128)(2,1)S(1)}) fusion(bf16[1,128,768]{2,1,0:T(8,128)(2,1)} %param.4), kind=kLoop, calls=%fused_computation.61 | loop fusion | bytes 393216 | tf_op jit(solution)/shard_map/slice | solution.py:20
  7.7 1.3 %collective-permute-start.1 = (bf16[1,64,768]{2,1,0:T(8,128)(2,1)S(1)}, bf16[1,64,768]{2,1,0:T(8,128)(2,1)S(1)}, u32[]{:S(2)}, u32[]{:S(2)}) collective-permute-start(bf16[1,64,768]{2,1,0:T(8,128)(2,1)S(1)} %get-tuple-element.20), channel_id=1, source_target_pairs={{8,0},{16,8},{24,16},{9,1},{17,9},{25,17},{10,2},{18,10},{26,18},{... | collective-permute-start | bytes 294920 | tf_op jit(solution)/shard_map/ppermute | solution.py:23
  9.0 3.0 %collective-permute-start = (bf16[1,64,768]{2,1,0:T(8,128)(2,1)S(1)}, bf16[1,64,768]{2,1,0:T(8,128)(2,1)S(1)}, u32[]{:S(2)}, u32[]{:S(2)}) collective-permute-start(bf16[1,64,768]{2,1,0:T(8,128)(2,1)S(1)} %get-tuple-element.19), channel_id=1, source_target_pairs={{0,8},{8,16},{16,24},{1,9},{9,17},{17,25},{2,10},{10,18},{18,26},{... | collective-permute-start | bytes 294920 | tf_op jit(solution)/shard_map/ppermute | solution.py:22
  12.1 9.1 %all_gather.3 = bf16[1,512,768]{2,1,0:T(8,128)(2,1)S(1)} all-gather(bf16[1,128,768]{2,1,0:T(8,128)(2,1)S(1)} %fusion.24), channel_id=1, replica_groups=mesh['seq'=4,'batch'=8] {'seq'}, dimensions={1}, use_global_device_ids=true | all-gather | bytes 983040 | tf_op jit(solution)/shard_map/all_gather | solution.py:95
  21.2 0.9 %fusion.20 = f32[128,768]{1,0:T(8,128)} fusion(bf16[1,128,768]{2,1,0:T(8,128)(2,1)S(1)} %copy-done.5), kind=kLoop, calls=%fused_computation.30 | loop fusion | flops 884736 | bytes 589824 | tf_op jit(solution)/shard_map/add | solution.py:31
  22.1 0.8 %maximum_bitcast_fusion = bf16[256,768]{1,0:T(8,128)(2,1)} fusion(bf16[1,64,768]{2,1,0:T(8,128)(2,1)S(1)} %collective-permute-done.1, bf16[1,128,768]{2,1,0:T(8,128)(2,1)S(1)} %copy-done, bf16[1,64,768]{2,1,0:T(8,128)(2,1)S(1)} %collective-permute-done), kind=kLoop, calls=%fused_computation.37 | loop fusion | flops 1179648 | bytes 786432 | tf_op jit(solution)/shard_map/squeeze | solution.py:108
  22.9 0.4 fusion.31
  23.3 0.4 fusion.14
  23.7 0.4 fusion.13
  24.1 0.2 maximum_multiply_fusion
  24.3 0.8 %fusion.1 = f32[]{:T(128)} fusion(f32[4,2,288,192]{3,2,1,0:T(8,128)S(1)} %bitcast.90, s32[]{:T(128)S(6)} %select_n.45), kind=kLoop, calls=%fused_computation.7 | loop fusion | flops 442367 | bytes 884744 | tf_op jit(solution)/shard_map/reduce_max | solution.py:36
  25.9 0.1 fusion.2
  26.0 0.4 copy.36
  26.6 2.1 %collective-permute-start.2 = (f16[1168,192]{0,1:T(8,128)(2,1)S(1)}, f16[1168,192]{0,1:T(8,128)(2,1)S(1)}, u32[]{:S(2)}, u32[]{:S(2)}) collective-permute-start(f16[1168,192]{0,1:T(8,128)(2,1)S(1)} %concatenate.20.clone), channel_id=1, source_target_pairs={{0,1},{1,0},{2,3},{3,2},{4,5},{5,4},{6,7},{7,6},{8,9},{9,8},{10,11... | collective-permute-start | bytes 1345544 | tf_op jit(solution)/shard_map/ppermute | solution.py:54
  28.6 1.7 %fusion.5 = f32[128,768]{1,0:T(8,128)S(1)} fusion(bf16[768,2304]{1,0:T(8,128)(2,1)} %param.5, bf16[256,768]{1,0:T(8,128)(2,1)} %maximum_bitcast_fusion), kind=kOutput, calls=%fused_computation.13 | convolution fusion | flops 150994944 | bytes 1769472 | tf_op jit(solution)/shard_map/dot_general | solution.py:114
  30.4 2.3 %convolution_add_fusion.1 = f32[128,768]{1,0:T(8,128)} fusion(f32[128,768]{1,0:T(8,128)S(1)} %fusion.5, bf16[768,2304]{1,0:T(8,128)(2,1)} %param.5, bf16[256,768]{1,0:T(8,128)(2,1)S(1)} %copy-done.2), kind=kOutput, calls=%fused_computation.2 | convolution fusion | flops 151093248 | bytes 2162688 | tf_op jit(solution)/shard_map/dot_general | solution.py:114
  32.7 7.5 %collective-permute-done.2 = f16[1168,192]{0,1:T(8,128)(2,1)S(1)} collective-permute-done((f16[1168,192]{0,1:T(8,128)(2,1)S(1)}, f16[1168,192]{0,1:T(8,128)(2,1)S(1)}, u32[]{:S(2)}, u32[]{:S(2)}) %collective-permute-start.2) | collective-permute-done | bytes 448544 | tf_op jit(solution)/shard_map/ppermute | solution.py:54
  40.2 0.8 %copy-done.6 = f16[1168,192]{0,1:T(8,128)(2,1)} copy-done((f16[1168,192]{0,1:T(8,128)(2,1)}, f16[1168,192]{0,1:T(8,128)(2,1)S(1)}, u32[]{:S(2)}) %copy-start.6) | copy-done | bytes 448536
  41.0 0.5 copy.34
  41.5 1.2 %slice.74 = f16[1,1]{0,1:T(2,128)(2,1)} slice(f16[1168,192]{0,1:T(8,128)(2,1)} %copy-done.6), slice={[1152:1153], [0:1]} | slice | bytes 4 | tf_op jit(solution)/shard_map/slice | solution.py:48
  43.5 0.8 %abs_reduce_fusion = (f32[]{:T(128)}, f32[4,288,192]{2,1,0:T(8,128)S(1)}) fusion(f32[4,288,192]{2,1,0:T(8,128)S(1)} %bitcast.95, f32[4,2,288,192]{3,2,1,0:T(8,128)S(1)} %bitcast.92, s32[]{:T(128)S(6)} %select_n.44), kind=kLoop, calls=%fused_computation.9 | loop fusion | flops 663551 | bytes 2654216 | tf_op jit(solution)/shard_map/reduce_max | solution.py:36
  45.4 2.9 %collective-permute-start.5 = (f16[304,192]{1,0:T(8,128)(2,1)S(1)}, f16[304,192]{1,0:T(8,128)(2,1)S(1)}, u32[]{:S(2)}, u32[]{:S(2)}) collective-permute-start(f16[304,192]{1,0:T(8,128)(2,1)S(1)} %concatenate.23), channel_id=1, source_target_pairs={{0,4},{1,5},{2,6},{3,7},{4,0},{5,1},{6,2},{7,3},{8,12},{9,13},{10,... | collective-permute-start | bytes 350216 | tf_op jit(solution)/shard_map/ppermute | solution.py:54
  48.3 1.6 %collective-permute-start.4 = (f16[304,192]{1,0:T(8,128)(2,1)S(1)}, f16[304,192]{1,0:T(8,128)(2,1)S(1)}, u32[]{:S(2)}, u32[]{:S(2)}) collective-permute-start(f16[304,192]{1,0:T(8,128)(2,1)S(1)} %concatenate.22), channel_id=1, source_target_pairs={{0,2},{1,3},{2,4},{3,5},{4,6},{5,7},{6,0},{7,1},{8,10},{9,11},{10,... | collective-permute-start | bytes 350216 | tf_op jit(solution)/shard_map/ppermute | solution.py:54
  50.0 2.3 %collective-permute-start.3 = (f16[304,192]{1,0:T(8,128)(2,1)S(1)}, f16[304,192]{1,0:T(8,128)(2,1)S(1)}, u32[]{:S(2)}, u32[]{:S(2)}) collective-permute-start(f16[304,192]{1,0:T(8,128)(2,1)S(1)} %concatenate.21), channel_id=1, source_target_pairs={{0,6},{1,7},{2,0},{3,1},{4,2},{5,3},{6,4},{7,5},{8,14},{9,15},{10,... | collective-permute-start | bytes 350216 | tf_op jit(solution)/shard_map/ppermute | solution.py:54
  52.3 2.3 %fusion.10 = bf16[1,128,768]{2,1,0:T(8,128)(2,1)} fusion(f32[128,768]{1,0:T(8,128)S(1)} %copy-done.1, f32[128,768]{1,0:T(8,128)S(1)} %copy-done.4, bf16[768,2304]{1,0:T(8,128)(2,1)} %param.5, bf16[256,768]{1,0:T(8,128)(2,1)S(1)} %copy-done.3), kind=kOutput, calls=%fused_computation.16 | convolution fusion | flops 151289856 | bytes 2359296 | tf_op jit(solution)/shard_map/dot_general | solution.py:114
  54.6 5.1 %collective-permute-done.5 = f16[304,192]{1,0:T(8,128)(2,1)S(1)} collective-permute-done((f16[304,192]{1,0:T(8,128)(2,1)S(1)}, f16[304,192]{1,0:T(8,128)(2,1)S(1)}, u32[]{:S(2)}, u32[]{:S(2)}) %collective-permute-start.5) | collective-permute-done | bytes 116768 | tf_op jit(solution)/shard_map/ppermute | solution.py:54
  59.7 0.5 slice.80
  60.9 0.5 slice.78
  62.1 0.5 slice.76
  63.4 0.9 %copy.28 = f32[192,288]{1,0:T(8,128)} copy(f32[192,288]{0,1:T(8,128)S(1)} %fusion.29) | data formatting | bytes 442368
  (27 shorter events, 0.7 us)
Async XLA Ops:
  0.6 11.4 %copy-start.5 = (bf16[1,128,768]{2,1,0:T(8,128)(2,1)S(1)}, bf16[1,128,768]{2,1,0:T(8,128)(2,1)}, u32[]{:S(2)}) copy-start(bf16[1,128,768]{2,1,0:T(8,128)(2,1)} %param.3) | copy-start | bytes 589828
  2.4 20.5 %all-to-all-start = ((bf16[4,192,128]{2,1,0:T(8,128)(2,1)}), bf16[4,192,128]{2,1,0:T(8,128)(2,1)S(1)}, u32[]{:S(2)}, u32[]{:S(2)}) async-start(bf16[4,192,128]{2,1,0:T(8,128)(2,1)} %bitcast.3), calls=%async_computation | async-start | bytes 393216 | tf_op jit(solution)/shard_map/all_to_all | solution.py:92
  6.7 15.5 %copy-start = (bf16[1,128,768]{2,1,0:T(8,128)(2,1)S(1)}, bf16[1,128,768]{2,1,0:T(8,128)(2,1)}, u32[]{:S(2)}) copy-start(bf16[1,128,768]{2,1,0:T(8,128)(2,1)} %param.4) | copy-start | bytes 589828
  7.7 14.4 %collective-permute-start.1 = (bf16[1,64,768]{2,1,0:T(8,128)(2,1)S(1)}, bf16[1,64,768]{2,1,0:T(8,128)(2,1)S(1)}, u32[]{:S(2)}, u32[]{:S(2)}) collective-permute-start(bf16[1,64,768]{2,1,0:T(8,128)(2,1)S(1)} %get-tuple-element.20), channel_id=1, source_target_pairs={{8,0},{16,8},{24,16},{9,1},{17,9},{25,17},{10,2},{18,10},{26,18},{... | collective-permute-start | bytes 294920 | tf_op jit(solution)/shard_map/ppermute | solution.py:23
  9.0 13.2 %collective-permute-start = (bf16[1,64,768]{2,1,0:T(8,128)(2,1)S(1)}, bf16[1,64,768]{2,1,0:T(8,128)(2,1)S(1)}, u32[]{:S(2)}, u32[]{:S(2)}) collective-permute-start(bf16[1,64,768]{2,1,0:T(8,128)(2,1)S(1)} %get-tuple-element.19), channel_id=1, source_target_pairs={{0,8},{8,16},{16,24},{1,9},{9,17},{17,25},{2,10},{10,18},{18,26},{... | collective-permute-start | bytes 294920 | tf_op jit(solution)/shard_map/ppermute | solution.py:22
  26.5 3.9 %copy-start.2 = (bf16[256,768]{1,0:T(8,128)(2,1)S(1)}, bf16[256,768]{1,0:T(8,128)(2,1)}, u32[]{:S(2)}) copy-start(bf16[256,768]{1,0:T(8,128)(2,1)} %maximum_bitcast_fusion) | copy-start | bytes 1179652
  26.6 13.6 %collective-permute-start.2 = (f16[1168,192]{0,1:T(8,128)(2,1)S(1)}, f16[1168,192]{0,1:T(8,128)(2,1)S(1)}, u32[]{:S(2)}, u32[]{:S(2)}) collective-permute-start(f16[1168,192]{0,1:T(8,128)(2,1)S(1)} %concatenate.20.clone), channel_id=1, source_target_pairs={{0,1},{1,0},{2,3},{3,2},{4,5},{5,4},{6,7},{7,6},{8,9},{9,8},{10,11... | collective-permute-start | bytes 1345544 | tf_op jit(solution)/shard_map/ppermute | solution.py:54
  40.2 0.8 %copy-start.6 = (f16[1168,192]{0,1:T(8,128)(2,1)}, f16[1168,192]{0,1:T(8,128)(2,1)S(1)}, u32[]{:S(2)}) copy-start(f16[1168,192]{0,1:T(8,128)(2,1)S(1)} %collective-permute-done.2) | copy-start | bytes 1345540
  44.4 7.9 %copy-start.1 = (f32[128,768]{1,0:T(8,128)S(1)}, f32[128,768]{1,0:T(8,128)}, u32[]{:S(2)}) copy-start(f32[128,768]{1,0:T(8,128)} %fusion.20) | copy-start | bytes 1179652
  44.4 7.9 %copy-start.3 = (bf16[256,768]{1,0:T(8,128)(2,1)S(1)}, bf16[256,768]{1,0:T(8,128)(2,1)}, u32[]{:S(2)}) copy-start(bf16[256,768]{1,0:T(8,128)(2,1)} %maximum_bitcast_fusion) | copy-start | bytes 1179652
  44.4 7.9 %copy-start.4 = (f32[128,768]{1,0:T(8,128)S(1)}, f32[128,768]{1,0:T(8,128)}, u32[]{:S(2)}) copy-start(f32[128,768]{1,0:T(8,128)} %convolution_add_fusion.1) | copy-start | bytes 1179652
  45.4 14.3 %collective-permute-start.5 = (f16[304,192]{1,0:T(8,128)(2,1)S(1)}, f16[304,192]{1,0:T(8,128)(2,1)S(1)}, u32[]{:S(2)}, u32[]{:S(2)}) collective-permute-start(f16[304,192]{1,0:T(8,128)(2,1)S(1)} %concatenate.23), channel_id=1, source_target_pairs={{0,4},{1,5},{2,6},{3,7},{4,0},{5,1},{6,2},{7,3},{8,12},{9,13},{10,... | collective-permute-start | bytes 350216 | tf_op jit(solution)/shard_map/ppermute | solution.py:54
  48.3 12.6 %collective-permute-start.4 = (f16[304,192]{1,0:T(8,128)(2,1)S(1)}, f16[304,192]{1,0:T(8,128)(2,1)S(1)}, u32[]{:S(2)}, u32[]{:S(2)}) collective-permute-start(f16[304,192]{1,0:T(8,128)(2,1)S(1)} %concatenate.22), channel_id=1, source_target_pairs={{0,2},{1,3},{2,4},{3,5},{4,6},{5,7},{6,0},{7,1},{8,10},{9,11},{10,... | collective-permute-start | bytes 350216 | tf_op jit(solution)/shard_map/ppermute | solution.py:54
  50.0 12.2 %collective-permute-start.3 = (f16[304,192]{1,0:T(8,128)(2,1)S(1)}, f16[304,192]{1,0:T(8,128)(2,1)S(1)}, u32[]{:S(2)}, u32[]{:S(2)}) collective-permute-start(f16[304,192]{1,0:T(8,128)(2,1)S(1)} %concatenate.21), channel_id=1, source_target_pairs={{0,6},{1,7},{2,0},{3,1},{4,2},{5,3},{6,4},{7,5},{8,14},{9,15},{10,... | collective-permute-start | bytes 350216 | tf_op jit(solution)/shard_map/ppermute | solution.py:54

commit v16 on v14

--- a/solution.py
+++ b/solution.py
@@ -81,6 +81,7 @@
     reach = middle_offset * TAP_SPACING
     length = inputs.shape[1]
     in_width = inputs.shape[2]
+    halo_source = cotangent
     values = inputs[0].astype(jnp.float32)
     activation, deriv = gelu_factors(values)
     act = activation.astype(jnp.bfloat16)
@@ -105,9 +106,8 @@
         )
     local_columns = jnp.concatenate(updated, axis=0) * factor
     local_columns = with_layout_constraint(local_columns, Layout((0, 1)))
-    local_columns, cotangent, deriv = lax.optimization_barrier((local_columns, cotangent, deriv))
-    padded_input = extended_2(cotangent, (("seq", 1),), reach)
-    extended = padded_input[0]
+    extended = extended_2(halo_source, (("seq", 1),), reach)[0]
+    local_columns, extended, deriv = lax.optimization_barrier((local_columns, extended, deriv))
     grad_act = jnp.zeros((length, in_width), jnp.float32)
     for tap_index in range(KW):
         window_start = (2 * middle_offset - tap_index) * TAP_SPACING

time: 67 us -> 64.9 us (0.969)
  local copies, waits for them, and re-layouts: 12.6 us -> 9.5 us
  waiting for transfers between devices: 10.9 us -> 12.2 us
    unnamed x12 -> x16, local copies, waits for them, and re-layouts: 6.01 us -> 3.61 us
    ppermute x4, waiting for transfers between devices: 10.9 us -> 12.2 us  [send(): arrived = lax.ppermute(encode(values, exponent), 'batch', perm)]
    convert_element_type x1, other arithmetic: 1.02 us -> 0.09 us  [body(): act = activation.astype(jnp.bfloat16)]
    squeeze x0 -> x1, other arithmetic: none -> 0.77 us  [body(): extended = extended_2(halo_source, (('seq', 1),), reach)[0]]
    slice x1, local copies, waits for them, and re-layouts: 1.85 us -> 1.09 us  [decode(): values = packed[:-TAG].astype(jnp.float32) * jnp.exp2(exponent - HEADROOM)]
  transfers between devices with their start and end apart: 7 -> 7, of which waited for: 2 -> 2; matrix products, arithmetic and copies ran while one was open for 27% -> 16% of each run, Pallas kernels for 0% -> 0%
where the time goes in v16:
time: 64.9 us; the launch traced here: 64.3 us
  starting transfers between devices  17.4 us (27%)
  waiting for transfers between devices  12.2 us (19%)
  local copies, waits for them, and re-layouts  9.5 us (15%)
  blocking collectives  9.08 us (14%)
  matrix products  7.58 us (12%)
  between operations  5.08 us (8%)
  other arithmetic  3.45 us (5%)
    ppermute x4, waiting for transfers between devices, send(): arrived = lax.ppermute(encode(values, exponent), 'batch', perm)  12.2 us
    all_gather x1, blocking collectives, body(): whole_act = lax.all_gather(act[None], 'seq', axis=1, tiled=True)[0]  9.08 us
    ppermute x4, starting transfers between devices, send(): arrived = lax.ppermute(encode(values, exponent), 'batch', perm)  8.84 us
    dot_general x3, matrix products, body(): jnp.dot(window, weight[:, tap_index * in_width:(tap_index + 1) * in_width...  6.37 us
    all_to_all x1, starting transfers between devices, body(): arrived = lax.all_to_all(channels, 'seq', 0, 0, tiled=True)  4.24 us
    unnamed x16, local copies, waits for them, and re-layouts  3.61 us
    ppermute x1, starting transfers between devices, extended_2(): before = lax.ppermute(last, axis, up)  3.05 us
    slice x4, local copies, waits for them, and re-layouts, decode(): exponent = packed[-TAG:1 - TAG, 0:1].astype(jnp.float32)  2.83 us
  transfers between devices with their start and end apart: 7, of which 2 were waited for; matrix products, arithmetic and copies ran while one was open for 16% of the time, Pallas kernels for 0%

profile of v16, /device:TPU:0, one launch (start us, length us, event | category | flops | bytes accessed | tf_op | source)
XLA Modules:
  0.0 64.3 jit_solution(5097522370744356640)
XLA Ops:
  0.6 1.8 %copy.19 = bf16[1,128,768]{1,2,0:T(8,128)(2,1)} copy(bf16[1,128,768]{2,1,0:T(8,128)(2,1)} %param.4) | data formatting | bytes 393216 | tf_op args[1]
  2.4 4.2 %all-to-all-start = ((bf16[4,192,128]{2,1,0:T(8,128)(2,1)}), bf16[4,192,128]{2,1,0:T(8,128)(2,1)S(1)}, u32[]{:S(2)}, u32[]{:S(2)}) async-start(bf16[4,192,128]{2,1,0:T(8,128)(2,1)} %bitcast.3), calls=%async_computation | async-start | bytes 393216 | tf_op jit(solution)/shard_map/all_to_all | solution.py:93
  6.7 1.0 %fusion.47 = (bf16[1,64,768]{2,1,0:T(8,128)(2,1)S(1)}, bf16[1,64,768]{2,1,0:T(8,128)(2,1)S(1)}) fusion(bf16[1,128,768]{2,1,0:T(8,128)(2,1)} %param.4), kind=kLoop, calls=%fused_computation.62 | loop fusion | bytes 393216 | tf_op jit(solution)/shard_map/slice | solution.py:20
  7.7 1.3 %collective-permute-start.1 = (bf16[1,64,768]{2,1,0:T(8,128)(2,1)S(1)}, bf16[1,64,768]{2,1,0:T(8,128)(2,1)S(1)}, u32[]{:S(2)}, u32[]{:S(2)}) collective-permute-start(bf16[1,64,768]{2,1,0:T(8,128)(2,1)S(1)} %get-tuple-element.20), channel_id=1, source_target_pairs={{8,0},{16,8},{24,16},{9,1},{17,9},{25,17},{10,2},{18,10},{26,18},{... | collective-permute-start | bytes 294920 | tf_op jit(solution)/shard_map/ppermute | solution.py:23
  9.0 3.0 %collective-permute-start = (bf16[1,64,768]{2,1,0:T(8,128)(2,1)S(1)}, bf16[1,64,768]{2,1,0:T(8,128)(2,1)S(1)}, u32[]{:S(2)}, u32[]{:S(2)}) collective-permute-start(bf16[1,64,768]{2,1,0:T(8,128)(2,1)S(1)} %get-tuple-element.19), channel_id=1, source_target_pairs={{0,8},{8,16},{16,24},{1,9},{9,17},{17,25},{2,10},{10,18},{18,26},{... | collective-permute-start | bytes 294920 | tf_op jit(solution)/shard_map/ppermute | solution.py:22
  12.1 9.1 %all_gather.3 = bf16[1,512,768]{2,1,0:T(8,128)(2,1)S(1)} all-gather(bf16[1,128,768]{2,1,0:T(8,128)(2,1)S(1)} %fusion.25), channel_id=1, replica_groups=mesh['seq'=4,'batch'=8] {'seq'}, dimensions={1}, use_global_device_ids=true | all-gather | bytes 983040 | tf_op jit(solution)/shard_map/all_gather | solution.py:96
  21.2 0.9 %fusion.21 = f32[128,768]{1,0:T(8,128)} fusion(bf16[1,128,768]{2,1,0:T(8,128)(2,1)S(1)} %copy-done.5), kind=kLoop, calls=%fused_computation.31 | loop fusion | flops 884736 | bytes 589824 | tf_op jit(solution)/shard_map/add | solution.py:31
  22.1 0.8 %maximum_bitcast_fusion = bf16[256,768]{1,0:T(8,128)(2,1)} fusion(bf16[1,64,768]{2,1,0:T(8,128)(2,1)S(1)} %collective-permute-done.1, bf16[1,128,768]{2,1,0:T(8,128)(2,1)S(1)} %copy-done, bf16[1,64,768]{2,1,0:T(8,128)(2,1)S(1)} %collective-permute-done), kind=kLoop, calls=%fused_computation.38 | loop fusion | flops 1179648 | bytes 786432 | tf_op jit(solution)/shard_map/squeeze | solution.py:109
  22.9 0.4 fusion.32
  23.3 0.4 fusion.15
  23.7 0.4 fusion.14
  24.1 0.2 maximum_multiply_fusion
  24.3 0.9 %fusion.1 = (f32[]{:T(128)}, f32[]{:T(128)}) fusion(f32[4,2,288,192]{3,2,1,0:T(8,128)S(1)} %bitcast.95, s32[]{:T(128)S(6)} %select_n.44, s32[]{:T(128)S(6)} %select_n.45), kind=kLoop, calls=%fused_computation.6 | loop fusion | flops 884734 | bytes 1769488 | tf_op jit(solution)/shard_map/reduce_max | solution.py:36
  26.1 0.4 copy.36
  26.5 0.9 %concatenate.20.clone = f16[1168,192]{0,1:T(8,128)(2,1)} pad(f16[1152,192]{0,1:T(8,128)(2,1)S(1)} %copy.36, f16[]{:T(256)S(6)} %convert_element_type.98), padding=0_16x0_0 | pad | bytes 890882 | tf_op jit(solution)/shard_map/concatenate | solution.py:44
  27.4 2.0 %collective-permute-start.2 = (f16[1168,192]{0,1:T(8,128)(2,1)}, f16[1168,192]{0,1:T(8,128)(2,1)}, u32[]{:S(2)}, u32[]{:S(2)}) collective-permute-start(f16[1168,192]{0,1:T(8,128)(2,1)} %concatenate.20.clone), channel_id=1, source_target_pairs={{0,1},{1,0},{2,3},{3,2},{4,5},{5,4},{6,7},{7,6},{8,9},{9,8},{10,11... | collective-permute-start | bytes 1345544 | tf_op jit(solution)/shard_map/ppermute | solution.py:54
  30.1 1.7 %fusion.6 = f32[128,768]{1,0:T(8,128)S(1)} fusion(bf16[768,2304]{1,0:T(8,128)(2,1)} %param.5, bf16[256,768]{1,0:T(8,128)(2,1)} %maximum_bitcast_fusion), kind=kOutput, calls=%fused_computation.14 | convolution fusion | flops 150994944 | bytes 1769472 | tf_op jit(solution)/shard_map/dot_general | solution.py:115
  31.8 2.4 %convolution_add_fusion.1 = f32[128,768]{1,0:T(8,128)} fusion(f32[128,768]{1,0:T(8,128)S(1)} %fusion.6, bf16[768,2304]{1,0:T(8,128)(2,1)} %param.5, bf16[256,768]{1,0:T(8,128)(2,1)S(1)} %copy-done.2), kind=kOutput, calls=%fused_computation.2 | convolution fusion | flops 151093248 | bytes 2162688 | tf_op jit(solution)/shard_map/dot_general | solution.py:115
  34.2 7.1 %collective-permute-done.2 = f16[1168,192]{0,1:T(8,128)(2,1)} collective-permute-done((f16[1168,192]{0,1:T(8,128)(2,1)}, f16[1168,192]{0,1:T(8,128)(2,1)}, u32[]{:S(2)}, u32[]{:S(2)}) %collective-permute-start.2) | collective-permute-done | bytes 448544 | tf_op jit(solution)/shard_map/ppermute | solution.py:54
  41.3 1.1 %slice.73 = f16[1152,192]{0,1:T(8,128)(2,1)S(1)} slice(f16[1168,192]{0,1:T(8,128)(2,1)} %collective-permute-done.2), slice={[0:1152], [0:192]} | slice | bytes 884736 | tf_op jit(solution)/shard_map/slice | solution.py:49
  42.4 0.5 copy.34
  42.9 1.2 %slice.74 = f16[1,1]{0,1:T(2,128)(2,1)} slice(f16[1168,192]{0,1:T(8,128)(2,1)} %collective-permute-done.2), slice={[1152:1153], [0:1]} | slice | bytes 4 | tf_op jit(solution)/shard_map/slice | solution.py:48
  44.9 0.2 bitcast_add_fusion
  45.3 2.9 %collective-permute-start.5 = (f16[304,192]{1,0:T(8,128)(2,1)S(1)}, f16[304,192]{1,0:T(8,128)(2,1)S(1)}, u32[]{:S(2)}, u32[]{:S(2)}) collective-permute-start(f16[304,192]{1,0:T(8,128)(2,1)S(1)} %concatenate.23), channel_id=1, source_target_pairs={{0,4},{1,5},{2,6},{3,7},{4,0},{5,1},{6,2},{7,3},{8,12},{9,13},{10,... | collective-permute-start | bytes 350216 | tf_op jit(solution)/shard_map/ppermute | solution.py:54
  48.2 1.6 %collective-permute-start.4 = (f16[304,192]{1,0:T(8,128)(2,1)S(1)}, f16[304,192]{1,0:T(8,128)(2,1)S(1)}, u32[]{:S(2)}, u32[]{:S(2)}) collective-permute-start(f16[304,192]{1,0:T(8,128)(2,1)S(1)} %concatenate.22), channel_id=1, source_target_pairs={{0,2},{1,3},{2,4},{3,5},{4,6},{5,7},{6,0},{7,1},{8,10},{9,11},{10,... | collective-permute-start | bytes 350216 | tf_op jit(solution)/shard_map/ppermute | solution.py:54
  49.9 2.3 %collective-permute-start.3 = (f16[304,192]{1,0:T(8,128)(2,1)S(1)}, f16[304,192]{1,0:T(8,128)(2,1)S(1)}, u32[]{:S(2)}, u32[]{:S(2)}) collective-permute-start(f16[304,192]{1,0:T(8,128)(2,1)S(1)} %concatenate.21), channel_id=1, source_target_pairs={{0,6},{1,7},{2,0},{3,1},{4,2},{5,3},{6,4},{7,5},{8,14},{9,15},{10,... | collective-permute-start | bytes 350216 | tf_op jit(solution)/shard_map/ppermute | solution.py:54
  52.2 2.3 %fusion.11 = bf16[1,128,768]{2,1,0:T(8,128)(2,1)} fusion(f32[128,768]{1,0:T(8,128)S(1)} %copy-done.1, f32[128,768]{1,0:T(8,128)S(1)} %copy-done.4, bf16[768,2304]{1,0:T(8,128)(2,1)} %param.5, bf16[256,768]{1,0:T(8,128)(2,1)S(1)} %copy-done.3), kind=kOutput, calls=%fused_computation.17 | convolution fusion | flops 151289856 | bytes 2359296 | tf_op jit(solution)/shard_map/dot_general | solution.py:115
  54.5 5.1 %collective-permute-done.5 = f16[304,192]{1,0:T(8,128)(2,1)S(1)} collective-permute-done((f16[304,192]{1,0:T(8,128)(2,1)S(1)}, f16[304,192]{1,0:T(8,128)(2,1)S(1)}, u32[]{:S(2)}, u32[]{:S(2)}) %collective-permute-start.5) | collective-permute-done | bytes 116768 | tf_op jit(solution)/shard_map/ppermute | solution.py:54
  59.6 0.5 slice.80
  60.8 0.6 slice.78
  62.1 0.5 slice.76
  63.4 0.9 %copy.28 = f32[192,288]{1,0:T(8,128)} copy(f32[192,288]{0,1:T(8,128)S(1)} %fusion.30) | data formatting | bytes 442368
  (25 shorter events, 0.7 us)
Async XLA Ops:
  0.6 11.4 %copy-start.5 = (bf16[1,128,768]{2,1,0:T(8,128)(2,1)S(1)}, bf16[1,128,768]{2,1,0:T(8,128)(2,1)}, u32[]{:S(2)}) copy-start(bf16[1,128,768]{2,1,0:T(8,128)(2,1)} %param.3) | copy-start | bytes 589828
  2.4 20.5 %all-to-all-start = ((bf16[4,192,128]{2,1,0:T(8,128)(2,1)}), bf16[4,192,128]{2,1,0:T(8,128)(2,1)S(1)}, u32[]{:S(2)}, u32[]{:S(2)}) async-start(bf16[4,192,128]{2,1,0:T(8,128)(2,1)} %bitcast.3), calls=%async_computation | async-start | bytes 393216 | tf_op jit(solution)/shard_map/all_to_all | solution.py:93
  6.7 15.5 %copy-start = (bf16[1,128,768]{2,1,0:T(8,128)(2,1)S(1)}, bf16[1,128,768]{2,1,0:T(8,128)(2,1)}, u32[]{:S(2)}) copy-start(bf16[1,128,768]{2,1,0:T(8,128)(2,1)} %param.4) | copy-start | bytes 589828
  7.7 14.5 %collective-permute-start.1 = (bf16[1,64,768]{2,1,0:T(8,128)(2,1)S(1)}, bf16[1,64,768]{2,1,0:T(8,128)(2,1)S(1)}, u32[]{:S(2)}, u32[]{:S(2)}) collective-permute-start(bf16[1,64,768]{2,1,0:T(8,128)(2,1)S(1)} %get-tuple-element.20), channel_id=1, source_target_pairs={{8,0},{16,8},{24,16},{9,1},{17,9},{25,17},{10,2},{18,10},{26,18},{... | collective-permute-start | bytes 294920 | tf_op jit(solution)/shard_map/ppermute | solution.py:23
  9.0 13.2 %collective-permute-start = (bf16[1,64,768]{2,1,0:T(8,128)(2,1)S(1)}, bf16[1,64,768]{2,1,0:T(8,128)(2,1)S(1)}, u32[]{:S(2)}, u32[]{:S(2)}) collective-permute-start(bf16[1,64,768]{2,1,0:T(8,128)(2,1)S(1)} %get-tuple-element.19), channel_id=1, source_target_pairs={{0,8},{8,16},{16,24},{1,9},{9,17},{17,25},{2,10},{10,18},{18,26},{... | collective-permute-start | bytes 294920 | tf_op jit(solution)/shard_map/ppermute | solution.py:22
  26.5 5.3 %copy-start.2 = (bf16[256,768]{1,0:T(8,128)(2,1)S(1)}, bf16[256,768]{1,0:T(8,128)(2,1)}, u32[]{:S(2)}) copy-start(bf16[256,768]{1,0:T(8,128)(2,1)} %maximum_bitcast_fusion) | copy-start | bytes 1179652
  27.4 13.9 %collective-permute-start.2 = (f16[1168,192]{0,1:T(8,128)(2,1)}, f16[1168,192]{0,1:T(8,128)(2,1)}, u32[]{:S(2)}, u32[]{:S(2)}) collective-permute-start(f16[1168,192]{0,1:T(8,128)(2,1)} %concatenate.20.clone), channel_id=1, source_target_pairs={{0,1},{1,0},{2,3},{3,2},{4,5},{5,4},{6,7},{7,6},{8,9},{9,8},{10,11... | collective-permute-start | bytes 1345544 | tf_op jit(solution)/shard_map/ppermute | solution.py:54
  45.0 7.2 %copy-start.1 = (f32[128,768]{1,0:T(8,128)S(1)}, f32[128,768]{1,0:T(8,128)}, u32[]{:S(2)}) copy-start(f32[128,768]{1,0:T(8,128)} %fusion.21) | copy-start | bytes 1179652
  45.0 7.2 %copy-start.3 = (bf16[256,768]{1,0:T(8,128)(2,1)S(1)}, bf16[256,768]{1,0:T(8,128)(2,1)}, u32[]{:S(2)}) copy-start(bf16[256,768]{1,0:T(8,128)(2,1)} %maximum_bitcast_fusion) | copy-start | bytes 1179652
  45.0 7.1 %copy-start.4 = (f32[128,768]{1,0:T(8,128)S(1)}, f32[128,768]{1,0:T(8,128)}, u32[]{:S(2)}) copy-start(f32[128,768]{1,0:T(8,128)} %convolution_add_fusion.1) | copy-start | bytes 1179652
  45.3 14.3 %collective-permute-start.5 = (f16[304,192]{1,0:T(8,128)(2,1)S(1)}, f16[304,192]{1,0:T(8,128)(2,1)S(1)}, u32[]{:S(2)}, u32[]{:S(2)}) collective-permute-start(f16[304,192]{1,0:T(8,128)(2,1)S(1)} %concatenate.23), channel_id=1, source_target_pairs={{0,4},{1,5},{2,6},{3,7},{4,0},{5,1},{6,2},{7,3},{8,12},{9,13},{10,... | collective-permute-start | bytes 350216 | tf_op jit(solution)/shard_map/ppermute | solution.py:54
  48.2 12.6 %collective-permute-start.4 = (f16[304,192]{1,0:T(8,128)(2,1)S(1)}, f16[304,192]{1,0:T(8,128)(2,1)S(1)}, u32[]{:S(2)}, u32[]{:S(2)}) collective-permute-start(f16[304,192]{1,0:T(8,128)(2,1)S(1)} %concatenate.22), channel_id=1, source_target_pairs={{0,2},{1,3},{2,4},{3,5},{4,6},{5,7},{6,0},{7,1},{8,10},{9,11},{10,... | collective-permute-start | bytes 350216 | tf_op jit(solution)/shard_map/ppermute | solution.py:54
  49.9 12.2 %collective-permute-start.3 = (f16[304,192]{1,0:T(8,128)(2,1)S(1)}, f16[304,192]{1,0:T(8,128)(2,1)S(1)}, u32[]{:S(2)}, u32[]{:S(2)}) collective-permute-start(f16[304,192]{1,0:T(8,128)(2,1)S(1)} %concatenate.21), channel_id=1, source_target_pairs={{0,6},{1,7},{2,0},{3,1},{4,2},{5,3},{6,4},{7,5},{8,14},{9,15},{10,... | collective-permute-start | bytes 350216 | tf_op jit(solution)/shard_map/ppermute | solution.py:54

commit v17 on v15

--- a/solution.py
+++ b/solution.py
@@ -75,6 +75,21 @@
     return with_layout_constraint(total, Layout((0, 1))).T
 
 
+def gather_over_seq(block):
+    count = lax.axis_size("seq")
+    me = lax.axis_index("seq")
+    bits = count.bit_length() - 1
+    if count != 1 << bits:
+        return lax.all_gather(block[None], "seq", axis=1, tiled=True)[0]
+    stack = block[None]
+    for bit in reversed(range(bits)):
+        pairs = [(i, i ^ (1 << bit)) for i in range(count)]
+        stack = jnp.concatenate([stack, lax.ppermute(stack, "seq", pairs)], axis=0)
+    reverse = jnp.array([int(format(v, "0%db" % bits)[::-1], 2) for v in range(count)], jnp.int32)
+    order = reverse[jnp.bitwise_xor(me, jnp.arange(count, dtype=jnp.int32))]
+    return jnp.take(stack, order, axis=0).reshape(-1, block.shape[-1])
+
+
 def body(inputs, cotangent, weight):
     middle_offset = KW // 2
     reach = middle_offset * TAP_SPACING
@@ -92,7 +107,7 @@
     arrived = lax.all_to_all(channels, "seq", 0, 0, tiled=True)
     own_rows = arrived.shape[1]
     owned = jnp.transpose(arrived, (1, 0, 2)).reshape(own_rows, -1)
-    whole_act = lax.all_gather(act[None], "seq", axis=1, tiled=True)[0]
+    whole_act = gather_over_seq(act)
     count = whole_act.shape[0]
     act_padded = jnp.pad(whole_act, ((reach, reach), (0, 0)))
     updated = []

time: 64.9 us -> 62.2 us (0.958)
  blocking collectives: 9.08 us -> 0 us
  starting transfers between devices: 17.5 us -> 20.6 us
  other arithmetic: 4.04 us -> 5.35 us
  waiting for transfers between devices: 12.6 us -> 13.9 us
    all_gather x1 -> x0, blocking collectives: 9.08 us -> none  [body(): whole_act = lax.all_gather(act[None], 'seq', axis=1, tiled=True)[0]]
    ppermute x0 -> x2, starting transfers between devices: none -> 4.79 us  [gather_over_seq(): stack = jnp.concatenate([stack, lax.ppermute(stack, 'seq', pairs)], axis=0)]
    unnamed x18 -> x17, local copies, waits for them, and re-layouts: 4.4 us -> 1.84 us
    transpose x0 -> x1, local copies, waits for them, and re-layouts: none -> 1.74 us  [body(): channels = cotangent[0].T.reshape(seq_count, -1, length)]
    gather x0 -> x2, local copies, waits for them, and re-layouts: none -> 1.24 us  [the longest x1 0.64 us: gather_over_seq(): order = reverse[jnp.bitwise_xor(me, jnp.arange(count, dtype=jnp.int32))]]
    slice x1, local copies, waits for them, and re-layouts: 0.08 us -> 1.09 us  [decode(): values = packed[:-TAG].astype(jnp.float32) * jnp.exp2(exponent - HEADROOM)]
    convert_element_type x1, other arithmetic: 0.09 us -> 1.08 us  [body(): act = activation.astype(jnp.bfloat16)]
    slice x1, local copies, waits for them, and re-layouts: 0.99 us -> 0.02 us  [extended_2(): last = lax.slice_in_dim(x, length - width, length, axis=dim)]
  transfers between devices with their start and end apart: 7 -> 9, of which waited for: 2 -> 3; matrix products, arithmetic and copies ran while one was open for 16% -> 20% of each run, Pallas kernels for 0% -> 0%
where the time goes in v17:
time: 62.2 us; the launch traced here: 61.7 us
  starting transfers between devices  20.6 us (33%)
  waiting for transfers between devices  13.9 us (22%)
  local copies, waits for them, and re-layouts  9.01 us (14%)
  matrix products  7.64 us (12%)
  other arithmetic  5.35 us (9%)
  between operations  5.24 us (8%)
    ppermute x4, waiting for transfers between devices, send(): arrived = lax.ppermute(encode(values, exponent), 'batch', perm)  13.4 us
    ppermute x4, starting transfers between devices, send(): arrived = lax.ppermute(encode(values, exponent), 'batch', perm)  8.15 us
    dot_general x3, matrix products, body(): jnp.dot(window, weight[:, tap_index * in_width:(tap_index + 1) * in_width...  6.33 us
    ppermute x2, starting transfers between devices, gather_over_seq(): stack = jnp.concatenate([stack, lax.ppermute(stack, 'seq', pairs)], axis=0)  4.79 us
    all_to_all x1, starting transfers between devices, body(): arrived = lax.all_to_all(channels, 'seq', 0, 0, tiled=True)  3.37 us
    ppermute x1, starting transfers between devices, extended_2(): before = lax.ppermute(last, axis, up)  3.04 us
    slice x4, local copies, waits for them, and re-layouts, decode(): exponent = packed[-TAG:1 - TAG, 0:1].astype(jnp.float32)  2.83 us
    unnamed x17, local copies, waits for them, and re-layouts  1.84 us
  transfers between devices with their start and end apart: 9, of which 3 were waited for; matrix products, arithmetic and copies ran while one was open for 20% of the time, Pallas kernels for 0%

profile of v17, /device:TPU:0, one launch (start us, length us, event | category | flops | bytes accessed | tf_op | source)
XLA Modules:
  0.0 61.7 jit_solution(13733553358274662568)
XLA Ops:
  0.7 1.1 %fusion.26 = bf16[1,128,768]{2,1,0:T(8,128)(2,1)S(1)} fusion(bf16[1,128,768]{2,1,0:T(8,128)(2,1)} %param.4), kind=kLoop, calls=%fused_computation.41 | loop fusion | flops 589824 | bytes 393216 | tf_op jit(solution)/shard_map/convert_element_type | solution.py:101
  1.7 3.0 %collective-permute-start = (bf16[1,128,768]{2,1,0:T(8,128)(2,1)S(1)}, bf16[1,128,768]{2,1,0:T(8,128)(2,1)S(1)}, u32[]{:S(2)}, u32[]{:S(2)}) collective-permute-start(bf16[1,128,768]{2,1,0:T(8,128)(2,1)S(1)} %fusion.26), channel_id=1, source_target_pairs={{0,16},{8,24},{16,0},{24,8},{1,17},{9,25},{17,1},{25,9},{2,18},{10... | collective-permute-start | bytes 589832 | tf_op jit(solution)/shard_map/ppermute | solution.py:87
  4.8 1.7 %copy.21 = bf16[768,128]{1,0:T(8,128)(2,1)} copy(bf16[768,128]{0,1:T(8,128)(2,1)} %bitcast.100) | data formatting | bytes 393216 | tf_op jit(solution)/shard_map/transpose | solution.py:106
  6.5 3.4 %all-to-all-start = ((bf16[4,192,128]{2,1,0:T(8,128)(2,1)}), bf16[4,192,128]{2,1,0:T(8,128)(2,1)S(1)}, u32[]{:S(2)}, u32[]{:S(2)}) async-start(bf16[4,192,128]{2,1,0:T(8,128)(2,1)} %bitcast.7), calls=%async_computation | async-start | bytes 393216 | tf_op jit(solution)/shard_map/all_to_all | solution.py:107
  9.9 1.3 %collective-permute-start.3 = (bf16[1,64,768]{2,1,0:T(8,128)(2,1)S(1)}, bf16[1,64,768]{2,1,0:T(8,128)(2,1)S(1)}, u32[]{:S(2)}, u32[]{:S(2)}) collective-permute-start(bf16[1,64,768]{2,1,0:T(8,128)(2,1)S(1)} %get-tuple-element.20), channel_id=1, source_target_pairs={{8,0},{16,8},{24,16},{9,1},{17,9},{25,17},{10,2},{18,10},{26,18},{... | collective-permute-start | bytes 294920 | tf_op jit(solution)/shard_map/ppermute | solution.py:23
  11.2 3.0 %collective-permute-start.2 = (bf16[1,64,768]{2,1,0:T(8,128)(2,1)S(1)}, bf16[1,64,768]{2,1,0:T(8,128)(2,1)S(1)}, u32[]{:S(2)}, u32[]{:S(2)}) collective-permute-start(bf16[1,64,768]{2,1,0:T(8,128)(2,1)S(1)} %get-tuple-element.19), channel_id=1, source_target_pairs={{0,8},{8,16},{16,24},{1,9},{9,17},{17,25},{2,10},{10,18},{18,26},{... | collective-permute-start | bytes 294920 | tf_op jit(solution)/shard_map/ppermute | solution.py:22
  14.3 0.9 %fusion.22 = f32[128,768]{1,0:T(8,128)} fusion(bf16[1,128,768]{2,1,0:T(8,128)(2,1)S(1)} %copy-done.6), kind=kLoop, calls=%fused_computation.37 | loop fusion | flops 884736 | bytes 589824 | tf_op jit(solution)/shard_map/add | solution.py:31
  15.2 0.6 %gather_fusion = s32[4]{0:T(128)S(1)} fusion(s32[4]{0:T(128)S(1)} %copy-done, s32[1024]{0:T(1024)S(1)} %pad_clamp_fusion.1), kind=kCustom, calls=%fused_computation | custom fusion | bytes 48 | tf_op jit(solution)/shard_map/gather | solution.py:89
  15.9 1.8 %collective-permute-start.1 = (bf16[2,128,768]{2,1,0:T(8,128)(2,1)S(1)}, bf16[2,128,768]{2,1,0:T(8,128)(2,1)S(1)}, u32[]{:S(2)}, u32[]{:S(2)}) collective-permute-start(bf16[2,128,768]{2,1,0:T(8,128)(2,1)S(1)} %pad_maximum_fusion.1), channel_id=1, source_target_pairs={{0,8},{8,0},{16,24},{24,16},{1,9},{9,1},{17,25},{25,17},{2,10},{10... | collective-permute-start | bytes 1179656 | tf_op jit(solution)/shard_map/ppermute | solution.py:87
  17.8 0.8 %maximum_bitcast_fusion = bf16[256,768]{1,0:T(8,128)(2,1)} fusion(bf16[1,64,768]{2,1,0:T(8,128)(2,1)S(1)} %collective-permute-done.3, bf16[1,128,768]{2,1,0:T(8,128)(2,1)S(1)} %copy-done.1, bf16[1,64,768]{2,1,0:T(8,128)(2,1)S(1)} %collective-permute-done.2), kind=kLoop, calls=%fused_computation.45 | loop fusion | flops 1179648 | bytes 786432 | tf_op jit(solution)/shard_map/squeeze | solution.py:123
  18.6 0.5 collective-permute-done.1
  19.1 0.6 gather_fusion.1
  19.9 0.5 convolution_bitcast_fusion
  21.4 0.8 %fusion.1 = f32[]{:T(128)} fusion(f32[4,2,288,192]{3,2,1,0:T(8,128)S(1)} %bitcast.95, s32[]{:T(128)S(6)} %select_n.83), kind=kLoop, calls=%fused_computation.10 | loop fusion | flops 442367 | bytes 884744 | tf_op jit(solution)/shard_map/reduce_max | solution.py:36
  23.1 0.4 copy.39
  23.6 1.6 %collective-permute-start.4 = (f16[1168,192]{0,1:T(8,128)(2,1)S(1)}, f16[1168,192]{0,1:T(8,128)(2,1)}, u32[]{:S(2)}, u32[]{:S(2)}) collective-permute-start(f16[1168,192]{0,1:T(8,128)(2,1)S(1)} %concatenate.29.clone), channel_id=1, source_target_pairs={{0,1},{1,0},{2,3},{3,2},{4,5},{5,4},{6,7},{7,6},{8,9},{9,8},{10,11... | collective-permute-start | bytes 1345544 | tf_op jit(solution)/shard_map/ppermute | solution.py:54
  25.2 1.7 %fusion.5 = f32[128,768]{1,0:T(8,128)S(1)} fusion(bf16[768,2304]{1,0:T(8,128)(2,1)} %param.6, bf16[256,768]{1,0:T(8,128)(2,1)} %maximum_bitcast_fusion), kind=kOutput, calls=%fused_computation.16 | convolution fusion | flops 150994944 | bytes 1769472 | tf_op jit(solution)/shard_map/dot_general | solution.py:129
  26.9 2.3 %convolution_add_fusion.1 = f32[128,768]{1,0:T(8,128)} fusion(f32[128,768]{1,0:T(8,128)S(1)} %fusion.5, bf16[768,2304]{1,0:T(8,128)(2,1)} %param.6, bf16[256,768]{1,0:T(8,128)(2,1)S(1)} %copy-done.3), kind=kOutput, calls=%fused_computation.5 | convolution fusion | flops 151093248 | bytes 2162688 | tf_op jit(solution)/shard_map/dot_general | solution.py:129
  29.3 8.0 %collective-permute-done.4 = f16[1168,192]{0,1:T(8,128)(2,1)} collective-permute-done((f16[1168,192]{0,1:T(8,128)(2,1)S(1)}, f16[1168,192]{0,1:T(8,128)(2,1)}, u32[]{:S(2)}, u32[]{:S(2)}) %collective-permute-start.4) | collective-permute-done | bytes 448544 | tf_op jit(solution)/shard_map/ppermute | solution.py:54
  37.3 1.1 %slice.77 = f16[1152,192]{0,1:T(8,128)(2,1)S(1)} slice(f16[1168,192]{0,1:T(8,128)(2,1)} %collective-permute-done.4), slice={[0:1152], [0:192]} | slice | bytes 884736 | tf_op jit(solution)/shard_map/slice | solution.py:49
  38.4 0.5 copy.37
  38.9 1.2 %slice.78 = f16[1,1]{0,1:T(2,128)(2,1)} slice(f16[1168,192]{0,1:T(8,128)(2,1)} %collective-permute-done.4), slice={[1152:1153], [0:1]} | slice | bytes 4 | tf_op jit(solution)/shard_map/slice | solution.py:48
  40.9 0.8 %abs_reduce_fusion = (f32[]{:T(128)}, f32[4,288,192]{2,1,0:T(8,128)S(1)}) fusion(f32[4,288,192]{2,1,0:T(8,128)S(1)} %bitcast.98, f32[4,2,288,192]{3,2,1,0:T(8,128)S(1)} %bitcast.97, s32[]{:T(128)S(6)} %select_n.82), kind=kLoop, calls=%fused_computation.12 | loop fusion | flops 663551 | bytes 2654216 | tf_op jit(solution)/shard_map/reduce_max | solution.py:36
  42.7 2.7 %collective-permute-start.7 = (f16[304,192]{1,0:T(8,128)(2,1)S(1)}, f16[304,192]{1,0:T(8,128)(2,1)S(1)}, u32[]{:S(2)}, u32[]{:S(2)}) collective-permute-start(f16[304,192]{1,0:T(8,128)(2,1)S(1)} %concatenate.32), channel_id=1, source_target_pairs={{0,4},{1,5},{2,6},{3,7},{4,0},{5,1},{6,2},{7,3},{8,12},{9,13},{10,... | collective-permute-start | bytes 350216 | tf_op jit(solution)/shard_map/ppermute | solution.py:54
  45.4 1.6 %collective-permute-start.6 = (f16[304,192]{1,0:T(8,128)(2,1)S(1)}, f16[304,192]{1,0:T(8,128)(2,1)S(1)}, u32[]{:S(2)}, u32[]{:S(2)}) collective-permute-start(f16[304,192]{1,0:T(8,128)(2,1)S(1)} %concatenate.31), channel_id=1, source_target_pairs={{0,2},{1,3},{2,4},{3,5},{4,6},{5,7},{6,0},{7,1},{8,10},{9,11},{10,... | collective-permute-start | bytes 350216 | tf_op jit(solution)/shard_map/ppermute | solution.py:54
  47.1 2.3 %collective-permute-start.5 = (f16[304,192]{1,0:T(8,128)(2,1)S(1)}, f16[304,192]{1,0:T(8,128)(2,1)S(1)}, u32[]{:S(2)}, u32[]{:S(2)}) collective-permute-start(f16[304,192]{1,0:T(8,128)(2,1)S(1)} %concatenate.30), channel_id=1, source_target_pairs={{0,6},{1,7},{2,0},{3,1},{4,2},{5,3},{6,4},{7,5},{8,14},{9,15},{10,... | collective-permute-start | bytes 350216 | tf_op jit(solution)/shard_map/ppermute | solution.py:54
  49.4 2.3 %fusion.10 = bf16[1,128,768]{2,1,0:T(8,128)(2,1)} fusion(f32[128,768]{1,0:T(8,128)S(1)} %copy-done.2, f32[128,768]{1,0:T(8,128)S(1)} %copy-done.5, bf16[768,2304]{1,0:T(8,128)(2,1)} %param.6, bf16[256,768]{1,0:T(8,128)(2,1)S(1)} %copy-done.4), kind=kOutput, calls=%fused_computation.19 | convolution fusion | flops 151289856 | bytes 2359296 | tf_op jit(solution)/shard_map/dot_general | solution.py:129
  51.7 5.4 %collective-permute-done.7 = f16[304,192]{1,0:T(8,128)(2,1)S(1)} collective-permute-done((f16[304,192]{1,0:T(8,128)(2,1)S(1)}, f16[304,192]{1,0:T(8,128)(2,1)S(1)}, u32[]{:S(2)}, u32[]{:S(2)}) %collective-permute-start.7) | collective-permute-done | bytes 116768 | tf_op jit(solution)/shard_map/ppermute | solution.py:54
  57.0 0.5 slice.84
  58.3 0.5 slice.82
  59.5 0.6 slice.80
  60.9 0.9 %copy.30 = f32[192,288]{1,0:T(8,128)} copy(f32[192,288]{0,1:T(8,128)S(1)} %fusion.32) | data formatting | bytes 442368
  (41 shorter events, 2.1 us)
Async XLA Ops:
  0.6 14.6 %copy-start = (s32[4]{0:T(128)S(1)}, s32[4]{0:T(128)}, u32[]{:S(2)}) copy-start(s32[4]{0:T(128)} %constant.122.clone) | copy-start | bytes 52
  0.6 13.6 %copy-start.6 = (bf16[1,128,768]{2,1,0:T(8,128)(2,1)S(1)}, bf16[1,128,768]{2,1,0:T(8,128)(2,1)}, u32[]{:S(2)}) copy-start(bf16[1,128,768]{2,1,0:T(8,128)(2,1)} %param.4) | copy-start | bytes 589828
  0.7 9.2 %copy-start.1 = (bf16[1,128,768]{2,1,0:T(8,128)(2,1)S(1)}, bf16[1,128,768]{2,1,0:T(8,128)(2,1)}, u32[]{:S(2)}) copy-start(bf16[1,128,768]{2,1,0:T(8,128)(2,1)} %param.5) | copy-start | bytes 589828
  1.7 14.1 %collective-permute-start = (bf16[1,128,768]{2,1,0:T(8,128)(2,1)S(1)}, bf16[1,128,768]{2,1,0:T(8,128)(2,1)S(1)}, u32[]{:S(2)}, u32[]{:S(2)}) collective-permute-start(bf16[1,128,768]{2,1,0:T(8,128)(2,1)S(1)} %fusion.26), channel_id=1, source_target_pairs={{0,16},{8,24},{16,0},{24,8},{1,17},{9,25},{17,1},{25,9},{2,18},{10... | collective-permute-start | bytes 589832 | tf_op jit(solution)/shard_map/ppermute | solution.py:87
  6.5 13.4 %all-to-all-start = ((bf16[4,192,128]{2,1,0:T(8,128)(2,1)}), bf16[4,192,128]{2,1,0:T(8,128)(2,1)S(1)}, u32[]{:S(2)}, u32[]{:S(2)}) async-start(bf16[4,192,128]{2,1,0:T(8,128)(2,1)} %bitcast.7), calls=%async_computation | async-start | bytes 393216 | tf_op jit(solution)/shard_map/all_to_all | solution.py:107
  9.9 7.8 %collective-permute-start.3 = (bf16[1,64,768]{2,1,0:T(8,128)(2,1)S(1)}, bf16[1,64,768]{2,1,0:T(8,128)(2,1)S(1)}, u32[]{:S(2)}, u32[]{:S(2)}) collective-permute-start(bf16[1,64,768]{2,1,0:T(8,128)(2,1)S(1)} %get-tuple-element.20), channel_id=1, source_target_pairs={{8,0},{16,8},{24,16},{9,1},{17,9},{25,17},{10,2},{18,10},{26,18},{... | collective-permute-start | bytes 294920 | tf_op jit(solution)/shard_map/ppermute | solution.py:23
  11.2 6.5 %collective-permute-start.2 = (bf16[1,64,768]{2,1,0:T(8,128)(2,1)S(1)}, bf16[1,64,768]{2,1,0:T(8,128)(2,1)S(1)}, u32[]{:S(2)}, u32[]{:S(2)}) collective-permute-start(bf16[1,64,768]{2,1,0:T(8,128)(2,1)S(1)} %get-tuple-element.19), channel_id=1, source_target_pairs={{0,8},{8,16},{16,24},{1,9},{9,17},{17,25},{2,10},{10,18},{18,26},{... | collective-permute-start | bytes 294920 | tf_op jit(solution)/shard_map/ppermute | solution.py:22
  15.9 3.1 %collective-permute-start.1 = (bf16[2,128,768]{2,1,0:T(8,128)(2,1)S(1)}, bf16[2,128,768]{2,1,0:T(8,128)(2,1)S(1)}, u32[]{:S(2)}, u32[]{:S(2)}) collective-permute-start(bf16[2,128,768]{2,1,0:T(8,128)(2,1)S(1)} %pad_maximum_fusion.1), channel_id=1, source_target_pairs={{0,8},{8,0},{16,24},{24,16},{1,9},{9,1},{17,25},{25,17},{2,10},{10... | collective-permute-start | bytes 1179656 | tf_op jit(solution)/shard_map/ppermute | solution.py:87
  23.5 3.4 %copy-start.3 = (bf16[256,768]{1,0:T(8,128)(2,1)S(1)}, bf16[256,768]{1,0:T(8,128)(2,1)}, u32[]{:S(2)}) copy-start(bf16[256,768]{1,0:T(8,128)(2,1)} %maximum_bitcast_fusion) | copy-start | bytes 1179652
  23.6 13.7 %collective-permute-start.4 = (f16[1168,192]{0,1:T(8,128)(2,1)S(1)}, f16[1168,192]{0,1:T(8,128)(2,1)}, u32[]{:S(2)}, u32[]{:S(2)}) collective-permute-start(f16[1168,192]{0,1:T(8,128)(2,1)S(1)} %concatenate.29.clone), channel_id=1, source_target_pairs={{0,1},{1,0},{2,3},{3,2},{4,5},{5,4},{6,7},{7,6},{8,9},{9,8},{10,11... | collective-permute-start | bytes 1345544 | tf_op jit(solution)/shard_map/ppermute | solution.py:54
  41.7 7.7 %copy-start.2 = (f32[128,768]{1,0:T(8,128)S(1)}, f32[128,768]{1,0:T(8,128)}, u32[]{:S(2)}) copy-start(f32[128,768]{1,0:T(8,128)} %fusion.22) | copy-start | bytes 1179652
  41.7 7.7 %copy-start.4 = (bf16[256,768]{1,0:T(8,128)(2,1)S(1)}, bf16[256,768]{1,0:T(8,128)(2,1)}, u32[]{:S(2)}) copy-start(bf16[256,768]{1,0:T(8,128)(2,1)} %maximum_bitcast_fusion) | copy-start | bytes 1179652
  41.7 7.7 %copy-start.5 = (f32[128,768]{1,0:T(8,128)S(1)}, f32[128,768]{1,0:T(8,128)}, u32[]{:S(2)}) copy-start(f32[128,768]{1,0:T(8,128)} %convolution_add_fusion.1) | copy-start | bytes 1179652
  42.7 14.3 %collective-permute-start.7 = (f16[304,192]{1,0:T(8,128)(2,1)S(1)}, f16[304,192]{1,0:T(8,128)(2,1)S(1)}, u32[]{:S(2)}, u32[]{:S(2)}) collective-permute-start(f16[304,192]{1,0:T(8,128)(2,1)S(1)} %concatenate.32), channel_id=1, source_target_pairs={{0,4},{1,5},{2,6},{3,7},{4,0},{5,1},{6,2},{7,3},{8,12},{9,13},{10,... | collective-permute-start | bytes 350216 | tf_op jit(solution)/shard_map/ppermute | solution.py:54
  45.4 12.8 %collective-permute-start.6 = (f16[304,192]{1,0:T(8,128)(2,1)S(1)}, f16[304,192]{1,0:T(8,128)(2,1)S(1)}, u32[]{:S(2)}, u32[]{:S(2)}) collective-permute-start(f16[304,192]{1,0:T(8,128)(2,1)S(1)} %concatenate.31), channel_id=1, source_target_pairs={{0,2},{1,3},{2,4},{3,5},{4,6},{5,7},{6,0},{7,1},{8,10},{9,11},{10,... | collective-permute-start | bytes 350216 | tf_op jit(solution)/shard_map/ppermute | solution.py:54
  47.1 12.4 %collective-permute-start.5 = (f16[304,192]{1,0:T(8,128)(2,1)S(1)}, f16[304,192]{1,0:T(8,128)(2,1)S(1)}, u32[]{:S(2)}, u32[]{:S(2)}) collective-permute-start(f16[304,192]{1,0:T(8,128)(2,1)S(1)} %concatenate.30), channel_id=1, source_target_pairs={{0,6},{1,7},{2,0},{3,1},{4,2},{5,3},{6,4},{7,5},{8,14},{9,15},{10,... | collective-permute-start | bytes 350216 | tf_op jit(solution)/shard_map/ppermute | solution.py:54

commit v18 on v17

--- a/solution.py
+++ b/solution.py
@@ -75,19 +75,31 @@
     return with_layout_constraint(total, Layout((0, 1))).T
 
 
-def gather_over_seq(block):
+def gather_over_seq(block, cot, width):
     count = lax.axis_size("seq")
     me = lax.axis_index("seq")
     bits = count.bit_length() - 1
-    if count != 1 << bits:
-        return lax.all_gather(block[None], "seq", axis=1, tiled=True)[0]
+    rows = cot.shape[0]
+    last = cot[rows - width :]
+    first = cot[:width]
+    odd = me % 2 == 1
     stack = block[None]
-    for bit in reversed(range(bits)):
+    for bit in reversed(range(1, bits)):
         pairs = [(i, i ^ (1 << bit)) for i in range(count)]
         stack = jnp.concatenate([stack, lax.ppermute(stack, "seq", pairs)], axis=0)
+    piece = jnp.where(odd, first, last)
+    outgoing = jnp.concatenate([stack.reshape(-1, block.shape[-1]), piece], axis=0)
+    incoming = lax.ppermute(outgoing, "seq", [(i, i ^ 1) for i in range(count)])
+    near = incoming[-width:]
+    stack = jnp.concatenate([stack, incoming[:-width].reshape(stack.shape)], axis=0)
+    across = [(i, i + 1) for i in range(1, count - 1, 2)] + [(i, i - 1) for i in range(2, count, 2)]
+    far = lax.ppermute(jnp.where(odd, last, first), "seq", across)
+    before = jnp.where(odd, near, far)
+    after = jnp.where(odd, far, near)
+    extended = jnp.concatenate([before, cot, after], axis=0)
     reverse = jnp.array([int(format(v, "0%db" % bits)[::-1], 2) for v in range(count)], jnp.int32)
     order = reverse[jnp.bitwise_xor(me, jnp.arange(count, dtype=jnp.int32))]
-    return jnp.take(stack, order, axis=0).reshape(-1, block.shape[-1])
+    return jnp.take(stack, order, axis=0).reshape(-1, block.shape[-1]), extended
 
 
 def body(inputs, cotangent, weight):
@@ -95,7 +107,6 @@
     reach = middle_offset * TAP_SPACING
     length = inputs.shape[1]
     in_width = inputs.shape[2]
-    halo_source = cotangent
     values = inputs[0].astype(jnp.float32)
     activation, deriv = gelu_factors(values)
     act = activation.astype(jnp.bfloat16)
@@ -107,7 +118,11 @@
     arrived = lax.all_to_all(channels, "seq", 0, 0, tiled=True)
     own_rows = arrived.shape[1]
     owned = jnp.transpose(arrived, (1, 0, 2)).reshape(own_rows, -1)
-    whole_act = gather_over_seq(act)
+    if seq_count >= 2 and seq_count & (seq_count - 1) == 0:
+        whole_act, extended = gather_over_seq(act, cotangent[0], reach)
+    else:
+        whole_act = lax.all_gather(act[None], "seq", axis=1, tiled=True)[0]
+        extended = extended_2(cotangent, (("seq", 1),), reach)[0]
     count = whole_act.shape[0]
     act_padded = jnp.pad(whole_act, ((reach, reach), (0, 0)))
     updated = []
@@ -120,7 +135,6 @@
         )
     local_columns = jnp.concatenate(updated, axis=0) * factor
     local_columns = with_layout_constraint(local_columns, Layout((0, 1)))
-    extended = extended_2(halo_source, (("seq", 1),), reach)[0]
     local_columns, extended, deriv = lax.optimization_barrier((local_columns, extended, deriv))
     grad_act = jnp.zeros((length, in_width), jnp.float32)
     for tap_index in range(KW):

time: 62.2 us -> 60.3 us (0.969)
  starting transfers between devices: 20.6 us -> 18.6 us
    ppermute x2 -> x1, starting transfers between devices: 4.79 us -> 3.03 us  [gather_over_seq(): stack = jnp.concatenate([stack, lax.ppermute(stack, 'seq', pairs)], axis=0)]
    concatenate x0 -> x3, other arithmetic: none -> 0.91 us  [the longest x1 0.8 us: gather_over_seq(): extended = jnp.concatenate([before, cot, after], axis=0)]
    squeeze x1 -> x0, other arithmetic: 0.8 us -> none  [body(): extended = extended_2(halo_source, (('seq', 1),), reach)[0]]
  transfers between devices with their start and end apart: 9 -> 8, of which waited for: 3 -> 3; matrix products, arithmetic and copies ran while one was open for 20% -> 22% of each run, Pallas kernels for 0% -> 0%
where the time goes in v18:
time: 60.3 us; the launch traced here: 59.8 us
  starting transfers between devices  18.6 us (31%)
  waiting for transfers between devices  13.9 us (23%)
  local copies, waits for them, and re-layouts  9.02 us (15%)
  matrix products  7.64 us (13%)
  other arithmetic  5.4 us (9%)
  between operations  5.27 us (9%)
    ppermute x4, waiting for transfers between devices, send(): arrived = lax.ppermute(encode(values, exponent), 'batch', perm)  13.4 us
    ppermute x4, starting transfers between devices, send(): arrived = lax.ppermute(encode(values, exponent), 'batch', perm)  8.15 us
    dot_general x3, matrix products, body(): jnp.dot(window, weight[:, tap_index * in_width:(tap_index + 1) * in_width...  6.33 us
    ppermute x1, starting transfers between devices, gather_over_seq(): incoming = lax.ppermute(outgoing, 'seq', [(i, i ^ 1) for i in range(count)])  3.38 us
    all_to_all x1, starting transfers between devices, body(): arrived = lax.all_to_all(channels, 'seq', 0, 0, tiled=True)  3.37 us
    ppermute x1, starting transfers between devices, gather_over_seq(): stack = jnp.concatenate([stack, lax.ppermute(stack, 'seq', pairs)], axis=0)  3.03 us
    slice x4, local copies, waits for them, and re-layouts, decode(): exponent = packed[-TAG:1 - TAG, 0:1].astype(jnp.float32)  2.83 us
    unnamed x17, local copies, waits for them, and re-layouts  1.84 us
  transfers between devices with their start and end apart: 8, of which 3 were waited for; matrix products, arithmetic and copies ran while one was open for 22% of the time, Pallas kernels for 0%

profile of v18, /device:TPU:0, one launch (start us, length us, event | category | flops | bytes accessed | tf_op | source)
XLA Modules:
  0.0 59.8 jit_solution(14577448478721871416)
XLA Ops:
  0.7 1.1 %fusion.26 = bf16[1,128,768]{2,1,0:T(8,128)(2,1)S(1)} fusion(bf16[1,128,768]{2,1,0:T(8,128)(2,1)} %param.4), kind=kLoop, calls=%fused_computation.42 | loop fusion | flops 589824 | bytes 393216 | tf_op jit(solution)/shard_map/convert_element_type | solution.py:112
  1.7 3.0 %collective-permute-start = (bf16[1,128,768]{2,1,0:T(8,128)(2,1)S(1)}, bf16[1,128,768]{2,1,0:T(8,128)(2,1)S(1)}, u32[]{:S(2)}, u32[]{:S(2)}) collective-permute-start(bf16[1,128,768]{2,1,0:T(8,128)(2,1)S(1)} %fusion.26), channel_id=1, source_target_pairs={{0,16},{8,24},{16,0},{24,8},{1,17},{9,25},{17,1},{25,9},{2,18},{10... | collective-permute-start | bytes 589832 | tf_op jit(solution)/shard_map/ppermute | solution.py:89
  4.7 1.7 %copy.21 = bf16[768,128]{1,0:T(8,128)(2,1)} copy(bf16[768,128]{0,1:T(8,128)(2,1)} %bitcast.104) | data formatting | bytes 393216 | tf_op jit(solution)/shard_map/transpose | solution.py:117
  6.5 3.4 %all-to-all-start = ((bf16[4,192,128]{2,1,0:T(8,128)(2,1)}), bf16[4,192,128]{2,1,0:T(8,128)(2,1)S(1)}, u32[]{:S(2)}, u32[]{:S(2)}) async-start(bf16[4,192,128]{2,1,0:T(8,128)(2,1)} %bitcast.10), calls=%async_computation | async-start | bytes 393216 | tf_op jit(solution)/shard_map/all_to_all | solution.py:118
  9.9 0.7 %collective-permute-start.2 = (bf16[64,768]{1,0:T(8,128)(2,1)S(1)}, bf16[64,768]{1,0:T(8,128)(2,1)S(1)}, u32[]{:S(2)}, u32[]{:S(2)}) collective-permute-start(bf16[64,768]{1,0:T(8,128)(2,1)S(1)} %get-tuple-element.21), channel_id=1, source_target_pairs={{8,16},{16,8},{9,17},{17,9},{10,18},{18,10},{11,19},{19,11},{12,20... | collective-permute-start | bytes 294920 | tf_op jit(solution)/shard_map/ppermute | solution.py:96
  10.6 0.6 %gather_fusion = s32[4]{0:T(128)S(1)} fusion(s32[4]{0:T(128)S(1)} %copy-done, s32[1024]{0:T(1024)S(1)} %pad_clamp_fusion.1), kind=kCustom, calls=%fused_computation | custom fusion | bytes 48 | tf_op jit(solution)/shard_map/gather | solution.py:101
  11.4 3.4 %collective-permute-start.1 = (bf16[320,768]{1,0:T(8,128)(2,1)S(1)}, bf16[320,768]{1,0:T(8,128)(2,1)S(1)}, u32[]{:S(2)}, u32[]{:S(2)}) collective-permute-start(bf16[320,768]{1,0:T(8,128)(2,1)S(1)} %pad_maximum_fusion.1), channel_id=1, source_target_pairs={{0,8},{8,0},{16,24},{24,16},{1,9},{9,1},{17,25},{25,17},{2,10},{10... | collective-permute-start | bytes 1474568 | tf_op jit(solution)/shard_map/ppermute | solution.py:92
  14.9 0.9 %fusion.22 = f32[128,768]{1,0:T(8,128)} fusion(bf16[1,128,768]{2,1,0:T(8,128)(2,1)S(1)} %copy-done.6), kind=kLoop, calls=%fused_computation.38 | loop fusion | flops 884736 | bytes 589824 | tf_op jit(solution)/shard_map/add | solution.py:31
  15.8 0.5 collective-permute-done.1
  16.4 0.6 gather_fusion.1
  17.2 0.5 convolution_bitcast_fusion
  18.1 0.4 fusion.13
  18.7 0.8 %pad_maximum_fusion.3 = bf16[256,768]{1,0:T(8,128)(2,1)} fusion(bf16[64,768]{1,0:T(8,128)(2,1)S(1)} %get-tuple-element.20, bf16[128,768]{1,0:T(8,128)(2,1)S(1)} %bitcast.105, bf16[64,768]{1,0:T(8,128)(2,1)S(1)} %get-tuple-element.19), kind=kLoop, calls=%fused_computation.46 | loop fusion | flops 1179648 | bytes 786432 | tf_op jit(solution)/shard_map/concatenate | solution.py:99
  19.5 0.8 %fusion.1 = f32[]{:T(128)} fusion(f32[4,2,288,192]{3,2,1,0:T(8,128)S(1)} %bitcast.99, s32[]{:T(128)S(6)} %select_n.124), kind=kLoop, calls=%fused_computation.10 | loop fusion | flops 442367 | bytes 884744 | tf_op jit(solution)/shard_map/reduce_max | solution.py:36
  21.2 0.4 copy.39
  21.7 1.6 %collective-permute-start.3 = (f16[1168,192]{0,1:T(8,128)(2,1)S(1)}, f16[1168,192]{0,1:T(8,128)(2,1)}, u32[]{:S(2)}, u32[]{:S(2)}) collective-permute-start(f16[1168,192]{0,1:T(8,128)(2,1)S(1)} %concatenate.33.clone), channel_id=1, source_target_pairs={{0,1},{1,0},{2,3},{3,2},{4,5},{5,4},{6,7},{7,6},{8,9},{9,8},{10,11... | collective-permute-start | bytes 1345544 | tf_op jit(solution)/shard_map/ppermute | solution.py:54
  23.3 1.7 %fusion.5 = f32[128,768]{1,0:T(8,128)S(1)} fusion(bf16[768,2304]{1,0:T(8,128)(2,1)} %param.6, bf16[256,768]{1,0:T(8,128)(2,1)} %pad_maximum_fusion.3), kind=kOutput, calls=%fused_computation.16 | convolution fusion | flops 150994944 | bytes 1769472 | tf_op jit(solution)/shard_map/dot_general | solution.py:143
  25.1 2.3 %convolution_add_fusion.1 = f32[128,768]{1,0:T(8,128)} fusion(f32[128,768]{1,0:T(8,128)S(1)} %fusion.5, bf16[768,2304]{1,0:T(8,128)(2,1)} %param.6, bf16[256,768]{1,0:T(8,128)(2,1)S(1)} %copy-done.3), kind=kOutput, calls=%fused_computation.5 | convolution fusion | flops 151093248 | bytes 2162688 | tf_op jit(solution)/shard_map/dot_general | solution.py:143
  27.4 8.0 %collective-permute-done.3 = f16[1168,192]{0,1:T(8,128)(2,1)} collective-permute-done((f16[1168,192]{0,1:T(8,128)(2,1)S(1)}, f16[1168,192]{0,1:T(8,128)(2,1)}, u32[]{:S(2)}, u32[]{:S(2)}) %collective-permute-start.3) | collective-permute-done | bytes 448544 | tf_op jit(solution)/shard_map/ppermute | solution.py:54
  35.4 1.1 %slice.89 = f16[1152,192]{0,1:T(8,128)(2,1)S(1)} slice(f16[1168,192]{0,1:T(8,128)(2,1)} %collective-permute-done.3), slice={[0:1152], [0:192]} | slice | bytes 884736 | tf_op jit(solution)/shard_map/slice | solution.py:49
  36.5 0.5 copy.37
  37.0 1.2 %slice.90 = f16[1,1]{0,1:T(2,128)(2,1)} slice(f16[1168,192]{0,1:T(8,128)(2,1)} %collective-permute-done.3), slice={[1152:1153], [0:1]} | slice | bytes 4 | tf_op jit(solution)/shard_map/slice | solution.py:48
  39.0 0.8 %abs_reduce_fusion = (f32[]{:T(128)}, f32[4,288,192]{2,1,0:T(8,128)S(1)}) fusion(f32[4,288,192]{2,1,0:T(8,128)S(1)} %bitcast.102, f32[4,2,288,192]{3,2,1,0:T(8,128)S(1)} %bitcast.101, s32[]{:T(128)S(6)} %select_n.123), kind=kLoop, calls=%fused_computation.12 | loop fusion | flops 663551 | bytes 2654216 | tf_op jit(solution)/shard_map/reduce_max | solution.py:36
  40.8 2.6 %collective-permute-start.6 = (f16[304,192]{1,0:T(8,128)(2,1)S(1)}, f16[304,192]{1,0:T(8,128)(2,1)S(1)}, u32[]{:S(2)}, u32[]{:S(2)}) collective-permute-start(f16[304,192]{1,0:T(8,128)(2,1)S(1)} %concatenate.36), channel_id=1, source_target_pairs={{0,4},{1,5},{2,6},{3,7},{4,0},{5,1},{6,2},{7,3},{8,12},{9,13},{10,... | collective-permute-start | bytes 350216 | tf_op jit(solution)/shard_map/ppermute | solution.py:54
  43.5 1.6 %collective-permute-start.5 = (f16[304,192]{1,0:T(8,128)(2,1)S(1)}, f16[304,192]{1,0:T(8,128)(2,1)S(1)}, u32[]{:S(2)}, u32[]{:S(2)}) collective-permute-start(f16[304,192]{1,0:T(8,128)(2,1)S(1)} %concatenate.35), channel_id=1, source_target_pairs={{0,2},{1,3},{2,4},{3,5},{4,6},{5,7},{6,0},{7,1},{8,10},{9,11},{10,... | collective-permute-start | bytes 350216 | tf_op jit(solution)/shard_map/ppermute | solution.py:54
  45.2 2.3 %collective-permute-start.4 = (f16[304,192]{1,0:T(8,128)(2,1)S(1)}, f16[304,192]{1,0:T(8,128)(2,1)S(1)}, u32[]{:S(2)}, u32[]{:S(2)}) collective-permute-start(f16[304,192]{1,0:T(8,128)(2,1)S(1)} %concatenate.34), channel_id=1, source_target_pairs={{0,6},{1,7},{2,0},{3,1},{4,2},{5,3},{6,4},{7,5},{8,14},{9,15},{10,... | collective-permute-start | bytes 350216 | tf_op jit(solution)/shard_map/ppermute | solution.py:54
  47.5 2.3 %fusion.10 = bf16[1,128,768]{2,1,0:T(8,128)(2,1)} fusion(f32[128,768]{1,0:T(8,128)S(1)} %copy-done.2, f32[128,768]{1,0:T(8,128)S(1)} %copy-done.5, bf16[768,2304]{1,0:T(8,128)(2,1)} %param.6, bf16[256,768]{1,0:T(8,128)(2,1)S(1)} %copy-done.4), kind=kOutput, calls=%fused_computation.19 | convolution fusion | flops 151289856 | bytes 2359296 | tf_op jit(solution)/shard_map/dot_general | solution.py:143
  49.8 5.3 %collective-permute-done.6 = f16[304,192]{1,0:T(8,128)(2,1)S(1)} collective-permute-done((f16[304,192]{1,0:T(8,128)(2,1)S(1)}, f16[304,192]{1,0:T(8,128)(2,1)S(1)}, u32[]{:S(2)}, u32[]{:S(2)}) %collective-permute-start.6) | collective-permute-done | bytes 116768 | tf_op jit(solution)/shard_map/ppermute | solution.py:54
  55.1 0.5 slice.96
  56.3 0.5 slice.94
  57.6 0.6 slice.92
  58.9 0.9 %copy.30 = f32[192,288]{1,0:T(8,128)} copy(f32[192,288]{0,1:T(8,128)S(1)} %fusion.32) | data formatting | bytes 442368
  (42 shorter events, 1.7 us)
Async XLA Ops:
  0.6 10.0 %copy-start = (s32[4]{0:T(128)S(1)}, s32[4]{0:T(128)}, u32[]{:S(2)}) copy-start(s32[4]{0:T(128)} %constant.126.clone) | copy-start | bytes 52
  0.6 9.2 %copy-start.1 = (bf16[1,128,768]{2,1,0:T(8,128)(2,1)S(1)}, bf16[1,128,768]{2,1,0:T(8,128)(2,1)}, u32[]{:S(2)}) copy-start(bf16[1,128,768]{2,1,0:T(8,128)(2,1)} %param.5) | copy-start | bytes 589828
  1.7 9.6 %collective-permute-start = (bf16[1,128,768]{2,1,0:T(8,128)(2,1)S(1)}, bf16[1,128,768]{2,1,0:T(8,128)(2,1)S(1)}, u32[]{:S(2)}, u32[]{:S(2)}) collective-permute-start(bf16[1,128,768]{2,1,0:T(8,128)(2,1)S(1)} %fusion.26), channel_id=1, source_target_pairs={{0,16},{8,24},{16,0},{24,8},{1,17},{9,25},{17,1},{25,9},{2,18},{10... | collective-permute-start | bytes 589832 | tf_op jit(solution)/shard_map/ppermute | solution.py:89
  6.5 10.7 %all-to-all-start = ((bf16[4,192,128]{2,1,0:T(8,128)(2,1)}), bf16[4,192,128]{2,1,0:T(8,128)(2,1)S(1)}, u32[]{:S(2)}, u32[]{:S(2)}) async-start(bf16[4,192,128]{2,1,0:T(8,128)(2,1)} %bitcast.10), calls=%async_computation | async-start | bytes 393216 | tf_op jit(solution)/shard_map/all_to_all | solution.py:118
  9.9 8.8 %collective-permute-start.2 = (bf16[64,768]{1,0:T(8,128)(2,1)S(1)}, bf16[64,768]{1,0:T(8,128)(2,1)S(1)}, u32[]{:S(2)}, u32[]{:S(2)}) collective-permute-start(bf16[64,768]{1,0:T(8,128)(2,1)S(1)} %get-tuple-element.21), channel_id=1, source_target_pairs={{8,16},{16,8},{9,17},{17,9},{10,18},{18,10},{11,19},{19,11},{12,20... | collective-permute-start | bytes 294920 | tf_op jit(solution)/shard_map/ppermute | solution.py:96
  10.6 4.2 %copy-start.6 = (bf16[1,128,768]{2,1,0:T(8,128)(2,1)S(1)}, bf16[1,128,768]{2,1,0:T(8,128)(2,1)}, u32[]{:S(2)}) copy-start(bf16[1,128,768]{2,1,0:T(8,128)(2,1)} %param.4) | copy-start | bytes 589828
  11.4 4.9 %collective-permute-start.1 = (bf16[320,768]{1,0:T(8,128)(2,1)S(1)}, bf16[320,768]{1,0:T(8,128)(2,1)S(1)}, u32[]{:S(2)}, u32[]{:S(2)}) collective-permute-start(bf16[320,768]{1,0:T(8,128)(2,1)S(1)} %pad_maximum_fusion.1), channel_id=1, source_target_pairs={{0,8},{8,0},{16,24},{24,16},{1,9},{9,1},{17,25},{25,17},{2,10},{10... | collective-permute-start | bytes 1474568 | tf_op jit(solution)/shard_map/ppermute | solution.py:92
  21.6 3.4 %copy-start.3 = (bf16[256,768]{1,0:T(8,128)(2,1)S(1)}, bf16[256,768]{1,0:T(8,128)(2,1)}, u32[]{:S(2)}) copy-start(bf16[256,768]{1,0:T(8,128)(2,1)} %pad_maximum_fusion.3) | copy-start | bytes 1179652
  21.7 13.7 %collective-permute-start.3 = (f16[1168,192]{0,1:T(8,128)(2,1)S(1)}, f16[1168,192]{0,1:T(8,128)(2,1)}, u32[]{:S(2)}, u32[]{:S(2)}) collective-permute-start(f16[1168,192]{0,1:T(8,128)(2,1)S(1)} %concatenate.33.clone), channel_id=1, source_target_pairs={{0,1},{1,0},{2,3},{3,2},{4,5},{5,4},{6,7},{7,6},{8,9},{9,8},{10,11... | collective-permute-start | bytes 1345544 | tf_op jit(solution)/shard_map/ppermute | solution.py:54
  39.8 7.7 %copy-start.2 = (f32[128,768]{1,0:T(8,128)S(1)}, f32[128,768]{1,0:T(8,128)}, u32[]{:S(2)}) copy-start(f32[128,768]{1,0:T(8,128)} %fusion.22) | copy-start | bytes 1179652
  39.8 7.7 %copy-start.4 = (bf16[256,768]{1,0:T(8,128)(2,1)S(1)}, bf16[256,768]{1,0:T(8,128)(2,1)}, u32[]{:S(2)}) copy-start(bf16[256,768]{1,0:T(8,128)(2,1)} %pad_maximum_fusion.3) | copy-start | bytes 1179652
  39.8 7.7 %copy-start.5 = (f32[128,768]{1,0:T(8,128)S(1)}, f32[128,768]{1,0:T(8,128)}, u32[]{:S(2)}) copy-start(f32[128,768]{1,0:T(8,128)} %convolution_add_fusion.1) | copy-start | bytes 1179652
  40.8 14.3 %collective-permute-start.6 = (f16[304,192]{1,0:T(8,128)(2,1)S(1)}, f16[304,192]{1,0:T(8,128)(2,1)S(1)}, u32[]{:S(2)}, u32[]{:S(2)}) collective-permute-start(f16[304,192]{1,0:T(8,128)(2,1)S(1)} %concatenate.36), channel_id=1, source_target_pairs={{0,4},{1,5},{2,6},{3,7},{4,0},{5,1},{6,2},{7,3},{8,12},{9,13},{10,... | collective-permute-start | bytes 350216 | tf_op jit(solution)/shard_map/ppermute | solution.py:54
  43.5 12.8 %collective-permute-start.5 = (f16[304,192]{1,0:T(8,128)(2,1)S(1)}, f16[304,192]{1,0:T(8,128)(2,1)S(1)}, u32[]{:S(2)}, u32[]{:S(2)}) collective-permute-start(f16[304,192]{1,0:T(8,128)(2,1)S(1)} %concatenate.35), channel_id=1, source_target_pairs={{0,2},{1,3},{2,4},{3,5},{4,6},{5,7},{6,0},{7,1},{8,10},{9,11},{10,... | collective-permute-start | bytes 350216 | tf_op jit(solution)/shard_map/ppermute | solution.py:54
  45.2 12.4 %collective-permute-start.4 = (f16[304,192]{1,0:T(8,128)(2,1)S(1)}, f16[304,192]{1,0:T(8,128)(2,1)S(1)}, u32[]{:S(2)}, u32[]{:S(2)}) collective-permute-start(f16[304,192]{1,0:T(8,128)(2,1)S(1)} %concatenate.34), channel_id=1, source_target_pairs={{0,6},{1,7},{2,0},{3,1},{4,2},{5,3},{6,4},{7,5},{8,14},{9,15},{10,... | collective-permute-start | bytes 350216 | tf_op jit(solution)/shard_map/ppermute | solution.py:54

commit v19 on v18

--- a/solution.py
+++ b/solution.py
@@ -102,6 +102,30 @@
     return jnp.take(stack, order, axis=0).reshape(-1, block.shape[-1]), extended
 
 
+def gather_over_seq4(block, cot, width):
+    me = lax.axis_index("seq")
+    rows = cot.shape[0]
+    last = cot[rows - width :]
+    first = cot[:width]
+    odd = me % 2 == 1
+    flat = lambda a: a.reshape(-1, block.shape[-1])
+    outgoing = jnp.concatenate([block, jnp.where(odd, last, first)], axis=0)
+    incoming = lax.ppermute(outgoing, "seq", [(i, 3 - i) for i in range(4)])
+    far = jnp.where((me == 0) | (me == 3), jnp.zeros_like(first), incoming[-width:])
+    stack = jnp.stack([block, incoming[:-width]])
+    outgoing = jnp.concatenate([flat(stack), jnp.where(odd, first, last)], axis=0)
+    incoming = lax.ppermute(outgoing, "seq", [(i, i ^ 1) for i in range(4)])
+    near = incoming[-width:]
+    stack = jnp.concatenate([stack, incoming[:-width].reshape(stack.shape)], axis=0)
+    before = jnp.where(odd, near, far)
+    after = jnp.where(odd, far, near)
+    extended = jnp.concatenate([before, cot, after], axis=0)
+    partner = jnp.bitwise_xor(me, 1)
+    sources = jnp.stack([me, 3 - me, partner, 3 - partner])
+    order = jnp.sum(jnp.arange(4)[None, :] * (sources[None, :] == jnp.arange(4)[:, None]), axis=1)
+    return flat(jnp.take(stack, order, axis=0)), extended
+
+
 def body(inputs, cotangent, weight):
     middle_offset = KW // 2
     reach = middle_offset * TAP_SPACING
@@ -118,7 +142,9 @@
     arrived = lax.all_to_all(channels, "seq", 0, 0, tiled=True)
     own_rows = arrived.shape[1]
     owned = jnp.transpose(arrived, (1, 0, 2)).reshape(own_rows, -1)
-    if seq_count >= 2 and seq_count & (seq_count - 1) == 0:
+    if seq_count == 4:
+        whole_act, extended = gather_over_seq4(act, cotangent[0], reach)
+    elif seq_count >= 2 and seq_count & (seq_count - 1) == 0:
         whole_act, extended = gather_over_seq(act, cotangent[0], reach)
     else:
         whole_act = lax.all_gather(act[None], "seq", axis=1, tiled=True)[0]

time: 60.3 us -> 63.1 us (1.046)
  waiting for transfers between devices: 13.9 us -> 21.6 us
  starting transfers between devices: 18.6 us -> 15.1 us
  local copies, waits for them, and re-layouts: 9.02 us -> 7.45 us
    ppermute x3 -> x2, waiting for transfers between devices: 0.51 us -> 8.89 us  [the longest x1 7.26 us: gather_over_seq4(): incoming = lax.ppermute(outgoing, 'seq', [(i, 3 - i) for i in range(4)])]
    ppermute x3 -> x2, starting transfers between devices: 7.08 us -> 2.06 us  [the longest x1 1.84 us: gather_over_seq4(): incoming = lax.ppermute(outgoing, 'seq', [(i, 3 - i) for i in range(4)])]
    slice x1, local copies, waits for them, and re-layouts: 1.09 us -> 0.08 us  [decode(): values = packed[:-TAG].astype(jnp.float32) * jnp.exp2(exponent - HEADROOM)]
    convert_element_type x1, other arithmetic: 1.06 us -> 0.09 us  [body(): act = activation.astype(jnp.bfloat16)]
    select_n x5 -> x4, other arithmetic: 0.22 us -> 1.15 us  [the longest x1 0.96 us: gather_over_seq4(): outgoing = jnp.concatenate([block, jnp.where(odd, last, first)], axis=0)]
    all_to_all x1, starting transfers between devices: 3.37 us -> 4.24 us  [body(): arrived = lax.all_to_all(channels, 'seq', 0, 0, tiled=True)]
    unnamed x17 -> x15, local copies, waits for them, and re-layouts: 1.84 us -> 2.55 us
    ppermute x4, starting transfers between devices: 8.15 us -> 8.84 us  [send(): arrived = lax.ppermute(encode(values, exponent), 'batch', perm)]
  transfers between devices with their start and end apart: 8 -> 7, of which waited for: 3 -> 4; matrix products, arithmetic and copies ran while one was open for 22% -> 18% of each run, Pallas kernels for 0% -> 0%
where the time goes in v19:
time: 63.1 us; the launch traced here: 62.6 us
  waiting for transfers between devices  21.6 us (34%)
  starting transfers between devices  15.1 us (24%)
  matrix products  7.65 us (12%)
  local copies, waits for them, and re-layouts  7.45 us (12%)
  other arithmetic  5.58 us (9%)
  between operations  5.21 us (8%)
    ppermute x4, waiting for transfers between devices, send(): arrived = lax.ppermute(encode(values, exponent), 'batch', perm)  12.7 us
    ppermute x4, starting transfers between devices, send(): arrived = lax.ppermute(encode(values, exponent), 'batch', perm)  8.84 us
    ppermute x1, waiting for transfers between devices, gather_over_seq4(): incoming = lax.ppermute(outgoing, 'seq', [(i, 3 - i) for i in range(4)])  7.26 us
    dot_general x3, matrix products, body(): jnp.dot(window, weight[:, tap_index * in_width:(tap_index + 1) * in_width...  6.35 us
    all_to_all x1, starting transfers between devices, body(): arrived = lax.all_to_all(channels, 'seq', 0, 0, tiled=True)  4.24 us
    unnamed x15, local copies, waits for them, and re-layouts  2.55 us
    slice x4, local copies, waits for them, and re-layouts, decode(): exponent = packed[-TAG:1 - TAG, 0:1].astype(jnp.float32)  2.15 us
    ppermute x1, starting transfers between devices, gather_over_seq4(): incoming = lax.ppermute(outgoing, 'seq', [(i, 3 - i) for i in range(4)])  1.84 us
  transfers between devices with their start and end apart: 7, of which 4 were waited for; matrix products, arithmetic and copies ran while one was open for 18% of the time, Pallas kernels for 0%

profile of v19, /device:TPU:0, one launch (start us, length us, event | category | flops | bytes accessed | tf_op | source)
XLA Modules:
  0.0 62.6 jit_solution(430225466653323542)
XLA Ops:
  0.6 1.8 %copy.30 = bf16[768,128]{1,0:T(8,128)(2,1)} copy(bf16[768,128]{0,1:T(8,128)(2,1)} %bitcast.114) | data formatting | bytes 393216 | tf_op jit(solution)/shard_map/transpose | solution.py:141
  2.4 4.2 %all-to-all-start = ((bf16[4,192,128]{2,1,0:T(8,128)(2,1)}), bf16[4,192,128]{2,1,0:T(8,128)(2,1)S(1)}, u32[]{:S(2)}, u32[]{:S(2)}) async-start(bf16[4,192,128]{2,1,0:T(8,128)(2,1)} %bitcast.16), calls=%async_computation | async-start | bytes 393216 | tf_op jit(solution)/shard_map/all_to_all | solution.py:142
  6.7 1.0 %select_bitcast_fusion.1 = (bf16[64,768]{1,0:T(8,128)(2,1)S(1)}, bf16[64,768]{1,0:T(8,128)(2,1)S(1)}) fusion(pred[]{:T(512)S(6)} %eq.31, bf16[1,128,768]{2,1,0:T(8,128)(2,1)} %param.4), kind=kLoop, calls=%fused_computation.71 | loop fusion | flops 98304 | bytes 393217 | tf_op jit(solution)/shard_map/jit(_where)/select_n | solution.py:112
  7.6 0.9 %fusion.24 = (f32[128,768]{1,0:T(8,128)}, bf16[128,768]{1,0:T(8,128)(2,1)S(1)}) fusion(bf16[1,128,768]{2,1,0:T(8,128)(2,1)S(1)} %copy-done.5), kind=kLoop, calls=%fused_computation.39 | loop fusion | flops 1081344 | bytes 786432 | tf_op jit(solution)/shard_map/add | solution.py:31
  8.6 1.8 %collective-permute-start = (bf16[192,768]{1,0:T(8,128)(2,1)S(1)}, bf16[192,768]{1,0:T(8,128)(2,1)S(1)}, u32[]{:S(2)}, u32[]{:S(2)}) collective-permute-start(bf16[192,768]{1,0:T(8,128)(2,1)S(1)} %pad_maximum_fusion.4), channel_id=1, source_target_pairs={{0,24},{8,16},{16,8},{24,0},{1,25},{9,17},{17,9},{25,1},{2,26},{10... | collective-permute-start | bytes 884744 | tf_op jit(solution)/shard_map/ppermute | solution.py:113
  10.7 7.3 %collective-permute-done = bf16[192,768]{1,0:T(8,128)(2,1)S(1)} collective-permute-done((bf16[192,768]{1,0:T(8,128)(2,1)S(1)}, bf16[192,768]{1,0:T(8,128)(2,1)S(1)}, u32[]{:S(2)}, u32[]{:S(2)}) %collective-permute-start) | collective-permute-done | bytes 294944 | tf_op jit(solution)/shard_map/ppermute | solution.py:113
  18.1 0.2 collective-permute-start.1
  18.4 1.6 %collective-permute-done.1 = bf16[320,768]{1,0:T(8,128)(2,1)S(1)} collective-permute-done((bf16[320,768]{1,0:T(8,128)(2,1)S(1)}, bf16[320,768]{1,0:T(8,128)(2,1)S(1)}, u32[]{:S(2)}, u32[]{:S(2)}) %collective-permute-start.1) | collective-permute-done | bytes 491552 | tf_op jit(solution)/shard_map/ppermute | solution.py:117
  20.1 0.6 gather_fusion
  21.0 0.7 %copy-done = bf16[1,128,768]{2,1,0:T(8,128)(2,1)S(1)} copy-done((bf16[1,128,768]{2,1,0:T(8,128)(2,1)S(1)}, bf16[1,128,768]{2,1,0:T(8,128)(2,1)}, u32[]{:S(2)}) %copy-start) | copy-done | bytes 196632
  21.7 0.8 %pad_maximum_fusion.3 = bf16[256,768]{1,0:T(8,128)(2,1)} fusion(bf16[64,768]{1,0:T(8,128)(2,1)S(1)} %get-tuple-element.22, bf16[128,768]{1,0:T(8,128)(2,1)S(1)} %bitcast.115, bf16[64,768]{1,0:T(8,128)(2,1)S(1)} %get-tuple-element.21), kind=kLoop, calls=%fused_computation.47 | loop fusion | flops 1179648 | bytes 786432 | tf_op jit(solution)/shard_map/concatenate | solution.py:122
  22.4 0.5 convolution_bitcast_fusion
  22.9 0.4 fusion.14
  23.3 0.4 fusion.13
  23.9 0.8 %fusion.1 = f32[]{:T(128)} fusion(f32[4,2,288,192]{3,2,1,0:T(8,128)S(1)} %bitcast.109, s32[]{:T(128)S(6)} %select_n.121), kind=kLoop, calls=%fused_computation.9 | loop fusion | flops 442367 | bytes 884744 | tf_op jit(solution)/shard_map/reduce_max | solution.py:36
  25.6 0.4 copy.48
  26.2 2.1 %collective-permute-start.2 = (f16[1168,192]{0,1:T(8,128)(2,1)S(1)}, f16[1168,192]{0,1:T(8,128)(2,1)S(1)}, u32[]{:S(2)}, u32[]{:S(2)}) collective-permute-start(f16[1168,192]{0,1:T(8,128)(2,1)S(1)} %concatenate.33.clone), channel_id=1, source_target_pairs={{0,1},{1,0},{2,3},{3,2},{4,5},{5,4},{6,7},{7,6},{8,9},{9,8},{10,11... | collective-permute-start | bytes 1345544 | tf_op jit(solution)/shard_map/ppermute | solution.py:54
  28.3 1.7 %fusion.5 = f32[128,768]{1,0:T(8,128)S(1)} fusion(bf16[768,2304]{1,0:T(8,128)(2,1)} %param.5, bf16[256,768]{1,0:T(8,128)(2,1)} %pad_maximum_fusion.3), kind=kOutput, calls=%fused_computation.15 | convolution fusion | flops 150994944 | bytes 1769472 | tf_op jit(solution)/shard_map/dot_general | solution.py:169
  30.0 2.4 %convolution_add_fusion.1 = f32[128,768]{1,0:T(8,128)} fusion(f32[128,768]{1,0:T(8,128)S(1)} %fusion.5, bf16[768,2304]{1,0:T(8,128)(2,1)} %param.5, bf16[256,768]{1,0:T(8,128)(2,1)S(1)} %copy-done.2), kind=kOutput, calls=%fused_computation.4 | convolution fusion | flops 151093248 | bytes 2162688 | tf_op jit(solution)/shard_map/dot_general | solution.py:169
  32.4 7.4 %collective-permute-done.2 = f16[1168,192]{0,1:T(8,128)(2,1)S(1)} collective-permute-done((f16[1168,192]{0,1:T(8,128)(2,1)S(1)}, f16[1168,192]{0,1:T(8,128)(2,1)S(1)}, u32[]{:S(2)}, u32[]{:S(2)}) %collective-permute-start.2) | collective-permute-done | bytes 448544 | tf_op jit(solution)/shard_map/ppermute | solution.py:54
  39.8 0.5 slice.98
  41.1 0.5 copy.46
  41.7 0.8 %abs_reduce_fusion = (f32[]{:T(128)}, f32[4,288,192]{2,1,0:T(8,128)S(1)}) fusion(f32[4,288,192]{2,1,0:T(8,128)S(1)} %bitcast.112, f32[4,2,288,192]{3,2,1,0:T(8,128)S(1)} %bitcast.111, s32[]{:T(128)S(6)} %select_n.120), kind=kLoop, calls=%fused_computation.11 | loop fusion | flops 663551 | bytes 2654216 | tf_op jit(solution)/shard_map/reduce_max | solution.py:36
  43.7 2.9 %collective-permute-start.5 = (f16[304,192]{1,0:T(8,128)(2,1)S(1)}, f16[304,192]{1,0:T(8,128)(2,1)S(1)}, u32[]{:S(2)}, u32[]{:S(2)}) collective-permute-start(f16[304,192]{1,0:T(8,128)(2,1)S(1)} %concatenate.36), channel_id=1, source_target_pairs={{0,4},{1,5},{2,6},{3,7},{4,0},{5,1},{6,2},{7,3},{8,12},{9,13},{10,... | collective-permute-start | bytes 350216 | tf_op jit(solution)/shard_map/ppermute | solution.py:54
  46.6 1.6 %collective-permute-start.4 = (f16[304,192]{1,0:T(8,128)(2,1)S(1)}, f16[304,192]{1,0:T(8,128)(2,1)S(1)}, u32[]{:S(2)}, u32[]{:S(2)}) collective-permute-start(f16[304,192]{1,0:T(8,128)(2,1)S(1)} %concatenate.35), channel_id=1, source_target_pairs={{0,2},{1,3},{2,4},{3,5},{4,6},{5,7},{6,0},{7,1},{8,10},{9,11},{10,... | collective-permute-start | bytes 350216 | tf_op jit(solution)/shard_map/ppermute | solution.py:54
  48.1 2.3 %collective-permute-start.3 = (f16[304,192]{1,0:T(8,128)(2,1)S(1)}, f16[304,192]{1,0:T(8,128)(2,1)S(1)}, u32[]{:S(2)}, u32[]{:S(2)}) collective-permute-start(f16[304,192]{1,0:T(8,128)(2,1)S(1)} %concatenate.34), channel_id=1, source_target_pairs={{0,6},{1,7},{2,0},{3,1},{4,2},{5,3},{6,4},{7,5},{8,14},{9,15},{10,... | collective-permute-start | bytes 350216 | tf_op jit(solution)/shard_map/ppermute | solution.py:54
  50.4 2.3 %fusion.10 = bf16[1,128,768]{2,1,0:T(8,128)(2,1)} fusion(f32[128,768]{1,0:T(8,128)S(1)} %copy-done.1, f32[128,768]{1,0:T(8,128)S(1)} %copy-done.4, bf16[768,2304]{1,0:T(8,128)(2,1)} %param.5, bf16[256,768]{1,0:T(8,128)(2,1)S(1)} %copy-done.3), kind=kOutput, calls=%fused_computation.18 | convolution fusion | flops 151289856 | bytes 2359296 | tf_op jit(solution)/shard_map/dot_general | solution.py:169
  52.7 5.3 %collective-permute-done.5 = f16[304,192]{1,0:T(8,128)(2,1)S(1)} collective-permute-done((f16[304,192]{1,0:T(8,128)(2,1)S(1)}, f16[304,192]{1,0:T(8,128)(2,1)S(1)}, u32[]{:S(2)}, u32[]{:S(2)}) %collective-permute-start.5) | collective-permute-done | bytes 116768 | tf_op jit(solution)/shard_map/ppermute | solution.py:54
  57.9 0.5 slice.104
  59.2 0.5 slice.102
  60.4 0.6 slice.100
  61.8 0.9 %copy.39 = f32[192,288]{1,0:T(8,128)} copy(f32[192,288]{0,1:T(8,128)S(1)} %fusion.34) | data formatting | bytes 442368
  (39 shorter events, 1.7 us)
Async XLA Ops:
  0.6 7.0 %copy-start.5 = (bf16[1,128,768]{2,1,0:T(8,128)(2,1)S(1)}, bf16[1,128,768]{2,1,0:T(8,128)(2,1)}, u32[]{:S(2)}) copy-start(bf16[1,128,768]{2,1,0:T(8,128)(2,1)} %param.3) | copy-start | bytes 589828
  2.4 20.0 %all-to-all-start = ((bf16[4,192,128]{2,1,0:T(8,128)(2,1)}), bf16[4,192,128]{2,1,0:T(8,128)(2,1)S(1)}, u32[]{:S(2)}, u32[]{:S(2)}) async-start(bf16[4,192,128]{2,1,0:T(8,128)(2,1)} %bitcast.16), calls=%async_computation | async-start | bytes 393216 | tf_op jit(solution)/shard_map/all_to_all | solution.py:142
  8.6 9.4 %collective-permute-start = (bf16[192,768]{1,0:T(8,128)(2,1)S(1)}, bf16[192,768]{1,0:T(8,128)(2,1)S(1)}, u32[]{:S(2)}, u32[]{:S(2)}) collective-permute-start(bf16[192,768]{1,0:T(8,128)(2,1)S(1)} %pad_maximum_fusion.4), channel_id=1, source_target_pairs={{0,24},{8,16},{16,8},{24,0},{1,25},{9,17},{17,9},{25,1},{2,26},{10... | collective-permute-start | bytes 884744 | tf_op jit(solution)/shard_map/ppermute | solution.py:113
  18.1 1.9 %collective-permute-start.1 = (bf16[320,768]{1,0:T(8,128)(2,1)S(1)}, bf16[320,768]{1,0:T(8,128)(2,1)S(1)}, u32[]{:S(2)}, u32[]{:S(2)}) collective-permute-start(bf16[320,768]{1,0:T(8,128)(2,1)S(1)} %pad_maximum_fusion.1), channel_id=1, source_target_pairs={{0,8},{8,0},{16,24},{24,16},{1,9},{9,1},{17,25},{25,17},{2,10},{10... | collective-permute-start | bytes 1474568 | tf_op jit(solution)/shard_map/ppermute | solution.py:117
  20.7 0.9 %copy-start = (bf16[1,128,768]{2,1,0:T(8,128)(2,1)S(1)}, bf16[1,128,768]{2,1,0:T(8,128)(2,1)}, u32[]{:S(2)}) copy-start(bf16[1,128,768]{2,1,0:T(8,128)(2,1)} %param.4) | copy-start | bytes 589828
  26.1 3.9 %copy-start.2 = (bf16[256,768]{1,0:T(8,128)(2,1)S(1)}, bf16[256,768]{1,0:T(8,128)(2,1)}, u32[]{:S(2)}) copy-start(bf16[256,768]{1,0:T(8,128)(2,1)} %pad_maximum_fusion.3) | copy-start | bytes 1179652
  26.2 13.6 %collective-permute-start.2 = (f16[1168,192]{0,1:T(8,128)(2,1)S(1)}, f16[1168,192]{0,1:T(8,128)(2,1)S(1)}, u32[]{:S(2)}, u32[]{:S(2)}) collective-permute-start(f16[1168,192]{0,1:T(8,128)(2,1)S(1)} %concatenate.33.clone), channel_id=1, source_target_pairs={{0,1},{1,0},{2,3},{3,2},{4,5},{5,4},{6,7},{7,6},{8,9},{9,8},{10,11... | collective-permute-start | bytes 1345544 | tf_op jit(solution)/shard_map/ppermute | solution.py:54
  42.6 7.8 %copy-start.1 = (f32[128,768]{1,0:T(8,128)S(1)}, f32[128,768]{1,0:T(8,128)}, u32[]{:S(2)}) copy-start(f32[128,768]{1,0:T(8,128)} %get-tuple-element.6) | copy-start | bytes 1179652
  42.6 7.8 %copy-start.3 = (bf16[256,768]{1,0:T(8,128)(2,1)S(1)}, bf16[256,768]{1,0:T(8,128)(2,1)}, u32[]{:S(2)}) copy-start(bf16[256,768]{1,0:T(8,128)(2,1)} %pad_maximum_fusion.3) | copy-start | bytes 1179652
  42.6 7.8 %copy-start.4 = (f32[128,768]{1,0:T(8,128)S(1)}, f32[128,768]{1,0:T(8,128)}, u32[]{:S(2)}) copy-start(f32[128,768]{1,0:T(8,128)} %convolution_add_fusion.1) | copy-start | bytes 1179652
  43.7 14.3 %collective-permute-start.5 = (f16[304,192]{1,0:T(8,128)(2,1)S(1)}, f16[304,192]{1,0:T(8,128)(2,1)S(1)}, u32[]{:S(2)}, u32[]{:S(2)}) collective-permute-start(f16[304,192]{1,0:T(8,128)(2,1)S(1)} %concatenate.36), channel_id=1, source_target_pairs={{0,4},{1,5},{2,6},{3,7},{4,0},{5,1},{6,2},{7,3},{8,12},{9,13},{10,... | collective-permute-start | bytes 350216 | tf_op jit(solution)/shard_map/ppermute | solution.py:54
  46.6 12.6 %collective-permute-start.4 = (f16[304,192]{1,0:T(8,128)(2,1)S(1)}, f16[304,192]{1,0:T(8,128)(2,1)S(1)}, u32[]{:S(2)}, u32[]{:S(2)}) collective-permute-start(f16[304,192]{1,0:T(8,128)(2,1)S(1)} %concatenate.35), channel_id=1, source_target_pairs={{0,2},{1,3},{2,4},{3,5},{4,6},{5,7},{6,0},{7,1},{8,10},{9,11},{10,... | collective-permute-start | bytes 350216 | tf_op jit(solution)/shard_map/ppermute | solution.py:54
  48.1 12.3 %collective-permute-start.3 = (f16[304,192]{1,0:T(8,128)(2,1)S(1)}, f16[304,192]{1,0:T(8,128)(2,1)S(1)}, u32[]{:S(2)}, u32[]{:S(2)}) collective-permute-start(f16[304,192]{1,0:T(8,128)(2,1)S(1)} %concatenate.34), channel_id=1, source_target_pairs={{0,6},{1,7},{2,0},{3,1},{4,2},{5,3},{6,4},{7,5},{8,14},{9,15},{10,... | collective-permute-start | bytes 350216 | tf_op jit(solution)/shard_map/ppermute | solution.py:54

commit v20 on v18

--- a/solution.py
+++ b/solution.py
@@ -102,6 +102,40 @@
     return jnp.take(stack, order, axis=0).reshape(-1, block.shape[-1]), extended
 
 
+def exchange_over_seq4(block, cot, channels, width):
+    me = lax.axis_index("seq")
+    rows = cot.shape[0]
+    last = cot[rows - width :]
+    first = cot[:width]
+    odd = me % 2 == 1
+    lanes = block.shape[-1]
+    flat = lambda a: a.reshape(-1, lanes)
+    pick = lambda j: lax.dynamic_index_in_dim(channels, j, axis=0, keepdims=False)
+    outgoing = jnp.stack([pick(me ^ 2), pick(me ^ 3)])
+    payload = jnp.concatenate([block, flat(outgoing)], axis=0)
+    incoming = lax.ppermute(payload, "seq", [(i, i ^ 2) for i in range(4)])
+    stack = jnp.stack([block, incoming[:rows]])
+    first_items = incoming[rows:].reshape(outgoing.shape)
+    outgoing = jnp.stack([pick(me ^ 1), first_items[1]])
+    piece = jnp.where(odd, first, last)
+    payload = jnp.concatenate([flat(stack), flat(outgoing), piece], axis=0)
+    incoming = lax.ppermute(payload, "seq", [(i, i ^ 1) for i in range(4)])
+    near = incoming[-width:]
+    stack = jnp.concatenate([stack, incoming[: 2 * rows].reshape(stack.shape)], axis=0)
+    second_items = incoming[2 * rows : -width].reshape(outgoing.shape)
+    across = [(1, 2), (2, 1)]
+    far = lax.ppermute(jnp.where(odd, last, first), "seq", across)
+    before = jnp.where(odd, near, far)
+    after = jnp.where(odd, far, near)
+    extended = jnp.concatenate([before, cot, after], axis=0)
+    items = jnp.stack([pick(me), first_items[0], second_items[0], second_items[1]])
+    reverse = jnp.array([0, 2, 1, 3], jnp.int32)
+    order = reverse[jnp.bitwise_xor(me, jnp.arange(4, dtype=jnp.int32))]
+    whole = flat(jnp.take(stack, order, axis=0))
+    owned = jnp.take(items, order, axis=0)
+    return whole, extended, jnp.transpose(owned, (1, 0, 2)).reshape(owned.shape[1], -1)
+
+
 def body(inputs, cotangent, weight):
     middle_offset = KW // 2
     reach = middle_offset * TAP_SPACING
@@ -115,14 +149,17 @@
     counted = batch_count * inputs.shape[0] * length * seq_count
     factor = 1.0 / math.sqrt(float(counted))
     channels = cotangent[0].T.reshape(seq_count, -1, length)
-    arrived = lax.all_to_all(channels, "seq", 0, 0, tiled=True)
-    own_rows = arrived.shape[1]
-    owned = jnp.transpose(arrived, (1, 0, 2)).reshape(own_rows, -1)
-    if seq_count >= 2 and seq_count & (seq_count - 1) == 0:
-        whole_act, extended = gather_over_seq(act, cotangent[0], reach)
+    own_rows = channels.shape[1]
+    if seq_count == 4:
+        whole_act, extended, owned = exchange_over_seq4(act, cotangent[0], channels, reach)
     else:
-        whole_act = lax.all_gather(act[None], "seq", axis=1, tiled=True)[0]
-        extended = extended_2(cotangent, (("seq", 1),), reach)[0]
+        arrived = lax.all_to_all(channels, "seq", 0, 0, tiled=True)
+        owned = jnp.transpose(arrived, (1, 0, 2)).reshape(own_rows, -1)
+        if seq_count >= 2 and seq_count & (seq_count - 1) == 0:
+            whole_act, extended = gather_over_seq(act, cotangent[0], reach)
+        else:
+            whole_act = lax.all_gather(act[None], "seq", axis=1, tiled=True)[0]
+            extended = extended_2(cotangent, (("seq", 1),), reach)[0]
     count = whole_act.shape[0]
     act_padded = jnp.pad(whole_act, ((reach, reach), (0, 0)))
     updated = []

time: 60.3 us -> 63.8 us (1.058)
  waiting for transfers between devices: 13.9 us -> 22.3 us
  starting transfers between devices: 18.6 us -> 13.2 us
  local copies, waits for them, and re-layouts: 9.02 us -> 10.4 us
  other arithmetic: 5.4 us -> 4.31 us
    ppermute x3, waiting for transfers between devices: 0.51 us -> 9.31 us  [the longest x1 7.63 us: exchange_over_seq4(): incoming = lax.ppermute(payload, 'seq', [(i, i ^ 2) for i in range(4)])]
    all_to_all x1 -> x0, starting transfers between devices: 3.37 us -> none  [body(): arrived = lax.all_to_all(channels, 'seq', 0, 0, tiled=True)]
    ppermute x3, starting transfers between devices: 7.08 us -> 5.18 us  [the longest x1 4.28 us: exchange_over_seq4(): incoming = lax.ppermute(payload, 'seq', [(i, i ^ 2) for i in range(4)])]
    unnamed x17 -> x16, local copies, waits for them, and re-layouts: 1.84 us -> 3.64 us
    transpose x1 -> x0, local copies, waits for them, and re-layouts: 1.74 us -> none  [body(): channels = cotangent[0].T.reshape(seq_count, -1, length)]
    concatenate x4, local copies, waits for them, and re-layouts: 0.18 us -> 1.19 us  [encode(): jnp.concatenate([scaled, tag], axis=0)]
    slice x1, local copies, waits for them, and re-layouts: 1.09 us -> 0.08 us  [decode(): values = packed[:-TAG].astype(jnp.float32) * jnp.exp2(exponent - HEADROOM)]
    convert_element_type x1, other arithmetic: 1.06 us -> 0.09 us  [body(): act = activation.astype(jnp.bfloat16)]
  transfers between devices with their start and end apart: 8 -> 7, of which waited for: 3 -> 4; matrix products, arithmetic and copies ran while one was open for 22% -> 22% of each run, Pallas kernels for 0% -> 0%
where the time goes in v20:
time: 63.8 us; the launch traced here: 63.4 us
  waiting for transfers between devices  22.3 us (35%)
  starting transfers between devices  13.2 us (21%)
  local copies, waits for them, and re-layouts  10.4 us (16%)
  matrix products  7.81 us (12%)
  between operations  5.39 us (8%)
  other arithmetic  4.31 us (7%)
    ppermute x4, waiting for transfers between devices, send(): arrived = lax.ppermute(encode(values, exponent), 'batch', perm)  13 us
    ppermute x4, starting transfers between devices, send(): arrived = lax.ppermute(encode(values, exponent), 'batch', perm)  8.03 us
    ppermute x1, waiting for transfers between devices, exchange_over_seq4(): incoming = lax.ppermute(payload, 'seq', [(i, i ^ 2) for i in range(4)])  7.63 us
    dot_general x3, matrix products, body(): jnp.dot(window, weight[:, tap_index * in_width:(tap_index + 1) * in_width...  6.37 us
    ppermute x1, starting transfers between devices, exchange_over_seq4(): incoming = lax.ppermute(payload, 'seq', [(i, i ^ 2) for i in range(4)])  4.28 us
    unnamed x16, local copies, waits for them, and re-layouts  3.64 us
    slice x4, local copies, waits for them, and re-layouts, decode(): exponent = packed[-TAG:1 - TAG, 0:1].astype(jnp.float32)  2.14 us
    ppermute x1, waiting for transfers between devices, exchange_over_seq4(): incoming = lax.ppermute(payload, 'seq', [(i, i ^ 1) for i in range(4)])  1.67 us
  transfers between devices with their start and end apart: 7, of which 4 were waited for; matrix products, arithmetic and copies ran while one was open for 22% of the time, Pallas kernels for 0%

profile of v20, /device:TPU:0, one launch (start us, length us, event | category | flops | bytes accessed | tf_op | source)
XLA Modules:
  0.0 63.4 jit_solution(1654074710826887737)
XLA Ops:
  0.7 1.1 %copy.47 = bf16[1,128,768]{1,2,0:T(8,128)(2,1)S(1)} copy(bf16[1,128,768]{2,1,0:T(8,128)(2,1)} %param.5) | data formatting | bytes 393216 | tf_op args[1]
  1.9 0.7 %collective-permute-start.2 = (bf16[64,768]{0,1:T(8,128)(2,1)S(1)}, bf16[64,768]{0,1:T(8,128)(2,1)S(1)}, u32[]{:S(2)}, u32[]{:S(2)}) collective-permute-start(bf16[64,768]{0,1:T(8,128)(2,1)S(1)} %get-tuple-element.29), channel_id=1, source_target_pairs={{8,16},{16,8},{9,17},{17,9},{10,18},{18,10},{11,19},{19,11},{12,20... | collective-permute-start | bytes 294920 | tf_op jit(solution)/shard_map/ppermute | solution.py:127
  2.8 0.9 %fusion.24 = (f32[128,768]{1,0:T(8,128)}, bf16[128,768]{1,0:T(8,128)(2,1)S(1)}) fusion(bf16[1,128,768]{2,1,0:T(8,128)(2,1)S(1)} %copy-done.5), kind=kLoop, calls=%fused_computation.41 | loop fusion | flops 1081344 | bytes 786432 | tf_op jit(solution)/shard_map/add | solution.py:31
  3.8 4.3 %collective-permute-start = (bf16[192,768]{1,0:T(8,128)(2,1)S(1)}, bf16[192,768]{1,0:T(8,128)(2,1)S(1)}, u32[]{:S(2)}, u32[]{:S(2)}) collective-permute-start(bf16[192,768]{1,0:T(8,128)(2,1)S(1)} %pad_maximum_fusion.4), channel_id=1, source_target_pairs={{0,16},{8,24},{16,0},{24,8},{1,17},{9,25},{17,1},{25,9},{2,18},{10... | collective-permute-start | bytes 884744 | tf_op jit(solution)/shard_map/ppermute | solution.py:116
  8.1 0.6 %gather_fusion = s32[4]{0:T(128)S(1)} fusion(s32[4]{0:T(128)S(1)} %copy-done, s32[1024]{0:T(1024)S(1)} %pad_clamp_fusion.1), kind=kCustom, calls=%fused_computation | custom fusion | bytes 48 | tf_op jit(solution)/shard_map/gather | solution.py:133
  8.8 7.6 %collective-permute-done = bf16[192,768]{1,0:T(8,128)(2,1)S(1)} collective-permute-done((bf16[192,768]{1,0:T(8,128)(2,1)S(1)}, bf16[192,768]{1,0:T(8,128)(2,1)S(1)}, u32[]{:S(2)}, u32[]{:S(2)}) %collective-permute-start) | collective-permute-done | bytes 294944 | tf_op jit(solution)/shard_map/ppermute | solution.py:116
  17.6 1.7 %collective-permute-done.1 = bf16[384,768]{0,1:T(8,128)(2,1)S(1)} collective-permute-done((bf16[384,768]{0,1:T(8,128)(2,1)S(1)}, bf16[384,768]{0,1:T(8,128)(2,1)S(1)}, u32[]{:S(2)}, u32[]{:S(2)}) %collective-permute-start.1) | collective-permute-done | bytes 589856 | tf_op jit(solution)/shard_map/ppermute | solution.py:122
  20.1 0.6 gather_fusion.1
  20.7 0.6 gather_fusion.2
  21.5 0.5 fusion.14
  22.0 0.5 fusion.13
  22.5 0.5 convolution_bitcast_fusion
  23.1 0.3 pad_maximum_fusion.3
  23.6 0.8 %fusion.1 = f32[]{:T(128)} fusion(f32[4,2,288,192]{3,2,1,0:T(8,128)S(1)} %bitcast.107, s32[]{:T(128)S(6)} %select_n.153), kind=kLoop, calls=%fused_computation.11 | loop fusion | flops 442367 | bytes 884744 | tf_op jit(solution)/shard_map/reduce_max | solution.py:36
  25.3 1.1 %copy.72 = f16[1152,192]{0,1:T(8,128)(2,1)} copy(f16[1152,192]{1,0:T(8,128)(2,1)S(1)} %bitcast.113) | data formatting | bytes 884736
  26.4 1.1 %concatenate.33.clone = f16[1168,192]{0,1:T(8,128)(2,1)S(1)} pad(f16[1152,192]{0,1:T(8,128)(2,1)} %copy.72, f16[]{:T(256)S(6)} %convert_element_type.101), padding=0_16x0_0 | pad | bytes 890882 | tf_op jit(solution)/shard_map/concatenate | solution.py:44
  27.5 1.6 %collective-permute-start.3 = (f16[1168,192]{0,1:T(8,128)(2,1)S(1)}, f16[1168,192]{0,1:T(8,128)(2,1)S(1)}, u32[]{:S(2)}, u32[]{:S(2)}) collective-permute-start(f16[1168,192]{0,1:T(8,128)(2,1)S(1)} %concatenate.33.clone), channel_id=1, source_target_pairs={{0,1},{1,0},{2,3},{3,2},{4,5},{5,4},{6,7},{7,6},{8,9},{9,8},{10,11... | collective-permute-start | bytes 1345544 | tf_op jit(solution)/shard_map/ppermute | solution.py:54
  29.0 1.6 %fusion.5 = f32[128,768]{1,0:T(8,128)S(1)} fusion(bf16[768,2304]{1,0:T(8,128)(2,1)} %param.6, bf16[256,768]{0,1:T(8,128)(2,1)S(1)} %pad_maximum_fusion.3), kind=kOutput, calls=%fused_computation.17 | convolution fusion | flops 150994944 | bytes 1769472 | tf_op jit(solution)/shard_map/dot_general | solution.py:180
  30.7 2.4 %convolution_add_fusion.1 = f32[128,768]{1,0:T(8,128)} fusion(f32[128,768]{1,0:T(8,128)S(1)} %fusion.5, bf16[768,2304]{1,0:T(8,128)(2,1)} %param.6, bf16[256,768]{0,1:T(8,128)(2,1)S(1)} %pad_maximum_fusion.3), kind=kOutput, calls=%fused_computation.6 | convolution fusion | flops 151093248 | bytes 2162688 | tf_op jit(solution)/shard_map/dot_general | solution.py:180
  33.1 7.7 %collective-permute-done.3 = f16[1168,192]{0,1:T(8,128)(2,1)S(1)} collective-permute-done((f16[1168,192]{0,1:T(8,128)(2,1)S(1)}, f16[1168,192]{0,1:T(8,128)(2,1)S(1)}, u32[]{:S(2)}, u32[]{:S(2)}) %collective-permute-start.3) | collective-permute-done | bytes 448544 | tf_op jit(solution)/shard_map/ppermute | solution.py:54
  40.8 0.5 slice.141
  42.1 0.5 copy.70
  42.7 0.8 %abs_reduce_fusion = (f32[]{:T(128)}, f32[4,288,192]{2,1,0:T(8,128)S(1)}) fusion(f32[4,288,192]{2,1,0:T(8,128)S(1)} %bitcast.112, f32[4,2,288,192]{3,2,1,0:T(8,128)S(1)} %bitcast.109, s32[]{:T(128)S(6)} %select_n.152), kind=kLoop, calls=%fused_computation.13 | loop fusion | flops 663551 | bytes 2654216 | tf_op jit(solution)/shard_map/reduce_max | solution.py:36
  44.7 2.7 %collective-permute-start.6 = (f16[304,192]{1,0:T(8,128)(2,1)S(1)}, f16[304,192]{1,0:T(8,128)(2,1)S(1)}, u32[]{:S(2)}, u32[]{:S(2)}) collective-permute-start(f16[304,192]{1,0:T(8,128)(2,1)S(1)} %concatenate.36), channel_id=1, source_target_pairs={{0,4},{1,5},{2,6},{3,7},{4,0},{5,1},{6,2},{7,3},{8,12},{9,13},{10,... | collective-permute-start | bytes 350216 | tf_op jit(solution)/shard_map/ppermute | solution.py:54
  47.3 1.6 %collective-permute-start.5 = (f16[304,192]{1,0:T(8,128)(2,1)S(1)}, f16[304,192]{1,0:T(8,128)(2,1)S(1)}, u32[]{:S(2)}, u32[]{:S(2)}) collective-permute-start(f16[304,192]{1,0:T(8,128)(2,1)S(1)} %concatenate.35), channel_id=1, source_target_pairs={{0,2},{1,3},{2,4},{3,5},{4,6},{5,7},{6,0},{7,1},{8,10},{9,11},{10,... | collective-permute-start | bytes 350216 | tf_op jit(solution)/shard_map/ppermute | solution.py:54
  48.9 2.2 %collective-permute-start.4 = (f16[304,192]{1,0:T(8,128)(2,1)S(1)}, f16[304,192]{1,0:T(8,128)(2,1)S(1)}, u32[]{:S(2)}, u32[]{:S(2)}) collective-permute-start(f16[304,192]{1,0:T(8,128)(2,1)S(1)} %concatenate.34), channel_id=1, source_target_pairs={{0,6},{1,7},{2,0},{3,1},{4,2},{5,3},{6,4},{7,5},{8,14},{9,15},{10,... | collective-permute-start | bytes 350216 | tf_op jit(solution)/shard_map/ppermute | solution.py:54
  51.1 2.3 %fusion.10 = bf16[1,128,768]{2,1,0:T(8,128)(2,1)} fusion(f32[128,768]{1,0:T(8,128)S(1)} %copy-done.3, f32[128,768]{1,0:T(8,128)S(1)} %copy-done.4, bf16[768,2304]{1,0:T(8,128)(2,1)} %param.6, bf16[256,768]{0,1:T(8,128)(2,1)S(1)} %copy-done.2), kind=kOutput, calls=%fused_computation.20 | convolution fusion | flops 151289856 | bytes 2359296 | tf_op jit(solution)/shard_map/dot_general | solution.py:180
  53.4 5.3 %collective-permute-done.6 = f16[304,192]{1,0:T(8,128)(2,1)S(1)} collective-permute-done((f16[304,192]{1,0:T(8,128)(2,1)S(1)}, f16[304,192]{1,0:T(8,128)(2,1)S(1)}, u32[]{:S(2)}, u32[]{:S(2)}) %collective-permute-start.6) | collective-permute-done | bytes 116768 | tf_op jit(solution)/shard_map/ppermute | solution.py:54
  58.7 0.5 slice.147
  60.0 0.6 slice.145
  61.2 0.5 slice.143
  62.5 0.9 %copy.63 = f32[192,288]{1,0:T(8,128)} copy(f32[192,288]{0,1:T(8,128)S(1)} %fusion.34) | data formatting | bytes 442368
  (58 shorter events, 3.4 us)
Async XLA Ops:
  0.6 2.2 %copy-start.5 = (bf16[1,128,768]{2,1,0:T(8,128)(2,1)S(1)}, bf16[1,128,768]{2,1,0:T(8,128)(2,1)}, u32[]{:S(2)}) copy-start(bf16[1,128,768]{2,1,0:T(8,128)(2,1)} %param.4) | copy-start | bytes 589828
  1.9 6.1 %copy-start = (s32[4]{0:T(128)S(1)}, s32[4]{0:T(128)}, u32[]{:S(2)}) copy-start(s32[4]{0:T(128)} %constant.148.clone) | copy-start | bytes 52
  1.9 21.0 %collective-permute-start.2 = (bf16[64,768]{0,1:T(8,128)(2,1)S(1)}, bf16[64,768]{0,1:T(8,128)(2,1)S(1)}, u32[]{:S(2)}, u32[]{:S(2)}) collective-permute-start(bf16[64,768]{0,1:T(8,128)(2,1)S(1)} %get-tuple-element.29), channel_id=1, source_target_pairs={{8,16},{16,8},{9,17},{17,9},{10,18},{18,10},{11,19},{19,11},{12,20... | collective-permute-start | bytes 294920 | tf_op jit(solution)/shard_map/ppermute | solution.py:127
  3.8 12.7 %collective-permute-start = (bf16[192,768]{1,0:T(8,128)(2,1)S(1)}, bf16[192,768]{1,0:T(8,128)(2,1)S(1)}, u32[]{:S(2)}, u32[]{:S(2)}) collective-permute-start(bf16[192,768]{1,0:T(8,128)(2,1)S(1)} %pad_maximum_fusion.4), channel_id=1, source_target_pairs={{0,16},{8,24},{16,0},{24,8},{1,17},{9,25},{17,1},{25,9},{2,18},{10... | collective-permute-start | bytes 884744 | tf_op jit(solution)/shard_map/ppermute | solution.py:116
  17.2 2.1 %collective-permute-start.1 = (bf16[384,768]{0,1:T(8,128)(2,1)S(1)}, bf16[384,768]{0,1:T(8,128)(2,1)S(1)}, u32[]{:S(2)}, u32[]{:S(2)}) collective-permute-start(bf16[384,768]{0,1:T(8,128)(2,1)S(1)} %pad_maximum_fusion.1), channel_id=1, source_target_pairs={{0,8},{8,0},{16,24},{24,16},{1,9},{9,1},{17,25},{25,17},{2,10},{10... | collective-permute-start | bytes 1769480 | tf_op jit(solution)/shard_map/ppermute | solution.py:122
  23.4 7.3 %copy-start.1 = (bf16[256,768]{0,1:T(8,128)(2,1)}, bf16[256,768]{0,1:T(8,128)(2,1)S(1)}, u32[]{:S(2)}) copy-start(bf16[256,768]{0,1:T(8,128)(2,1)S(1)} %pad_maximum_fusion.3) | copy-start | bytes 1179652
  27.5 13.4 %collective-permute-start.3 = (f16[1168,192]{0,1:T(8,128)(2,1)S(1)}, f16[1168,192]{0,1:T(8,128)(2,1)S(1)}, u32[]{:S(2)}, u32[]{:S(2)}) collective-permute-start(f16[1168,192]{0,1:T(8,128)(2,1)S(1)} %concatenate.33.clone), channel_id=1, source_target_pairs={{0,1},{1,0},{2,3},{3,2},{4,5},{5,4},{6,7},{7,6},{8,9},{9,8},{10,11... | collective-permute-start | bytes 1345544 | tf_op jit(solution)/shard_map/ppermute | solution.py:54
  43.6 7.6 %copy-start.2 = (bf16[256,768]{0,1:T(8,128)(2,1)S(1)}, bf16[256,768]{0,1:T(8,128)(2,1)}, u32[]{:S(2)}) copy-start(bf16[256,768]{0,1:T(8,128)(2,1)} %copy-done.1) | copy-start | bytes 1179652
  43.6 7.6 %copy-start.3 = (f32[128,768]{1,0:T(8,128)S(1)}, f32[128,768]{1,0:T(8,128)}, u32[]{:S(2)}) copy-start(f32[128,768]{1,0:T(8,128)} %get-tuple-element.6) | copy-start | bytes 1179652
  43.6 7.6 %copy-start.4 = (f32[128,768]{1,0:T(8,128)S(1)}, f32[128,768]{1,0:T(8,128)}, u32[]{:S(2)}) copy-start(f32[128,768]{1,0:T(8,128)} %convolution_add_fusion.1) | copy-start | bytes 1179652
  44.7 14.1 %collective-permute-start.6 = (f16[304,192]{1,0:T(8,128)(2,1)S(1)}, f16[304,192]{1,0:T(8,128)(2,1)S(1)}, u32[]{:S(2)}, u32[]{:S(2)}) collective-permute-start(f16[304,192]{1,0:T(8,128)(2,1)S(1)} %concatenate.36), channel_id=1, source_target_pairs={{0,4},{1,5},{2,6},{3,7},{4,0},{5,1},{6,2},{7,3},{8,12},{9,13},{10,... | collective-permute-start | bytes 350216 | tf_op jit(solution)/shard_map/ppermute | solution.py:54
  47.3 12.6 %collective-permute-start.5 = (f16[304,192]{1,0:T(8,128)(2,1)S(1)}, f16[304,192]{1,0:T(8,128)(2,1)S(1)}, u32[]{:S(2)}, u32[]{:S(2)}) collective-permute-start(f16[304,192]{1,0:T(8,128)(2,1)S(1)} %concatenate.35), channel_id=1, source_target_pairs={{0,2},{1,3},{2,4},{3,5},{4,6},{5,7},{6,0},{7,1},{8,10},{9,11},{10,... | collective-permute-start | bytes 350216 | tf_op jit(solution)/shard_map/ppermute | solution.py:54
  48.9 12.3 %collective-permute-start.4 = (f16[304,192]{1,0:T(8,128)(2,1)S(1)}, f16[304,192]{1,0:T(8,128)(2,1)S(1)}, u32[]{:S(2)}, u32[]{:S(2)}) collective-permute-start(f16[304,192]{1,0:T(8,128)(2,1)S(1)} %concatenate.34), channel_id=1, source_target_pairs={{0,6},{1,7},{2,0},{3,1},{4,2},{5,3},{6,4},{7,5},{8,14},{9,15},{10,... | collective-permute-start | bytes 350216 | tf_op jit(solution)/shard_map/ppermute | solution.py:54

commit v21 on v18

--- a/solution.py
+++ b/solution.py
@@ -65,7 +65,10 @@
     blocks = columns.reshape(outer, 2, -1, columns.shape[1])
     mine = lax.dynamic_index_in_dim(blocks, x, axis=1, keepdims=False)
     theirs = lax.dynamic_index_in_dim(blocks, 1 - x, axis=1, keepdims=False)
-    summed = with_layout_constraint(mine + send(theirs, pairs, exponent_of(theirs)), Layout((0, 1, 2)))
+    flipped = jnp.transpose(theirs, (2, 0, 1)).reshape(theirs.shape[2], -1)
+    received = send(flipped, pairs, exponent_of(flipped))
+    received = jnp.transpose(received.reshape(theirs.shape[2], theirs.shape[0], theirs.shape[1]), (1, 2, 0))
+    summed = with_layout_constraint(mine + received, Layout((0, 1, 2)))
     spread = exponent_of(summed)
     total = lax.dynamic_index_in_dim(summed, z, axis=0, keepdims=False)
     for shift in sorted(range(1, outer), key=lambda d: (min(d, outer - d), -d)):

time: 60.3 us -> 67.8 us (1.12)
  other arithmetic: 5.4 us -> 9.53 us
  local copies, waits for them, and re-layouts: 9.02 us -> 12.9 us
    reduce_max x2, other arithmetic: 1.63 us -> 3.31 us  [exponent_of(): jnp.max(jnp.max(jnp.abs(flat), axis=0, keepdims=True), axis=1, keepdims=T...]
    convert_element_type x0 -> x1, local copies, waits for them, and re-layouts: none -> 1.62 us  [encode(): scaled = (flat * jnp.exp2(HEADROOM - exponent)).astype(jnp.float16)]
    unnamed x17 -> x20, local copies, waits for them, and re-layouts: 1.84 us -> 3.44 us
    mul x0 -> x1, local copies, waits for them, and re-layouts: none -> 1.4 us  [decode(): values = packed[:-TAG].astype(jnp.float32) * jnp.exp2(exponent - HEADROOM)]
    dynamic_slice x0 -> x1, local copies, waits for them, and re-layouts: none -> 1.11 us  [reduce_over_batch(): theirs = lax.dynamic_index_in_dim(blocks, 1 - x, axis=1, keepdims=False)]
    slice x1 -> x0, local copies, waits for them, and re-layouts: 1.09 us -> none  [decode(): values = packed[:-TAG].astype(jnp.float32) * jnp.exp2(exponent - HEADROOM)]
    select_n x1, other arithmetic: 0.02 us -> 0.96 us  [gather_over_seq(): before = jnp.where(odd, near, far)]
    convert_element_type x2, other arithmetic: 0.25 us -> 1.15 us  [encode(): scaled = (flat * jnp.exp2(HEADROOM - exponent)).astype(jnp.float16)]
  transfers between devices with their start and end apart: 8 -> 8, of which waited for: 3 -> 3; matrix products, arithmetic and copies ran while one was open for 22% -> 21% of each run, Pallas kernels for 0% -> 0%
where the time goes in v21:
time: 67.8 us; the launch traced here: 67.3 us
  starting transfers between devices  18.6 us (27%)
  waiting for transfers between devices  13.6 us (20%)
  local copies, waits for them, and re-layouts  12.9 us (19%)
  other arithmetic  9.53 us (14%)
  matrix products  7.53 us (11%)
  between operations  5.15 us (8%)
    ppermute x4, waiting for transfers between devices, send(): arrived = lax.ppermute(encode(values, exponent), 'batch', perm)  13.1 us
    ppermute x4, starting transfers between devices, send(): arrived = lax.ppermute(encode(values, exponent), 'batch', perm)  8.16 us
    dot_general x3, matrix products, body(): jnp.dot(window, weight[:, tap_index * in_width:(tap_index + 1) * in_width...  6.23 us
    unnamed x20, local copies, waits for them, and re-layouts  3.44 us
    all_to_all x1, starting transfers between devices, body(): arrived = lax.all_to_all(channels, 'seq', 0, 0, tiled=True)  3.37 us
    reduce_max x2, other arithmetic, exponent_of(): jnp.max(jnp.max(jnp.abs(flat), axis=0, keepdims=True), axis=1, keepdims=T...  3.31 us
    ppermute x1, starting transfers between devices, gather_over_seq(): stack = jnp.concatenate([stack, lax.ppermute(stack, 'seq', pairs)], axis=0)  3.03 us
    ppermute x1, starting transfers between devices, gather_over_seq(): incoming = lax.ppermute(outgoing, 'seq', [(i, i ^ 1) for i in range(count)])  2.77 us
  transfers between devices with their start and end apart: 8, of which 3 were waited for; matrix products, arithmetic and copies ran while one was open for 21% of the time, Pallas kernels for 0%

profile of v21, /device:TPU:0, one launch (start us, length us, event | category | flops | bytes accessed | tf_op | source)
XLA Modules:
  0.0 67.3 jit_solution(18300506381102227655)
XLA Ops:
  0.7 1.1 %fusion.25 = bf16[1,128,768]{2,1,0:T(8,128)(2,1)S(1)} fusion(bf16[1,128,768]{2,1,0:T(8,128)(2,1)} %param.4), kind=kLoop, calls=%fused_computation.41 | loop fusion | flops 589824 | bytes 393216 | tf_op jit(solution)/shard_map/convert_element_type | solution.py:115
  1.7 3.0 %collective-permute-start = (bf16[1,128,768]{2,1,0:T(8,128)(2,1)S(1)}, bf16[1,128,768]{2,1,0:T(8,128)(2,1)S(1)}, u32[]{:S(2)}, u32[]{:S(2)}) collective-permute-start(bf16[1,128,768]{2,1,0:T(8,128)(2,1)S(1)} %fusion.25), channel_id=1, source_target_pairs={{0,16},{8,24},{16,0},{24,8},{1,17},{9,25},{17,1},{25,9},{2,18},{10... | collective-permute-start | bytes 589832 | tf_op jit(solution)/shard_map/ppermute | solution.py:92
  4.7 1.7 %copy.14 = bf16[768,128]{1,0:T(8,128)(2,1)} copy(bf16[768,128]{0,1:T(8,128)(2,1)} %bitcast.99) | data formatting | bytes 393216 | tf_op jit(solution)/shard_map/transpose | solution.py:120
  6.5 3.4 %all-to-all-start = ((bf16[4,192,128]{2,1,0:T(8,128)(2,1)}), bf16[4,192,128]{2,1,0:T(8,128)(2,1)S(1)}, u32[]{:S(2)}, u32[]{:S(2)}) async-start(bf16[4,192,128]{2,1,0:T(8,128)(2,1)} %bitcast.10), calls=%async_computation | async-start | bytes 393216 | tf_op jit(solution)/shard_map/all_to_all | solution.py:121
  9.9 0.7 select_bitcast_fusion
  10.5 1.3 %collective-permute-start.2 = (bf16[64,768]{1,0:T(8,128)(2,1)}, bf16[64,768]{1,0:T(8,128)(2,1)}, u32[]{:S(2)}, u32[]{:S(2)}) collective-permute-start(bf16[64,768]{1,0:T(8,128)(2,1)} %get-tuple-element.19), channel_id=1, source_target_pairs={{8,16},{16,8},{9,17},{17,9},{10,18},{18,10},{11,19},{19,11},{12,20... | collective-permute-start | bytes 294920 | tf_op jit(solution)/shard_map/ppermute | solution.py:99
  11.9 0.6 gather_fusion
  12.6 2.8 %collective-permute-start.1 = (bf16[320,768]{1,0:T(8,128)(2,1)S(1)}, bf16[320,768]{1,0:T(8,128)(2,1)S(1)}, u32[]{:S(2)}, u32[]{:S(2)}) collective-permute-start(bf16[320,768]{1,0:T(8,128)(2,1)S(1)} %pad_maximum_fusion.1), channel_id=1, source_target_pairs={{0,8},{8,0},{16,24},{24,16},{1,9},{9,1},{17,25},{25,17},{2,10},{10... | collective-permute-start | bytes 1474568 | tf_op jit(solution)/shard_map/ppermute | solution.py:95
  15.5 0.9 %fusion.21 = f32[128,768]{1,0:T(8,128)} fusion(bf16[1,128,768]{2,1,0:T(8,128)(2,1)S(1)} %copy-done.7), kind=kLoop, calls=%fused_computation.37 | loop fusion | flops 884736 | bytes 589824 | tf_op jit(solution)/shard_map/add | solution.py:31
  16.9 0.7 %copy-done.8 = bf16[320,768]{1,0:T(8,128)(2,1)} copy-done((bf16[320,768]{1,0:T(8,128)(2,1)}, bf16[320,768]{1,0:T(8,128)(2,1)S(1)}, u32[]{:S(2)}) %copy-start.8) | copy-done | bytes 491544
  17.8 0.6 gather_fusion.1
  20.1 1.0 %broadcast_select_fusion.1 = (bf16[64,768]{1,0:T(8,128)(2,1)S(1)}, bf16[64,768]{1,0:T(8,128)(2,1)S(1)}) fusion(bf16[64,768]{1,0:T(8,128)(2,1)} %collective-permute-done.2, pred[]{:T(512)S(6)} %eq.9, bf16[320,768]{1,0:T(8,128)(2,1)} %copy-done.8), kind=kLoop, calls=%fused_computation.68 | loop fusion | flops 98304 | bytes 393217 | tf_op jit(solution)/shard_map/jit(_where)/select_n | solution.py:100
  21.0 0.8 %pad_maximum_fusion.3 = bf16[256,768]{1,0:T(8,128)(2,1)} fusion(bf16[64,768]{1,0:T(8,128)(2,1)S(1)} %get-tuple-element.18, bf16[128,768]{1,0:T(8,128)(2,1)S(1)} %bitcast.100, bf16[64,768]{1,0:T(8,128)(2,1)S(1)} %get-tuple-element.17), kind=kLoop, calls=%fused_computation.45 | loop fusion | flops 1179648 | bytes 786432 | tf_op jit(solution)/shard_map/concatenate | solution.py:102
  21.8 1.1 %constant_dynamic-slice_fusion = f32[4,1,288,192]{3,2,1,0:T(8,128)} fusion(f32[4,2,288,192]{3,2,1,0:T(8,128)S(1)} %bitcast.96, s32[]{:T(128)S(6)} %select_n.124), kind=kLoop, calls=%fused_computation.75 | loop fusion | bytes 1769476 | tf_op jit(solution)/shard_map/jit(dynamic_index_in_dim)/dynamic_slice | solution.py:67
  22.9 1.8 %copy.28 = f32[4,1,288,192]{2,0,3,1:T(4,128)S(1)} copy(f32[4,1,288,192]{3,2,1,0:T(8,128)} %constant_dynamic-slice_fusion) | data formatting | bytes 1769472
  24.7 1.2 %abs_reduce_fusion.1 = f32[]{:T(128)} fusion(f32[4,1,288,192]{2,0,3,1:T(4,128)S(1)} %copy.28), kind=kLoop, calls=%fused_computation.10 | loop fusion | flops 442367 | bytes 884740 | tf_op jit(solution)/shard_map/reduce_max | solution.py:36
  26.7 1.0 %fusion.17 = f16[192,4,288]{2,1,0:T(4,128)(2,1)} fusion(f32[4,1,288,192]{2,0,3,1:T(4,128)S(1)} %copy.28, f32[]{:T(128)S(6)} %exp2.54), kind=kLoop, calls=%fused_computation.32 | loop fusion | flops 442368 | bytes 1327108 | tf_op jit(solution)/shard_map/convert_element_type | solution.py:42
  27.7 1.6 %convert_element_type.88 = f16[192,1152]{1,0:T(8,128)(2,1)S(1)} reshape(f16[192,4,288]{2,1,0:T(4,128)(2,1)} %fusion.17) | data formatting | bytes 884736 | tf_op jit(solution)/shard_map/convert_element_type | solution.py:42
  29.4 1.6 %collective-permute-start.3 = (f16[208,1152]{1,0:T(8,128)(2,1)S(1)}, f16[208,1152]{1,0:T(8,128)(2,1)S(1)}, u32[]{:S(2)}, u32[]{:S(2)}) collective-permute-start(f16[208,1152]{1,0:T(8,128)(2,1)S(1)} %concatenate.33), channel_id=1, source_target_pairs={{0,1},{1,0},{2,3},{3,2},{4,5},{5,4},{6,7},{7,6},{8,9},{9,8},{10,11... | collective-permute-start | bytes 1437704 | tf_op jit(solution)/shard_map/ppermute | solution.py:54
  31.0 1.6 %fusion.3 = f32[128,768]{1,0:T(8,128)S(1)} fusion(bf16[768,2304]{1,0:T(8,128)(2,1)} %param.6, bf16[256,768]{1,0:T(8,128)(2,1)S(1)} %copy-done.4), kind=kOutput, calls=%fused_computation.13 | convolution fusion | flops 150994944 | bytes 1769472 | tf_op jit(solution)/shard_map/dot_general | solution.py:146
  32.6 2.4 %convolution_add_fusion.1 = f32[128,768]{1,0:T(8,128)} fusion(f32[128,768]{1,0:T(8,128)S(1)} %fusion.3, bf16[768,2304]{1,0:T(8,128)(2,1)} %param.6, bf16[256,768]{1,0:T(8,128)(2,1)S(1)} %copy-done.4), kind=kOutput, calls=%fused_computation.5 | convolution fusion | flops 151093248 | bytes 2162688 | tf_op jit(solution)/shard_map/dot_general | solution.py:146
  35.0 7.8 %collective-permute-done.3 = f16[208,1152]{1,0:T(8,128)(2,1)S(1)} collective-permute-done((f16[208,1152]{1,0:T(8,128)(2,1)S(1)}, f16[208,1152]{1,0:T(8,128)(2,1)S(1)}, u32[]{:S(2)}, u32[]{:S(2)}) %collective-permute-start.3) | collective-permute-done | bytes 479264 | tf_op jit(solution)/shard_map/ppermute | solution.py:54
  42.7 0.5 slice.90
  44.0 1.4 %copy.21 = f32[192,1152]{0,1:T(8,128)} copy(f32[192,1152]{1,0:T(8,128)S(1)} %convert_multiply_fusion) | data formatting | bytes 1769472 | tf_op jit(solution)/shard_map/mul | solution.py:49
  45.4 2.1 %abs_reduce_fusion = (f32[]{:T(128)}, f32[4,288,192]{2,1,0:T(8,128)S(1)}) fusion(f32[4,288,192]{2,1,0:T(8,128)} %bitcast.98, f32[4,2,288,192]{3,2,1,0:T(8,128)S(1)} %bitcast.97, s32[]{:T(128)S(6)} %select_n.123), kind=kLoop, calls=%fused_computation.8 | loop fusion | flops 663551 | bytes 2654216 | tf_op jit(solution)/shard_map/reduce_max | solution.py:36
  48.5 2.7 %collective-permute-start.6 = (f16[304,192]{1,0:T(8,128)(2,1)S(1)}, f16[304,192]{1,0:T(8,128)(2,1)S(1)}, u32[]{:S(2)}, u32[]{:S(2)}) collective-permute-start(f16[304,192]{1,0:T(8,128)(2,1)S(1)} %concatenate.36), channel_id=1, source_target_pairs={{0,4},{1,5},{2,6},{3,7},{4,0},{5,1},{6,2},{7,3},{8,12},{9,13},{10,... | collective-permute-start | bytes 350216 | tf_op jit(solution)/shard_map/ppermute | solution.py:54
  51.2 1.6 %collective-permute-start.5 = (f16[304,192]{1,0:T(8,128)(2,1)S(1)}, f16[304,192]{1,0:T(8,128)(2,1)S(1)}, u32[]{:S(2)}, u32[]{:S(2)}) collective-permute-start(f16[304,192]{1,0:T(8,128)(2,1)S(1)} %concatenate.35), channel_id=1, source_target_pairs={{0,2},{1,3},{2,4},{3,5},{4,6},{5,7},{6,0},{7,1},{8,10},{9,11},{10,... | collective-permute-start | bytes 350216 | tf_op jit(solution)/shard_map/ppermute | solution.py:54
  52.9 2.3 %collective-permute-start.4 = (f16[304,192]{1,0:T(8,128)(2,1)S(1)}, f16[304,192]{1,0:T(8,128)(2,1)S(1)}, u32[]{:S(2)}, u32[]{:S(2)}) collective-permute-start(f16[304,192]{1,0:T(8,128)(2,1)S(1)} %concatenate.34), channel_id=1, source_target_pairs={{0,6},{1,7},{2,0},{3,1},{4,2},{5,3},{6,4},{7,5},{8,14},{9,15},{10,... | collective-permute-start | bytes 350216 | tf_op jit(solution)/shard_map/ppermute | solution.py:54
  55.2 2.3 %fusion.8 = bf16[1,128,768]{2,1,0:T(8,128)(2,1)} fusion(f32[128,768]{1,0:T(8,128)S(1)} %copy-done.3, f32[128,768]{1,0:T(8,128)S(1)} %copy-done.6, bf16[768,2304]{1,0:T(8,128)(2,1)} %param.6, bf16[256,768]{1,0:T(8,128)(2,1)S(1)} %copy-done.5), kind=kOutput, calls=%fused_computation.16 | convolution fusion | flops 151289856 | bytes 2359296 | tf_op jit(solution)/shard_map/dot_general | solution.py:146
  57.5 5.3 %collective-permute-done.6 = f16[304,192]{1,0:T(8,128)(2,1)S(1)} collective-permute-done((f16[304,192]{1,0:T(8,128)(2,1)S(1)}, f16[304,192]{1,0:T(8,128)(2,1)S(1)}, u32[]{:S(2)}, u32[]{:S(2)}) %collective-permute-start.6) | collective-permute-done | bytes 116768 | tf_op jit(solution)/shard_map/ppermute | solution.py:54
  64.0 0.5 slice.94
  66.4 0.9 %copy.22 = f32[192,288]{1,0:T(8,128)} copy(f32[192,288]{0,1:T(8,128)S(1)} %fusion.31) | data formatting | bytes 442368
  (47 shorter events, 3.9 us)
Async XLA Ops:
  0.6 11.2 %copy-start = (s32[4]{0:T(128)S(1)}, s32[4]{0:T(128)}, u32[]{:S(2)}) copy-start(s32[4]{0:T(128)} %constant.126.clone) | copy-start | bytes 52
  0.6 9.2 %copy-start.1 = (bf16[1,128,768]{2,1,0:T(8,128)(2,1)S(1)}, bf16[1,128,768]{2,1,0:T(8,128)(2,1)}, u32[]{:S(2)}) copy-start(bf16[1,128,768]{2,1,0:T(8,128)(2,1)} %param.5) | copy-start | bytes 589828
  1.7 10.8 %collective-permute-start = (bf16[1,128,768]{2,1,0:T(8,128)(2,1)S(1)}, bf16[1,128,768]{2,1,0:T(8,128)(2,1)S(1)}, u32[]{:S(2)}, u32[]{:S(2)}) collective-permute-start(bf16[1,128,768]{2,1,0:T(8,128)(2,1)S(1)} %fusion.25), channel_id=1, source_target_pairs={{0,16},{8,24},{16,0},{24,8},{1,17},{9,25},{17,1},{25,9},{2,18},{10... | collective-permute-start | bytes 589832 | tf_op jit(solution)/shard_map/ppermute | solution.py:92
  6.5 12.0 %all-to-all-start = ((bf16[4,192,128]{2,1,0:T(8,128)(2,1)}), bf16[4,192,128]{2,1,0:T(8,128)(2,1)S(1)}, u32[]{:S(2)}, u32[]{:S(2)}) async-start(bf16[4,192,128]{2,1,0:T(8,128)(2,1)} %bitcast.10), calls=%async_computation | async-start | bytes 393216 | tf_op jit(solution)/shard_map/all_to_all | solution.py:121
  10.5 9.5 %collective-permute-start.2 = (bf16[64,768]{1,0:T(8,128)(2,1)}, bf16[64,768]{1,0:T(8,128)(2,1)}, u32[]{:S(2)}, u32[]{:S(2)}) collective-permute-start(bf16[64,768]{1,0:T(8,128)(2,1)} %get-tuple-element.19), channel_id=1, source_target_pairs={{8,16},{16,8},{9,17},{17,9},{10,18},{18,10},{11,19},{19,11},{12,20... | collective-permute-start | bytes 294920 | tf_op jit(solution)/shard_map/ppermute | solution.py:99
  11.9 3.6 %copy-start.7 = (bf16[1,128,768]{2,1,0:T(8,128)(2,1)S(1)}, bf16[1,128,768]{2,1,0:T(8,128)(2,1)}, u32[]{:S(2)}) copy-start(bf16[1,128,768]{2,1,0:T(8,128)(2,1)} %param.4) | copy-start | bytes 589828
  12.6 4.3 %collective-permute-start.1 = (bf16[320,768]{1,0:T(8,128)(2,1)S(1)}, bf16[320,768]{1,0:T(8,128)(2,1)S(1)}, u32[]{:S(2)}, u32[]{:S(2)}) collective-permute-start(bf16[320,768]{1,0:T(8,128)(2,1)S(1)} %pad_maximum_fusion.1), channel_id=1, source_target_pairs={{0,8},{8,0},{16,24},{24,16},{1,9},{9,1},{17,25},{25,17},{2,10},{10... | collective-permute-start | bytes 1474568 | tf_op jit(solution)/shard_map/ppermute | solution.py:95
  16.9 0.8 %copy-start.8 = (bf16[320,768]{1,0:T(8,128)(2,1)}, bf16[320,768]{1,0:T(8,128)(2,1)S(1)}, u32[]{:S(2)}) copy-start(bf16[320,768]{1,0:T(8,128)(2,1)S(1)} %collective-permute-done.1) | copy-start | bytes 1474564
  19.9 1.2 %copy-start.2 = (bf16[1,128,768]{2,1,0:T(8,128)(2,1)S(1)}, bf16[1,128,768]{2,1,0:T(8,128)(2,1)}, u32[]{:S(2)}) copy-start(bf16[1,128,768]{2,1,0:T(8,128)(2,1)} %param.5) | copy-start | bytes 589828
  27.7 3.3 %copy-start.4 = (bf16[256,768]{1,0:T(8,128)(2,1)S(1)}, bf16[256,768]{1,0:T(8,128)(2,1)}, u32[]{:S(2)}) copy-start(bf16[256,768]{1,0:T(8,128)(2,1)} %pad_maximum_fusion.3) | copy-start | bytes 1179652
  29.4 13.3 %collective-permute-start.3 = (f16[208,1152]{1,0:T(8,128)(2,1)S(1)}, f16[208,1152]{1,0:T(8,128)(2,1)S(1)}, u32[]{:S(2)}, u32[]{:S(2)}) collective-permute-start(f16[208,1152]{1,0:T(8,128)(2,1)S(1)} %concatenate.33), channel_id=1, source_target_pairs={{0,1},{1,0},{2,3},{3,2},{4,5},{5,4},{6,7},{7,6},{8,9},{9,8},{10,11... | collective-permute-start | bytes 1437704 | tf_op jit(solution)/shard_map/ppermute | solution.py:54
  47.5 7.7 %copy-start.3 = (f32[128,768]{1,0:T(8,128)S(1)}, f32[128,768]{1,0:T(8,128)}, u32[]{:S(2)}) copy-start(f32[128,768]{1,0:T(8,128)} %fusion.21) | copy-start | bytes 1179652
  47.5 7.7 %copy-start.5 = (bf16[256,768]{1,0:T(8,128)(2,1)S(1)}, bf16[256,768]{1,0:T(8,128)(2,1)}, u32[]{:S(2)}) copy-start(bf16[256,768]{1,0:T(8,128)(2,1)} %pad_maximum_fusion.3) | copy-start | bytes 1179652
  47.5 7.7 %copy-start.6 = (f32[128,768]{1,0:T(8,128)S(1)}, f32[128,768]{1,0:T(8,128)}, u32[]{:S(2)}) copy-start(f32[128,768]{1,0:T(8,128)} %convolution_add_fusion.1) | copy-start | bytes 1179652
  48.5 14.3 %collective-permute-start.6 = (f16[304,192]{1,0:T(8,128)(2,1)S(1)}, f16[304,192]{1,0:T(8,128)(2,1)S(1)}, u32[]{:S(2)}, u32[]{:S(2)}) collective-permute-start(f16[304,192]{1,0:T(8,128)(2,1)S(1)} %concatenate.36), channel_id=1, source_target_pairs={{0,4},{1,5},{2,6},{3,7},{4,0},{5,1},{6,2},{7,3},{8,12},{9,13},{10,... | collective-permute-start | bytes 350216 | tf_op jit(solution)/shard_map/ppermute | solution.py:54
  51.2 12.8 %collective-permute-start.5 = (f16[304,192]{1,0:T(8,128)(2,1)S(1)}, f16[304,192]{1,0:T(8,128)(2,1)S(1)}, u32[]{:S(2)}, u32[]{:S(2)}) collective-permute-start(f16[304,192]{1,0:T(8,128)(2,1)S(1)} %concatenate.35), channel_id=1, source_target_pairs={{0,2},{1,3},{2,4},{3,5},{4,6},{5,7},{6,0},{7,1},{8,10},{9,11},{10,... | collective-permute-start | bytes 350216 | tf_op jit(solution)/shard_map/ppermute | solution.py:54
  52.9 12.4 %collective-permute-start.4 = (f16[304,192]{1,0:T(8,128)(2,1)S(1)}, f16[304,192]{1,0:T(8,128)(2,1)S(1)}, u32[]{:S(2)}, u32[]{:S(2)}) collective-permute-start(f16[304,192]{1,0:T(8,128)(2,1)S(1)} %concatenate.34), channel_id=1, source_target_pairs={{0,6},{1,7},{2,0},{3,1},{4,2},{5,3},{6,4},{7,5},{8,14},{9,15},{10,... | collective-permute-start | bytes 350216 | tf_op jit(solution)/shard_map/ppermute | solution.py:54

commit v22 on v18

--- a/solution.py
+++ b/solution.py
@@ -65,7 +65,12 @@
     blocks = columns.reshape(outer, 2, -1, columns.shape[1])
     mine = lax.dynamic_index_in_dim(blocks, x, axis=1, keepdims=False)
     theirs = lax.dynamic_index_in_dim(blocks, 1 - x, axis=1, keepdims=False)
-    summed = with_layout_constraint(mine + send(theirs, pairs, exponent_of(theirs)), Layout((0, 1, 2)))
+    half = outer // 2
+    exponent = exponent_of(theirs)
+    received = jnp.concatenate(
+        [send(theirs[:half], pairs, exponent), send(theirs[half:], pairs, exponent)], axis=0
+    )
+    summed = with_layout_constraint(mine + received, Layout((0, 1, 2)))
     spread = exponent_of(summed)
     total = lax.dynamic_index_in_dim(summed, z, axis=0, keepdims=False)
     for shift in sorted(range(1, outer), key=lambda d: (min(d, outer - d), -d)):

time: 60.3 us -> 59.8 us (level)
  local copies, waits for them, and re-layouts: 9.02 us -> 6.84 us
  between operations: 5.27 us -> 5.94 us
    slice x1 -> x0, local copies, waits for them, and re-layouts: 1.09 us -> none  [decode(): values = packed[:-TAG].astype(jnp.float32) * jnp.exp2(exponent - HEADROOM)]
    unnamed x17 -> x15, local copies, waits for them, and re-layouts: 1.84 us -> 0.9 us
    ppermute x4 -> x5, starting transfers between devices: 8.15 us -> 8.75 us  [send(): arrived = lax.ppermute(encode(values, exponent), 'batch', perm)]
    ppermute x4 -> x5, waiting for transfers between devices: 13.4 us -> 13.9 us  [send(): arrived = lax.ppermute(encode(values, exponent), 'batch', perm)]
    slice x4 -> x5, local copies, waits for them, and re-layouts: 2.83 us -> 2.62 us  [decode(): exponent = packed[-TAG:1 - TAG, 0:1].astype(jnp.float32)]
  transfers between devices with their start and end apart: 8 -> 9, of which waited for: 3 -> 4; matrix products, arithmetic and copies ran while one was open for 22% -> 23% of each run, Pallas kernels for 0% -> 0%
where the time goes in v22:
time: 59.8 us; the launch traced here: 59.3 us
  starting transfers between devices  19.2 us (32%)
  waiting for transfers between devices  14.5 us (24%)
  matrix products  7.53 us (13%)
  local copies, waits for them, and re-layouts  6.84 us (11%)
  between operations  5.94 us (10%)
  other arithmetic  5.37 us (9%)
    ppermute x5, waiting for transfers between devices, send(): arrived = lax.ppermute(encode(values, exponent), 'batch', perm)  13.9 us
    ppermute x5, starting transfers between devices, send(): arrived = lax.ppermute(encode(values, exponent), 'batch', perm)  8.75 us
    dot_general x3, matrix products, body(): jnp.dot(window, weight[:, tap_index * in_width:(tap_index + 1) * in_width...  6.23 us
    ppermute x1, starting transfers between devices, gather_over_seq(): incoming = lax.ppermute(outgoing, 'seq', [(i, i ^ 1) for i in range(count)])  3.38 us
    all_to_all x1, starting transfers between devices, body(): arrived = lax.all_to_all(channels, 'seq', 0, 0, tiled=True)  3.37 us
    ppermute x1, starting transfers between devices, gather_over_seq(): stack = jnp.concatenate([stack, lax.ppermute(stack, 'seq', pairs)], axis=0)  3.03 us
    slice x5, local copies, waits for them, and re-layouts, decode(): exponent = packed[-TAG:1 - TAG, 0:1].astype(jnp.float32)  2.62 us
    transpose x1, local copies, waits for them, and re-layouts, body(): channels = cotangent[0].T.reshape(seq_count, -1, length)  1.74 us
  transfers between devices with their start and end apart: 9, of which 4 were waited for; matrix products, arithmetic and copies ran while one was open for 23% of the time, Pallas kernels for 0%

profile of v22, /device:TPU:0, one launch (start us, length us, event | category | flops | bytes accessed | tf_op | source)
XLA Modules:
  0.0 59.3 jit_solution(17891872389711770579)
XLA Ops:
  0.7 1.1 %fusion.26 = bf16[1,128,768]{2,1,0:T(8,128)(2,1)S(1)} fusion(bf16[1,128,768]{2,1,0:T(8,128)(2,1)} %param.4), kind=kLoop, calls=%fused_computation.45 | loop fusion | flops 589824 | bytes 393216 | tf_op jit(solution)/shard_map/convert_element_type | solution.py:117
  1.7 3.0 %collective-permute-start = (bf16[1,128,768]{2,1,0:T(8,128)(2,1)S(1)}, bf16[1,128,768]{2,1,0:T(8,128)(2,1)S(1)}, u32[]{:S(2)}, u32[]{:S(2)}) collective-permute-start(bf16[1,128,768]{2,1,0:T(8,128)(2,1)S(1)} %fusion.26), channel_id=1, source_target_pairs={{0,16},{8,24},{16,0},{24,8},{1,17},{9,25},{17,1},{25,9},{2,18},{10... | collective-permute-start | bytes 589832 | tf_op jit(solution)/shard_map/ppermute | solution.py:94
  4.7 1.7 %copy.13 = bf16[768,128]{1,0:T(8,128)(2,1)} copy(bf16[768,128]{0,1:T(8,128)(2,1)} %bitcast.101) | data formatting | bytes 393216 | tf_op jit(solution)/shard_map/transpose | solution.py:122
  6.5 3.4 %all-to-all-start = ((bf16[4,192,128]{2,1,0:T(8,128)(2,1)}), bf16[4,192,128]{2,1,0:T(8,128)(2,1)S(1)}, u32[]{:S(2)}, u32[]{:S(2)}) async-start(bf16[4,192,128]{2,1,0:T(8,128)(2,1)} %bitcast.10), calls=%async_computation | async-start | bytes 393216 | tf_op jit(solution)/shard_map/all_to_all | solution.py:123
  9.9 0.7 %collective-permute-start.2 = (bf16[64,768]{1,0:T(8,128)(2,1)S(1)}, bf16[64,768]{1,0:T(8,128)(2,1)S(1)}, u32[]{:S(2)}, u32[]{:S(2)}) collective-permute-start(bf16[64,768]{1,0:T(8,128)(2,1)S(1)} %get-tuple-element.23), channel_id=1, source_target_pairs={{8,16},{16,8},{9,17},{17,9},{10,18},{18,10},{11,19},{19,11},{12,20... | collective-permute-start | bytes 294920 | tf_op jit(solution)/shard_map/ppermute | solution.py:101
  10.6 0.6 %gather_fusion = s32[4]{0:T(128)S(1)} fusion(s32[4]{0:T(128)S(1)} %copy-done, s32[1024]{0:T(1024)S(1)} %pad_clamp_fusion.1), kind=kCustom, calls=%fused_computation | custom fusion | bytes 48 | tf_op jit(solution)/shard_map/gather | solution.py:106
  11.4 3.4 %collective-permute-start.1 = (bf16[320,768]{1,0:T(8,128)(2,1)S(1)}, bf16[320,768]{1,0:T(8,128)(2,1)S(1)}, u32[]{:S(2)}, u32[]{:S(2)}) collective-permute-start(bf16[320,768]{1,0:T(8,128)(2,1)S(1)} %pad_maximum_fusion.1), channel_id=1, source_target_pairs={{0,8},{8,0},{16,24},{24,16},{1,9},{9,1},{17,25},{25,17},{2,10},{10... | collective-permute-start | bytes 1474568 | tf_op jit(solution)/shard_map/ppermute | solution.py:97
  14.9 0.9 %fusion.22 = f32[128,768]{1,0:T(8,128)} fusion(bf16[1,128,768]{2,1,0:T(8,128)(2,1)S(1)} %copy-done.6), kind=kLoop, calls=%fused_computation.41 | loop fusion | flops 884736 | bytes 589824 | tf_op jit(solution)/shard_map/add | solution.py:31
  15.8 0.5 collective-permute-done.1
  16.4 0.6 %gather_fusion.1 = bf16[4,128,768]{2,1,0:T(8,128)(2,1)S(1)} fusion(bf16[4,128,768]{2,1,0:T(8,128)(2,1)S(1)} %pad_maximum_fusion, s32[1024]{0:T(1024)S(1)} %pad_clamp_fusion), kind=kCustom, calls=%fused_computation.1 | custom fusion | bytes 1572880 | tf_op jit(solution)/shard_map/jit(_take)/gather | solution.py:107
  17.2 0.5 convolution_bitcast_fusion
  18.1 0.4 fusion.11
  18.7 0.8 %pad_maximum_fusion.3 = bf16[256,768]{1,0:T(8,128)(2,1)} fusion(bf16[64,768]{1,0:T(8,128)(2,1)S(1)} %get-tuple-element.22, bf16[128,768]{1,0:T(8,128)(2,1)S(1)} %bitcast.102, bf16[64,768]{1,0:T(8,128)(2,1)S(1)} %get-tuple-element.21), kind=kLoop, calls=%fused_computation.49 | loop fusion | flops 1179648 | bytes 786432 | tf_op jit(solution)/shard_map/concatenate | solution.py:104
  19.5 0.8 %abs_reduce_fusion.1 = (f32[]{:T(128)}, f32[4,1,288,192]{3,2,0,1:T(8,128)S(1)}) fusion(f32[4,2,288,192]{3,2,1,0:T(8,128)S(1)} %bitcast.97, s32[]{:T(128)S(6)} %select_n.124), kind=kLoop, calls=%fused_computation.9 | loop fusion | flops 442367 | bytes 1769480 | tf_op jit(solution)/shard_map/reduce_max | solution.py:36
  21.3 1.6 %collective-permute-start.4 = (f16[592,192]{1,0:T(8,128)(2,1)S(1)}, f16[592,192]{1,0:T(8,128)(2,1)S(1)}, u32[]{:S(2)}, u32[]{:S(2)}) collective-permute-start(f16[592,192]{1,0:T(8,128)(2,1)S(1)} %concatenate.40), channel_id=1, source_target_pairs={{0,1},{1,0},{2,3},{3,2},{4,5},{5,4},{6,7},{7,6},{8,9},{9,8},{10,11... | collective-permute-start | bytes 681992 | tf_op jit(solution)/shard_map/ppermute | solution.py:54
  22.9 0.6 %collective-permute-start.3 = (f16[592,192]{1,0:T(8,128)(2,1)S(1)}, f16[592,192]{1,0:T(8,128)(2,1)S(1)}, u32[]{:S(2)}, u32[]{:S(2)}) collective-permute-start(f16[592,192]{1,0:T(8,128)(2,1)S(1)} %concatenate.39), channel_id=1, source_target_pairs={{0,1},{1,0},{2,3},{3,2},{4,5},{5,4},{6,7},{7,6},{8,9},{9,8},{10,11... | collective-permute-start | bytes 681992 | tf_op jit(solution)/shard_map/ppermute | solution.py:54
  23.5 1.6 %fusion.3 = f32[128,768]{1,0:T(8,128)S(1)} fusion(bf16[768,2304]{1,0:T(8,128)(2,1)} %param.6, bf16[256,768]{1,0:T(8,128)(2,1)S(1)} %copy-done.3), kind=kOutput, calls=%fused_computation.13 | convolution fusion | flops 150994944 | bytes 1769472 | tf_op jit(solution)/shard_map/dot_general | solution.py:148
  25.1 2.4 %convolution_add_fusion.1 = f32[128,768]{1,0:T(8,128)} fusion(f32[128,768]{1,0:T(8,128)S(1)} %fusion.3, bf16[768,2304]{1,0:T(8,128)(2,1)} %param.6, bf16[256,768]{1,0:T(8,128)(2,1)S(1)} %copy-done.3), kind=kOutput, calls=%fused_computation.5 | convolution fusion | flops 151093248 | bytes 2162688 | tf_op jit(solution)/shard_map/dot_general | solution.py:148
  27.5 3.9 %collective-permute-done.4 = f16[592,192]{1,0:T(8,128)(2,1)S(1)} collective-permute-done((f16[592,192]{1,0:T(8,128)(2,1)S(1)}, f16[592,192]{1,0:T(8,128)(2,1)S(1)}, u32[]{:S(2)}, u32[]{:S(2)}) %collective-permute-start.4) | collective-permute-done | bytes 227360 | tf_op jit(solution)/shard_map/ppermute | solution.py:54
  31.3 0.5 slice.112
  32.5 4.7 %collective-permute-done.3 = f16[592,192]{1,0:T(8,128)(2,1)S(1)} collective-permute-done((f16[592,192]{1,0:T(8,128)(2,1)S(1)}, f16[592,192]{1,0:T(8,128)(2,1)S(1)}, u32[]{:S(2)}, u32[]{:S(2)}) %collective-permute-start.3) | collective-permute-done | bytes 227360 | tf_op jit(solution)/shard_map/ppermute | solution.py:54
  37.3 0.5 slice.109
  38.6 0.8 %abs_reduce_fusion = (f32[]{:T(128)}, f32[4,288,192]{2,1,0:T(8,128)S(1)}) fusion(f32[2,288,192]{2,1,0:T(8,128)S(1)} %bitcast.99, f32[2,288,192]{2,1,0:T(8,128)S(1)} %bitcast.100, f32[4,2,288,192]{3,2,1,0:T(8,128)S(1)} %bitcast.98, s32[]{:T(128)S(6)} %select_n.123), kind=kLoop, calls=%fused_computation.8 | loop fusion | flops 884735 | bytes 2654216 | tf_op jit(solution)/shard_map/reduce_max | solution.py:36
  40.4 2.6 %collective-permute-start.7 = (f16[304,192]{1,0:T(8,128)(2,1)S(1)}, f16[304,192]{1,0:T(8,128)(2,1)S(1)}, u32[]{:S(2)}, u32[]{:S(2)}) collective-permute-start(f16[304,192]{1,0:T(8,128)(2,1)S(1)} %concatenate.44), channel_id=1, source_target_pairs={{0,4},{1,5},{2,6},{3,7},{4,0},{5,1},{6,2},{7,3},{8,12},{9,13},{10,... | collective-permute-start | bytes 350216 | tf_op jit(solution)/shard_map/ppermute | solution.py:54
  43.1 1.6 %collective-permute-start.6 = (f16[304,192]{1,0:T(8,128)(2,1)S(1)}, f16[304,192]{1,0:T(8,128)(2,1)S(1)}, u32[]{:S(2)}, u32[]{:S(2)}) collective-permute-start(f16[304,192]{1,0:T(8,128)(2,1)S(1)} %concatenate.43), channel_id=1, source_target_pairs={{0,2},{1,3},{2,4},{3,5},{4,6},{5,7},{6,0},{7,1},{8,10},{9,11},{10,... | collective-permute-start | bytes 350216 | tf_op jit(solution)/shard_map/ppermute | solution.py:54
  44.8 2.3 %collective-permute-start.5 = (f16[304,192]{1,0:T(8,128)(2,1)S(1)}, f16[304,192]{1,0:T(8,128)(2,1)S(1)}, u32[]{:S(2)}, u32[]{:S(2)}) collective-permute-start(f16[304,192]{1,0:T(8,128)(2,1)S(1)} %concatenate.42), channel_id=1, source_target_pairs={{0,6},{1,7},{2,0},{3,1},{4,2},{5,3},{6,4},{7,5},{8,14},{9,15},{10,... | collective-permute-start | bytes 350216 | tf_op jit(solution)/shard_map/ppermute | solution.py:54
  47.1 2.3 %fusion.8 = bf16[1,128,768]{2,1,0:T(8,128)(2,1)} fusion(f32[128,768]{1,0:T(8,128)S(1)} %copy-done.2, f32[128,768]{1,0:T(8,128)S(1)} %copy-done.5, bf16[768,2304]{1,0:T(8,128)(2,1)} %param.6, bf16[256,768]{1,0:T(8,128)(2,1)S(1)} %copy-done.4), kind=kOutput, calls=%fused_computation.16 | convolution fusion | flops 151289856 | bytes 2359296 | tf_op jit(solution)/shard_map/dot_general | solution.py:148
  49.4 5.3 %collective-permute-done.7 = f16[304,192]{1,0:T(8,128)(2,1)S(1)} collective-permute-done((f16[304,192]{1,0:T(8,128)(2,1)S(1)}, f16[304,192]{1,0:T(8,128)(2,1)S(1)}, u32[]{:S(2)}, u32[]{:S(2)}) %collective-permute-start.7) | collective-permute-done | bytes 116768 | tf_op jit(solution)/shard_map/ppermute | solution.py:54
  54.7 0.5 slice.118
  55.9 0.5 slice.116
  57.0 0.6 slice.114
  58.5 0.9 %copy.20 = f32[192,288]{1,0:T(8,128)} copy(f32[192,288]{0,1:T(8,128)S(1)} %fusion.32) | data formatting | bytes 442368
  (44 shorter events, 1.8 us)
Async XLA Ops:
  0.6 10.0 %copy-start = (s32[4]{0:T(128)S(1)}, s32[4]{0:T(128)}, u32[]{:S(2)}) copy-start(s32[4]{0:T(128)} %constant.127.clone) | copy-start | bytes 52
  0.6 9.2 %copy-start.1 = (bf16[1,128,768]{2,1,0:T(8,128)(2,1)S(1)}, bf16[1,128,768]{2,1,0:T(8,128)(2,1)}, u32[]{:S(2)}) copy-start(bf16[1,128,768]{2,1,0:T(8,128)(2,1)} %param.5) | copy-start | bytes 589828
  1.7 9.6 %collective-permute-start = (bf16[1,128,768]{2,1,0:T(8,128)(2,1)S(1)}, bf16[1,128,768]{2,1,0:T(8,128)(2,1)S(1)}, u32[]{:S(2)}, u32[]{:S(2)}) collective-permute-start(bf16[1,128,768]{2,1,0:T(8,128)(2,1)S(1)} %fusion.26), channel_id=1, source_target_pairs={{0,16},{8,24},{16,0},{24,8},{1,17},{9,25},{17,1},{25,9},{2,18},{10... | collective-permute-start | bytes 589832 | tf_op jit(solution)/shard_map/ppermute | solution.py:94
  6.5 10.7 %all-to-all-start = ((bf16[4,192,128]{2,1,0:T(8,128)(2,1)}), bf16[4,192,128]{2,1,0:T(8,128)(2,1)S(1)}, u32[]{:S(2)}, u32[]{:S(2)}) async-start(bf16[4,192,128]{2,1,0:T(8,128)(2,1)} %bitcast.10), calls=%async_computation | async-start | bytes 393216 | tf_op jit(solution)/shard_map/all_to_all | solution.py:123
  9.9 8.8 %collective-permute-start.2 = (bf16[64,768]{1,0:T(8,128)(2,1)S(1)}, bf16[64,768]{1,0:T(8,128)(2,1)S(1)}, u32[]{:S(2)}, u32[]{:S(2)}) collective-permute-start(bf16[64,768]{1,0:T(8,128)(2,1)S(1)} %get-tuple-element.23), channel_id=1, source_target_pairs={{8,16},{16,8},{9,17},{17,9},{10,18},{18,10},{11,19},{19,11},{12,20... | collective-permute-start | bytes 294920 | tf_op jit(solution)/shard_map/ppermute | solution.py:101
  10.6 4.2 %copy-start.6 = (bf16[1,128,768]{2,1,0:T(8,128)(2,1)S(1)}, bf16[1,128,768]{2,1,0:T(8,128)(2,1)}, u32[]{:S(2)}) copy-start(bf16[1,128,768]{2,1,0:T(8,128)(2,1)} %param.4) | copy-start | bytes 589828
  11.4 4.9 %collective-permute-start.1 = (bf16[320,768]{1,0:T(8,128)(2,1)S(1)}, bf16[320,768]{1,0:T(8,128)(2,1)S(1)}, u32[]{:S(2)}, u32[]{:S(2)}) collective-permute-start(bf16[320,768]{1,0:T(8,128)(2,1)S(1)} %pad_maximum_fusion.1), channel_id=1, source_target_pairs={{0,8},{8,0},{16,24},{24,16},{1,9},{9,1},{17,25},{25,17},{2,10},{10... | collective-permute-start | bytes 1474568 | tf_op jit(solution)/shard_map/ppermute | solution.py:97
  21.0 2.5 %copy-start.3 = (bf16[256,768]{1,0:T(8,128)(2,1)S(1)}, bf16[256,768]{1,0:T(8,128)(2,1)}, u32[]{:S(2)}) copy-start(bf16[256,768]{1,0:T(8,128)(2,1)} %pad_maximum_fusion.3) | copy-start | bytes 1179652
  21.3 10.1 %collective-permute-start.4 = (f16[592,192]{1,0:T(8,128)(2,1)S(1)}, f16[592,192]{1,0:T(8,128)(2,1)S(1)}, u32[]{:S(2)}, u32[]{:S(2)}) collective-permute-start(f16[592,192]{1,0:T(8,128)(2,1)S(1)} %concatenate.40), channel_id=1, source_target_pairs={{0,1},{1,0},{2,3},{3,2},{4,5},{5,4},{6,7},{7,6},{8,9},{9,8},{10,11... | collective-permute-start | bytes 681992 | tf_op jit(solution)/shard_map/ppermute | solution.py:54
  22.9 14.4 %collective-permute-start.3 = (f16[592,192]{1,0:T(8,128)(2,1)S(1)}, f16[592,192]{1,0:T(8,128)(2,1)S(1)}, u32[]{:S(2)}, u32[]{:S(2)}) collective-permute-start(f16[592,192]{1,0:T(8,128)(2,1)S(1)} %concatenate.39), channel_id=1, source_target_pairs={{0,1},{1,0},{2,3},{3,2},{4,5},{5,4},{6,7},{7,6},{8,9},{9,8},{10,11... | collective-permute-start | bytes 681992 | tf_op jit(solution)/shard_map/ppermute | solution.py:54
  39.4 7.7 %copy-start.2 = (f32[128,768]{1,0:T(8,128)S(1)}, f32[128,768]{1,0:T(8,128)}, u32[]{:S(2)}) copy-start(f32[128,768]{1,0:T(8,128)} %fusion.22) | copy-start | bytes 1179652
  39.4 7.7 %copy-start.4 = (bf16[256,768]{1,0:T(8,128)(2,1)S(1)}, bf16[256,768]{1,0:T(8,128)(2,1)}, u32[]{:S(2)}) copy-start(bf16[256,768]{1,0:T(8,128)(2,1)} %pad_maximum_fusion.3) | copy-start | bytes 1179652
  39.4 7.7 %copy-start.5 = (f32[128,768]{1,0:T(8,128)S(1)}, f32[128,768]{1,0:T(8,128)}, u32[]{:S(2)}) copy-start(f32[128,768]{1,0:T(8,128)} %convolution_add_fusion.1) | copy-start | bytes 1179652
  40.4 14.3 %collective-permute-start.7 = (f16[304,192]{1,0:T(8,128)(2,1)S(1)}, f16[304,192]{1,0:T(8,128)(2,1)S(1)}, u32[]{:S(2)}, u32[]{:S(2)}) collective-permute-start(f16[304,192]{1,0:T(8,128)(2,1)S(1)} %concatenate.44), channel_id=1, source_target_pairs={{0,4},{1,5},{2,6},{3,7},{4,0},{5,1},{6,2},{7,3},{8,12},{9,13},{10,... | collective-permute-start | bytes 350216 | tf_op jit(solution)/shard_map/ppermute | solution.py:54
  43.1 12.8 %collective-permute-start.6 = (f16[304,192]{1,0:T(8,128)(2,1)S(1)}, f16[304,192]{1,0:T(8,128)(2,1)S(1)}, u32[]{:S(2)}, u32[]{:S(2)}) collective-permute-start(f16[304,192]{1,0:T(8,128)(2,1)S(1)} %concatenate.43), channel_id=1, source_target_pairs={{0,2},{1,3},{2,4},{3,5},{4,6},{5,7},{6,0},{7,1},{8,10},{9,11},{10,... | collective-permute-start | bytes 350216 | tf_op jit(solution)/shard_map/ppermute | solution.py:54
  44.8 12.2 %collective-permute-start.5 = (f16[304,192]{1,0:T(8,128)(2,1)S(1)}, f16[304,192]{1,0:T(8,128)(2,1)S(1)}, u32[]{:S(2)}, u32[]{:S(2)}) collective-permute-start(f16[304,192]{1,0:T(8,128)(2,1)S(1)} %concatenate.42), channel_id=1, source_target_pairs={{0,6},{1,7},{2,0},{3,1},{4,2},{5,3},{6,4},{7,5},{8,14},{9,15},{10,... | collective-permute-start | bytes 350216 | tf_op jit(solution)/shard_map/ppermute | solution.py:54

commit v23 on v18

--- a/solution.py
+++ b/solution.py
@@ -61,17 +61,17 @@
     me = lax.axis_index("batch")
     x = me % 2
     z = me // 2
-    pairs = [(i, i ^ 1) for i in range(count)]
     blocks = columns.reshape(outer, 2, -1, columns.shape[1])
-    mine = lax.dynamic_index_in_dim(blocks, x, axis=1, keepdims=False)
-    theirs = lax.dynamic_index_in_dim(blocks, 1 - x, axis=1, keepdims=False)
-    summed = with_layout_constraint(mine + send(theirs, pairs, exponent_of(theirs)), Layout((0, 1, 2)))
-    spread = exponent_of(summed)
-    total = lax.dynamic_index_in_dim(summed, z, axis=0, keepdims=False)
+    exponent = exponent_of(columns)
+    acc = lax.dynamic_index_in_dim(blocks, z, axis=0, keepdims=False)
     for shift in sorted(range(1, outer), key=lambda d: (min(d, outer - d), -d)):
-        target = lax.dynamic_index_in_dim(summed, (z + shift) % outer, axis=0, keepdims=False)
+        target = lax.dynamic_index_in_dim(blocks, (z + shift) % outer, axis=0, keepdims=False)
         perm = [(2 * q + p, 2 * ((q + shift) % outer) + p) for q in range(outer) for p in range(2)]
-        total = total + send(target, perm, spread)
+        acc = acc + send(target, perm, exponent)
+    acc = with_layout_constraint(acc, Layout((0, 1, 2)))
+    mine = lax.dynamic_index_in_dim(acc, x, axis=0, keepdims=False)
+    theirs = lax.dynamic_index_in_dim(acc, 1 - x, axis=0, keepdims=False)
+    total = mine + send(theirs, [(i, i ^ 1) for i in range(count)], exponent_of(theirs))
     return with_layout_constraint(total, Layout((0, 1))).T
 
 

time: 60.3 us -> 64.4 us (1.068)
  the two profiles are of different devices: /device:TPU:0 before, /device:TPU:16 now
where the time goes in v23:
time: 64.4 us; the launch traced here: 64 us
  waiting for transfers between devices  27.2 us (42%)
  starting transfers between devices  13.8 us (21%)
  local copies, waits for them, and re-layouts  7.63 us (12%)
  between operations  5.19 us (8%)
  matrix products  5.14 us (8%)
  other arithmetic  4.99 us (8%)
    ppermute x4, waiting for transfers between devices, send(): arrived = lax.ppermute(encode(values, exponent), 'batch', perm)  26 us
    ppermute x4, starting transfers between devices, send(): arrived = lax.ppermute(encode(values, exponent), 'batch', perm)  4.79 us
    dot_general x3, matrix products, body(): jnp.dot(window, weight[:, tap_index * in_width:(tap_index + 1) * in_width...  3.83 us
    ppermute x1, starting transfers between devices, gather_over_seq(): incoming = lax.ppermute(outgoing, 'seq', [(i, i ^ 1) for i in range(count)])  3.39 us
    all_to_all x1, starting transfers between devices, body(): arrived = lax.all_to_all(channels, 'seq', 0, 0, tiled=True)  3.37 us
    slice x4, local copies, waits for them, and re-layouts, decode(): exponent = packed[-TAG:1 - TAG, 0:1].astype(jnp.float32)  2.09 us
    transpose x1, local copies, waits for them, and re-layouts, body(): channels = cotangent[0].T.reshape(seq_count, -1, length)  1.74 us
    reduce_max x2, other arithmetic, exponent_of(): jnp.max(jnp.max(jnp.abs(flat), axis=0, keepdims=True), axis=1, keepdims=T...  1.63 us
  transfers between devices with their start and end apart: 8, of which 4 were waited for; matrix products, arithmetic and copies ran while one was open for 18% of the time, Pallas kernels for 0%

profile of v23, /device:TPU:16, one launch (start us, length us, event | category | flops | bytes accessed | tf_op | source)
XLA Modules:
  0.0 64.0 jit_solution(608355086046756595)
XLA Ops:
  0.6 1.1 %fusion.26 = bf16[1,128,768]{2,1,0:T(8,128)(2,1)S(1)} fusion(bf16[1,128,768]{2,1,0:T(8,128)(2,1)} %param.4), kind=kLoop, calls=%fused_computation.45 | loop fusion | flops 589824 | bytes 393216 | tf_op jit(solution)/shard_map/convert_element_type | solution.py:112
  1.7 1.6 %collective-permute-start = (bf16[1,128,768]{2,1,0:T(8,128)(2,1)S(1)}, bf16[1,128,768]{2,1,0:T(8,128)(2,1)S(1)}, u32[]{:S(2)}, u32[]{:S(2)}) collective-permute-start(bf16[1,128,768]{2,1,0:T(8,128)(2,1)S(1)} %fusion.26), channel_id=1, source_target_pairs={{0,16},{8,24},{16,0},{24,8},{1,17},{9,25},{17,1},{25,9},{2,18},{10... | collective-permute-start | bytes 589832 | tf_op jit(solution)/shard_map/ppermute | solution.py:89
  3.3 1.7 %copy.11 = bf16[768,128]{1,0:T(8,128)(2,1)} copy(bf16[768,128]{0,1:T(8,128)(2,1)} %bitcast.93) | data formatting | bytes 393216 | tf_op jit(solution)/shard_map/transpose | solution.py:117
  5.0 3.4 %all-to-all-start = ((bf16[4,192,128]{2,1,0:T(8,128)(2,1)}), bf16[4,192,128]{2,1,0:T(8,128)(2,1)S(1)}, u32[]{:S(2)}, u32[]{:S(2)}) async-start(bf16[4,192,128]{2,1,0:T(8,128)(2,1)} %bitcast.10), calls=%async_computation | async-start | bytes 393216 | tf_op jit(solution)/shard_map/all_to_all | solution.py:118
  8.4 1.0 %select_bitcast_fusion = (bf16[64,768]{1,0:T(8,128)(2,1)S(1)}, bf16[64,768]{1,0:T(8,128)(2,1)S(1)}) fusion(pred[]{:T(512)S(6)} %eq.9, bf16[1,128,768]{2,1,0:T(8,128)(2,1)} %param.5), kind=kLoop, calls=%fused_computation.64 | loop fusion | flops 98304 | bytes 393217 | tf_op jit(solution)/shard_map/jit(_where)/select_n | solution.py:96
  9.4 0.7 %collective-permute-start.2 = (bf16[64,768]{1,0:T(8,128)(2,1)S(1)}, bf16[64,768]{1,0:T(8,128)(2,1)S(1)}, u32[]{:S(2)}, u32[]{:S(2)}) collective-permute-start(bf16[64,768]{1,0:T(8,128)(2,1)S(1)} %get-tuple-element.17), channel_id=1, source_target_pairs={{8,16},{16,8},{9,17},{17,9},{10,18},{18,10},{11,19},{19,11},{12,20... | collective-permute-start | bytes 294920 | tf_op jit(solution)/shard_map/ppermute | solution.py:96
  10.1 1.3 %gather_fusion = s32[4]{0:T(128)S(1)} fusion(s32[4]{0:T(128)} %constant.126.clone, s32[1024]{0:T(1024)S(1)} %pad_clamp_fusion.1), kind=kCustom, calls=%fused_computation | custom fusion | bytes 48 | tf_op jit(solution)/shard_map/gather | solution.py:101
  11.5 3.4 %collective-permute-start.1 = (bf16[320,768]{1,0:T(8,128)(2,1)S(1)}, bf16[320,768]{1,0:T(8,128)(2,1)S(1)}, u32[]{:S(2)}, u32[]{:S(2)}) collective-permute-start(bf16[320,768]{1,0:T(8,128)(2,1)S(1)} %pad_maximum_fusion.1), channel_id=1, source_target_pairs={{0,8},{8,0},{16,24},{24,16},{1,9},{9,1},{17,25},{25,17},{2,10},{10... | collective-permute-start | bytes 1474568 | tf_op jit(solution)/shard_map/ppermute | solution.py:92
  15.1 1.2 %collective-permute-done.1 = bf16[320,768]{1,0:T(8,128)(2,1)S(1)} collective-permute-done((bf16[320,768]{1,0:T(8,128)(2,1)S(1)}, bf16[320,768]{1,0:T(8,128)(2,1)S(1)}, u32[]{:S(2)}, u32[]{:S(2)}) %collective-permute-start.1) | collective-permute-done | bytes 491552 | tf_op jit(solution)/shard_map/ppermute | solution.py:92
  16.5 0.6 gather_fusion.1
  17.3 0.5 convolution_bitcast_fusion
  17.8 0.4 fusion.12
  18.2 0.4 fusion.11
  18.9 0.7 %copy-done = bf16[1,128,768]{2,1,0:T(8,128)(2,1)S(1)} copy-done((bf16[1,128,768]{2,1,0:T(8,128)(2,1)S(1)}, bf16[1,128,768]{2,1,0:T(8,128)(2,1)}, u32[]{:S(2)}) %copy-start) | copy-done | bytes 196632
  19.6 1.0 %abs_reduce_fusion = f32[]{:T(128)} fusion(f32[2304,192]{1,0:T(8,128)S(1)} %maximum_multiply_fusion), kind=kLoop, calls=%fused_computation.3 | loop fusion | flops 884735 | bytes 1769476 | tf_op jit(solution)/shard_map/reduce_max | solution.py:36
  21.3 0.2 multiply_convert_fusion.2
  21.6 0.4 collective-permute-start.5
  22.1 1.6 %collective-permute-start.4 = (f16[592,192]{1,0:T(8,128)(2,1)S(1)}, f16[592,192]{1,0:T(8,128)(2,1)S(1)}, u32[]{:S(2)}, u32[]{:S(2)}) collective-permute-start(f16[592,192]{1,0:T(8,128)(2,1)S(1)} %concatenate.34), channel_id=1, source_target_pairs={{0,2},{1,3},{2,4},{3,5},{4,6},{5,7},{6,0},{7,1},{8,10},{9,11},{10,... | collective-permute-start | bytes 681992 | tf_op jit(solution)/shard_map/ppermute | solution.py:54
  23.8 1.2 %collective-permute-start.3 = (f16[592,192]{1,0:T(8,128)(2,1)S(1)}, f16[592,192]{1,0:T(8,128)(2,1)S(1)}, u32[]{:S(2)}, u32[]{:S(2)}) collective-permute-start(f16[592,192]{1,0:T(8,128)(2,1)S(1)} %concatenate.33), channel_id=1, source_target_pairs={{0,6},{1,7},{2,0},{3,1},{4,2},{5,3},{6,4},{7,5},{8,14},{9,15},{10,... | collective-permute-start | bytes 681992 | tf_op jit(solution)/shard_map/ppermute | solution.py:54
  25.0 0.3 fusion.3
  25.3 1.1 %convolution_add_fusion.1 = f32[128,768]{1,0:T(8,128)} fusion(f32[128,768]{1,0:T(8,128)S(1)} %fusion.3, bf16[768,2304]{1,0:T(8,128)(2,1)S(1)} %copy-done.2, bf16[256,768]{1,0:T(8,128)(2,1)S(1)} %pad_maximum_fusion.3), kind=kOutput, calls=%fused_computation.6 | convolution fusion | flops 151093248 | bytes 2162688 | tf_op jit(solution)/shard_map/dot_general | solution.py:143
  26.4 16.2 %collective-permute-done.5 = f16[592,192]{1,0:T(8,128)(2,1)S(1)} collective-permute-done((f16[592,192]{1,0:T(8,128)(2,1)S(1)}, f16[592,192]{1,0:T(8,128)(2,1)S(1)}, u32[]{:S(2)}, u32[]{:S(2)}) %collective-permute-start.5) | collective-permute-done | bytes 227360 | tf_op jit(solution)/shard_map/ppermute | solution.py:54
  42.6 0.5 slice.94
  43.8 7.7 %collective-permute-done.4 = f16[592,192]{1,0:T(8,128)(2,1)S(1)} collective-permute-done((f16[592,192]{1,0:T(8,128)(2,1)S(1)}, f16[592,192]{1,0:T(8,128)(2,1)S(1)}, u32[]{:S(2)}, u32[]{:S(2)}) %collective-permute-start.4) | collective-permute-done | bytes 227360 | tf_op jit(solution)/shard_map/ppermute | solution.py:54
  51.5 0.5 slice.92
  52.8 0.5 slice.90
  54.3 0.7 %abs_reduce_fusion.1 = f32[]{:T(128)} fusion(f32[2,288,192]{2,1,0:T(8,128)S(1)} %fusion.18, s32[]{:T(128)S(6)} %select_n.132), kind=kLoop, calls=%fused_computation.54 | loop fusion | flops 110591 | bytes 221192 | tf_op jit(solution)/shard_map/reduce_max | solution.py:36
  55.8 1.6 %collective-permute-start.6 = (f16[304,192]{1,0:T(8,128)(2,1)S(1)}, f16[304,192]{1,0:T(8,128)(2,1)S(1)}, u32[]{:S(2)}, u32[]{:S(2)}) collective-permute-start(f16[304,192]{1,0:T(8,128)(2,1)S(1)} %concatenate.36), channel_id=1, source_target_pairs={{0,1},{1,0},{2,3},{3,2},{4,5},{5,4},{6,7},{7,6},{8,9},{9,8},{10,11... | collective-permute-start | bytes 350216 | tf_op jit(solution)/shard_map/ppermute | solution.py:54
  57.4 2.4 %fusion.8 = bf16[1,128,768]{2,1,0:T(8,128)(2,1)} fusion(f32[128,768]{1,0:T(8,128)S(1)} %fusion.22, f32[128,768]{1,0:T(8,128)} %convolution_add_fusion.1, bf16[768,2304]{1,0:T(8,128)(2,1)} %param.6, bf16[256,768]{1,0:T(8,128)(2,1)} %copy-done.1), kind=kOutput, calls=%fused_computation.13 | convolution fusion | flops 151289856 | bytes 2359296 | tf_op jit(solution)/shard_map/dot_general | solution.py:143
  59.8 2.1 %collective-permute-done.6 = f16[304,192]{1,0:T(8,128)(2,1)S(1)} collective-permute-done((f16[304,192]{1,0:T(8,128)(2,1)S(1)}, f16[304,192]{1,0:T(8,128)(2,1)S(1)}, u32[]{:S(2)}, u32[]{:S(2)}) %collective-permute-start.6) | collective-permute-done | bytes 116768 | tf_op jit(solution)/shard_map/ppermute | solution.py:54
  61.9 0.5 slice.96
  63.1 0.9 %copy.16 = f32[192,288]{1,0:T(8,128)} copy(f32[192,288]{0,1:T(8,128)S(1)} %fusion.30) | data formatting | bytes 442368
  (36 shorter events, 1.5 us)
Async XLA Ops:
  0.6 14.4 %copy-start.3 = (bf16[1,128,768]{2,1,0:T(8,128)(2,1)S(1)}, bf16[1,128,768]{2,1,0:T(8,128)(2,1)}, u32[]{:S(2)}) copy-start(bf16[1,128,768]{2,1,0:T(8,128)(2,1)} %param.4) | copy-start | bytes 589828
  1.7 9.7 %collective-permute-start = (bf16[1,128,768]{2,1,0:T(8,128)(2,1)S(1)}, bf16[1,128,768]{2,1,0:T(8,128)(2,1)S(1)}, u32[]{:S(2)}, u32[]{:S(2)}) collective-permute-start(bf16[1,128,768]{2,1,0:T(8,128)(2,1)S(1)} %fusion.26), channel_id=1, source_target_pairs={{0,16},{8,24},{16,0},{24,8},{1,17},{9,25},{17,1},{25,9},{2,18},{10... | collective-permute-start | bytes 589832 | tf_op jit(solution)/shard_map/ppermute | solution.py:89
  5.0 12.2 %all-to-all-start = ((bf16[4,192,128]{2,1,0:T(8,128)(2,1)}), bf16[4,192,128]{2,1,0:T(8,128)(2,1)S(1)}, u32[]{:S(2)}, u32[]{:S(2)}) async-start(bf16[4,192,128]{2,1,0:T(8,128)(2,1)} %bitcast.10), calls=%async_computation | async-start | bytes 393216 | tf_op jit(solution)/shard_map/all_to_all | solution.py:118
  9.4 9.4 %collective-permute-start.2 = (bf16[64,768]{1,0:T(8,128)(2,1)S(1)}, bf16[64,768]{1,0:T(8,128)(2,1)S(1)}, u32[]{:S(2)}, u32[]{:S(2)}) collective-permute-start(bf16[64,768]{1,0:T(8,128)(2,1)S(1)} %get-tuple-element.17), channel_id=1, source_target_pairs={{8,16},{16,8},{9,17},{17,9},{10,18},{18,10},{11,19},{19,11},{12,20... | collective-permute-start | bytes 294920 | tf_op jit(solution)/shard_map/ppermute | solution.py:96
  11.5 4.9 %collective-permute-start.1 = (bf16[320,768]{1,0:T(8,128)(2,1)S(1)}, bf16[320,768]{1,0:T(8,128)(2,1)S(1)}, u32[]{:S(2)}, u32[]{:S(2)}) collective-permute-start(bf16[320,768]{1,0:T(8,128)(2,1)S(1)} %pad_maximum_fusion.1), channel_id=1, source_target_pairs={{0,8},{8,0},{16,24},{24,16},{1,9},{9,1},{17,25},{25,17},{2,10},{10... | collective-permute-start | bytes 1474568 | tf_op jit(solution)/shard_map/ppermute | solution.py:92
  18.6 0.9 %copy-start = (bf16[1,128,768]{2,1,0:T(8,128)(2,1)S(1)}, bf16[1,128,768]{2,1,0:T(8,128)(2,1)}, u32[]{:S(2)}) copy-start(bf16[1,128,768]{2,1,0:T(8,128)(2,1)} %param.5) | copy-start | bytes 589828
  19.6 34.6 %copy-start.1 = (bf16[256,768]{1,0:T(8,128)(2,1)}, bf16[256,768]{1,0:T(8,128)(2,1)S(1)}, u32[]{:S(2)}) copy-start(bf16[256,768]{1,0:T(8,128)(2,1)S(1)} %pad_maximum_fusion.3) | copy-start | bytes 1179652
  21.3 3.7 %copy-start.2 = (bf16[768,2304]{1,0:T(8,128)(2,1)S(1)}, bf16[768,2304]{1,0:T(8,128)(2,1)}, u32[]{:S(2)}) copy-start(bf16[768,2304]{1,0:T(8,128)(2,1)} %param.6) | copy-start | bytes 10616836
  21.6 21.0 %collective-permute-start.5 = (f16[592,192]{1,0:T(8,128)(2,1)S(1)}, f16[592,192]{1,0:T(8,128)(2,1)S(1)}, u32[]{:S(2)}, u32[]{:S(2)}) collective-permute-start(f16[592,192]{1,0:T(8,128)(2,1)S(1)} %concatenate.35), channel_id=1, source_target_pairs={{0,4},{1,5},{2,6},{3,7},{4,0},{5,1},{6,2},{7,3},{8,12},{9,13},{10,... | collective-permute-start | bytes 681992 | tf_op jit(solution)/shard_map/ppermute | solution.py:54
  22.1 29.4 %collective-permute-start.4 = (f16[592,192]{1,0:T(8,128)(2,1)S(1)}, f16[592,192]{1,0:T(8,128)(2,1)S(1)}, u32[]{:S(2)}, u32[]{:S(2)}) collective-permute-start(f16[592,192]{1,0:T(8,128)(2,1)S(1)} %concatenate.34), channel_id=1, source_target_pairs={{0,2},{1,3},{2,4},{3,5},{4,6},{5,7},{6,0},{7,1},{8,10},{9,11},{10,... | collective-permute-start | bytes 681992 | tf_op jit(solution)/shard_map/ppermute | solution.py:54
  23.8 28.9 %collective-permute-start.3 = (f16[592,192]{1,0:T(8,128)(2,1)S(1)}, f16[592,192]{1,0:T(8,128)(2,1)S(1)}, u32[]{:S(2)}, u32[]{:S(2)}) collective-permute-start(f16[592,192]{1,0:T(8,128)(2,1)S(1)} %concatenate.33), channel_id=1, source_target_pairs={{0,6},{1,7},{2,0},{3,1},{4,2},{5,3},{6,4},{7,5},{8,14},{9,15},{10,... | collective-permute-start | bytes 681992 | tf_op jit(solution)/shard_map/ppermute | solution.py:54
  55.8 6.0 %collective-permute-start.6 = (f16[304,192]{1,0:T(8,128)(2,1)S(1)}, f16[304,192]{1,0:T(8,128)(2,1)S(1)}, u32[]{:S(2)}, u32[]{:S(2)}) collective-permute-start(f16[304,192]{1,0:T(8,128)(2,1)S(1)} %concatenate.36), channel_id=1, source_target_pairs={{0,1},{1,0},{2,3},{3,2},{4,5},{5,4},{6,7},{7,6},{8,9},{9,8},{10,11... | collective-permute-start | bytes 350216 | tf_op jit(solution)/shard_map/ppermute | solution.py:54

commit v24 on v18

--- a/solution.py
+++ b/solution.py
@@ -45,7 +45,7 @@
 
 
 def decode(packed, shape):
-    exponent = packed[-TAG:1 - TAG, 0:1].astype(jnp.float32)
+    exponent = packed[-TAG:1 - TAG].astype(jnp.float32)
     values = packed[:-TAG].astype(jnp.float32) * jnp.exp2(exponent - HEADROOM)
     return values.reshape(shape)
 

time: 60.3 us -> 57.8 us (0.959)
  local copies, waits for them, and re-layouts: 9.02 us -> 6.26 us
  between operations: 5.27 us -> 2.52 us
  waiting for transfers between devices: 13.9 us -> 16 us
  other arithmetic: 5.4 us -> 6.26 us
    slice x4 -> x0, local copies, waits for them, and re-layouts: 2.83 us -> none  [decode(): exponent = packed[-TAG:1 - TAG, 0:1].astype(jnp.float32)]
    ppermute x4, waiting for transfers between devices: 13.4 us -> 15.5 us  [send(): arrived = lax.ppermute(encode(values, exponent), 'batch', perm)]
    exp2 x0 -> x4, other arithmetic: none -> 0.85 us  [decode(): values = packed[:-TAG].astype(jnp.float32) * jnp.exp2(exponent - HEADROOM)]
    unnamed x17 -> x18, local copies, waits for them, and re-layouts: 1.84 us -> 1.92 us
  transfers between devices with their start and end apart: 8 -> 8, of which waited for: 3 -> 4; matrix products, arithmetic and copies ran while one was open for 22% -> 21% of each run, Pallas kernels for 0% -> 0%
where the time goes in v24:
time: 57.8 us; the launch traced here: 57.3 us
  starting transfers between devices  18.6 us (32%)
  waiting for transfers between devices  16 us (28%)
  matrix products  7.63 us (13%)
  local copies, waits for them, and re-layouts  6.26 us (11%)
  other arithmetic  6.26 us (11%)
  between operations  2.52 us (4%)
    ppermute x4, waiting for transfers between devices, send(): arrived = lax.ppermute(encode(values, exponent), 'batch', perm)  15.5 us
    ppermute x4, starting transfers between devices, send(): arrived = lax.ppermute(encode(values, exponent), 'batch', perm)  8.15 us
    dot_general x3, matrix products, body(): jnp.dot(window, weight[:, tap_index * in_width:(tap_index + 1) * in_width...  6.33 us
    ppermute x1, starting transfers between devices, gather_over_seq(): incoming = lax.ppermute(outgoing, 'seq', [(i, i ^ 1) for i in range(count)])  3.38 us
    all_to_all x1, starting transfers between devices, body(): arrived = lax.all_to_all(channels, 'seq', 0, 0, tiled=True)  3.37 us
    ppermute x1, starting transfers between devices, gather_over_seq(): stack = jnp.concatenate([stack, lax.ppermute(stack, 'seq', pairs)], axis=0)  3.03 us
    unnamed x18, local copies, waits for them, and re-layouts  1.92 us
    transpose x1, local copies, waits for them, and re-layouts, body(): channels = cotangent[0].T.reshape(seq_count, -1, length)  1.74 us
  transfers between devices with their start and end apart: 8, of which 4 were waited for; matrix products, arithmetic and copies ran while one was open for 21% of the time, Pallas kernels for 0%

profile of v24, /device:TPU:0, one launch (start us, length us, event | category | flops | bytes accessed | tf_op | source)
XLA Modules:
  0.0 57.3 jit_solution(1727838163693574983)
XLA Ops:
  0.7 1.1 %fusion.26 = bf16[1,128,768]{2,1,0:T(8,128)(2,1)S(1)} fusion(bf16[1,128,768]{2,1,0:T(8,128)(2,1)} %param.4), kind=kLoop, calls=%fused_computation.42 | loop fusion | flops 589824 | bytes 393216 | tf_op jit(solution)/shard_map/convert_element_type | solution.py:112
  1.7 3.0 %collective-permute-start = (bf16[1,128,768]{2,1,0:T(8,128)(2,1)S(1)}, bf16[1,128,768]{2,1,0:T(8,128)(2,1)S(1)}, u32[]{:S(2)}, u32[]{:S(2)}) collective-permute-start(bf16[1,128,768]{2,1,0:T(8,128)(2,1)S(1)} %fusion.26), channel_id=1, source_target_pairs={{0,16},{8,24},{16,0},{24,8},{1,17},{9,25},{17,1},{25,9},{2,18},{10... | collective-permute-start | bytes 589832 | tf_op jit(solution)/shard_map/ppermute | solution.py:89
  4.7 1.7 %copy.21 = bf16[768,128]{1,0:T(8,128)(2,1)} copy(bf16[768,128]{0,1:T(8,128)(2,1)} %bitcast.103) | data formatting | bytes 393216 | tf_op jit(solution)/shard_map/transpose | solution.py:117
  6.5 3.4 %all-to-all-start = ((bf16[4,192,128]{2,1,0:T(8,128)(2,1)}), bf16[4,192,128]{2,1,0:T(8,128)(2,1)S(1)}, u32[]{:S(2)}, u32[]{:S(2)}) async-start(bf16[4,192,128]{2,1,0:T(8,128)(2,1)} %bitcast.10), calls=%async_computation | async-start | bytes 393216 | tf_op jit(solution)/shard_map/all_to_all | solution.py:118
  9.9 0.7 %collective-permute-start.2 = (bf16[64,768]{1,0:T(8,128)(2,1)S(1)}, bf16[64,768]{1,0:T(8,128)(2,1)S(1)}, u32[]{:S(2)}, u32[]{:S(2)}) collective-permute-start(bf16[64,768]{1,0:T(8,128)(2,1)S(1)} %get-tuple-element.21), channel_id=1, source_target_pairs={{8,16},{16,8},{9,17},{17,9},{10,18},{18,10},{11,19},{19,11},{12,20... | collective-permute-start | bytes 294920 | tf_op jit(solution)/shard_map/ppermute | solution.py:96
  10.6 0.6 %gather_fusion = s32[4]{0:T(128)S(1)} fusion(s32[4]{0:T(128)S(1)} %copy-done, s32[1024]{0:T(1024)S(1)} %pad_clamp_fusion.1), kind=kCustom, calls=%fused_computation | custom fusion | bytes 48 | tf_op jit(solution)/shard_map/gather | solution.py:101
  11.4 3.4 %collective-permute-start.1 = (bf16[320,768]{1,0:T(8,128)(2,1)S(1)}, bf16[320,768]{1,0:T(8,128)(2,1)S(1)}, u32[]{:S(2)}, u32[]{:S(2)}) collective-permute-start(bf16[320,768]{1,0:T(8,128)(2,1)S(1)} %pad_maximum_fusion.1), channel_id=1, source_target_pairs={{0,8},{8,0},{16,24},{24,16},{1,9},{9,1},{17,25},{25,17},{2,10},{10... | collective-permute-start | bytes 1474568 | tf_op jit(solution)/shard_map/ppermute | solution.py:92
  14.9 0.9 %fusion.22 = f32[128,768]{1,0:T(8,128)} fusion(bf16[1,128,768]{2,1,0:T(8,128)(2,1)S(1)} %copy-done.6), kind=kLoop, calls=%fused_computation.38 | loop fusion | flops 884736 | bytes 589824 | tf_op jit(solution)/shard_map/add | solution.py:31
  15.8 0.5 collective-permute-done.1
  16.4 0.6 %gather_fusion.1 = bf16[4,128,768]{2,1,0:T(8,128)(2,1)S(1)} fusion(bf16[4,128,768]{2,1,0:T(8,128)(2,1)S(1)} %pad_maximum_fusion, s32[1024]{0:T(1024)S(1)} %pad_clamp_fusion), kind=kCustom, calls=%fused_computation.1 | custom fusion | bytes 1572880 | tf_op jit(solution)/shard_map/jit(_take)/gather | solution.py:102
  17.2 0.5 convolution_bitcast_fusion
  17.7 0.4 fusion.14
  18.1 0.4 fusion.13
  18.5 0.2 maximum_multiply_fusion
  18.7 0.8 %pad_maximum_fusion.3 = bf16[256,768]{1,0:T(8,128)(2,1)} fusion(bf16[64,768]{1,0:T(8,128)(2,1)S(1)} %get-tuple-element.20, bf16[128,768]{1,0:T(8,128)(2,1)S(1)} %bitcast.104, bf16[64,768]{1,0:T(8,128)(2,1)S(1)} %get-tuple-element.19), kind=kLoop, calls=%fused_computation.46 | loop fusion | flops 1179648 | bytes 786432 | tf_op jit(solution)/shard_map/concatenate | solution.py:99
  19.5 0.8 %fusion.1 = f32[]{:T(128)} fusion(f32[4,2,288,192]{3,2,1,0:T(8,128)S(1)} %bitcast.98, s32[]{:T(128)S(6)} %select_n.124), kind=kLoop, calls=%fused_computation.10 | loop fusion | flops 442367 | bytes 884744 | tf_op jit(solution)/shard_map/reduce_max | solution.py:36
  21.2 0.4 copy.39
  21.7 1.6 %collective-permute-start.3 = (f16[1168,192]{0,1:T(8,128)(2,1)S(1)}, f16[1168,192]{0,1:T(8,128)(2,1)}, u32[]{:S(2)}, u32[]{:S(2)}) collective-permute-start(f16[1168,192]{0,1:T(8,128)(2,1)S(1)} %concatenate.33.clone), channel_id=1, source_target_pairs={{0,1},{1,0},{2,3},{3,2},{4,5},{5,4},{6,7},{7,6},{8,9},{9,8},{10,11... | collective-permute-start | bytes 1345544 | tf_op jit(solution)/shard_map/ppermute | solution.py:54
  23.3 1.7 %fusion.5 = f32[128,768]{1,0:T(8,128)S(1)} fusion(bf16[768,2304]{1,0:T(8,128)(2,1)} %param.6, bf16[256,768]{1,0:T(8,128)(2,1)} %pad_maximum_fusion.3), kind=kOutput, calls=%fused_computation.16 | convolution fusion | flops 150994944 | bytes 1769472 | tf_op jit(solution)/shard_map/dot_general | solution.py:143
  25.1 2.3 %convolution_add_fusion.1 = f32[128,768]{1,0:T(8,128)} fusion(f32[128,768]{1,0:T(8,128)S(1)} %fusion.5, bf16[768,2304]{1,0:T(8,128)(2,1)} %param.6, bf16[256,768]{1,0:T(8,128)(2,1)S(1)} %copy-done.3), kind=kOutput, calls=%fused_computation.5 | convolution fusion | flops 151093248 | bytes 2162688 | tf_op jit(solution)/shard_map/dot_general | solution.py:143
  27.4 8.0 %collective-permute-done.3 = f16[1168,192]{0,1:T(8,128)(2,1)} collective-permute-done((f16[1168,192]{0,1:T(8,128)(2,1)S(1)}, f16[1168,192]{0,1:T(8,128)(2,1)}, u32[]{:S(2)}, u32[]{:S(2)}) %collective-permute-start.3) | collective-permute-done | bytes 448544 | tf_op jit(solution)/shard_map/ppermute | solution.py:54
  35.4 1.1 %slice.89 = f16[1152,192]{0,1:T(8,128)(2,1)S(1)} slice(f16[1168,192]{0,1:T(8,128)(2,1)} %collective-permute-done.3), slice={[0:1152], [0:192]} | slice | bytes 884736 | tf_op jit(solution)/shard_map/slice | solution.py:49
  36.5 0.5 copy.37
  37.0 0.8 %multiply_exponential_fusion = f32[1,192]{0,1:T(8,128)S(1)} fusion(f16[1168,192]{0,1:T(8,128)(2,1)} %collective-permute-done.3), kind=kLoop, calls=%fused_computation.66 | loop fusion | flops 576 | bytes 1152 | tf_op jit(solution)/shard_map/exp2 | solution.py:49
  38.0 0.8 %abs_reduce_fusion = (f32[]{:T(128)}, f32[4,288,192]{2,1,0:T(8,128)S(1)}) fusion(f32[4,288,192]{2,1,0:T(8,128)S(1)} %bitcast.101, f32[4,2,288,192]{3,2,1,0:T(8,128)S(1)} %bitcast.100, s32[]{:T(128)S(6)} %select_n.123), kind=kLoop, calls=%fused_computation.12 | loop fusion | flops 663551 | bytes 2654216 | tf_op jit(solution)/shard_map/reduce_max | solution.py:36
  39.9 2.6 %collective-permute-start.6 = (f16[304,192]{1,0:T(8,128)(2,1)S(1)}, f16[304,192]{1,0:T(8,128)(2,1)S(1)}, u32[]{:S(2)}, u32[]{:S(2)}) collective-permute-start(f16[304,192]{1,0:T(8,128)(2,1)S(1)} %concatenate.36), channel_id=1, source_target_pairs={{0,4},{1,5},{2,6},{3,7},{4,0},{5,1},{6,2},{7,3},{8,12},{9,13},{10,... | collective-permute-start | bytes 350216 | tf_op jit(solution)/shard_map/ppermute | solution.py:54
  42.5 2.3 %fusion.10 = bf16[1,128,768]{2,1,0:T(8,128)(2,1)} fusion(f32[128,768]{1,0:T(8,128)S(1)} %copy-done.2, f32[128,768]{1,0:T(8,128)S(1)} %copy-done.5, bf16[768,2304]{1,0:T(8,128)(2,1)} %param.6, bf16[256,768]{1,0:T(8,128)(2,1)S(1)} %copy-done.4), kind=kOutput, calls=%fused_computation.19 | convolution fusion | flops 151289856 | bytes 2359296 | tf_op jit(solution)/shard_map/dot_general | solution.py:143
  44.8 1.6 %collective-permute-start.5 = (f16[304,192]{1,0:T(8,128)(2,1)S(1)}, f16[304,192]{1,0:T(8,128)(2,1)S(1)}, u32[]{:S(2)}, u32[]{:S(2)}) collective-permute-start(f16[304,192]{1,0:T(8,128)(2,1)S(1)} %concatenate.35), channel_id=1, source_target_pairs={{0,2},{1,3},{2,4},{3,5},{4,6},{5,7},{6,0},{7,1},{8,10},{9,11},{10,... | collective-permute-start | bytes 350216 | tf_op jit(solution)/shard_map/ppermute | solution.py:54
  46.5 2.3 %collective-permute-start.4 = (f16[304,192]{1,0:T(8,128)(2,1)S(1)}, f16[304,192]{1,0:T(8,128)(2,1)S(1)}, u32[]{:S(2)}, u32[]{:S(2)}) collective-permute-start(f16[304,192]{1,0:T(8,128)(2,1)S(1)} %concatenate.34), channel_id=1, source_target_pairs={{0,6},{1,7},{2,0},{3,1},{4,2},{5,3},{6,4},{7,5},{8,14},{9,15},{10,... | collective-permute-start | bytes 350216 | tf_op jit(solution)/shard_map/ppermute | solution.py:54
  48.8 5.3 %collective-permute-done.6 = f16[304,192]{1,0:T(8,128)(2,1)S(1)} collective-permute-done((f16[304,192]{1,0:T(8,128)(2,1)S(1)}, f16[304,192]{1,0:T(8,128)(2,1)S(1)}, u32[]{:S(2)}, u32[]{:S(2)}) %collective-permute-start.6) | collective-permute-done | bytes 116768 | tf_op jit(solution)/shard_map/ppermute | solution.py:54
  54.2 2.2 %collective-permute-done.4 = f16[304,192]{1,0:T(8,128)(2,1)S(1)} collective-permute-done((f16[304,192]{1,0:T(8,128)(2,1)S(1)}, f16[304,192]{1,0:T(8,128)(2,1)S(1)}, u32[]{:S(2)}, u32[]{:S(2)}) %collective-permute-start.4) | collective-permute-done | bytes 116768 | tf_op jit(solution)/shard_map/ppermute | solution.py:54
  56.4 0.9 %copy.30 = f32[192,288]{1,0:T(8,128)} copy(f32[192,288]{0,1:T(8,128)S(1)} %fusion.32) | data formatting | bytes 442368
  (43 shorter events, 1.3 us)
Async XLA Ops:
  0.6 10.0 %copy-start = (s32[4]{0:T(128)S(1)}, s32[4]{0:T(128)}, u32[]{:S(2)}) copy-start(s32[4]{0:T(128)} %constant.129.clone) | copy-start | bytes 52
  0.6 9.2 %copy-start.1 = (bf16[1,128,768]{2,1,0:T(8,128)(2,1)S(1)}, bf16[1,128,768]{2,1,0:T(8,128)(2,1)}, u32[]{:S(2)}) copy-start(bf16[1,128,768]{2,1,0:T(8,128)(2,1)} %param.5) | copy-start | bytes 589828
  1.7 9.6 %collective-permute-start = (bf16[1,128,768]{2,1,0:T(8,128)(2,1)S(1)}, bf16[1,128,768]{2,1,0:T(8,128)(2,1)S(1)}, u32[]{:S(2)}, u32[]{:S(2)}) collective-permute-start(bf16[1,128,768]{2,1,0:T(8,128)(2,1)S(1)} %fusion.26), channel_id=1, source_target_pairs={{0,16},{8,24},{16,0},{24,8},{1,17},{9,25},{17,1},{25,9},{2,18},{10... | collective-permute-start | bytes 589832 | tf_op jit(solution)/shard_map/ppermute | solution.py:89
  6.5 10.7 %all-to-all-start = ((bf16[4,192,128]{2,1,0:T(8,128)(2,1)}), bf16[4,192,128]{2,1,0:T(8,128)(2,1)S(1)}, u32[]{:S(2)}, u32[]{:S(2)}) async-start(bf16[4,192,128]{2,1,0:T(8,128)(2,1)} %bitcast.10), calls=%async_computation | async-start | bytes 393216 | tf_op jit(solution)/shard_map/all_to_all | solution.py:118
  9.9 8.8 %collective-permute-start.2 = (bf16[64,768]{1,0:T(8,128)(2,1)S(1)}, bf16[64,768]{1,0:T(8,128)(2,1)S(1)}, u32[]{:S(2)}, u32[]{:S(2)}) collective-permute-start(bf16[64,768]{1,0:T(8,128)(2,1)S(1)} %get-tuple-element.21), channel_id=1, source_target_pairs={{8,16},{16,8},{9,17},{17,9},{10,18},{18,10},{11,19},{19,11},{12,20... | collective-permute-start | bytes 294920 | tf_op jit(solution)/shard_map/ppermute | solution.py:96
  10.6 4.2 %copy-start.6 = (bf16[1,128,768]{2,1,0:T(8,128)(2,1)S(1)}, bf16[1,128,768]{2,1,0:T(8,128)(2,1)}, u32[]{:S(2)}) copy-start(bf16[1,128,768]{2,1,0:T(8,128)(2,1)} %param.4) | copy-start | bytes 589828
  11.4 4.9 %collective-permute-start.1 = (bf16[320,768]{1,0:T(8,128)(2,1)S(1)}, bf16[320,768]{1,0:T(8,128)(2,1)S(1)}, u32[]{:S(2)}, u32[]{:S(2)}) collective-permute-start(bf16[320,768]{1,0:T(8,128)(2,1)S(1)} %pad_maximum_fusion.1), channel_id=1, source_target_pairs={{0,8},{8,0},{16,24},{24,16},{1,9},{9,1},{17,25},{25,17},{2,10},{10... | collective-permute-start | bytes 1474568 | tf_op jit(solution)/shard_map/ppermute | solution.py:92
  21.6 3.4 %copy-start.3 = (bf16[256,768]{1,0:T(8,128)(2,1)S(1)}, bf16[256,768]{1,0:T(8,128)(2,1)}, u32[]{:S(2)}) copy-start(bf16[256,768]{1,0:T(8,128)(2,1)} %pad_maximum_fusion.3) | copy-start | bytes 1179652
  21.7 13.7 %collective-permute-start.3 = (f16[1168,192]{0,1:T(8,128)(2,1)S(1)}, f16[1168,192]{0,1:T(8,128)(2,1)}, u32[]{:S(2)}, u32[]{:S(2)}) collective-permute-start(f16[1168,192]{0,1:T(8,128)(2,1)S(1)} %concatenate.33.clone), channel_id=1, source_target_pairs={{0,1},{1,0},{2,3},{3,2},{4,5},{5,4},{6,7},{7,6},{8,9},{9,8},{10,11... | collective-permute-start | bytes 1345544 | tf_op jit(solution)/shard_map/ppermute | solution.py:54
  38.9 3.7 %copy-start.2 = (f32[128,768]{1,0:T(8,128)S(1)}, f32[128,768]{1,0:T(8,128)}, u32[]{:S(2)}) copy-start(f32[128,768]{1,0:T(8,128)} %fusion.22) | copy-start | bytes 1179652
  38.9 3.7 %copy-start.4 = (bf16[256,768]{1,0:T(8,128)(2,1)S(1)}, bf16[256,768]{1,0:T(8,128)(2,1)}, u32[]{:S(2)}) copy-start(bf16[256,768]{1,0:T(8,128)(2,1)} %pad_maximum_fusion.3) | copy-start | bytes 1179652
  38.9 3.7 %copy-start.5 = (f32[128,768]{1,0:T(8,128)S(1)}, f32[128,768]{1,0:T(8,128)}, u32[]{:S(2)}) copy-start(f32[128,768]{1,0:T(8,128)} %convolution_add_fusion.1) | copy-start | bytes 1179652
  39.9 14.3 %collective-permute-start.6 = (f16[304,192]{1,0:T(8,128)(2,1)S(1)}, f16[304,192]{1,0:T(8,128)(2,1)S(1)}, u32[]{:S(2)}, u32[]{:S(2)}) collective-permute-start(f16[304,192]{1,0:T(8,128)(2,1)S(1)} %concatenate.36), channel_id=1, source_target_pairs={{0,4},{1,5},{2,6},{3,7},{4,0},{5,1},{6,2},{7,3},{8,12},{9,13},{10,... | collective-permute-start | bytes 350216 | tf_op jit(solution)/shard_map/ppermute | solution.py:54
  44.8 9.3 %collective-permute-start.5 = (f16[304,192]{1,0:T(8,128)(2,1)S(1)}, f16[304,192]{1,0:T(8,128)(2,1)S(1)}, u32[]{:S(2)}, u32[]{:S(2)}) collective-permute-start(f16[304,192]{1,0:T(8,128)(2,1)S(1)} %concatenate.35), channel_id=1, source_target_pairs={{0,2},{1,3},{2,4},{3,5},{4,6},{5,7},{6,0},{7,1},{8,10},{9,11},{10,... | collective-permute-start | bytes 350216 | tf_op jit(solution)/shard_map/ppermute | solution.py:54
  46.5 9.8 %collective-permute-start.4 = (f16[304,192]{1,0:T(8,128)(2,1)S(1)}, f16[304,192]{1,0:T(8,128)(2,1)S(1)}, u32[]{:S(2)}, u32[]{:S(2)}) collective-permute-start(f16[304,192]{1,0:T(8,128)(2,1)S(1)} %concatenate.34), channel_id=1, source_target_pairs={{0,6},{1,7},{2,0},{3,1},{4,2},{5,3},{6,4},{7,5},{8,14},{9,15},{10,... | collective-permute-start | bytes 350216 | tf_op jit(solution)/shard_map/ppermute | solution.py:54

commit v25 on v24

--- a/solution.py
+++ b/solution.py
@@ -33,7 +33,7 @@
 
 def exponent_of(values):
     flat = values.reshape(-1, values.shape[-1])
-    biggest = jnp.max(jnp.max(jnp.abs(flat), axis=0, keepdims=True), axis=1, keepdims=True)
+    biggest = jnp.max(jnp.abs(flat), axis=0, keepdims=True)
     return jnp.floor(jnp.log2(jnp.maximum(biggest, 1e-30)))
 
 

time: 57.8 us -> 56 us (0.969)
  between operations: 2.52 us -> 0.94 us
  other arithmetic: 6.26 us -> 5.31 us
  local copies, waits for them, and re-layouts: 6.26 us -> 6.84 us
    another operation x0 -> x1, local copies, waits for them, and re-layouts: none -> 1.19 us  [encode(): with_layout_constraint(jnp.concatenate([scaled, tag], axis=0), Layout((0,...]
    reduce_max x2, other arithmetic: 1.63 us -> 0.47 us  [exponent_of(): biggest = jnp.max(jnp.abs(flat), axis=0, keepdims=True)]
    concatenate x1, other arithmetic: 0.8 us -> 0.03 us  [gather_over_seq(): extended = jnp.concatenate([before, cot, after], axis=0)]
    select_n x1, other arithmetic: 0.02 us -> 0.66 us  [gather_over_seq(): far = lax.ppermute(jnp.where(odd, last, first), 'seq', across)]
    unnamed x18 -> x17, local copies, waits for them, and re-layouts: 1.92 us -> 1.47 us
  transfers between devices with their start and end apart: 8 -> 8, of which waited for: 4 -> 4; matrix products, arithmetic and copies ran while one was open for 21% -> 23% of each run, Pallas kernels for 0% -> 0%
where the time goes in v25:
time: 56 us; the launch traced here: 55.5 us
  starting transfers between devices  18.4 us (33%)
  waiting for transfers between devices  16.5 us (29%)
  matrix products  7.56 us (14%)
  local copies, waits for them, and re-layouts  6.84 us (12%)
  other arithmetic  5.31 us (9%)
  between operations  0.94 us (2%)
    ppermute x4, waiting for transfers between devices, send(): arrived = lax.ppermute(encode(values, exponent), 'batch', perm)  16 us
    ppermute x4, starting transfers between devices, send(): arrived = lax.ppermute(encode(values, exponent), 'batch', perm)  7.98 us
    dot_general x3, matrix products, body(): jnp.dot(window, weight[:, tap_index * in_width:(tap_index + 1) * in_width...  6.25 us
    ppermute x1, starting transfers between devices, gather_over_seq(): incoming = lax.ppermute(outgoing, 'seq', [(i, i ^ 1) for i in range(count)])  3.39 us
    all_to_all x1, starting transfers between devices, body(): arrived = lax.all_to_all(channels, 'seq', 0, 0, tiled=True)  3.37 us
    ppermute x1, starting transfers between devices, gather_over_seq(): stack = jnp.concatenate([stack, lax.ppermute(stack, 'seq', pairs)], axis=0)  3.03 us
    transpose x1, local copies, waits for them, and re-layouts, body(): channels = cotangent[0].T.reshape(seq_count, -1, length)  1.74 us
    unnamed x17, local copies, waits for them, and re-layouts  1.47 us
  transfers between devices with their start and end apart: 8, of which 4 were waited for; matrix products, arithmetic and copies ran while one was open for 23% of the time, Pallas kernels for 0%

profile of v25, /device:TPU:0, one launch (start us, length us, event | category | flops | bytes accessed | tf_op | source)
XLA Modules:
  0.0 55.5 jit_solution(8973208887329479059)
XLA Ops:
  0.7 1.1 %fusion.26 = bf16[1,128,768]{2,1,0:T(8,128)(2,1)S(1)} fusion(bf16[1,128,768]{2,1,0:T(8,128)(2,1)} %param.4), kind=kLoop, calls=%fused_computation.43 | loop fusion | flops 589824 | bytes 393216 | tf_op jit(solution)/shard_map/convert_element_type | solution.py:112
  1.7 3.0 %collective-permute-start = (bf16[1,128,768]{2,1,0:T(8,128)(2,1)S(1)}, bf16[1,128,768]{2,1,0:T(8,128)(2,1)S(1)}, u32[]{:S(2)}, u32[]{:S(2)}) collective-permute-start(bf16[1,128,768]{2,1,0:T(8,128)(2,1)S(1)} %fusion.26), channel_id=1, source_target_pairs={{0,16},{8,24},{16,0},{24,8},{1,17},{9,25},{17,1},{25,9},{2,18},{10... | collective-permute-start | bytes 589832 | tf_op jit(solution)/shard_map/ppermute | solution.py:89
  4.7 1.7 %copy.21 = bf16[768,128]{1,0:T(8,128)(2,1)} copy(bf16[768,128]{0,1:T(8,128)(2,1)} %bitcast.108) | data formatting | bytes 393216 | tf_op jit(solution)/shard_map/transpose | solution.py:117
  6.5 3.4 %all-to-all-start = ((bf16[4,192,128]{2,1,0:T(8,128)(2,1)}), bf16[4,192,128]{2,1,0:T(8,128)(2,1)S(1)}, u32[]{:S(2)}, u32[]{:S(2)}) async-start(bf16[4,192,128]{2,1,0:T(8,128)(2,1)} %bitcast.10), calls=%async_computation | async-start | bytes 393216 | tf_op jit(solution)/shard_map/all_to_all | solution.py:118
  9.9 0.7 %select_bitcast_fusion = (bf16[64,768]{1,0:T(8,128)(2,1)}, bf16[64,768]{1,0:T(8,128)(2,1)S(1)}) fusion(pred[]{:T(512)S(6)} %eq.9, bf16[1,128,768]{2,1,0:T(8,128)(2,1)S(1)} %copy-done.1), kind=kLoop, calls=%fused_computation.71 | loop fusion | flops 98304 | bytes 393217 | tf_op jit(solution)/shard_map/jit(_where)/select_n | solution.py:96
  10.5 0.7 %collective-permute-start.2 = (bf16[64,768]{1,0:T(8,128)(2,1)}, bf16[64,768]{1,0:T(8,128)(2,1)S(1)}, u32[]{:S(2)}, u32[]{:S(2)}) collective-permute-start(bf16[64,768]{1,0:T(8,128)(2,1)} %get-tuple-element.23), channel_id=1, source_target_pairs={{8,16},{16,8},{9,17},{17,9},{10,18},{18,10},{11,19},{19,11},{12,20... | collective-permute-start | bytes 294920 | tf_op jit(solution)/shard_map/ppermute | solution.py:96
  11.3 0.6 %gather_fusion = s32[4]{0:T(128)S(1)} fusion(s32[4]{0:T(128)S(1)} %copy-done, s32[1024]{0:T(1024)S(1)} %pad_clamp_fusion.1), kind=kCustom, calls=%fused_computation | custom fusion | bytes 48 | tf_op jit(solution)/shard_map/gather | solution.py:101
  12.0 3.4 %collective-permute-start.1 = (bf16[320,768]{1,0:T(8,128)(2,1)S(1)}, bf16[320,768]{1,0:T(8,128)(2,1)S(1)}, u32[]{:S(2)}, u32[]{:S(2)}) collective-permute-start(bf16[320,768]{1,0:T(8,128)(2,1)S(1)} %pad_maximum_fusion.2), channel_id=1, source_target_pairs={{0,8},{8,0},{16,24},{24,16},{1,9},{9,1},{17,25},{25,17},{2,10},{10... | collective-permute-start | bytes 1474568 | tf_op jit(solution)/shard_map/ppermute | solution.py:92
  15.5 0.9 %fusion.22 = f32[128,768]{1,0:T(8,128)} fusion(bf16[1,128,768]{2,1,0:T(8,128)(2,1)S(1)} %copy-done.6), kind=kLoop, calls=%fused_computation.39 | loop fusion | flops 884736 | bytes 589824 | tf_op jit(solution)/shard_map/add | solution.py:31
  16.4 0.5 collective-permute-done.1
  17.0 0.6 %gather_fusion.1 = bf16[4,128,768]{2,1,0:T(8,128)(2,1)S(1)} fusion(bf16[4,128,768]{2,1,0:T(8,128)(2,1)S(1)} %pad_maximum_fusion, s32[1024]{0:T(1024)S(1)} %pad_clamp_fusion), kind=kCustom, calls=%fused_computation.1 | custom fusion | bytes 1572880 | tf_op jit(solution)/shard_map/jit(_take)/gather | solution.py:102
  17.8 0.5 convolution_bitcast_fusion
  18.3 0.4 fusion.14
  18.7 0.4 fusion.13
  19.1 0.2 maximum_multiply_fusion
  19.4 0.2 fusion.2
  19.9 1.2 %copy.28 = f16[1168,192]{0,1:T(8,128)(2,1)} copy(f16[1168,192]{1,0:T(8,128)(2,1)S(1)} %pad_maximum_fusion.1) | data formatting | bytes 897024 | tf_op jit(solution)/shard_map/layout_constraint | solution.py:44
  21.1 1.5 %collective-permute-start.3 = (f16[1168,192]{0,1:T(8,128)(2,1)}, f16[1168,192]{0,1:T(8,128)(2,1)}, u32[]{:S(2)}, u32[]{:S(2)}) collective-permute-start(f16[1168,192]{0,1:T(8,128)(2,1)} %copy.28), channel_id=1, source_target_pairs={{0,1},{1,0},{2,3},{3,2},{4,5},{5,4},{6,7},{7,6},{8,9},{9,8},{10,11... | collective-permute-start | bytes 1345544 | tf_op jit(solution)/shard_map/ppermute | solution.py:54
  22.6 1.6 %fusion.5 = f32[128,768]{1,0:T(8,128)S(1)} fusion(bf16[768,2304]{1,0:T(8,128)(2,1)} %param.6, bf16[256,768]{1,0:T(8,128)(2,1)S(1)} %pad_maximum_fusion.4), kind=kOutput, calls=%fused_computation.16 | convolution fusion | flops 150994944 | bytes 1769472 | tf_op jit(solution)/shard_map/dot_general | solution.py:143
  24.2 2.4 %convolution_add_fusion.1 = f32[128,768]{1,0:T(8,128)} fusion(f32[128,768]{1,0:T(8,128)S(1)} %fusion.5, bf16[768,2304]{1,0:T(8,128)(2,1)} %param.6, bf16[256,768]{1,0:T(8,128)(2,1)S(1)} %pad_maximum_fusion.4), kind=kOutput, calls=%fused_computation.5 | convolution fusion | flops 151093248 | bytes 2162688 | tf_op jit(solution)/shard_map/dot_general | solution.py:143
  26.6 8.3 %collective-permute-done.3 = f16[1168,192]{0,1:T(8,128)(2,1)} collective-permute-done((f16[1168,192]{0,1:T(8,128)(2,1)}, f16[1168,192]{0,1:T(8,128)(2,1)}, u32[]{:S(2)}, u32[]{:S(2)}) %collective-permute-start.3) | collective-permute-done | bytes 448544 | tf_op jit(solution)/shard_map/ppermute | solution.py:54
  34.9 1.1 %slice.89 = f16[1152,192]{0,1:T(8,128)(2,1)S(1)} slice(f16[1168,192]{0,1:T(8,128)(2,1)} %collective-permute-done.3), slice={[0:1152], [0:192]} | slice | bytes 884736 | tf_op jit(solution)/shard_map/slice | solution.py:49
  36.0 0.5 copy.37
  36.5 0.8 %multiply_exponential_fusion = f32[1,192]{0,1:T(8,128)S(1)} fusion(f16[1168,192]{0,1:T(8,128)(2,1)} %collective-permute-done.3), kind=kLoop, calls=%fused_computation.70 | loop fusion | flops 576 | bytes 1152 | tf_op jit(solution)/shard_map/exp2 | solution.py:49
  37.5 0.3 abs_reduce_fusion
  38.1 2.7 %collective-permute-start.6 = (f16[304,192]{1,0:T(8,128)(2,1)S(1)}, f16[304,192]{1,0:T(8,128)(2,1)S(1)}, u32[]{:S(2)}, u32[]{:S(2)}) collective-permute-start(f16[304,192]{1,0:T(8,128)(2,1)S(1)} %get-tuple-element.27), channel_id=1, source_target_pairs={{0,4},{1,5},{2,6},{3,7},{4,0},{5,1},{6,2},{7,3},{8,12},{9,13},{10,... | collective-permute-start | bytes 350216 | tf_op jit(solution)/shard_map/ppermute | solution.py:54
  40.8 2.3 %fusion.10 = bf16[1,128,768]{2,1,0:T(8,128)(2,1)} fusion(f32[128,768]{1,0:T(8,128)S(1)} %copy-done.2, f32[128,768]{1,0:T(8,128)S(1)} %copy-done.5, bf16[768,2304]{1,0:T(8,128)(2,1)} %param.6, bf16[256,768]{1,0:T(8,128)(2,1)S(1)} %copy-done.4), kind=kOutput, calls=%fused_computation.19 | convolution fusion | flops 151289856 | bytes 2359296 | tf_op jit(solution)/shard_map/dot_general | solution.py:143
  43.0 1.6 %collective-permute-start.5 = (f16[304,192]{1,0:T(8,128)(2,1)S(1)}, f16[304,192]{1,0:T(8,128)(2,1)S(1)}, u32[]{:S(2)}, u32[]{:S(2)}) collective-permute-start(f16[304,192]{1,0:T(8,128)(2,1)S(1)} %get-tuple-element.26), channel_id=1, source_target_pairs={{0,2},{1,3},{2,4},{3,5},{4,6},{5,7},{6,0},{7,1},{8,10},{9,11},{10,... | collective-permute-start | bytes 350216 | tf_op jit(solution)/shard_map/ppermute | solution.py:54
  44.6 2.2 %collective-permute-start.4 = (f16[304,192]{1,0:T(8,128)(2,1)S(1)}, f16[304,192]{1,0:T(8,128)(2,1)S(1)}, u32[]{:S(2)}, u32[]{:S(2)}) collective-permute-start(f16[304,192]{1,0:T(8,128)(2,1)S(1)} %get-tuple-element.25), channel_id=1, source_target_pairs={{0,6},{1,7},{2,0},{3,1},{4,2},{5,3},{6,4},{7,5},{8,14},{9,15},{10,... | collective-permute-start | bytes 350216 | tf_op jit(solution)/shard_map/ppermute | solution.py:54
  46.9 5.5 %collective-permute-done.6 = f16[304,192]{1,0:T(8,128)(2,1)S(1)} collective-permute-done((f16[304,192]{1,0:T(8,128)(2,1)S(1)}, f16[304,192]{1,0:T(8,128)(2,1)S(1)}, u32[]{:S(2)}, u32[]{:S(2)}) %collective-permute-start.6) | collective-permute-done | bytes 116768 | tf_op jit(solution)/shard_map/ppermute | solution.py:54
  52.4 2.1 %collective-permute-done.4 = f16[304,192]{1,0:T(8,128)(2,1)S(1)} collective-permute-done((f16[304,192]{1,0:T(8,128)(2,1)S(1)}, f16[304,192]{1,0:T(8,128)(2,1)S(1)}, u32[]{:S(2)}, u32[]{:S(2)}) %collective-permute-start.4) | collective-permute-done | bytes 116768 | tf_op jit(solution)/shard_map/ppermute | solution.py:54
  54.7 0.9 %copy.30 = f32[192,288]{1,0:T(8,128)} copy(f32[192,288]{0,1:T(8,128)S(1)} %fusion.35) | data formatting | bytes 442368
  (45 shorter events, 1.4 us)
Async XLA Ops:
  0.6 10.6 %copy-start = (s32[4]{0:T(128)S(1)}, s32[4]{0:T(128)}, u32[]{:S(2)}) copy-start(s32[4]{0:T(128)} %constant.122.clone) | copy-start | bytes 52
  0.6 9.2 %copy-start.1 = (bf16[1,128,768]{2,1,0:T(8,128)(2,1)S(1)}, bf16[1,128,768]{2,1,0:T(8,128)(2,1)}, u32[]{:S(2)}) copy-start(bf16[1,128,768]{2,1,0:T(8,128)(2,1)} %param.5) | copy-start | bytes 589828
  1.7 10.2 %collective-permute-start = (bf16[1,128,768]{2,1,0:T(8,128)(2,1)S(1)}, bf16[1,128,768]{2,1,0:T(8,128)(2,1)S(1)}, u32[]{:S(2)}, u32[]{:S(2)}) collective-permute-start(bf16[1,128,768]{2,1,0:T(8,128)(2,1)S(1)} %fusion.26), channel_id=1, source_target_pairs={{0,16},{8,24},{16,0},{24,8},{1,17},{9,25},{17,1},{25,9},{2,18},{10... | collective-permute-start | bytes 589832 | tf_op jit(solution)/shard_map/ppermute | solution.py:89
  6.5 11.3 %all-to-all-start = ((bf16[4,192,128]{2,1,0:T(8,128)(2,1)}), bf16[4,192,128]{2,1,0:T(8,128)(2,1)S(1)}, u32[]{:S(2)}, u32[]{:S(2)}) async-start(bf16[4,192,128]{2,1,0:T(8,128)(2,1)} %bitcast.10), calls=%async_computation | async-start | bytes 393216 | tf_op jit(solution)/shard_map/all_to_all | solution.py:118
  10.5 8.8 %collective-permute-start.2 = (bf16[64,768]{1,0:T(8,128)(2,1)}, bf16[64,768]{1,0:T(8,128)(2,1)S(1)}, u32[]{:S(2)}, u32[]{:S(2)}) collective-permute-start(bf16[64,768]{1,0:T(8,128)(2,1)} %get-tuple-element.23), channel_id=1, source_target_pairs={{8,16},{16,8},{9,17},{17,9},{10,18},{18,10},{11,19},{19,11},{12,20... | collective-permute-start | bytes 294920 | tf_op jit(solution)/shard_map/ppermute | solution.py:96
  11.2 4.2 %copy-start.6 = (bf16[1,128,768]{2,1,0:T(8,128)(2,1)S(1)}, bf16[1,128,768]{2,1,0:T(8,128)(2,1)}, u32[]{:S(2)}) copy-start(bf16[1,128,768]{2,1,0:T(8,128)(2,1)} %param.4) | copy-start | bytes 589828
  12.0 4.9 %collective-permute-start.1 = (bf16[320,768]{1,0:T(8,128)(2,1)S(1)}, bf16[320,768]{1,0:T(8,128)(2,1)S(1)}, u32[]{:S(2)}, u32[]{:S(2)}) collective-permute-start(bf16[320,768]{1,0:T(8,128)(2,1)S(1)} %pad_maximum_fusion.2), channel_id=1, source_target_pairs={{0,8},{8,0},{16,24},{24,16},{1,9},{9,1},{17,25},{25,17},{2,10},{10... | collective-permute-start | bytes 1474568 | tf_op jit(solution)/shard_map/ppermute | solution.py:92
  19.4 4.8 %copy-start.3 = (bf16[256,768]{1,0:T(8,128)(2,1)}, bf16[256,768]{1,0:T(8,128)(2,1)S(1)}, u32[]{:S(2)}) copy-start(bf16[256,768]{1,0:T(8,128)(2,1)S(1)} %pad_maximum_fusion.4) | copy-start | bytes 1179652
  21.1 13.8 %collective-permute-start.3 = (f16[1168,192]{0,1:T(8,128)(2,1)}, f16[1168,192]{0,1:T(8,128)(2,1)}, u32[]{:S(2)}, u32[]{:S(2)}) collective-permute-start(f16[1168,192]{0,1:T(8,128)(2,1)} %copy.28), channel_id=1, source_target_pairs={{0,1},{1,0},{2,3},{3,2},{4,5},{5,4},{6,7},{7,6},{8,9},{9,8},{10,11... | collective-permute-start | bytes 1345544 | tf_op jit(solution)/shard_map/ppermute | solution.py:54
  37.8 3.0 %copy-start.2 = (f32[128,768]{1,0:T(8,128)S(1)}, f32[128,768]{1,0:T(8,128)}, u32[]{:S(2)}) copy-start(f32[128,768]{1,0:T(8,128)} %fusion.22) | copy-start | bytes 1179652
  37.8 3.0 %copy-start.4 = (bf16[256,768]{1,0:T(8,128)(2,1)S(1)}, bf16[256,768]{1,0:T(8,128)(2,1)}, u32[]{:S(2)}) copy-start(bf16[256,768]{1,0:T(8,128)(2,1)} %copy-done.3) | copy-start | bytes 1179652
  37.8 3.0 %copy-start.5 = (f32[128,768]{1,0:T(8,128)S(1)}, f32[128,768]{1,0:T(8,128)}, u32[]{:S(2)}) copy-start(f32[128,768]{1,0:T(8,128)} %convolution_add_fusion.1) | copy-start | bytes 1179652
  38.1 14.3 %collective-permute-start.6 = (f16[304,192]{1,0:T(8,128)(2,1)S(1)}, f16[304,192]{1,0:T(8,128)(2,1)S(1)}, u32[]{:S(2)}, u32[]{:S(2)}) collective-permute-start(f16[304,192]{1,0:T(8,128)(2,1)S(1)} %get-tuple-element.27), channel_id=1, source_target_pairs={{0,4},{1,5},{2,6},{3,7},{4,0},{5,1},{6,2},{7,3},{8,12},{9,13},{10,... | collective-permute-start | bytes 350216 | tf_op jit(solution)/shard_map/ppermute | solution.py:54
  43.0 9.4 %collective-permute-start.5 = (f16[304,192]{1,0:T(8,128)(2,1)S(1)}, f16[304,192]{1,0:T(8,128)(2,1)S(1)}, u32[]{:S(2)}, u32[]{:S(2)}) collective-permute-start(f16[304,192]{1,0:T(8,128)(2,1)S(1)} %get-tuple-element.26), channel_id=1, source_target_pairs={{0,2},{1,3},{2,4},{3,5},{4,6},{5,7},{6,0},{7,1},{8,10},{9,11},{10,... | collective-permute-start | bytes 350216 | tf_op jit(solution)/shard_map/ppermute | solution.py:54
  44.6 9.9 %collective-permute-start.4 = (f16[304,192]{1,0:T(8,128)(2,1)S(1)}, f16[304,192]{1,0:T(8,128)(2,1)S(1)}, u32[]{:S(2)}, u32[]{:S(2)}) collective-permute-start(f16[304,192]{1,0:T(8,128)(2,1)S(1)} %get-tuple-element.25), channel_id=1, source_target_pairs={{0,6},{1,7},{2,0},{3,1},{4,2},{5,3},{6,4},{7,5},{8,14},{9,15},{10,... | collective-permute-start | bytes 350216 | tf_op jit(solution)/shard_map/ppermute | solution.py:54

commit v26 on v25

--- a/solution.py
+++ b/solution.py
@@ -65,7 +65,12 @@
     blocks = columns.reshape(outer, 2, -1, columns.shape[1])
     mine = lax.dynamic_index_in_dim(blocks, x, axis=1, keepdims=False)
     theirs = lax.dynamic_index_in_dim(blocks, 1 - x, axis=1, keepdims=False)
-    summed = with_layout_constraint(mine + send(theirs, pairs, exponent_of(theirs)), Layout((0, 1, 2)))
+    half = outer // 2
+    received = jnp.concatenate(
+        [send(theirs[:half], pairs, exponent_of(theirs[:half])),
+         send(theirs[half:], pairs, exponent_of(theirs[half:]))], axis=0
+    )
+    summed = with_layout_constraint(mine + received, Layout((0, 1, 2)))
     spread = exponent_of(summed)
     total = lax.dynamic_index_in_dim(summed, z, axis=0, keepdims=False)
     for shift in sorted(range(1, outer), key=lambda d: (min(d, outer - d), -d)):

time: 56 us -> 55.1 us (0.984)
  waiting for transfers between devices: 16.5 us -> 22.4 us
  matrix products: 7.56 us -> 2.96 us
  local copies, waits for them, and re-layouts: 6.84 us -> 5.33 us
  other arithmetic: 5.31 us -> 4.04 us
  starting transfers between devices: 18.4 us -> 19.1 us
    ppermute x4 -> x5, waiting for transfers between devices: 16 us -> 21.1 us  [send(): arrived = lax.ppermute(encode(values, exponent), 'batch', perm)]
    dot_general x3, matrix products: 6.25 us -> 1.66 us  [body(): jnp.dot(window, weight[:, tap_index * in_width:(tap_index + 1) * in_width...]
    another operation x1 -> x0, local copies, waits for them, and re-layouts: 1.19 us -> none  [encode(): with_layout_constraint(jnp.concatenate([scaled, tag], axis=0), Layout((0,...]
    slice x1 -> x0, local copies, waits for them, and re-layouts: 1.09 us -> none  [decode(): values = packed[:-TAG].astype(jnp.float32) * jnp.exp2(exponent - HEADROOM)]
    exp2 x4 -> x5, other arithmetic: 0.85 us -> 0.04 us  [decode(): values = packed[:-TAG].astype(jnp.float32) * jnp.exp2(exponent - HEADROOM)]
    add x1, other arithmetic: 0.92 us -> 0.16 us  [gelu_factors(): return (values * normal_cdf, normal_cdf + values * density)]
    ppermute x1, waiting for transfers between devices: 0.49 us -> 1.24 us  [gather_over_seq(): incoming = lax.ppermute(outgoing, 'seq', [(i, i ^ 1) for i in range(count)])]
    ppermute x4 -> x5, starting transfers between devices: 7.98 us -> 8.65 us  [send(): arrived = lax.ppermute(encode(values, exponent), 'batch', perm)]
  transfers between devices with their start and end apart: 8 -> 9, of which waited for: 4 -> 5; matrix products, arithmetic and copies ran while one was open for 23% -> 16% of each run, Pallas kernels for 0% -> 0%
where the time goes in v26:
time: 55.1 us; the launch traced here: 54.8 us
  waiting for transfers between devices  22.4 us (41%)
  starting transfers between devices  19.1 us (35%)
  local copies, waits for them, and re-layouts  5.33 us (10%)
  other arithmetic  4.04 us (7%)
  matrix products  2.96 us (5%)
  between operations  0.93 us (2%)
    ppermute x5, waiting for transfers between devices, send(): arrived = lax.ppermute(encode(values, exponent), 'batch', perm)  21.1 us
    ppermute x5, starting transfers between devices, send(): arrived = lax.ppermute(encode(values, exponent), 'batch', perm)  8.65 us
    ppermute x1, starting transfers between devices, gather_over_seq(): incoming = lax.ppermute(outgoing, 'seq', [(i, i ^ 1) for i in range(count)])  3.39 us
    all_to_all x1, starting transfers between devices, body(): arrived = lax.all_to_all(channels, 'seq', 0, 0, tiled=True)  3.37 us
    ppermute x1, starting transfers between devices, gather_over_seq(): stack = jnp.concatenate([stack, lax.ppermute(stack, 'seq', pairs)], axis=0)  3.03 us
    transpose x1, local copies, waits for them, and re-layouts, body(): channels = cotangent[0].T.reshape(seq_count, -1, length)  1.74 us
    dot_general x3, matrix products, body(): jnp.dot(window, weight[:, tap_index * in_width:(tap_index + 1) * in_width...  1.66 us
    unnamed x7, local copies, waits for them, and re-layouts  1.57 us
  transfers between devices with their start and end apart: 9, of which 5 were waited for; matrix products, arithmetic and copies ran while one was open for 16% of the time, Pallas kernels for 0%

profile of v26, /device:TPU:0, one launch (start us, length us, event | category | flops | bytes accessed | tf_op | source)
XLA Modules:
  0.0 54.8 jit_solution(10538124624055871205)
XLA Ops:
  0.6 1.1 %fusion.28 = bf16[1,128,768]{2,1,0:T(8,128)(2,1)S(1)} fusion(bf16[1,128,768]{2,1,0:T(8,128)(2,1)} %param.4), kind=kLoop, calls=%fused_computation.47 | loop fusion | flops 589824 | bytes 393216 | tf_op jit(solution)/shard_map/convert_element_type | solution.py:117
  1.7 3.0 %collective-permute-start = (bf16[1,128,768]{2,1,0:T(8,128)(2,1)S(1)}, bf16[1,128,768]{2,1,0:T(8,128)(2,1)S(1)}, u32[]{:S(2)}, u32[]{:S(2)}) collective-permute-start(bf16[1,128,768]{2,1,0:T(8,128)(2,1)S(1)} %fusion.28), channel_id=1, source_target_pairs={{0,16},{8,24},{16,0},{24,8},{1,17},{9,25},{17,1},{25,9},{2,18},{10... | collective-permute-start | bytes 589832 | tf_op jit(solution)/shard_map/ppermute | solution.py:94
  4.8 1.7 %copy.13 = bf16[768,128]{1,0:T(8,128)(2,1)} copy(bf16[768,128]{0,1:T(8,128)(2,1)} %bitcast.121) | data formatting | bytes 393216 | tf_op jit(solution)/shard_map/transpose | solution.py:122
  6.5 3.4 %all-to-all-start = ((bf16[4,192,128]{2,1,0:T(8,128)(2,1)}), bf16[4,192,128]{2,1,0:T(8,128)(2,1)S(1)}, u32[]{:S(2)}, u32[]{:S(2)}) async-start(bf16[4,192,128]{2,1,0:T(8,128)(2,1)} %bitcast.10), calls=%async_computation | async-start | bytes 393216 | tf_op jit(solution)/shard_map/all_to_all | solution.py:123
  9.9 1.0 %select_bitcast_fusion = (bf16[64,768]{1,0:T(8,128)(2,1)S(1)}, bf16[64,768]{1,0:T(8,128)(2,1)S(1)}) fusion(pred[]{:T(512)S(6)} %eq.9, bf16[1,128,768]{2,1,0:T(8,128)(2,1)} %param.5), kind=kLoop, calls=%fused_computation.76 | loop fusion | flops 98304 | bytes 393217 | tf_op jit(solution)/shard_map/jit(_where)/select_n | solution.py:101
  10.8 0.7 %collective-permute-start.2 = (bf16[64,768]{1,0:T(8,128)(2,1)S(1)}, bf16[64,768]{1,0:T(8,128)(2,1)S(1)}, u32[]{:S(2)}, u32[]{:S(2)}) collective-permute-start(bf16[64,768]{1,0:T(8,128)(2,1)S(1)} %get-tuple-element.25), channel_id=1, source_target_pairs={{8,16},{16,8},{9,17},{17,9},{10,18},{18,10},{11,19},{19,11},{12,20... | collective-permute-start | bytes 294920 | tf_op jit(solution)/shard_map/ppermute | solution.py:101
  11.5 1.3 %gather_fusion = s32[4]{0:T(128)S(1)} fusion(s32[4]{0:T(128)} %constant.123.clone, s32[1024]{0:T(1024)S(1)} %pad_clamp_fusion.1), kind=kCustom, calls=%fused_computation | custom fusion | bytes 48 | tf_op jit(solution)/shard_map/gather | solution.py:106
  13.0 3.4 %collective-permute-start.1 = (bf16[320,768]{1,0:T(8,128)(2,1)S(1)}, bf16[320,768]{1,0:T(8,128)(2,1)S(1)}, u32[]{:S(2)}, u32[]{:S(2)}) collective-permute-start(bf16[320,768]{1,0:T(8,128)(2,1)S(1)} %pad_maximum_fusion.1), channel_id=1, source_target_pairs={{0,8},{8,0},{16,24},{24,16},{1,9},{9,1},{17,25},{25,17},{2,10},{10... | collective-permute-start | bytes 1474568 | tf_op jit(solution)/shard_map/ppermute | solution.py:97
  16.4 0.2 fusion.24
  16.6 1.2 %collective-permute-done.1 = bf16[320,768]{1,0:T(8,128)(2,1)S(1)} collective-permute-done((bf16[320,768]{1,0:T(8,128)(2,1)S(1)}, bf16[320,768]{1,0:T(8,128)(2,1)S(1)}, u32[]{:S(2)}, u32[]{:S(2)}) %collective-permute-start.1) | collective-permute-done | bytes 491552 | tf_op jit(solution)/shard_map/ppermute | solution.py:97
  18.0 0.6 %gather_fusion.1 = bf16[4,128,768]{2,1,0:T(8,128)(2,1)S(1)} fusion(bf16[4,128,768]{2,1,0:T(8,128)(2,1)S(1)} %pad_maximum_fusion, s32[1024]{0:T(1024)S(1)} %pad_clamp_fusion), kind=kCustom, calls=%fused_computation.1 | custom fusion | bytes 1572880 | tf_op jit(solution)/shard_map/jit(_take)/gather | solution.py:107
  18.6 0.2 bitcast_select_fusion
  18.7 0.5 convolution_bitcast_fusion
  19.2 0.4 fusion.12
  19.7 0.4 fusion.11
  20.1 0.2 maximum_multiply_fusion
  20.3 0.7 %copy-done = bf16[1,128,768]{2,1,0:T(8,128)(2,1)S(1)} copy-done((bf16[1,128,768]{2,1,0:T(8,128)(2,1)S(1)}, bf16[1,128,768]{2,1,0:T(8,128)(2,1)}, u32[]{:S(2)}) %copy-start) | copy-done | bytes 196632
  21.0 0.2 fusion.20
  21.4 1.6 %collective-permute-start.4 = (f16[592,192]{1,0:T(8,128)(2,1)S(1)}, f16[592,192]{1,0:T(8,128)(2,1)S(1)}, u32[]{:S(2)}, u32[]{:S(2)}) collective-permute-start(f16[592,192]{1,0:T(8,128)(2,1)S(1)} %pad_maximum_fusion.5), channel_id=1, source_target_pairs={{0,1},{1,0},{2,3},{3,2},{4,5},{5,4},{6,7},{7,6},{8,9},{9,8},{10,11... | collective-permute-start | bytes 681992 | tf_op jit(solution)/shard_map/ppermute | solution.py:54
  23.2 0.6 %collective-permute-start.3 = (f16[592,192]{1,0:T(8,128)(2,1)S(1)}, f16[592,192]{1,0:T(8,128)(2,1)S(1)}, u32[]{:S(2)}, u32[]{:S(2)}) collective-permute-start(f16[592,192]{1,0:T(8,128)(2,1)S(1)} %pad_maximum_fusion.4), channel_id=1, source_target_pairs={{0,1},{1,0},{2,3},{3,2},{4,5},{5,4},{6,7},{7,6},{8,9},{9,8},{10,11... | collective-permute-start | bytes 681992 | tf_op jit(solution)/shard_map/ppermute | solution.py:54
  23.8 0.3 fusion.3
  24.1 0.3 convolution_add_fusion.1
  24.4 7.1 %collective-permute-done.4 = f16[592,192]{1,0:T(8,128)(2,1)S(1)} collective-permute-done((f16[592,192]{1,0:T(8,128)(2,1)S(1)}, f16[592,192]{1,0:T(8,128)(2,1)S(1)}, u32[]{:S(2)}, u32[]{:S(2)}) %collective-permute-start.4) | collective-permute-done | bytes 227360 | tf_op jit(solution)/shard_map/ppermute | solution.py:54
  31.5 5.9 %collective-permute-done.3 = f16[592,192]{1,0:T(8,128)(2,1)S(1)} collective-permute-done((f16[592,192]{1,0:T(8,128)(2,1)S(1)}, f16[592,192]{1,0:T(8,128)(2,1)S(1)}, u32[]{:S(2)}, u32[]{:S(2)}) %collective-permute-start.3) | collective-permute-done | bytes 227360 | tf_op jit(solution)/shard_map/ppermute | solution.py:54
  37.5 0.3 abs_reduce_fusion
  38.0 2.7 %collective-permute-start.7 = (f16[304,192]{1,0:T(8,128)(2,1)S(1)}, f16[304,192]{1,0:T(8,128)(2,1)S(1)}, u32[]{:S(2)}, u32[]{:S(2)}) collective-permute-start(f16[304,192]{1,0:T(8,128)(2,1)S(1)} %get-tuple-element.29), channel_id=1, source_target_pairs={{0,4},{1,5},{2,6},{3,7},{4,0},{5,1},{6,2},{7,3},{8,12},{9,13},{10,... | collective-permute-start | bytes 350216 | tf_op jit(solution)/shard_map/ppermute | solution.py:54
  40.7 1.0 %fusion.8 = bf16[1,128,768]{2,1,0:T(8,128)(2,1)} fusion(f32[128,768]{1,0:T(8,128)S(1)} %fusion.24, f32[128,768]{1,0:T(8,128)S(1)} %convolution_add_fusion.1, bf16[768,2304]{1,0:T(8,128)(2,1)S(1)} %copy-done.1, bf16[256,768]{1,0:T(8,128)(2,1)S(1)} %pad_maximum_fusion.3), kind=kOutput, calls=%fused_computation.14 | convolution fusion | flops 151289856 | bytes 2359296 | tf_op jit(solution)/shard_map/dot_general | solution.py:148
  41.7 1.6 %collective-permute-start.6 = (f16[304,192]{1,0:T(8,128)(2,1)S(1)}, f16[304,192]{1,0:T(8,128)(2,1)S(1)}, u32[]{:S(2)}, u32[]{:S(2)}) collective-permute-start(f16[304,192]{1,0:T(8,128)(2,1)S(1)} %get-tuple-element.28), channel_id=1, source_target_pairs={{0,2},{1,3},{2,4},{3,5},{4,6},{5,7},{6,0},{7,1},{8,10},{9,11},{10,... | collective-permute-start | bytes 350216 | tf_op jit(solution)/shard_map/ppermute | solution.py:54
  43.3 2.3 %collective-permute-start.5 = (f16[304,192]{1,0:T(8,128)(2,1)S(1)}, f16[304,192]{1,0:T(8,128)(2,1)S(1)}, u32[]{:S(2)}, u32[]{:S(2)}) collective-permute-start(f16[304,192]{1,0:T(8,128)(2,1)S(1)} %get-tuple-element.27), channel_id=1, source_target_pairs={{0,6},{1,7},{2,0},{3,1},{4,2},{5,3},{6,4},{7,5},{8,14},{9,15},{10,... | collective-permute-start | bytes 350216 | tf_op jit(solution)/shard_map/ppermute | solution.py:54
  45.5 6.8 %collective-permute-done.7 = f16[304,192]{1,0:T(8,128)(2,1)S(1)} collective-permute-done((f16[304,192]{1,0:T(8,128)(2,1)S(1)}, f16[304,192]{1,0:T(8,128)(2,1)S(1)}, u32[]{:S(2)}, u32[]{:S(2)}) %collective-permute-start.7) | collective-permute-done | bytes 116768 | tf_op jit(solution)/shard_map/ppermute | solution.py:54
  52.4 1.4 %collective-permute-done.5 = f16[304,192]{1,0:T(8,128)(2,1)S(1)} collective-permute-done((f16[304,192]{1,0:T(8,128)(2,1)S(1)}, f16[304,192]{1,0:T(8,128)(2,1)S(1)}, u32[]{:S(2)}, u32[]{:S(2)}) %collective-permute-start.5) | collective-permute-done | bytes 116768 | tf_op jit(solution)/shard_map/ppermute | solution.py:54
  53.9 0.9 %copy.20 = f32[192,288]{1,0:T(8,128)} copy(f32[192,288]{0,1:T(8,128)S(1)} %fusion.37) | data formatting | bytes 442368
  (41 shorter events, 1.2 us)
Async XLA Ops:
  0.6 15.8 %copy-start.2 = (bf16[1,128,768]{2,1,0:T(8,128)(2,1)S(1)}, bf16[1,128,768]{2,1,0:T(8,128)(2,1)}, u32[]{:S(2)}) copy-start(bf16[1,128,768]{2,1,0:T(8,128)(2,1)} %param.4) | copy-start | bytes 589828
  1.7 11.1 %collective-permute-start = (bf16[1,128,768]{2,1,0:T(8,128)(2,1)S(1)}, bf16[1,128,768]{2,1,0:T(8,128)(2,1)S(1)}, u32[]{:S(2)}, u32[]{:S(2)}) collective-permute-start(bf16[1,128,768]{2,1,0:T(8,128)(2,1)S(1)} %fusion.28), channel_id=1, source_target_pairs={{0,16},{8,24},{16,0},{24,8},{1,17},{9,25},{17,1},{25,9},{2,18},{10... | collective-permute-start | bytes 589832 | tf_op jit(solution)/shard_map/ppermute | solution.py:94
  6.5 12.2 %all-to-all-start = ((bf16[4,192,128]{2,1,0:T(8,128)(2,1)}), bf16[4,192,128]{2,1,0:T(8,128)(2,1)S(1)}, u32[]{:S(2)}, u32[]{:S(2)}) async-start(bf16[4,192,128]{2,1,0:T(8,128)(2,1)} %bitcast.10), calls=%async_computation | async-start | bytes 393216 | tf_op jit(solution)/shard_map/all_to_all | solution.py:123
  10.8 9.4 %collective-permute-start.2 = (bf16[64,768]{1,0:T(8,128)(2,1)S(1)}, bf16[64,768]{1,0:T(8,128)(2,1)S(1)}, u32[]{:S(2)}, u32[]{:S(2)}) collective-permute-start(bf16[64,768]{1,0:T(8,128)(2,1)S(1)} %get-tuple-element.25), channel_id=1, source_target_pairs={{8,16},{16,8},{9,17},{17,9},{10,18},{18,10},{11,19},{19,11},{12,20... | collective-permute-start | bytes 294920 | tf_op jit(solution)/shard_map/ppermute | solution.py:101
  13.0 4.9 %collective-permute-start.1 = (bf16[320,768]{1,0:T(8,128)(2,1)S(1)}, bf16[320,768]{1,0:T(8,128)(2,1)S(1)}, u32[]{:S(2)}, u32[]{:S(2)}) collective-permute-start(bf16[320,768]{1,0:T(8,128)(2,1)S(1)} %pad_maximum_fusion.1), channel_id=1, source_target_pairs={{0,8},{8,0},{16,24},{24,16},{1,9},{9,1},{17,25},{25,17},{2,10},{10... | collective-permute-start | bytes 1474568 | tf_op jit(solution)/shard_map/ppermute | solution.py:97
  20.1 0.9 %copy-start = (bf16[1,128,768]{2,1,0:T(8,128)(2,1)S(1)}, bf16[1,128,768]{2,1,0:T(8,128)(2,1)}, u32[]{:S(2)}) copy-start(bf16[1,128,768]{2,1,0:T(8,128)(2,1)} %param.5) | copy-start | bytes 589828
  21.0 2.7 %copy-start.1 = (bf16[768,2304]{1,0:T(8,128)(2,1)S(1)}, bf16[768,2304]{1,0:T(8,128)(2,1)}, u32[]{:S(2)}) copy-start(bf16[768,2304]{1,0:T(8,128)(2,1)} %param.6) | copy-start | bytes 10616836
  21.4 10.1 %collective-permute-start.4 = (f16[592,192]{1,0:T(8,128)(2,1)S(1)}, f16[592,192]{1,0:T(8,128)(2,1)S(1)}, u32[]{:S(2)}, u32[]{:S(2)}) collective-permute-start(f16[592,192]{1,0:T(8,128)(2,1)S(1)} %pad_maximum_fusion.5), channel_id=1, source_target_pairs={{0,1},{1,0},{2,3},{3,2},{4,5},{5,4},{6,7},{7,6},{8,9},{9,8},{10,11... | collective-permute-start | bytes 681992 | tf_op jit(solution)/shard_map/ppermute | solution.py:54
  23.2 14.3 %collective-permute-start.3 = (f16[592,192]{1,0:T(8,128)(2,1)S(1)}, f16[592,192]{1,0:T(8,128)(2,1)S(1)}, u32[]{:S(2)}, u32[]{:S(2)}) collective-permute-start(f16[592,192]{1,0:T(8,128)(2,1)S(1)} %pad_maximum_fusion.4), channel_id=1, source_target_pairs={{0,1},{1,0},{2,3},{3,2},{4,5},{5,4},{6,7},{7,6},{8,9},{9,8},{10,11... | collective-permute-start | bytes 681992 | tf_op jit(solution)/shard_map/ppermute | solution.py:54
  38.0 14.3 %collective-permute-start.7 = (f16[304,192]{1,0:T(8,128)(2,1)S(1)}, f16[304,192]{1,0:T(8,128)(2,1)S(1)}, u32[]{:S(2)}, u32[]{:S(2)}) collective-permute-start(f16[304,192]{1,0:T(8,128)(2,1)S(1)} %get-tuple-element.29), channel_id=1, source_target_pairs={{0,4},{1,5},{2,6},{3,7},{4,0},{5,1},{6,2},{7,3},{8,12},{9,13},{10,... | collective-permute-start | bytes 350216 | tf_op jit(solution)/shard_map/ppermute | solution.py:54
  41.7 10.7 %collective-permute-start.6 = (f16[304,192]{1,0:T(8,128)(2,1)S(1)}, f16[304,192]{1,0:T(8,128)(2,1)S(1)}, u32[]{:S(2)}, u32[]{:S(2)}) collective-permute-start(f16[304,192]{1,0:T(8,128)(2,1)S(1)} %get-tuple-element.28), channel_id=1, source_target_pairs={{0,2},{1,3},{2,4},{3,5},{4,6},{5,7},{6,0},{7,1},{8,10},{9,11},{10,... | collective-permute-start | bytes 350216 | tf_op jit(solution)/shard_map/ppermute | solution.py:54
  43.3 10.5 %collective-permute-start.5 = (f16[304,192]{1,0:T(8,128)(2,1)S(1)}, f16[304,192]{1,0:T(8,128)(2,1)S(1)}, u32[]{:S(2)}, u32[]{:S(2)}) collective-permute-start(f16[304,192]{1,0:T(8,128)(2,1)S(1)} %get-tuple-element.27), channel_id=1, source_target_pairs={{0,6},{1,7},{2,0},{3,1},{4,2},{5,3},{6,4},{7,5},{8,14},{9,15},{10,... | collective-permute-start | bytes 350216 | tf_op jit(solution)/shard_map/ppermute | solution.py:54

commit v27 on v26

--- a/solution.py
+++ b/solution.py
@@ -55,7 +55,7 @@
     return decode(with_layout_constraint(arrived, Layout((0, 1))), values.shape)
 
 
-def reduce_over_batch(columns):
+def reduce_over_batch(columns, rider):
     count = lax.axis_size("batch")
     outer = count // 2
     me = lax.axis_index("batch")
@@ -70,6 +70,7 @@
         [send(theirs[:half], pairs, exponent_of(theirs[:half])),
          send(theirs[half:], pairs, exponent_of(theirs[half:]))], axis=0
     )
+    received, rider = lax.optimization_barrier((received, rider))
     summed = with_layout_constraint(mine + received, Layout((0, 1, 2)))
     spread = exponent_of(summed)
     total = lax.dynamic_index_in_dim(summed, z, axis=0, keepdims=False)
@@ -77,7 +78,7 @@
         target = lax.dynamic_index_in_dim(summed, (z + shift) % outer, axis=0, keepdims=False)
         perm = [(2 * q + p, 2 * ((q + shift) % outer) + p) for q in range(outer) for p in range(2)]
         total = total + send(target, perm, spread)
-    return with_layout_constraint(total, Layout((0, 1))).T
+    return with_layout_constraint(total, Layout((0, 1))).T, rider
 
 
 def gather_over_seq(block, cot, width):
@@ -152,7 +153,7 @@
         )
     grad_input = (grad_act * deriv).astype(jnp.bfloat16)[None]
     if batch_count == 8:
-        grad_weight = reduce_over_batch(local_columns)
+        grad_weight, grad_input = reduce_over_batch(local_columns, grad_input)
     else:
         pieces = local_columns.reshape(batch_count, -1, own_rows)
         swapped = lax.all_to_all(pieces, "batch", split_axis=0, concat_axis=0, tiled=True)

time: 55.1 us -> 57.8 us (1.049)
  waiting for transfers between devices: 22.4 us -> 25.7 us
  starting transfers between devices: 19.1 us -> 17.3 us
  local copies, waits for them, and re-layouts: 5.33 us -> 6.47 us
    ppermute x5, waiting for transfers between devices: 21.1 us -> 24.5 us  [send(): arrived = lax.ppermute(encode(values, exponent), 'batch', perm)]
    ppermute x5, starting transfers between devices: 8.65 us -> 6.84 us  [send(): arrived = lax.ppermute(encode(values, exponent), 'batch', perm)]
    unnamed x7, local copies, waits for them, and re-layouts: 1.57 us -> 2.72 us
  transfers between devices with their start and end apart: 9 -> 9, of which waited for: 5 -> 6; matrix products, arithmetic and copies ran while one was open for 16% -> 14% of each run, Pallas kernels for 0% -> 0%
where the time goes in v27:
time: 57.8 us; the launch traced here: 57.5 us
  waiting for transfers between devices  25.7 us (44%)
  starting transfers between devices  17.3 us (30%)
  local copies, waits for them, and re-layouts  6.47 us (11%)
  other arithmetic  4.14 us (7%)
  matrix products  2.96 us (5%)
  between operations  0.93 us (2%)
    ppermute x5, waiting for transfers between devices, send(): arrived = lax.ppermute(encode(values, exponent), 'batch', perm)  24.5 us
    ppermute x5, starting transfers between devices, send(): arrived = lax.ppermute(encode(values, exponent), 'batch', perm)  6.84 us
    ppermute x1, starting transfers between devices, gather_over_seq(): incoming = lax.ppermute(outgoing, 'seq', [(i, i ^ 1) for i in range(count)])  3.39 us
    all_to_all x1, starting transfers between devices, body(): arrived = lax.all_to_all(channels, 'seq', 0, 0, tiled=True)  3.37 us
    ppermute x1, starting transfers between devices, gather_over_seq(): stack = jnp.concatenate([stack, lax.ppermute(stack, 'seq', pairs)], axis=0)  3.03 us
    unnamed x7, local copies, waits for them, and re-layouts  2.72 us
    transpose x1, local copies, waits for them, and re-layouts, body(): channels = cotangent[0].T.reshape(seq_count, -1, length)  1.74 us
    dot_general x3, matrix products, body(): jnp.dot(window, weight[:, tap_index * in_width:(tap_index + 1) * in_width...  1.66 us
  transfers between devices with their start and end apart: 9, of which 6 were waited for; matrix products, arithmetic and copies ran while one was open for 14% of the time, Pallas kernels for 0%

profile of v27, /device:TPU:0, one launch (start us, length us, event | category | flops | bytes accessed | tf_op | source)
XLA Modules:
  0.0 57.5 jit_solution(6278476354485291332)
XLA Ops:
  0.6 1.1 %fusion.28 = bf16[1,128,768]{2,1,0:T(8,128)(2,1)S(1)} fusion(bf16[1,128,768]{2,1,0:T(8,128)(2,1)} %param.4), kind=kLoop, calls=%fused_computation.48 | loop fusion | flops 589824 | bytes 393216 | tf_op jit(solution)/shard_map/convert_element_type | solution.py:118
  1.7 3.0 %collective-permute-start = (bf16[1,128,768]{2,1,0:T(8,128)(2,1)S(1)}, bf16[1,128,768]{2,1,0:T(8,128)(2,1)S(1)}, u32[]{:S(2)}, u32[]{:S(2)}) collective-permute-start(bf16[1,128,768]{2,1,0:T(8,128)(2,1)S(1)} %fusion.28), channel_id=1, source_target_pairs={{0,16},{8,24},{16,0},{24,8},{1,17},{9,25},{17,1},{25,9},{2,18},{10... | collective-permute-start | bytes 589832 | tf_op jit(solution)/shard_map/ppermute | solution.py:95
  4.8 1.7 %copy.13 = bf16[768,128]{1,0:T(8,128)(2,1)} copy(bf16[768,128]{0,1:T(8,128)(2,1)} %bitcast.121) | data formatting | bytes 393216 | tf_op jit(solution)/shard_map/transpose | solution.py:123
  6.5 3.4 %all-to-all-start = ((bf16[4,192,128]{2,1,0:T(8,128)(2,1)}), bf16[4,192,128]{2,1,0:T(8,128)(2,1)S(1)}, u32[]{:S(2)}, u32[]{:S(2)}) async-start(bf16[4,192,128]{2,1,0:T(8,128)(2,1)} %bitcast.10), calls=%async_computation | async-start | bytes 393216 | tf_op jit(solution)/shard_map/all_to_all | solution.py:124
  9.9 1.0 %select_bitcast_fusion = (bf16[64,768]{1,0:T(8,128)(2,1)S(1)}, bf16[64,768]{1,0:T(8,128)(2,1)S(1)}) fusion(pred[]{:T(512)S(6)} %eq.9, bf16[1,128,768]{2,1,0:T(8,128)(2,1)} %param.5), kind=kLoop, calls=%fused_computation.77 | loop fusion | flops 98304 | bytes 393217 | tf_op jit(solution)/shard_map/jit(_where)/select_n | solution.py:102
  10.8 0.7 %collective-permute-start.2 = (bf16[64,768]{1,0:T(8,128)(2,1)S(1)}, bf16[64,768]{1,0:T(8,128)(2,1)S(1)}, u32[]{:S(2)}, u32[]{:S(2)}) collective-permute-start(bf16[64,768]{1,0:T(8,128)(2,1)S(1)} %get-tuple-element.29), channel_id=1, source_target_pairs={{8,16},{16,8},{9,17},{17,9},{10,18},{18,10},{11,19},{19,11},{12,20... | collective-permute-start | bytes 294920 | tf_op jit(solution)/shard_map/ppermute | solution.py:102
  11.5 1.3 %gather_fusion = s32[4]{0:T(128)S(1)} fusion(s32[4]{0:T(128)} %constant.123.clone, s32[1024]{0:T(1024)S(1)} %pad_clamp_fusion.1), kind=kCustom, calls=%fused_computation | custom fusion | bytes 48 | tf_op jit(solution)/shard_map/gather | solution.py:107
  13.0 3.4 %collective-permute-start.1 = (bf16[320,768]{1,0:T(8,128)(2,1)S(1)}, bf16[320,768]{1,0:T(8,128)(2,1)S(1)}, u32[]{:S(2)}, u32[]{:S(2)}) collective-permute-start(bf16[320,768]{1,0:T(8,128)(2,1)S(1)} %pad_maximum_fusion.2), channel_id=1, source_target_pairs={{0,8},{8,0},{16,24},{24,16},{1,9},{9,1},{17,25},{25,17},{2,10},{10... | collective-permute-start | bytes 1474568 | tf_op jit(solution)/shard_map/ppermute | solution.py:98
  16.6 1.2 %collective-permute-done.1 = bf16[320,768]{1,0:T(8,128)(2,1)S(1)} collective-permute-done((bf16[320,768]{1,0:T(8,128)(2,1)S(1)}, bf16[320,768]{1,0:T(8,128)(2,1)S(1)}, u32[]{:S(2)}, u32[]{:S(2)}) %collective-permute-start.1) | collective-permute-done | bytes 491552 | tf_op jit(solution)/shard_map/ppermute | solution.py:98
  18.0 0.6 %gather_fusion.1 = bf16[4,128,768]{2,1,0:T(8,128)(2,1)S(1)} fusion(bf16[4,128,768]{2,1,0:T(8,128)(2,1)S(1)} %pad_maximum_fusion.1, s32[1024]{0:T(1024)S(1)} %pad_clamp_fusion), kind=kCustom, calls=%fused_computation.1 | custom fusion | bytes 1572880 | tf_op jit(solution)/shard_map/jit(_take)/gather | solution.py:108
  18.6 0.2 bitcast_select_fusion
  18.7 0.4 fusion.11
  19.2 0.4 fusion.12
  19.6 0.5 convolution_bitcast_fusion
  20.1 0.2 maximum_multiply_fusion
  20.3 0.7 %copy-done = bf16[1,128,768]{2,1,0:T(8,128)(2,1)S(1)} copy-done((bf16[1,128,768]{2,1,0:T(8,128)(2,1)S(1)}, bf16[1,128,768]{2,1,0:T(8,128)(2,1)}, u32[]{:S(2)}) %copy-start) | copy-done | bytes 196632
  21.0 1.2 %copy-done.1 = bf16[768,2304]{1,0:T(8,128)(2,1)S(1)} copy-done((bf16[768,2304]{1,0:T(8,128)(2,1)S(1)}, bf16[768,2304]{1,0:T(8,128)(2,1)}, u32[]{:S(2)}) %copy-start.1) | copy-done | bytes 3538968
  22.2 0.3 fusion.3
  22.5 0.3 convolution_add_fusion.1
  22.9 0.2 fusion.20
  23.2 1.6 %collective-permute-start.3 = (f16[592,192]{1,0:T(8,128)(2,1)S(1)}, f16[592,192]{1,0:T(8,128)(2,1)S(1)}, u32[]{:S(2)}, u32[]{:S(2)}) collective-permute-start(f16[592,192]{1,0:T(8,128)(2,1)S(1)} %pad_maximum_fusion.5), channel_id=1, source_target_pairs={{0,1},{1,0},{2,3},{3,2},{4,5},{5,4},{6,7},{7,6},{8,9},{9,8},{10,11... | collective-permute-start | bytes 681992 | tf_op jit(solution)/shard_map/ppermute | solution.py:54
  25.0 0.6 %collective-permute-start.4 = (f16[592,192]{1,0:T(8,128)(2,1)S(1)}, f16[592,192]{1,0:T(8,128)(2,1)S(1)}, u32[]{:S(2)}, u32[]{:S(2)}) collective-permute-start(f16[592,192]{1,0:T(8,128)(2,1)S(1)} %pad_maximum_fusion.6), channel_id=1, source_target_pairs={{0,1},{1,0},{2,3},{3,2},{4,5},{5,4},{6,7},{7,6},{8,9},{9,8},{10,11... | collective-permute-start | bytes 681992 | tf_op jit(solution)/shard_map/ppermute | solution.py:54
  25.6 1.0 %fusion.8 = bf16[1,128,768]{2,1,0:T(8,128)(2,1)} fusion(f32[128,768]{1,0:T(8,128)S(1)} %fusion.24, f32[128,768]{1,0:T(8,128)S(1)} %convolution_add_fusion.1, bf16[768,2304]{1,0:T(8,128)(2,1)S(1)} %copy-done.1, bf16[256,768]{1,0:T(8,128)(2,1)S(1)} %pad_maximum_fusion.4), kind=kOutput, calls=%fused_computation.15 | convolution fusion | flops 151289856 | bytes 2359296 | tf_op jit(solution)/shard_map/dot_general | solution.py:149
  26.6 6.7 %collective-permute-done.3 = f16[592,192]{1,0:T(8,128)(2,1)S(1)} collective-permute-done((f16[592,192]{1,0:T(8,128)(2,1)S(1)}, f16[592,192]{1,0:T(8,128)(2,1)S(1)}, u32[]{:S(2)}, u32[]{:S(2)}) %collective-permute-start.3) | collective-permute-done | bytes 227360 | tf_op jit(solution)/shard_map/ppermute | solution.py:54
  33.4 5.9 %collective-permute-done.4 = f16[592,192]{1,0:T(8,128)(2,1)S(1)} collective-permute-done((f16[592,192]{1,0:T(8,128)(2,1)S(1)}, f16[592,192]{1,0:T(8,128)(2,1)S(1)}, u32[]{:S(2)}, u32[]{:S(2)}) %collective-permute-start.4) | collective-permute-done | bytes 227360 | tf_op jit(solution)/shard_map/ppermute | solution.py:54
  39.4 0.3 abs_reduce_fusion
  40.0 3.7 %collective-permute-start.5 = (f16[304,192]{1,0:T(8,128)(2,1)S(1)}, f16[304,192]{1,0:T(8,128)(2,1)S(1)}, u32[]{:S(2)}, u32[]{:S(2)}) collective-permute-start(f16[304,192]{1,0:T(8,128)(2,1)S(1)} %get-tuple-element.31), channel_id=1, source_target_pairs={{0,6},{1,7},{2,0},{3,1},{4,2},{5,3},{6,4},{7,5},{8,14},{9,15},{10,... | collective-permute-start | bytes 350216 | tf_op jit(solution)/shard_map/ppermute | solution.py:54
  43.6 1.0 %collective-permute-start.7 = (f16[304,192]{1,0:T(8,128)(2,1)S(1)}, f16[304,192]{1,0:T(8,128)(2,1)S(1)}, u32[]{:S(2)}, u32[]{:S(2)}) collective-permute-start(f16[304,192]{1,0:T(8,128)(2,1)S(1)} %get-tuple-element.33), channel_id=1, source_target_pairs={{0,4},{1,5},{2,6},{3,7},{4,0},{5,1},{6,2},{7,3},{8,12},{9,13},{10,... | collective-permute-start | bytes 350216 | tf_op jit(solution)/shard_map/ppermute | solution.py:54
  44.6 3.5 %collective-permute-done.5 = f16[304,192]{1,0:T(8,128)(2,1)S(1)} collective-permute-done((f16[304,192]{1,0:T(8,128)(2,1)S(1)}, f16[304,192]{1,0:T(8,128)(2,1)S(1)}, u32[]{:S(2)}, u32[]{:S(2)}) %collective-permute-start.5) | collective-permute-done | bytes 116768 | tf_op jit(solution)/shard_map/ppermute | solution.py:54
  48.1 4.3 %collective-permute-done.6 = f16[304,192]{1,0:T(8,128)(2,1)S(1)} collective-permute-done((f16[304,192]{1,0:T(8,128)(2,1)S(1)}, f16[304,192]{1,0:T(8,128)(2,1)S(1)}, u32[]{:S(2)}, u32[]{:S(2)}) %collective-permute-start.6) | collective-permute-done | bytes 116768 | tf_op jit(solution)/shard_map/ppermute | solution.py:54
  52.4 4.1 %collective-permute-done.7 = f16[304,192]{1,0:T(8,128)(2,1)S(1)} collective-permute-done((f16[304,192]{1,0:T(8,128)(2,1)S(1)}, f16[304,192]{1,0:T(8,128)(2,1)S(1)}, u32[]{:S(2)}, u32[]{:S(2)}) %collective-permute-start.7) | collective-permute-done | bytes 116768 | tf_op jit(solution)/shard_map/ppermute | solution.py:54
  56.7 0.9 %copy.20 = f32[192,288]{1,0:T(8,128)} copy(f32[192,288]{0,1:T(8,128)S(1)} %fusion.37) | data formatting | bytes 442368
  (42 shorter events, 1.4 us)
Async XLA Ops:
  0.6 15.8 %copy-start.2 = (bf16[1,128,768]{2,1,0:T(8,128)(2,1)S(1)}, bf16[1,128,768]{2,1,0:T(8,128)(2,1)}, u32[]{:S(2)}) copy-start(bf16[1,128,768]{2,1,0:T(8,128)(2,1)} %param.4) | copy-start | bytes 589828
  1.7 11.1 %collective-permute-start = (bf16[1,128,768]{2,1,0:T(8,128)(2,1)S(1)}, bf16[1,128,768]{2,1,0:T(8,128)(2,1)S(1)}, u32[]{:S(2)}, u32[]{:S(2)}) collective-permute-start(bf16[1,128,768]{2,1,0:T(8,128)(2,1)S(1)} %fusion.28), channel_id=1, source_target_pairs={{0,16},{8,24},{16,0},{24,8},{1,17},{9,25},{17,1},{25,9},{2,18},{10... | collective-permute-start | bytes 589832 | tf_op jit(solution)/shard_map/ppermute | solution.py:95
  6.5 12.2 %all-to-all-start = ((bf16[4,192,128]{2,1,0:T(8,128)(2,1)}), bf16[4,192,128]{2,1,0:T(8,128)(2,1)S(1)}, u32[]{:S(2)}, u32[]{:S(2)}) async-start(bf16[4,192,128]{2,1,0:T(8,128)(2,1)} %bitcast.10), calls=%async_computation | async-start | bytes 393216 | tf_op jit(solution)/shard_map/all_to_all | solution.py:124
  10.8 9.4 %collective-permute-start.2 = (bf16[64,768]{1,0:T(8,128)(2,1)S(1)}, bf16[64,768]{1,0:T(8,128)(2,1)S(1)}, u32[]{:S(2)}, u32[]{:S(2)}) collective-permute-start(bf16[64,768]{1,0:T(8,128)(2,1)S(1)} %get-tuple-element.29), channel_id=1, source_target_pairs={{8,16},{16,8},{9,17},{17,9},{10,18},{18,10},{11,19},{19,11},{12,20... | collective-permute-start | bytes 294920 | tf_op jit(solution)/shard_map/ppermute | solution.py:102
  13.0 4.9 %collective-permute-start.1 = (bf16[320,768]{1,0:T(8,128)(2,1)S(1)}, bf16[320,768]{1,0:T(8,128)(2,1)S(1)}, u32[]{:S(2)}, u32[]{:S(2)}) collective-permute-start(bf16[320,768]{1,0:T(8,128)(2,1)S(1)} %pad_maximum_fusion.2), channel_id=1, source_target_pairs={{0,8},{8,0},{16,24},{24,16},{1,9},{9,1},{17,25},{25,17},{2,10},{10... | collective-permute-start | bytes 1474568 | tf_op jit(solution)/shard_map/ppermute | solution.py:98
  20.1 0.9 %copy-start = (bf16[1,128,768]{2,1,0:T(8,128)(2,1)S(1)}, bf16[1,128,768]{2,1,0:T(8,128)(2,1)}, u32[]{:S(2)}) copy-start(bf16[1,128,768]{2,1,0:T(8,128)(2,1)} %param.5) | copy-start | bytes 589828
  20.1 2.1 %copy-start.1 = (bf16[768,2304]{1,0:T(8,128)(2,1)S(1)}, bf16[768,2304]{1,0:T(8,128)(2,1)}, u32[]{:S(2)}) copy-start(bf16[768,2304]{1,0:T(8,128)(2,1)} %param.6) | copy-start | bytes 10616836
  23.2 10.1 %collective-permute-start.3 = (f16[592,192]{1,0:T(8,128)(2,1)S(1)}, f16[592,192]{1,0:T(8,128)(2,1)S(1)}, u32[]{:S(2)}, u32[]{:S(2)}) collective-permute-start(f16[592,192]{1,0:T(8,128)(2,1)S(1)} %pad_maximum_fusion.5), channel_id=1, source_target_pairs={{0,1},{1,0},{2,3},{3,2},{4,5},{5,4},{6,7},{7,6},{8,9},{9,8},{10,11... | collective-permute-start | bytes 681992 | tf_op jit(solution)/shard_map/ppermute | solution.py:54
  25.0 14.3 %collective-permute-start.4 = (f16[592,192]{1,0:T(8,128)(2,1)S(1)}, f16[592,192]{1,0:T(8,128)(2,1)S(1)}, u32[]{:S(2)}, u32[]{:S(2)}) collective-permute-start(f16[592,192]{1,0:T(8,128)(2,1)S(1)} %pad_maximum_fusion.6), channel_id=1, source_target_pairs={{0,1},{1,0},{2,3},{3,2},{4,5},{5,4},{6,7},{7,6},{8,9},{9,8},{10,11... | collective-permute-start | bytes 681992 | tf_op jit(solution)/shard_map/ppermute | solution.py:54
  40.0 8.1 %collective-permute-start.5 = (f16[304,192]{1,0:T(8,128)(2,1)S(1)}, f16[304,192]{1,0:T(8,128)(2,1)S(1)}, u32[]{:S(2)}, u32[]{:S(2)}) collective-permute-start(f16[304,192]{1,0:T(8,128)(2,1)S(1)} %get-tuple-element.31), channel_id=1, source_target_pairs={{0,6},{1,7},{2,0},{3,1},{4,2},{5,3},{6,4},{7,5},{8,14},{9,15},{10,... | collective-permute-start | bytes 350216 | tf_op jit(solution)/shard_map/ppermute | solution.py:54
  43.6 8.8 %collective-permute-start.6 = (f16[304,192]{1,0:T(8,128)(2,1)S(1)}, f16[304,192]{1,0:T(8,128)(2,1)S(1)}, u32[]{:S(2)}, u32[]{:S(2)}) collective-permute-start(f16[304,192]{1,0:T(8,128)(2,1)S(1)} %get-tuple-element.32), channel_id=1, source_target_pairs={{0,2},{1,3},{2,4},{3,5},{4,6},{5,7},{6,0},{7,1},{8,10},{9,11},{10,... | collective-permute-start | bytes 350216 | tf_op jit(solution)/shard_map/ppermute | solution.py:54
  43.6 12.9 %collective-permute-start.7 = (f16[304,192]{1,0:T(8,128)(2,1)S(1)}, f16[304,192]{1,0:T(8,128)(2,1)S(1)}, u32[]{:S(2)}, u32[]{:S(2)}) collective-permute-start(f16[304,192]{1,0:T(8,128)(2,1)S(1)} %get-tuple-element.33), channel_id=1, source_target_pairs={{0,4},{1,5},{2,6},{3,7},{4,0},{5,1},{6,2},{7,3},{8,12},{9,13},{10,... | collective-permute-start | bytes 350216 | tf_op jit(solution)/shard_map/ppermute | solution.py:54
